TPU v7x, 32 devices: a whole 2x2x4 slice. The times are simulated.
32 devices in a mesh: species: 4 (over z), space: 8 (over y, x, core).
Axes of the slice: x: 2, y: 2, z: 4, core: 2. Of those that a mesh axis runs over, the one named last changes fastest.
Arguments:
- density: float32 [4, 32, 16, 32, 128], P('species', None, 'space'), may hold values from 0 to 2
- space_factor: float32 [16, 32, 128], P('space'), may hold values from 0.5 to 1
- diff_rate: float32 [4, 32], P('species'), may hold values from 0.02 to 0.08
- loss_inverse: float32 [4, 32, 32], P('species'), may hold values from 0 to 1, as said below
- chain_yield: float32 [4, 32], P('species'), may hold values from 0.25 to 0.95
- survival: float32 [4, 32], P('species'), may hold values from 0.6 to 1
- gamma_yield: float32 [4, 32], P('species'), may hold values from 0.1 to 1
- sky_weight: bfloat16 [8, 8, 64, 128], P('space'), may hold values from -0.75 to 0.75
- sky_blocks: int32 [8, 8], P('space'), may hold values from 0 to 383
Outputs:
- propagated: float32 [4, 32, 16, 32, 128], P('species', None, 'space')
- sky: float32 [384, 128], P('space')
Inputs may be any that keep to these rules, and one draw needn't show every extreme that they name: `loss_inverse`: each matrix is upper triangular with a diagonal of 0.5 to 1 and nonnegative entries.
All inputs are finite; a program needn't handle non-finite values.
Results may differ from a plain program's by a relative error of at most 0.0011.
Values sent between devices are 32-bit elements; how exact they have to be, the bound alone decides.
No kernel may reach another device: no remote copies, remote signals or barrier semaphores. Data moves between devices by JAX's collectives and lax.ppermute only.
A program may use at most 64 MiB of HBM per device.

v0:
```python
import jax
import jax.numpy as jnp
from jax import lax
from jax.sharding import PartitionSpec as P

SUBSTEPS = 2
NB = 384


def padded_2(cells, sides, width):
    for axis, dim in sides:
        count = lax.axis_size(axis)
        ends = count - 1
        head = lax.slice_in_dim(cells, 0, width, axis=dim)
        tail = lax.slice_in_dim(cells, cells.shape[dim] - width, cells.shape[dim], axis=dim)
        cells = jnp.concatenate(
            [
                lax.ppermute(tail, axis, [(i, (i + 1) % count) for i in range(ends)]),
                cells,
                lax.ppermute(head, axis, [((i + 1) % count, i) for i in range(ends)]),
            ],
            axis=dim,
        )
    return cells


def from_behind(block, axis, distance):
    devices = range(lax.axis_size(axis))
    route = [(i - distance, i) for i in devices if i - distance in devices]
    return lax.ppermute(block, axis, route)


def cross_sum(field):
    padded = jnp.pad(field, ((0, 0), (0, 0), (1, 1), (1, 1)))
    beside = padded[:, :, 2:, 1:-1] + padded[:, :, :-2, 1:-1]
    beside = beside + padded[:, :, 1:-1, 2:] + padded[:, :, 1:-1, :-2]
    return beside


def body(
    density,
    space_factor,
    diff_rate,
    loss_inverse,
    chain_yield,
    survival,
    gamma_yield,
    sky_weight,
    sky_blocks,
):
    field = density[0]
    bins = field.shape[0]
    width = field.shape[1]
    rate = diff_rate[0][:, None, None, None]
    factor = rate * space_factor[None]
    for step in range(SUBSTEPS):
        wider = padded_2(field, (("space", 1),), 1)
        beside = wider[:, 2:] + wider[:, :-2] + cross_sum(field)
        field = field + factor * (beside - 6.0 * field)
    solved = jnp.dot(
        loss_inverse[0],
        field.reshape(bins, -1),
        precision=lax.Precision.HIGHEST,
        preferred_element_type=jnp.float32,
    ).reshape(field.shape)
    factor_chain = chain_yield[0][:, None, None, None]
    own_part = survival[0][:, None, None, None] * solved
    carried = own_part
    for section in range(lax.axis_size("species") - 1):
        carried = factor_chain * from_behind(carried, "species", 1) + own_part
    weighted = jnp.dot(
        gamma_yield[0],
        carried.reshape(bins, -1),
        precision=lax.Precision.HIGHEST,
        preferred_element_type=jnp.float32,
    )
    depth = carried.shape[3]
    emission = (
        jnp.sum(weighted.reshape(width, carried.shape[2], depth), axis=2) / (bins * depth)
    ).astype(jnp.bfloat16)
    columns = emission.reshape(-1)
    contribution = jnp.einsum(
        "c,lcb->lb", columns, sky_weight[0], preferred_element_type=jnp.float32
    )
    onehot = (sky_blocks[0][:, None] == jnp.arange(NB, dtype=jnp.int32)[None, :]).astype(
        jnp.float32
    )
    dense_map = jnp.dot(
        onehot.T, contribution, precision=lax.Precision.HIGHEST, preferred_element_type=jnp.float32
    )
    summed = lax.psum(dense_map, "species")
    sky = lax.psum_scatter(summed, "space", scatter_dimension=0, tiled=True)
    return (carried[None], sky)


def solution(mesh):
    placed = (
        P("species", None, "space", None, None),
        P("space", None, None),
        P("species", None),
        P("species", None, None),
        P("species", None),
        P("species", None),
        P("species", None),
        P("space", None, None, None),
        P("space", None),
    )
    return jax.shard_map(
        body,
        mesh=mesh,
        in_specs=placed,
        out_specs=(P("species", None, "space", None, None), P("space", None)),
        check_vma=False,
    )
```

profile of v0, /device:TPU:0, one launch (start us, length us, event | category | flops | bytes accessed | tf_op | source)
XLA Modules:
  0.0 190.8 jit_solution(6497044509966995586)
XLA Ops:
  7.3 1.4 fusion.25
  8.6 1.3 collective-permute-start
  9.9 3.1 %collective-permute-start.1 = (f32[32,1,32,128]{3,2,1,0:T(8,128)S(1)}, f32[32,1,32,128]{3,2,1,0:T(8,128)S(1)}, u32[]{:S(2)}, u32[]{:S(2)}) collective-permute-start(f32[32,1,32,128]{3,2,1,0:T(8,128)S(1)} %get-tuple-element.5), channel_id=1, source_target_pairs={{0,1},{1,2},{2,3},{3,4},{4,5},{5,6},{6,7},{8,9},{9,10},{10,11},{11... | collective-permute-start | bytes 1572872 | tf_op jit(solution)/shard_map/ppermute | solution.py:18
  13.0 1.5 collective-permute-done.1
  14.5 0.8 fusion
  15.4 1.3 collective-permute-start.2
  16.7 10.4 %collective-permute-start.3 = (f32[32,1,32,128]{3,2,1,0:T(8,128)S(1)}, f32[32,1,32,128]{3,2,1,0:T(8,128)S(1)}, u32[]{:S(2)}, u32[]{:S(2)}) collective-permute-start(f32[32,1,32,128]{3,2,1,0:T(8,128)S(1)} %get-tuple-element.3), channel_id=1, source_target_pairs={{0,1},{1,2},{2,3},{3,4},{4,5},{5,6},{6,7},{8,9},{9,10},{10,11},{11... | collective-permute-start | bytes 1572872 | tf_op jit(solution)/shard_map/ppermute | solution.py:18
  27.1 1.5 collective-permute-done.3
  28.6 0.8 fusion.1
  29.4 1.7 convolution_bitcast_fusion
  31.1 0.2 copy.16
  31.3 0.5 copy-done.5
  31.7 0.1 broadcast_multiply_fusion
  31.9 3.5 %collective-permute-start.4 = (f32[32,2,32,128]{3,2,1,0:T(8,128)S(1)}, f32[32,2,32,128]{3,2,1,0:T(8,128)S(1)}, u32[]{:S(2)}, u32[]{:S(2)}) collective-permute-start(f32[32,2,32,128]{3,2,1,0:T(8,128)S(1)} %broadcast_multiply_fusion), channel_id=1, source_target_pairs={{0,8},{8,16},{16,24},{1,9},{9,17},{17,25},{2,10},{10,18},{18,26},{... | collective-permute-start | bytes 3145736 | tf_op jit(solution)/shard_map/ppermute | solution.py:30
  35.4 18.0 %collective-permute-done.4 = f32[32,2,32,128]{3,2,1,0:T(8,128)S(1)} collective-permute-done((f32[32,2,32,128]{3,2,1,0:T(8,128)S(1)}, f32[32,2,32,128]{3,2,1,0:T(8,128)S(1)}, u32[]{:S(2)}, u32[]{:S(2)}) %collective-permute-start.4) | collective-permute-done | bytes 1048608 | tf_op jit(solution)/shard_map/ppermute | solution.py:30
  53.4 0.2 multiply_add_fusion.2
  53.6 4.5 %collective-permute-start.5 = (f32[32,2,32,128]{3,2,1,0:T(8,128)S(1)}, f32[32,2,32,128]{3,2,1,0:T(8,128)S(1)}, u32[]{:S(2)}, u32[]{:S(2)}) collective-permute-start(f32[32,2,32,128]{3,2,1,0:T(8,128)S(1)} %multiply_add_fusion.2), channel_id=1, source_target_pairs={{0,8},{8,16},{16,24},{1,9},{9,17},{17,25},{2,10},{10,18},{18,26},{... | collective-permute-start | bytes 3145736 | tf_op jit(solution)/shard_map/ppermute | solution.py:30
  58.1 19.1 %collective-permute-done.5 = f32[32,2,32,128]{3,2,1,0:T(8,128)S(1)} collective-permute-done((f32[32,2,32,128]{3,2,1,0:T(8,128)S(1)}, f32[32,2,32,128]{3,2,1,0:T(8,128)S(1)}, u32[]{:S(2)}, u32[]{:S(2)}) %collective-permute-start.5) | collective-permute-done | bytes 1048608 | tf_op jit(solution)/shard_map/ppermute | solution.py:30
  77.1 0.2 multiply_add_fusion.1
  77.3 4.5 %collective-permute-start.6 = (f32[32,2,32,128]{3,2,1,0:T(8,128)S(1)}, f32[32,2,32,128]{3,2,1,0:T(8,128)S(1)}, u32[]{:S(2)}, u32[]{:S(2)}) collective-permute-start(f32[32,2,32,128]{3,2,1,0:T(8,128)S(1)} %multiply_add_fusion.1), channel_id=1, source_target_pairs={{0,8},{8,16},{16,24},{1,9},{9,17},{17,25},{2,10},{10,18},{18,26},{... | collective-permute-start | bytes 3145736 | tf_op jit(solution)/shard_map/ppermute | solution.py:30
  81.8 20.1 %collective-permute-done.6 = f32[32,2,32,128]{3,2,1,0:T(8,128)S(1)} collective-permute-done((f32[32,2,32,128]{3,2,1,0:T(8,128)S(1)}, f32[32,2,32,128]{3,2,1,0:T(8,128)S(1)}, u32[]{:S(2)}, u32[]{:S(2)}) %collective-permute-start.6) | collective-permute-done | bytes 1048608 | tf_op jit(solution)/shard_map/ppermute | solution.py:30
  101.9 0.2 multiply_add_fusion
  102.1 0.6 copy.26
  102.7 0.3 copy-done.2
  103.1 0.2 copy.18
  103.3 0.5 copy-done.8
  103.7 1.2 fusion.16
  105.0 0.1 reduce_sum.9
  105.2 0.1 fusion.18
  105.3 1.1 fusion.21
  106.4 57.4 %reduce-scatter.2.cloned.1.call-done = f32[48,128]{1,0:T(8,128)} async-done(((f32[384,128]{1,0:T(8,128)}), f32[48,128]{1,0:T(8,128)}) %reduce-scatter.2.cloned.1.call-update) | async-done | bytes 24592 | tf_op jit(solution)/shard_map/reduce_scatter | solution.py:92
  163.8 20.2 %psum.8 = f32[48,128]{1,0:T(8,128)} all-reduce(f32[48,128]{1,0:T(8,128)} %reduce-scatter.2.cloned.1.call-done), channel_id=1, replica_groups=mesh['species'=4,'space'=8] {'species'}, use_global_device_ids=true, to_apply=%region_1.2 | all-reduce | flops 6144 | bytes 49152 | tf_op jit(solution)/shard_map/psum | solution.py:91
  (24 shorter events, 0.3 us)
Async XLA Ops:
  7.2 98.0 %copy-start = (bf16[1,8,64,128]{3,2,1,0:T(8,128)(2,1)S(1)}, bf16[1,8,64,128]{3,2,1,0:T(8,128)(2,1)}, u32[]{:S(2)}) copy-start(bf16[1,8,64,128]{3,2,1,0:T(8,128)(2,1)} %param.16) | copy-start | bytes 393220
  7.2 156.6 %reduce-scatter.2.cloned.1.call-start = ((), (), s32[]{:S(2)}) async-start(), calls=%async_computation.1 | async-start | bytes 221184 | tf_op jit(solution)/shard_map/reduce_scatter | solution.py:92
  7.2 7.3 %copy-start.1 = (f32[1,32,2,32,128]{4,3,2,1,0:T(8,128)S(1)}, f32[1,32,2,32,128]{4,3,2,1,0:T(8,128)}, u32[]{:S(2)}) copy-start(f32[1,32,2,32,128]{4,3,2,1,0:T(8,128)} %param.9) | copy-start | bytes 3145732
  7.2 7.3 %copy-start.3 = (f32[2,32,128]{2,1,0:T(8,128)S(1)}, f32[2,32,128]{2,1,0:T(8,128)}, u32[]{:S(2)}) copy-start(f32[2,32,128]{2,1,0:T(8,128)} %param.10) | copy-start | bytes 98308
  7.2 7.2 %copy-start.7 = (f32[1,32]{1,0:T(1,128)S(1)}, f32[1,32]{1,0:T(1,128)}, u32[]{:S(2)}) copy-start(f32[1,32]{1,0:T(1,128)} %param.11) | copy-start | bytes 388
  8.6 4.4 %collective-permute-start = (f32[32,1,32,128]{3,2,1,0:T(8,128)S(1)}, f32[32,1,32,128]{3,2,1,0:T(8,128)S(1)}, u32[]{:S(2)}, u32[]{:S(2)}) collective-permute-start(f32[32,1,32,128]{3,2,1,0:T(8,128)S(1)} %get-tuple-element.4), channel_id=1, source_target_pairs={{1,0},{2,1},{3,2},{4,3},{5,4},{6,5},{7,6},{9,8},{10,9},{11,10},{12... | collective-permute-start | bytes 1572872 | tf_op jit(solution)/shard_map/ppermute | solution.py:20
  9.9 4.6 %collective-permute-start.1 = (f32[32,1,32,128]{3,2,1,0:T(8,128)S(1)}, f32[32,1,32,128]{3,2,1,0:T(8,128)S(1)}, u32[]{:S(2)}, u32[]{:S(2)}) collective-permute-start(f32[32,1,32,128]{3,2,1,0:T(8,128)S(1)} %get-tuple-element.5), channel_id=1, source_target_pairs={{0,1},{1,2},{2,3},{3,4},{4,5},{5,6},{6,7},{8,9},{9,10},{10,11},{11... | collective-permute-start | bytes 1572872 | tf_op jit(solution)/shard_map/ppermute | solution.py:18
  15.4 11.7 %collective-permute-start.2 = (f32[32,1,32,128]{3,2,1,0:T(8,128)S(1)}, f32[32,1,32,128]{3,2,1,0:T(8,128)S(1)}, u32[]{:S(2)}, u32[]{:S(2)}) collective-permute-start(f32[32,1,32,128]{3,2,1,0:T(8,128)S(1)} %get-tuple-element.2), channel_id=1, source_target_pairs={{1,0},{2,1},{3,2},{4,3},{5,4},{6,5},{7,6},{9,8},{10,9},{11,10},{12... | collective-permute-start | bytes 1572872 | tf_op jit(solution)/shard_map/ppermute | solution.py:20
  16.7 12.7 %copy-start.4 = (f32[1,32,32]{2,1,0:T(8,128)S(1)}, f32[1,32,32]{2,1,0:T(8,128)}, u32[]{:S(2)}) copy-start(f32[1,32,32]{2,1,0:T(8,128)} %param.12) | copy-start | bytes 12292
  16.7 11.9 %collective-permute-start.3 = (f32[32,1,32,128]{3,2,1,0:T(8,128)S(1)}, f32[32,1,32,128]{3,2,1,0:T(8,128)S(1)}, u32[]{:S(2)}, u32[]{:S(2)}) collective-permute-start(f32[32,1,32,128]{3,2,1,0:T(8,128)S(1)} %get-tuple-element.3), channel_id=1, source_target_pairs={{0,1},{1,2},{2,3},{3,4},{4,5},{5,6},{6,7},{8,9},{9,10},{10,11},{11... | collective-permute-start | bytes 1572872 | tf_op jit(solution)/shard_map/ppermute | solution.py:18
  31.1 0.7 copy-start.5
  31.7 21.7 %copy-start.6 = (f32[1,32]{1,0:T(1,128)S(1)}, f32[1,32]{1,0:T(1,128)}, u32[]{:S(2)}) copy-start(f32[1,32]{1,0:T(1,128)} %param.13) | copy-start | bytes 388
  31.9 21.5 %collective-permute-start.4 = (f32[32,2,32,128]{3,2,1,0:T(8,128)S(1)}, f32[32,2,32,128]{3,2,1,0:T(8,128)S(1)}, u32[]{:S(2)}, u32[]{:S(2)}) collective-permute-start(f32[32,2,32,128]{3,2,1,0:T(8,128)S(1)} %broadcast_multiply_fusion), channel_id=1, source_target_pairs={{0,8},{8,16},{16,24},{1,9},{9,17},{17,25},{2,10},{10,18},{18,26},{... | collective-permute-start | bytes 3145736 | tf_op jit(solution)/shard_map/ppermute | solution.py:30
  53.6 23.5 %collective-permute-start.5 = (f32[32,2,32,128]{3,2,1,0:T(8,128)S(1)}, f32[32,2,32,128]{3,2,1,0:T(8,128)S(1)}, u32[]{:S(2)}, u32[]{:S(2)}) collective-permute-start(f32[32,2,32,128]{3,2,1,0:T(8,128)S(1)} %multiply_add_fusion.2), channel_id=1, source_target_pairs={{0,8},{8,16},{16,24},{1,9},{9,17},{17,25},{2,10},{10,18},{18,26},{... | collective-permute-start | bytes 3145736 | tf_op jit(solution)/shard_map/ppermute | solution.py:30
  77.3 24.6 %collective-permute-start.6 = (f32[32,2,32,128]{3,2,1,0:T(8,128)S(1)}, f32[32,2,32,128]{3,2,1,0:T(8,128)S(1)}, u32[]{:S(2)}, u32[]{:S(2)}) collective-permute-start(f32[32,2,32,128]{3,2,1,0:T(8,128)S(1)} %multiply_add_fusion.1), channel_id=1, source_target_pairs={{0,8},{8,16},{16,24},{1,9},{9,17},{17,25},{2,10},{10,18},{18,26},{... | collective-permute-start | bytes 3145736 | tf_op jit(solution)/shard_map/ppermute | solution.py:30
  102.1 1.0 copy-start.2
  103.1 0.7 copy-start.8
  103.3 2.0 %copy-start.9 = (s32[1,8]{1,0:T(1,128)S(1)}, s32[1,8]{1,0:T(1,128)}, u32[]{:S(2)}) copy-start(s32[1,8]{1,0:T(1,128)} %param.17) | copy-start | bytes 100
Sparse Core Ops, SparseCore 0:
  106.6 57.1 reduce-scatter.1
where the time goes:
time: 191 us
  waiting for transfers between devices  118 us (62%)
  starting transfers between devices  28.5 us (15%)
  blocking collectives  20.2 us (11%)
  between operations  14.3 us (7%)
  matrix products  4.16 us (2%)
  local copies, waits for them, and re-layouts  3.81 us (2%)
  other arithmetic  2.35 us (1%)
    reduce_scatter x1, waiting for transfers between devices, body(): sky = lax.psum_scatter(summed, 'space', scatter_dimension=0, tiled=True)  57.4 us
    ppermute x3, waiting for transfers between devices, from_behind(): return lax.ppermute(block, axis, route)  57.2 us
    psum x1, blocking collectives, body(): summed = lax.psum(dense_map, 'species')  20.2 us
    ppermute x2, starting transfers between devices, padded_2(): lax.ppermute(tail, axis, [(i, (i + 1) % count) for i in range(ends)])  13.5 us
    ppermute x3, starting transfers between devices, from_behind(): return lax.ppermute(block, axis, route)  12.5 us
  transfers between devices with their start and end apart: 8, of which 6 were waited for; matrix products, arithmetic and copies ran while one was open for 0% of the time, Pallas kernels for 0%

commit v1 on v0

--- a/solution.py
+++ b/solution.py
@@ -5,6 +5,7 @@
 
 SUBSTEPS = 2
 NB = 384
+HIGH = lax.Precision.HIGHEST
 
 
 def padded_2(cells, sides, width):
@@ -37,6 +38,16 @@
     return beside
 
 
+def emission_weights(chain_all, gamma_all, me):
+    groups = chain_all.shape[0]
+    g = jnp.arange(groups)[:, None]
+    k = jnp.arange(groups)[None, :]
+    live = (k > me) & (k <= g)
+    factors = jnp.where(live[:, :, None], chain_all[None, :, :], 1.0)
+    spread = jnp.prod(factors, axis=1)
+    return jnp.where(g >= me, gamma_all * spread, 0.0)
+
+
 def body(
     density,
     space_factor,
@@ -48,9 +59,16 @@
     sky_weight,
     sky_blocks,
 ):
+    tiles = lax.axis_size("space")
+    rows = NB // tiles
+    params = jnp.stack([chain_yield[0], gamma_yield[0]])
+    params_all = lax.all_gather(params, "species")
+    blocks_all = lax.all_gather(sky_blocks[0].astype(jnp.float32), "space")
+
     field = density[0]
     bins = field.shape[0]
     width = field.shape[1]
+    depth = field.shape[3]
     rate = diff_rate[0][:, None, None, None]
     factor = rate * space_factor[None]
     for step in range(SUBSTEPS):
@@ -60,36 +78,38 @@
     solved = jnp.dot(
         loss_inverse[0],
         field.reshape(bins, -1),
-        precision=lax.Precision.HIGHEST,
+        precision=HIGH,
         preferred_element_type=jnp.float32,
     ).reshape(field.shape)
     factor_chain = chain_yield[0][:, None, None, None]
     own_part = survival[0][:, None, None, None] * solved
+
+    me = lax.axis_index("species")
+    weights = emission_weights(params_all[:, 0], params_all[:, 1], me)
+    own_columns = jnp.sum(own_part, axis=3).reshape(bins, -1)
+    partial = jnp.dot(weights, own_columns, precision=HIGH, preferred_element_type=jnp.float32)
+    sums = lax.psum(partial, "species")
+    emission = (sums / (bins * depth)).astype(jnp.bfloat16).astype(jnp.float32)
+    columns = jnp.sum(emission, axis=0)
+    contribution = jnp.einsum(
+        "c,lcb->lb", columns, sky_weight[0].astype(jnp.float32), precision=HIGH
+    )
+    gathered = lax.all_gather(contribution, "space")
+    lines = gathered.shape[1]
+    mine = lax.axis_index("space") * rows + jnp.arange(rows, dtype=jnp.int32)
+    onehot = (
+        blocks_all.reshape(1, tiles * lines) == mine.astype(jnp.float32)[:, None]
+    ).astype(jnp.float32)
+    sky = jnp.dot(
+        onehot,
+        gathered.reshape(tiles * lines, -1),
+        precision=HIGH,
+        preferred_element_type=jnp.float32,
+    )
+
     carried = own_part
     for section in range(lax.axis_size("species") - 1):
         carried = factor_chain * from_behind(carried, "species", 1) + own_part
-    weighted = jnp.dot(
-        gamma_yield[0],
-        carried.reshape(bins, -1),
-        precision=lax.Precision.HIGHEST,
-        preferred_element_type=jnp.float32,
-    )
-    depth = carried.shape[3]
-    emission = (
-        jnp.sum(weighted.reshape(width, carried.shape[2], depth), axis=2) / (bins * depth)
-    ).astype(jnp.bfloat16)
-    columns = emission.reshape(-1)
-    contribution = jnp.einsum(
-        "c,lcb->lb", columns, sky_weight[0], preferred_element_type=jnp.float32
-    )
-    onehot = (sky_blocks[0][:, None] == jnp.arange(NB, dtype=jnp.int32)[None, :]).astype(
-        jnp.float32
-    )
-    dense_map = jnp.dot(
-        onehot.T, contribution, precision=lax.Precision.HIGHEST, preferred_element_type=jnp.float32
-    )
-    summed = lax.psum(dense_map, "species")
-    sky = lax.psum_scatter(summed, "space", scatter_dimension=0, tiled=True)
     return (carried[None], sky)
 
 

time: 191 us -> 140 us (0.73)
  waiting for transfers between devices: 118 us -> 20.9 us
  blocking collectives: 20.2 us -> 79.9 us
  between operations: 14.3 us -> 0.86 us
  other arithmetic: 2.35 us -> 5.66 us
  starting transfers between devices: 28.5 us -> 26.3 us
    all_gather x0 -> x3, blocking collectives: none -> 71 us  [the longest x1 29.6 us: body(): blocks_all = lax.all_gather(sky_blocks[0].astype(jnp.float32), 'space')]
    reduce_scatter x1 -> x0, waiting for transfers between devices: 57.4 us -> none  [body(): sky = lax.psum_scatter(summed, 'space', scatter_dimension=0, tiled=True)]
    ppermute x3, waiting for transfers between devices: 57.2 us -> 18 us  [from_behind(): return lax.ppermute(block, axis, route)]
    psum x1, blocking collectives: 20.2 us -> 8.89 us  [body(): sums = lax.psum(partial, 'species')]
    ppermute x3, starting transfers between devices: 12.5 us -> 10.3 us  [from_behind(): return lax.ppermute(block, axis, route)]
  transfers between devices with their start and end apart: 8 -> 7, of which waited for: 6 -> 3; matrix products, arithmetic and copies ran while one was open for 0% -> 2% of each run, Pallas kernels for 0% -> 0%
where the time goes in v1:
time: 140 us; the launch traced here: 139 us
  blocking collectives  79.9 us (57%)
  starting transfers between devices  26.3 us (19%)
  waiting for transfers between devices  20.9 us (15%)
  other arithmetic  5.66 us (4%)
  matrix products  2.84 us (2%)
  local copies, waits for them, and re-layouts  2.81 us (2%)
    all_gather x1, blocking collectives, body(): blocks_all = lax.all_gather(sky_blocks[0].astype(jnp.float32), 'space')  29.6 us
    all_gather x1, blocking collectives, body(): params_all = lax.all_gather(params, 'species')  24.3 us
    ppermute x3, waiting for transfers between devices, from_behind(): return lax.ppermute(block, axis, route)  18 us
    all_gather x1, blocking collectives, body(): gathered = lax.all_gather(contribution, 'space')  17.1 us
    ppermute x2, starting transfers between devices, padded_2(): lax.ppermute(tail, axis, [(i, (i + 1) % count) for i in range(ends)])  13.5 us
    ppermute x3, starting transfers between devices, from_behind(): return lax.ppermute(block, axis, route)  10.3 us
    psum x1, blocking collectives, body(): sums = lax.psum(partial, 'species')  8.89 us
    ppermute x2, waiting for transfers between devices, padded_2(): lax.ppermute(tail, axis, [(i, (i + 1) % count) for i in range(ends)])  2.95 us
  transfers between devices with their start and end apart: 7, of which 3 were waited for; matrix products, arithmetic and copies ran while one was open for 2% of the time, Pallas kernels for 0%

profile of v1, /device:TPU:0, one launch (start us, length us, event | category | flops | bytes accessed | tf_op | source)
XLA Modules:
  0.0 139.3 jit_solution(8967124272913731241)
XLA Ops:
  0.7 1.4 fusion.34
  2.0 1.3 collective-permute-start
  3.4 3.1 %collective-permute-start.1 = (f32[32,1,32,128]{3,2,1,0:T(8,128)S(1)}, f32[32,1,32,128]{3,2,1,0:T(8,128)S(1)}, u32[]{:S(2)}, u32[]{:S(2)}) collective-permute-start(f32[32,1,32,128]{3,2,1,0:T(8,128)S(1)} %get-tuple-element.7), channel_id=1, source_target_pairs={{0,1},{1,2},{2,3},{3,4},{4,5},{5,6},{6,7},{8,9},{9,10},{10,11},{11... | collective-permute-start | bytes 1572872 | tf_op jit(solution)/shard_map/ppermute | solution.py:19
  6.4 1.5 %collective-permute-done.1 = f32[32,1,32,128]{3,2,1,0:T(8,128)S(1)} collective-permute-done((f32[32,1,32,128]{3,2,1,0:T(8,128)S(1)}, f32[32,1,32,128]{3,2,1,0:T(8,128)S(1)}, u32[]{:S(2)}, u32[]{:S(2)}) %collective-permute-start.1) | collective-permute-done | bytes 524320 | tf_op jit(solution)/shard_map/ppermute | solution.py:19
  7.9 0.8 fusion
  8.8 1.3 collective-permute-start.2
  10.1 10.4 %collective-permute-start.3 = (f32[32,1,32,128]{3,2,1,0:T(8,128)S(1)}, f32[32,1,32,128]{3,2,1,0:T(8,128)S(1)}, u32[]{:S(2)}, u32[]{:S(2)}) collective-permute-start(f32[32,1,32,128]{3,2,1,0:T(8,128)S(1)} %get-tuple-element.5), channel_id=1, source_target_pairs={{0,1},{1,2},{2,3},{3,4},{4,5},{5,6},{6,7},{8,9},{9,10},{10,11},{11... | collective-permute-start | bytes 1572872 | tf_op jit(solution)/shard_map/ppermute | solution.py:19
  20.5 1.5 %collective-permute-done.3 = f32[32,1,32,128]{3,2,1,0:T(8,128)S(1)} collective-permute-done((f32[32,1,32,128]{3,2,1,0:T(8,128)S(1)}, f32[32,1,32,128]{3,2,1,0:T(8,128)S(1)}, u32[]{:S(2)}, u32[]{:S(2)}) %collective-permute-start.3) | collective-permute-done | bytes 524320 | tf_op jit(solution)/shard_map/ppermute | solution.py:19
  22.0 0.8 fusion.1
  22.8 1.7 %convolution_bitcast_fusion = f32[4,8,64,128]{3,1,2,0:T(8,128)S(1)} fusion(f32[4,8,64,128]{3,2,1,0:T(8,128)S(1)} %bitcast.49, f32[1,32,32]{2,1,0:T(8,128)S(1)} %copy-done.3), kind=kOutput, calls=%fused_computation.10 | convolution fusion | flops 100663296 | bytes 2101248 | tf_op jit(solution)/shard_map/dot_general | solution.py:78
  24.5 0.2 copy.17
  24.7 0.5 copy-done.6
  25.2 0.5 fusion.32
  25.7 3.6 %collective-permute-start.4 = (f32[32,2,32,128]{3,2,1,0:T(8,128)S(1)}, f32[32,2,32,128]{3,2,1,0:T(8,128)S(1)}, u32[]{:S(2)}, u32[]{:S(2)}) collective-permute-start(f32[32,2,32,128]{3,2,1,0:T(8,128)S(1)} %get-tuple-element.3), channel_id=1, source_target_pairs={{0,8},{8,16},{16,24},{1,9},{9,17},{17,25},{2,10},{10,18},{18,26},{... | collective-permute-start | bytes 3145736 | tf_op jit(solution)/shard_map/ppermute | solution.py:31
  29.2 18.0 %collective-permute-done.4 = f32[32,2,32,128]{3,2,1,0:T(8,128)S(1)} collective-permute-done((f32[32,2,32,128]{3,2,1,0:T(8,128)S(1)}, f32[32,2,32,128]{3,2,1,0:T(8,128)S(1)}, u32[]{:S(2)}, u32[]{:S(2)}) %collective-permute-start.4) | collective-permute-done | bytes 1048608 | tf_op jit(solution)/shard_map/ppermute | solution.py:31
  47.2 0.2 multiply_add_fusion.1
  47.5 5.4 %collective-permute-start.5 = (f32[32,2,32,128]{3,2,1,0:T(8,128)S(1)}, f32[32,2,32,128]{3,2,1,0:T(8,128)}, u32[]{:S(2)}, u32[]{:S(2)}) collective-permute-start(f32[32,2,32,128]{3,2,1,0:T(8,128)S(1)} %multiply_add_fusion.1), channel_id=1, source_target_pairs={{0,8},{8,16},{16,24},{1,9},{9,17},{17,25},{2,10},{10,18},{18,26},{... | collective-permute-start | bytes 3145736 | tf_op jit(solution)/shard_map/ppermute | solution.py:31
  52.8 24.3 %all-gather.3 = f32[4,2,32]{2,1,0:T(2,128)S(1)} all-gather(f32[1,2,32]{2,1,0:T(2,128)S(1)} %maximum_bitcast_fusion), channel_id=2, replica_groups=mesh['species'=4,'space'=8] {'species'}, dimensions={0}, use_global_device_ids=true | all-gather | bytes 1280 | tf_op jit(solution)/shard_map/all_gather | solution.py:65
  77.2 1.4 multiply_add_fusion
  78.6 1.4 collective-permute-start.6
  80.0 29.6 %all-gather.2 = f32[8,1,8]{2,1,0:T(1,128)S(1)} all-gather(f32[1,1,8]{2,1,0:T(1,128)S(1)} %convert_bitcast_fusion), channel_id=1, replica_groups=mesh['species'=4,'space'=8] {'space'}, dimensions={0}, use_global_device_ids=true | all-gather | bytes 288 | tf_op jit(solution)/shard_map/all_gather | solution.py:66
  109.6 0.5 broadcast.46
  110.1 0.7 reduce.3
  110.8 0.1 eq.15
  110.9 0.1 select_reduce_fusion
  111.0 0.1 reshape.73
  111.0 0.2 fusion.23
  111.2 8.9 %psum.7 = f32[4,64]{1,0:T(4,128)S(1)} all-reduce(f32[4,64]{1,0:T(4,128)S(1)} %fusion.23), channel_id=1, replica_groups=mesh['species'=4,'space'=8] {'species'}, use_global_device_ids=true, to_apply=%region_2.3 | all-reduce | flops 256 | bytes 2048 | tf_op jit(solution)/shard_map/psum | solution.py:91
  120.2 0.2 fusion.16
  120.3 17.1 %all-gather.1 = f32[64,128]{1,0:T(8,128)S(1)} all-gather(f32[8,128]{1,0:T(8,128)S(1)} %bitcast.50), channel_id=3, replica_groups=mesh['species'=4,'space'=8] {'space'}, dimensions={0}, use_global_device_ids=true | all-gather | bytes 36864 | tf_op jit(solution)/shard_map/all_gather | solution.py:97
  137.4 0.8 fusion.18
  138.2 1.1 add_bitcast_fusion
  (30 shorter events, 0.2 us)
Async XLA Ops:
  0.6 119.5 %copy-start = (bf16[1,8,64,128]{3,2,1,0:T(8,128)(2,1)S(1)}, bf16[1,8,64,128]{3,2,1,0:T(8,128)(2,1)}, u32[]{:S(2)}) copy-start(bf16[1,8,64,128]{3,2,1,0:T(8,128)(2,1)} %param.16) | copy-start | bytes 393220
  0.6 7.3 %copy-start.1 = (f32[1,32,2,32,128]{4,3,2,1,0:T(8,128)S(1)}, f32[1,32,2,32,128]{4,3,2,1,0:T(8,128)}, u32[]{:S(2)}) copy-start(f32[1,32,2,32,128]{4,3,2,1,0:T(8,128)} %param.9) | copy-start | bytes 3145732
  0.7 7.3 %copy-start.2 = (f32[2,32,128]{2,1,0:T(8,128)S(1)}, f32[2,32,128]{2,1,0:T(8,128)}, u32[]{:S(2)}) copy-start(f32[2,32,128]{2,1,0:T(8,128)} %param.10) | copy-start | bytes 98308
  0.7 7.2 %copy-start.5 = (f32[1,32]{1,0:T(1,128)S(1)}, f32[1,32]{1,0:T(1,128)}, u32[]{:S(2)}) copy-start(f32[1,32]{1,0:T(1,128)} %param.11) | copy-start | bytes 388
  2.0 4.4 %collective-permute-start = (f32[32,1,32,128]{3,2,1,0:T(8,128)S(1)}, f32[32,1,32,128]{3,2,1,0:T(8,128)S(1)}, u32[]{:S(2)}, u32[]{:S(2)}) collective-permute-start(f32[32,1,32,128]{3,2,1,0:T(8,128)S(1)} %get-tuple-element.6), channel_id=1, source_target_pairs={{1,0},{2,1},{3,2},{4,3},{5,4},{6,5},{7,6},{9,8},{10,9},{11,10},{12... | collective-permute-start | bytes 1572872 | tf_op jit(solution)/shard_map/ppermute | solution.py:21
  3.4 4.6 %collective-permute-start.1 = (f32[32,1,32,128]{3,2,1,0:T(8,128)S(1)}, f32[32,1,32,128]{3,2,1,0:T(8,128)S(1)}, u32[]{:S(2)}, u32[]{:S(2)}) collective-permute-start(f32[32,1,32,128]{3,2,1,0:T(8,128)S(1)} %get-tuple-element.7), channel_id=1, source_target_pairs={{0,1},{1,2},{2,3},{3,4},{4,5},{5,6},{6,7},{8,9},{9,10},{10,11},{11... | collective-permute-start | bytes 1572872 | tf_op jit(solution)/shard_map/ppermute | solution.py:19
  8.8 11.7 %collective-permute-start.2 = (f32[32,1,32,128]{3,2,1,0:T(8,128)S(1)}, f32[32,1,32,128]{3,2,1,0:T(8,128)S(1)}, u32[]{:S(2)}, u32[]{:S(2)}) collective-permute-start(f32[32,1,32,128]{3,2,1,0:T(8,128)S(1)} %get-tuple-element.4), channel_id=1, source_target_pairs={{1,0},{2,1},{3,2},{4,3},{5,4},{6,5},{7,6},{9,8},{10,9},{11,10},{12... | collective-permute-start | bytes 1572872 | tf_op jit(solution)/shard_map/ppermute | solution.py:21
  10.1 12.7 %copy-start.3 = (f32[1,32,32]{2,1,0:T(8,128)S(1)}, f32[1,32,32]{2,1,0:T(8,128)}, u32[]{:S(2)}) copy-start(f32[1,32,32]{2,1,0:T(8,128)} %param.12) | copy-start | bytes 12292
  10.1 11.9 %collective-permute-start.3 = (f32[32,1,32,128]{3,2,1,0:T(8,128)S(1)}, f32[32,1,32,128]{3,2,1,0:T(8,128)S(1)}, u32[]{:S(2)}, u32[]{:S(2)}) collective-permute-start(f32[32,1,32,128]{3,2,1,0:T(8,128)S(1)} %get-tuple-element.5), channel_id=1, source_target_pairs={{0,1},{1,2},{2,3},{3,4},{4,5},{5,6},{6,7},{8,9},{9,10},{10,11},{11... | collective-permute-start | bytes 1572872 | tf_op jit(solution)/shard_map/ppermute | solution.py:19
  24.5 0.7 copy-start.6
  25.2 22.0 %copy-start.4 = (f32[1,32]{1,0:T(1,128)S(1)}, f32[1,32]{1,0:T(1,128)}, u32[]{:S(2)}) copy-start(f32[1,32]{1,0:T(1,128)} %param.13) | copy-start | bytes 388
  25.7 21.5 %collective-permute-start.4 = (f32[32,2,32,128]{3,2,1,0:T(8,128)S(1)}, f32[32,2,32,128]{3,2,1,0:T(8,128)S(1)}, u32[]{:S(2)}, u32[]{:S(2)}) collective-permute-start(f32[32,2,32,128]{3,2,1,0:T(8,128)S(1)} %get-tuple-element.3), channel_id=1, source_target_pairs={{0,8},{8,16},{16,24},{1,9},{9,17},{17,25},{2,10},{10,18},{18,26},{... | collective-permute-start | bytes 3145736 | tf_op jit(solution)/shard_map/ppermute | solution.py:31
  47.2 5.6 %copy-start.7 = (f32[1,32]{1,0:T(1,128)S(1)}, f32[1,32]{1,0:T(1,128)}, u32[]{:S(2)}) copy-start(f32[1,32]{1,0:T(1,128)} %param.15) | copy-start | bytes 388
  47.2 30.0 %copy-start.8 = (s32[1,8]{1,0:T(1,128)S(1)}, s32[1,8]{1,0:T(1,128)}, u32[]{:S(2)}) copy-start(s32[1,8]{1,0:T(1,128)} %param.17) | copy-start | bytes 100
  47.5 29.7 %collective-permute-start.5 = (f32[32,2,32,128]{3,2,1,0:T(8,128)S(1)}, f32[32,2,32,128]{3,2,1,0:T(8,128)}, u32[]{:S(2)}, u32[]{:S(2)}) collective-permute-start(f32[32,2,32,128]{3,2,1,0:T(8,128)S(1)} %multiply_add_fusion.1), channel_id=1, source_target_pairs={{0,8},{8,16},{16,24},{1,9},{9,17},{17,25},{2,10},{10,18},{18,26},{... | collective-permute-start | bytes 3145736 | tf_op jit(solution)/shard_map/ppermute | solution.py:31
  78.6 59.6 %collective-permute-start.6 = (f32[32,2,32,128]{3,2,1,0:T(8,128)S(1)}, f32[32,2,32,128]{3,2,1,0:T(8,128)S(1)}, u32[]{:S(2)}, u32[]{:S(2)}) collective-permute-start(f32[32,2,32,128]{3,2,1,0:T(8,128)S(1)} %multiply_add_fusion), channel_id=1, source_target_pairs={{0,8},{8,16},{16,24},{1,9},{9,17},{17,25},{2,10},{10,18},{18,26},{... | collective-permute-start | bytes 3145736 | tf_op jit(solution)/shard_map/ppermute | solution.py:31

commit v2 on v1

v2 whole, which is shorter than its diff:
```python
import jax
import jax.numpy as jnp
from jax import lax
from jax.sharding import PartitionSpec as P

SUBSTEPS = 2
NB = 384
CHUNKS = 4
HIGH = lax.Precision.HIGHEST


def padded_2(cells, sides, width):
    for axis, dim in sides:
        count = lax.axis_size(axis)
        ends = count - 1
        head = lax.slice_in_dim(cells, 0, width, axis=dim)
        tail = lax.slice_in_dim(cells, cells.shape[dim] - width, cells.shape[dim], axis=dim)
        cells = jnp.concatenate(
            [
                lax.ppermute(tail, axis, [(i, (i + 1) % count) for i in range(ends)]),
                cells,
                lax.ppermute(head, axis, [((i + 1) % count, i) for i in range(ends)]),
            ],
            axis=dim,
        )
    return cells


def cross_sum(field):
    padded = jnp.pad(field, ((0, 0), (0, 0), (1, 1), (1, 1)))
    beside = padded[:, :, 2:, 1:-1] + padded[:, :, :-2, 1:-1]
    beside = beside + padded[:, :, 1:-1, 2:] + padded[:, :, 1:-1, :-2]
    return beside


def gather_all(block, axis):
    count = lax.axis_size(axis)
    if count & (count - 1):
        return lax.all_gather(block, axis)
    me = lax.axis_index(axis)
    held = block[None]
    span = 1
    while span < count:
        other = lax.ppermute(held, axis, [(i, i ^ span) for i in range(count)])
        low = (me & span) == 0
        held = jnp.where(
            low,
            jnp.concatenate([held, other], axis=0),
            jnp.concatenate([other, held], axis=0),
        )
        span *= 2
    return held


def body(
    density,
    space_factor,
    diff_rate,
    loss_inverse,
    chain_yield,
    survival,
    gamma_yield,
    sky_weight,
    sky_blocks,
):
    groups = lax.axis_size("species")
    tiles = lax.axis_size("space")
    rows = NB // tiles

    field = density[0]
    bins = field.shape[0]
    depth = field.shape[3]
    rate = diff_rate[0][:, None, None, None]
    factor = rate * space_factor[None]
    for step in range(SUBSTEPS):
        wider = padded_2(field, (("space", 1),), 1)
        beside = wider[:, 2:] + wider[:, :-2] + cross_sum(field)
        field = field + factor * (beside - 6.0 * field)
    solved = jnp.dot(
        loss_inverse[0],
        field.reshape(bins, -1),
        precision=HIGH,
        preferred_element_type=jnp.float32,
    ).reshape(field.shape)
    chain = chain_yield[0]
    own_part = survival[0][:, None, None, None] * solved

    own_columns = jnp.sum(own_part, axis=3).reshape(bins, -1)
    cols = own_columns.shape[1]
    packed = jnp.concatenate(
        [own_columns, jnp.concatenate([chain, gamma_yield[0]]).reshape(1, -1)[:, :cols]], axis=0
    ) if cols == 2 * bins else None
    everyone = gather_all(packed, "species")
    sums = everyone[0, :bins]
    total = jnp.zeros((cols,), jnp.float32)
    for group in range(groups):
        if group > 0:
            sums = everyone[group, bins, :bins][:, None] * sums + everyone[group, :bins]
        weighted = jnp.dot(
            everyone[group, bins, bins:], sums, precision=HIGH, preferred_element_type=jnp.float32
        )
        emission = lax.reduce_precision(weighted / (bins * depth), exponent_bits=8, mantissa_bits=7)
        total = total + emission
    contribution = jnp.einsum(
        "c,lcb->lb", total, sky_weight[0].astype(jnp.float32), precision=HIGH
    )
    lines, pixels = contribution.shape
    ids = jnp.zeros((1, pixels), jnp.float32).at[0, :lines].set(sky_blocks[0].astype(jnp.float32))
    gathered = gather_all(jnp.concatenate([contribution, ids], axis=0), "space")
    mine = lax.axis_index("space") * rows + jnp.arange(rows, dtype=jnp.int32)
    onehot = (
        gathered[:, lines, :lines].reshape(1, tiles * lines) == mine.astype(jnp.float32)[:, None]
    ).astype(jnp.float32)
    sky = jnp.dot(
        onehot,
        gathered[:, :lines].reshape(tiles * lines, pixels),
        precision=HIGH,
        preferred_element_type=jnp.float32,
    )

    base = bins // CHUNKS
    bounds = [0]
    for c in range(CHUNKS):
        bounds.append(bounds[-1] + base + 2 * c - (CHUNKS - 1))
    bounds[-1] = bins
    pieces = [own_part[bounds[c]:bounds[c + 1]] for c in range(CHUNKS)]
    scales = [chain[bounds[c]:bounds[c + 1]][:, None, None, None] for c in range(CHUNKS)]
    for wave in range(CHUNKS + groups - 2):
        for c in range(CHUNKS):
            s = wave - c
            if 0 <= s < groups - 1:
                arrived = lax.ppermute(pieces[c], "species", [(s, s + 1)])
                pieces[c] = pieces[c] + scales[c] * arrived
    carried = jnp.concatenate(pieces, axis=0)
    return (carried[None], sky)


def solution(mesh):
    placed = (
        P("species", None, "space", None, None),
        P("space", None, None),
        P("species", None),
        P("species", None, None),
        P("species", None),
        P("species", None),
        P("species", None),
        P("space", None, None, None),
        P("space", None),
    )
    return jax.shard_map(
        body,
        mesh=mesh,
        in_specs=placed,
        out_specs=(P("species", None, "space", None, None), P("space", None)),
        check_vma=False,
    )
```

time: 140 us -> 98.9 us (0.71)
  the two profiles are of different devices: /device:TPU:0 before, /device:TPU:26 now
where the time goes in v2:
time: 98.9 us; the launch traced here: 98.5 us
  waiting for transfers between devices  55.1 us (56%)
  starting transfers between devices  30.4 us (31%)
  other arithmetic  5.77 us (6%)
  matrix products  3.48 us (4%)
  local copies, waits for them, and re-layouts  2.61 us (3%)
  between operations  1.11 us (1%)
    ppermute x12, waiting for transfers between devices, body(): arrived = lax.ppermute(pieces[c], 'species', [(s, s + 1)])  29.6 us
    ppermute x5, waiting for transfers between devices, gather_all(): other = lax.ppermute(held, axis, [(i, i ^ span) for i in range(count)])  11.3 us
    ppermute x12, starting transfers between devices, body(): arrived = lax.ppermute(pieces[c], 'species', [(s, s + 1)])  10.6 us
    ppermute x5, starting transfers between devices, gather_all(): other = lax.ppermute(held, axis, [(i, i ^ span) for i in range(count)])  9.31 us
    ppermute x2, waiting for transfers between devices, padded_2(): lax.ppermute(head, axis, [((i + 1) % count, i) for i in range(ends)])  8.39 us
    ppermute x2, starting transfers between devices, padded_2(): lax.ppermute(tail, axis, [(i, (i + 1) % count) for i in range(ends)])  6.71 us
    ppermute x2, waiting for transfers between devices, padded_2(): lax.ppermute(tail, axis, [(i, (i + 1) % count) for i in range(ends)])  5.79 us
    ppermute x2, starting transfers between devices, padded_2(): lax.ppermute(head, axis, [((i + 1) % count, i) for i in range(ends)])  3.84 us
  transfers between devices with their start and end apart: 21, of which 12 were waited for; matrix products, arithmetic and copies ran while one was open for 4% of the time, Pallas kernels for 0%

profile of v2, /device:TPU:26, one launch (start us, length us, event | category | flops | bytes accessed | tf_op | source)
XLA Modules:
  0.0 98.5 jit_solution(5766678334430735213)
XLA Ops:
  0.7 1.4 %fusion.46 = (f32[32,1,32,128]{3,2,1,0:T(8,128)S(1)}, f32[32,1,32,128]{3,2,1,0:T(8,128)S(1)}) fusion(f32[32,2,32,128]{3,2,1,0:T(8,128)} %bitcast.117), kind=kLoop, calls=%fused_computation.106 | loop fusion | bytes 2097152 | tf_op jit(solution)/shard_map/slice | solution.py:16
  2.1 1.9 %collective-permute-start = (f32[32,1,32,128]{3,2,1,0:T(8,128)S(1)}, f32[32,1,32,128]{3,2,1,0:T(8,128)S(1)}, u32[]{:S(2)}, u32[]{:S(2)}) collective-permute-start(f32[32,1,32,128]{3,2,1,0:T(8,128)S(1)} %get-tuple-element.18), channel_id=1, source_target_pairs={{1,0},{2,1},{3,2},{4,3},{5,4},{6,5},{7,6},{9,8},{10,9},{11,10},{12... | collective-permute-start | bytes 1572872 | tf_op jit(solution)/shard_map/ppermute | solution.py:22
  4.0 2.4 %collective-permute-start.1 = (f32[32,1,32,128]{3,2,1,0:T(8,128)S(1)}, f32[32,1,32,128]{3,2,1,0:T(8,128)S(1)}, u32[]{:S(2)}, u32[]{:S(2)}) collective-permute-start(f32[32,1,32,128]{3,2,1,0:T(8,128)S(1)} %get-tuple-element.19), channel_id=1, source_target_pairs={{0,1},{1,2},{2,3},{3,4},{4,5},{5,6},{6,7},{8,9},{9,10},{10,11},{11... | collective-permute-start | bytes 1572872 | tf_op jit(solution)/shard_map/ppermute | solution.py:20
  6.4 6.1 %collective-permute-done = f32[32,1,32,128]{3,2,1,0:T(8,128)S(1)} collective-permute-done((f32[32,1,32,128]{3,2,1,0:T(8,128)S(1)}, f32[32,1,32,128]{3,2,1,0:T(8,128)S(1)}, u32[]{:S(2)}, u32[]{:S(2)}) %collective-permute-start) | collective-permute-done | bytes 524320 | tf_op jit(solution)/shard_map/ppermute | solution.py:22
  12.5 2.0 %collective-permute-done.1 = f32[32,1,32,128]{3,2,1,0:T(8,128)S(1)} collective-permute-done((f32[32,1,32,128]{3,2,1,0:T(8,128)S(1)}, f32[32,1,32,128]{3,2,1,0:T(8,128)S(1)}, u32[]{:S(2)}, u32[]{:S(2)}) %collective-permute-start.1) | collective-permute-done | bytes 524320 | tf_op jit(solution)/shard_map/ppermute | solution.py:20
  14.5 0.8 fusion.12
  15.4 1.9 %collective-permute-start.2 = (f32[32,1,32,128]{3,2,1,0:T(8,128)S(1)}, f32[32,1,32,128]{3,2,1,0:T(8,128)S(1)}, u32[]{:S(2)}, u32[]{:S(2)}) collective-permute-start(f32[32,1,32,128]{3,2,1,0:T(8,128)S(1)} %get-tuple-element.16), channel_id=1, source_target_pairs={{1,0},{2,1},{3,2},{4,3},{5,4},{6,5},{7,6},{9,8},{10,9},{11,10},{12... | collective-permute-start | bytes 1572872 | tf_op jit(solution)/shard_map/ppermute | solution.py:22
  17.3 4.3 %collective-permute-start.3 = (f32[32,1,32,128]{3,2,1,0:T(8,128)S(1)}, f32[32,1,32,128]{3,2,1,0:T(8,128)S(1)}, u32[]{:S(2)}, u32[]{:S(2)}) collective-permute-start(f32[32,1,32,128]{3,2,1,0:T(8,128)S(1)} %get-tuple-element.17), channel_id=1, source_target_pairs={{0,1},{1,2},{2,3},{3,4},{4,5},{5,6},{6,7},{8,9},{9,10},{10,11},{11... | collective-permute-start | bytes 1572872 | tf_op jit(solution)/shard_map/ppermute | solution.py:20
  21.7 2.3 %collective-permute-done.2 = f32[32,1,32,128]{3,2,1,0:T(8,128)S(1)} collective-permute-done((f32[32,1,32,128]{3,2,1,0:T(8,128)S(1)}, f32[32,1,32,128]{3,2,1,0:T(8,128)S(1)}, u32[]{:S(2)}, u32[]{:S(2)}) %collective-permute-start.2) | collective-permute-done | bytes 524320 | tf_op jit(solution)/shard_map/ppermute | solution.py:22
  24.0 3.8 %collective-permute-done.3 = f32[32,1,32,128]{3,2,1,0:T(8,128)S(1)} collective-permute-done((f32[32,1,32,128]{3,2,1,0:T(8,128)S(1)}, f32[32,1,32,128]{3,2,1,0:T(8,128)S(1)}, u32[]{:S(2)}, u32[]{:S(2)}) %collective-permute-start.3) | collective-permute-done | bytes 524320 | tf_op jit(solution)/shard_map/ppermute | solution.py:20
  27.8 0.8 fusion.13
  28.6 1.7 %convolution_bitcast_fusion = f32[4,8,64,128]{3,1,2,0:T(8,128)S(1)} fusion(f32[4,8,64,128]{3,2,1,0:T(8,128)S(1)} %bitcast.119, f32[1,32,32]{2,1,0:T(8,128)S(1)} %copy-done.3), kind=kOutput, calls=%fused_computation.10 | convolution fusion | flops 100663296 | bytes 2101248 | tf_op jit(solution)/shard_map/dot_general | solution.py:79
  32.8 2.6 %collective-permute-done.16 = f32[1,33,64]{2,1,0:T(8,128)S(1)} collective-permute-done((f32[1,33,64]{2,1,0:T(8,128)S(1)}, f32[1,33,64]{2,1,0:T(8,128)S(1)}, u32[]{:S(2)}, u32[]{:S(2)}) %collective-permute-start.16) | collective-permute-done | bytes 8480 | tf_op jit(solution)/shard_map/ppermute | solution.py:44
  36.5 4.2 %collective-permute-done.17 = f32[2,33,64]{2,1,0:T(8,128)S(1)} collective-permute-done((f32[2,33,64]{2,1,0:T(8,128)S(1)}, f32[2,33,64]{2,1,0:T(8,128)S(1)}, u32[]{:S(2)}, u32[]{:S(2)}) %collective-permute-start.17) | collective-permute-done | bytes 16928 | tf_op jit(solution)/shard_map/ppermute | solution.py:44
  41.8 2.1 %collective-permute-start.18 = (f32[1,9,128]{2,1,0:T(8,128)S(1)}, f32[1,9,128]{2,1,0:T(8,128)S(1)}, u32[]{:S(2)}, u32[]{:S(2)}) collective-permute-start(f32[1,9,128]{2,1,0:T(8,128)S(1)} %fusion.42), channel_id=1, source_target_pairs={{0,1},{1,0},{2,3},{3,2},{4,5},{5,4},{6,7},{7,6},{8,9},{9,8},{10,11... | collective-permute-start | bytes 13832 | tf_op jit(solution)/shard_map/ppermute | solution.py:44
  44.1 0.8 collective-permute-done.18
  44.9 3.7 %collective-permute-done.19 = f32[2,9,128]{2,1,0:T(8,128)S(1)} collective-permute-done((f32[2,9,128]{2,1,0:T(8,128)S(1)}, f32[2,9,128]{2,1,0:T(8,128)S(1)}, u32[]{:S(2)}, u32[]{:S(2)}) %collective-permute-start.19) | collective-permute-done | bytes 9248 | tf_op jit(solution)/shard_map/ppermute | solution.py:44
  48.6 6.2 %collective-permute-start.20 = (f32[4,9,128]{2,1,0:T(8,128)S(1)}, f32[4,9,128]{2,1,0:T(8,128)S(1)}, u32[]{:S(2)}, u32[]{:S(2)}) collective-permute-start(f32[4,9,128]{2,1,0:T(8,128)S(1)} %maximum_select_fusion.3), channel_id=1, source_target_pairs={{0,4},{1,5},{2,6},{3,7},{4,0},{5,1},{6,2},{7,3},{8,12},{9,13},{10,... | collective-permute-start | bytes 55304 | tf_op jit(solution)/shard_map/ppermute | solution.py:44
  56.3 0.7 collective-permute-start.10
  57.0 0.7 collective-permute-start.13
  57.8 0.8 fusion.30
  60.3 0.7 collective-permute-start.11
  61.1 1.3 %collective-permute-start.6 = (f32[5,2,32,128]{3,2,1,0:T(8,128)S(1)}, f32[5,2,32,128]{3,2,1,0:T(8,128)S(1)}, u32[]{:S(2)}, u32[]{:S(2)}) collective-permute-start(f32[5,2,32,128]{3,2,1,0:T(8,128)S(1)} %multiply_add_fusion.10), channel_id=1, source_target_pairs={{16,24},{17,25},{18,26},{19,27},{20,28},{21,29},{22,30},{23,31}} | collective-permute-start | bytes 491528 | tf_op jit(solution)/shard_map/ppermute | solution.py:132
  62.5 0.7 collective-permute-start.14
  63.3 1.3 %collective-permute-start.9 = (f32[7,2,32,128]{3,2,1,0:T(8,128)S(1)}, f32[7,2,32,128]{3,2,1,0:T(8,128)S(1)}, u32[]{:S(2)}, u32[]{:S(2)}) collective-permute-start(f32[7,2,32,128]{3,2,1,0:T(8,128)S(1)} %multiply_add_fusion.7), channel_id=1, source_target_pairs={{16,24},{17,25},{18,26},{19,27},{20,28},{21,29},{22,30},{23,31}} | collective-permute-start | bytes 688136 | tf_op jit(solution)/shard_map/ppermute | solution.py:132
  64.6 12.7 %collective-permute-done.6 = f32[5,2,32,128]{3,2,1,0:T(8,128)S(1)} collective-permute-done((f32[5,2,32,128]{3,2,1,0:T(8,128)S(1)}, f32[5,2,32,128]{3,2,1,0:T(8,128)S(1)}, u32[]{:S(2)}, u32[]{:S(2)}) %collective-permute-start.6) | collective-permute-done | bytes 163872 | tf_op jit(solution)/shard_map/ppermute | solution.py:132
  77.5 1.3 %collective-permute-start.12 = (f32[9,2,32,128]{3,2,1,0:T(8,128)S(1)}, f32[9,2,32,128]{3,2,1,0:T(8,128)S(1)}, u32[]{:S(2)}, u32[]{:S(2)}) collective-permute-start(f32[9,2,32,128]{3,2,1,0:T(8,128)S(1)} %multiply_add_fusion.4), channel_id=1, source_target_pairs={{16,24},{17,25},{18,26},{19,27},{20,28},{21,29},{22,30},{23,31}} | collective-permute-start | bytes 884744 | tf_op jit(solution)/shard_map/ppermute | solution.py:132
  78.9 1.3 %collective-permute-start.15 = (f32[11,2,32,128]{3,2,1,0:T(8,128)S(1)}, f32[11,2,32,128]{3,2,1,0:T(8,128)S(1)}, u32[]{:S(2)}, u32[]{:S(2)}) collective-permute-start(f32[11,2,32,128]{3,2,1,0:T(8,128)S(1)} %multiply_add_fusion.1), channel_id=1, source_target_pairs={{16,24},{17,25},{18,26},{19,27},{20,28},{21,29},{22,30},{23,31}} | collective-permute-start | bytes 1081352 | tf_op jit(solution)/shard_map/ppermute | solution.py:132
  80.2 2.7 %collective-permute-done.9 = f32[7,2,32,128]{3,2,1,0:T(8,128)S(1)} collective-permute-done((f32[7,2,32,128]{3,2,1,0:T(8,128)S(1)}, f32[7,2,32,128]{3,2,1,0:T(8,128)S(1)}, u32[]{:S(2)}, u32[]{:S(2)}) %collective-permute-start.9) | collective-permute-done | bytes 229408 | tf_op jit(solution)/shard_map/ppermute | solution.py:132
  83.0 5.4 %collective-permute-done.12 = f32[9,2,32,128]{3,2,1,0:T(8,128)S(1)} collective-permute-done((f32[9,2,32,128]{3,2,1,0:T(8,128)S(1)}, f32[9,2,32,128]{3,2,1,0:T(8,128)S(1)}, u32[]{:S(2)}, u32[]{:S(2)}) %collective-permute-start.12) | collective-permute-done | bytes 294944 | tf_op jit(solution)/shard_map/ppermute | solution.py:132
  88.6 8.7 %collective-permute-done.15 = f32[11,2,32,128]{3,2,1,0:T(8,128)S(1)} collective-permute-done((f32[11,2,32,128]{3,2,1,0:T(8,128)S(1)}, f32[11,2,32,128]{3,2,1,0:T(8,128)S(1)}, u32[]{:S(2)}, u32[]{:S(2)}) %collective-permute-start.15) | collective-permute-done | bytes 360480 | tf_op jit(solution)/shard_map/ppermute | solution.py:132
  97.4 1.1 %maximum_bitcast_fusion = f32[1,32,2,32,128]{4,3,2,1,0:T(8,128)} fusion(f32[11,2,32,128]{3,2,1,0:T(8,128)S(1)} %multiply_add_fusion, f32[9,2,32,128]{3,2,1,0:T(8,128)S(1)} %multiply_add_fusion.3, f32[7,2,32,128]{3,2,1,0:T(8,128)S(1)} %multiply_add_fusion.6, f32[5,2,32,128]{3,2,1,0:T(8,128)S(1)} %multiply_add_fusion.9), kind=kLoop, calls=%fused_computation.47 | loop fusion | flops 786432 | bytes 2097152 | tf_op jit(solution)/shard_map/broadcast_in_dim | solution.py:135
  (78 shorter events, 9.0 us)
Async XLA Ops:
  0.6 41.0 %copy-start = (bf16[1,8,64,128]{3,2,1,0:T(8,128)(2,1)S(1)}, bf16[1,8,64,128]{3,2,1,0:T(8,128)(2,1)}, u32[]{:S(2)}) copy-start(bf16[1,8,64,128]{3,2,1,0:T(8,128)(2,1)} %param.18) | copy-start | bytes 393220
  0.6 13.8 %copy-start.1 = (f32[1,32,2,32,128]{4,3,2,1,0:T(8,128)S(1)}, f32[1,32,2,32,128]{4,3,2,1,0:T(8,128)}, u32[]{:S(2)}) copy-start(f32[1,32,2,32,128]{4,3,2,1,0:T(8,128)} %param.11) | copy-start | bytes 3145732
  0.7 13.8 %copy-start.2 = (f32[2,32,128]{2,1,0:T(8,128)S(1)}, f32[2,32,128]{2,1,0:T(8,128)}, u32[]{:S(2)}) copy-start(f32[2,32,128]{2,1,0:T(8,128)} %param.12) | copy-start | bytes 98308
  0.7 13.8 %copy-start.4 = (f32[1,32]{1,0:T(1,128)S(1)}, f32[1,32]{1,0:T(1,128)}, u32[]{:S(2)}) copy-start(f32[1,32]{1,0:T(1,128)} %param.13) | copy-start | bytes 388
  2.1 10.5 %collective-permute-start = (f32[32,1,32,128]{3,2,1,0:T(8,128)S(1)}, f32[32,1,32,128]{3,2,1,0:T(8,128)S(1)}, u32[]{:S(2)}, u32[]{:S(2)}) collective-permute-start(f32[32,1,32,128]{3,2,1,0:T(8,128)S(1)} %get-tuple-element.18), channel_id=1, source_target_pairs={{1,0},{2,1},{3,2},{4,3},{5,4},{6,5},{7,6},{9,8},{10,9},{11,10},{12... | collective-permute-start | bytes 1572872 | tf_op jit(solution)/shard_map/ppermute | solution.py:22
  4.0 10.5 %collective-permute-start.1 = (f32[32,1,32,128]{3,2,1,0:T(8,128)S(1)}, f32[32,1,32,128]{3,2,1,0:T(8,128)S(1)}, u32[]{:S(2)}, u32[]{:S(2)}) collective-permute-start(f32[32,1,32,128]{3,2,1,0:T(8,128)S(1)} %get-tuple-element.19), channel_id=1, source_target_pairs={{0,1},{1,2},{2,3},{3,4},{4,5},{5,6},{6,7},{8,9},{9,10},{10,11},{11... | collective-permute-start | bytes 1572872 | tf_op jit(solution)/shard_map/ppermute | solution.py:20
  15.3 6.3 %copy-start.6 = (f32[1,32]{1,0:T(1,128)S(1)}, f32[1,32]{1,0:T(1,128)}, u32[]{:S(2)}) copy-start(f32[1,32]{1,0:T(1,128)} %param.17) | copy-start | bytes 388
  15.3 6.3 %copy-start.8 = (f32[1,32]{1,0:T(1,128)S(1)}, f32[1,32]{1,0:T(1,128)}, u32[]{:S(2)}) copy-start(f32[1,32]{1,0:T(1,128)} %param.15) | copy-start | bytes 388
  15.4 8.6 %collective-permute-start.2 = (f32[32,1,32,128]{3,2,1,0:T(8,128)S(1)}, f32[32,1,32,128]{3,2,1,0:T(8,128)S(1)}, u32[]{:S(2)}, u32[]{:S(2)}) collective-permute-start(f32[32,1,32,128]{3,2,1,0:T(8,128)S(1)} %get-tuple-element.16), channel_id=1, source_target_pairs={{1,0},{2,1},{3,2},{4,3},{5,4},{6,5},{7,6},{9,8},{10,9},{11,10},{12... | collective-permute-start | bytes 1572872 | tf_op jit(solution)/shard_map/ppermute | solution.py:22
  17.3 10.5 %collective-permute-start.3 = (f32[32,1,32,128]{3,2,1,0:T(8,128)S(1)}, f32[32,1,32,128]{3,2,1,0:T(8,128)S(1)}, u32[]{:S(2)}, u32[]{:S(2)}) collective-permute-start(f32[32,1,32,128]{3,2,1,0:T(8,128)S(1)} %get-tuple-element.17), channel_id=1, source_target_pairs={{0,1},{1,2},{2,3},{3,4},{4,5},{5,6},{6,7},{8,9},{9,10},{10,11},{11... | collective-permute-start | bytes 1572872 | tf_op jit(solution)/shard_map/ppermute | solution.py:20
  21.7 6.9 %copy-start.3 = (f32[1,32,32]{2,1,0:T(8,128)S(1)}, f32[1,32,32]{2,1,0:T(8,128)}, u32[]{:S(2)}) copy-start(f32[1,32,32]{2,1,0:T(8,128)} %param.14) | copy-start | bytes 12292
  30.3 0.7 copy-start.5
  31.0 4.9 %copy-start.7 = (s32[1,8]{1,0:T(1,128)S(1)}, s32[1,8]{1,0:T(1,128)}, u32[]{:S(2)}) copy-start(s32[1,8]{1,0:T(1,128)} %param.19) | copy-start | bytes 100
  31.6 3.8 %collective-permute-start.16 = (f32[1,33,64]{2,1,0:T(8,128)S(1)}, f32[1,33,64]{2,1,0:T(8,128)S(1)}, u32[]{:S(2)}, u32[]{:S(2)}) collective-permute-start(f32[1,33,64]{2,1,0:T(8,128)S(1)} %maximum_bitcast_fusion.1), channel_id=1, source_target_pairs={{0,8},{8,0},{16,24},{24,16},{1,9},{9,1},{17,25},{25,17},{2,10},{10... | collective-permute-start | bytes 25352 | tf_op jit(solution)/shard_map/ppermute | solution.py:44
  35.4 5.3 %collective-permute-start.17 = (f32[2,33,64]{2,1,0:T(8,128)S(1)}, f32[2,33,64]{2,1,0:T(8,128)S(1)}, u32[]{:S(2)}, u32[]{:S(2)}) collective-permute-start(f32[2,33,64]{2,1,0:T(8,128)S(1)} %maximum_select_fusion.2), channel_id=1, source_target_pairs={{0,16},{8,24},{16,0},{24,8},{1,17},{9,25},{17,1},{25,9},{2,18},{10... | collective-permute-start | bytes 50696 | tf_op jit(solution)/shard_map/ppermute | solution.py:44
  41.8 3.0 %collective-permute-start.18 = (f32[1,9,128]{2,1,0:T(8,128)S(1)}, f32[1,9,128]{2,1,0:T(8,128)S(1)}, u32[]{:S(2)}, u32[]{:S(2)}) collective-permute-start(f32[1,9,128]{2,1,0:T(8,128)S(1)} %fusion.42), channel_id=1, source_target_pairs={{0,1},{1,0},{2,3},{3,2},{4,5},{5,4},{6,7},{7,6},{8,9},{9,8},{10,11... | collective-permute-start | bytes 13832 | tf_op jit(solution)/shard_map/ppermute | solution.py:44
  44.8 3.7 %collective-permute-start.19 = (f32[2,9,128]{2,1,0:T(8,128)S(1)}, f32[2,9,128]{2,1,0:T(8,128)S(1)}, u32[]{:S(2)}, u32[]{:S(2)}) collective-permute-start(f32[2,9,128]{2,1,0:T(8,128)S(1)} %maximum_select_fusion.4), channel_id=1, source_target_pairs={{0,2},{1,3},{2,0},{3,1},{4,6},{5,7},{6,4},{7,5},{8,10},{9,11},{10,... | collective-permute-start | bytes 27656 | tf_op jit(solution)/shard_map/ppermute | solution.py:44
  48.6 9.1 %collective-permute-start.20 = (f32[4,9,128]{2,1,0:T(8,128)S(1)}, f32[4,9,128]{2,1,0:T(8,128)S(1)}, u32[]{:S(2)}, u32[]{:S(2)}) collective-permute-start(f32[4,9,128]{2,1,0:T(8,128)S(1)} %maximum_select_fusion.3), channel_id=1, source_target_pairs={{0,4},{1,5},{2,6},{3,7},{4,0},{5,1},{6,2},{7,3},{8,12},{9,13},{10,... | collective-permute-start | bytes 55304 | tf_op jit(solution)/shard_map/ppermute | solution.py:44
  54.9 3.7 %collective-permute-start.4 = (f32[5,2,32,128]{3,2,1,0:T(8,128)S(1)}, f32[5,2,32,128]{3,2,1,0:T(8,128)S(1)}, u32[]{:S(2)}, u32[]{:S(2)}) collective-permute-start(f32[5,2,32,128]{3,2,1,0:T(8,128)S(1)} %slice.176), channel_id=1, source_target_pairs={{0,8},{1,9},{2,10},{3,11},{4,12},{5,13},{6,14},{7,15}} | collective-permute-start | bytes 491528 | tf_op jit(solution)/shard_map/ppermute | solution.py:132
  55.6 3.8 %collective-permute-start.7 = (f32[7,2,32,128]{3,2,1,0:T(8,128)S(1)}, f32[7,2,32,128]{3,2,1,0:T(8,128)S(1)}, u32[]{:S(2)}, u32[]{:S(2)}) collective-permute-start(f32[7,2,32,128]{3,2,1,0:T(8,128)S(1)} %slice.177), channel_id=1, source_target_pairs={{0,8},{1,9},{2,10},{3,11},{4,12},{5,13},{6,14},{7,15}} | collective-permute-start | bytes 688136 | tf_op jit(solution)/shard_map/ppermute | solution.py:132
  56.3 3.9 %collective-permute-start.10 = (f32[9,2,32,128]{3,2,1,0:T(8,128)S(1)}, f32[9,2,32,128]{3,2,1,0:T(8,128)S(1)}, u32[]{:S(2)}, u32[]{:S(2)}) collective-permute-start(f32[9,2,32,128]{3,2,1,0:T(8,128)S(1)} %slice.178), channel_id=1, source_target_pairs={{0,8},{1,9},{2,10},{3,11},{4,12},{5,13},{6,14},{7,15}} | collective-permute-start | bytes 884744 | tf_op jit(solution)/shard_map/ppermute | solution.py:132
  57.0 5.4 %collective-permute-start.13 = (f32[11,2,32,128]{3,2,1,0:T(8,128)S(1)}, f32[11,2,32,128]{3,2,1,0:T(8,128)S(1)}, u32[]{:S(2)}, u32[]{:S(2)}) collective-permute-start(f32[11,2,32,128]{3,2,1,0:T(8,128)S(1)} %slice.179), channel_id=1, source_target_pairs={{0,8},{1,9},{2,10},{3,11},{4,12},{5,13},{6,14},{7,15}} | collective-permute-start | bytes 1081352 | tf_op jit(solution)/shard_map/ppermute | solution.py:132
  58.7 2.3 %collective-permute-start.5 = (f32[5,2,32,128]{3,2,1,0:T(8,128)S(1)}, f32[5,2,32,128]{3,2,1,0:T(8,128)S(1)}, u32[]{:S(2)}, u32[]{:S(2)}) collective-permute-start(f32[5,2,32,128]{3,2,1,0:T(8,128)S(1)} %multiply_add_fusion.11), channel_id=1, source_target_pairs={{8,16},{9,17},{10,18},{11,19},{12,20},{13,21},{14,22},{15,23}} | collective-permute-start | bytes 491528 | tf_op jit(solution)/shard_map/ppermute | solution.py:132
  59.5 3.7 %collective-permute-start.8 = (f32[7,2,32,128]{3,2,1,0:T(8,128)S(1)}, f32[7,2,32,128]{3,2,1,0:T(8,128)S(1)}, u32[]{:S(2)}, u32[]{:S(2)}) collective-permute-start(f32[7,2,32,128]{3,2,1,0:T(8,128)S(1)} %multiply_add_fusion.8), channel_id=1, source_target_pairs={{8,16},{9,17},{10,18},{11,19},{12,20},{13,21},{14,22},{15,23}} | collective-permute-start | bytes 688136 | tf_op jit(solution)/shard_map/ppermute | solution.py:132
  60.3 17.1 %collective-permute-start.11 = (f32[9,2,32,128]{3,2,1,0:T(8,128)S(1)}, f32[9,2,32,128]{3,2,1,0:T(8,128)S(1)}, u32[]{:S(2)}, u32[]{:S(2)}) collective-permute-start(f32[9,2,32,128]{3,2,1,0:T(8,128)S(1)} %multiply_add_fusion.5), channel_id=1, source_target_pairs={{8,16},{9,17},{10,18},{11,19},{12,20},{13,21},{14,22},{15,23}} | collective-permute-start | bytes 884744 | tf_op jit(solution)/shard_map/ppermute | solution.py:132
  61.1 16.2 %collective-permute-start.6 = (f32[5,2,32,128]{3,2,1,0:T(8,128)S(1)}, f32[5,2,32,128]{3,2,1,0:T(8,128)S(1)}, u32[]{:S(2)}, u32[]{:S(2)}) collective-permute-start(f32[5,2,32,128]{3,2,1,0:T(8,128)S(1)} %multiply_add_fusion.10), channel_id=1, source_target_pairs={{16,24},{17,25},{18,26},{19,27},{20,28},{21,29},{22,30},{23,31}} | collective-permute-start | bytes 491528 | tf_op jit(solution)/shard_map/ppermute | solution.py:132
  62.5 16.3 %collective-permute-start.14 = (f32[11,2,32,128]{3,2,1,0:T(8,128)S(1)}, f32[11,2,32,128]{3,2,1,0:T(8,128)S(1)}, u32[]{:S(2)}, u32[]{:S(2)}) collective-permute-start(f32[11,2,32,128]{3,2,1,0:T(8,128)S(1)} %multiply_add_fusion.2), channel_id=1, source_target_pairs={{8,16},{9,17},{10,18},{11,19},{12,20},{13,21},{14,22},{15,23}} | collective-permute-start | bytes 1081352 | tf_op jit(solution)/shard_map/ppermute | solution.py:132
  63.3 19.6 %collective-permute-start.9 = (f32[7,2,32,128]{3,2,1,0:T(8,128)S(1)}, f32[7,2,32,128]{3,2,1,0:T(8,128)S(1)}, u32[]{:S(2)}, u32[]{:S(2)}) collective-permute-start(f32[7,2,32,128]{3,2,1,0:T(8,128)S(1)} %multiply_add_fusion.7), channel_id=1, source_target_pairs={{16,24},{17,25},{18,26},{19,27},{20,28},{21,29},{22,30},{23,31}} | collective-permute-start | bytes 688136 | tf_op jit(solution)/shard_map/ppermute | solution.py:132
  77.5 11.0 %collective-permute-start.12 = (f32[9,2,32,128]{3,2,1,0:T(8,128)S(1)}, f32[9,2,32,128]{3,2,1,0:T(8,128)S(1)}, u32[]{:S(2)}, u32[]{:S(2)}) collective-permute-start(f32[9,2,32,128]{3,2,1,0:T(8,128)S(1)} %multiply_add_fusion.4), channel_id=1, source_target_pairs={{16,24},{17,25},{18,26},{19,27},{20,28},{21,29},{22,30},{23,31}} | collective-permute-start | bytes 884744 | tf_op jit(solution)/shard_map/ppermute | solution.py:132
  78.9 18.4 %collective-permute-start.15 = (f32[11,2,32,128]{3,2,1,0:T(8,128)S(1)}, f32[11,2,32,128]{3,2,1,0:T(8,128)S(1)}, u32[]{:S(2)}, u32[]{:S(2)}) collective-permute-start(f32[11,2,32,128]{3,2,1,0:T(8,128)S(1)} %multiply_add_fusion.1), channel_id=1, source_target_pairs={{16,24},{17,25},{18,26},{19,27},{20,28},{21,29},{22,30},{23,31}} | collective-permute-start | bytes 1081352 | tf_op jit(solution)/shard_map/ppermute | solution.py:132

commit v3 on v2

--- a/solution.py
+++ b/solution.py
@@ -87,17 +87,29 @@
 
     own_columns = jnp.sum(own_part, axis=3).reshape(bins, -1)
     cols = own_columns.shape[1]
-    packed = jnp.concatenate(
-        [own_columns, jnp.concatenate([chain, gamma_yield[0]]).reshape(1, -1)[:, :cols]], axis=0
-    ) if cols == 2 * bins else None
-    everyone = gather_all(packed, "species")
+    extra = jnp.zeros((2, cols), jnp.float32).at[0, :bins].set(chain).at[1, :bins].set(gamma_yield[0])
+    packed = jnp.concatenate([own_columns, extra], axis=0)
+    me_g = lax.axis_index("species")
+    everyone = packed[None]
+    span = 1
+    while span < groups:
+        other = lax.ppermute(everyone, "species", [(i, i ^ span) for i in range(groups)])
+        if span == 1:
+            own_part, other = lax.optimization_barrier((own_part, other))
+        low = (me_g & span) == 0
+        everyone = jnp.where(
+            low,
+            jnp.concatenate([everyone, other], axis=0),
+            jnp.concatenate([other, everyone], axis=0),
+        )
+        span *= 2
     sums = everyone[0, :bins]
     total = jnp.zeros((cols,), jnp.float32)
     for group in range(groups):
         if group > 0:
             sums = everyone[group, bins, :bins][:, None] * sums + everyone[group, :bins]
         weighted = jnp.dot(
-            everyone[group, bins, bins:], sums, precision=HIGH, preferred_element_type=jnp.float32
+            everyone[group, bins + 1, :bins], sums, precision=HIGH, preferred_element_type=jnp.float32
         )
         emission = lax.reduce_precision(weighted / (bins * depth), exponent_bits=8, mantissa_bits=7)
         total = total + emission
@@ -106,18 +118,7 @@
     )
     lines, pixels = contribution.shape
     ids = jnp.zeros((1, pixels), jnp.float32).at[0, :lines].set(sky_blocks[0].astype(jnp.float32))
-    gathered = gather_all(jnp.concatenate([contribution, ids], axis=0), "space")
-    mine = lax.axis_index("space") * rows + jnp.arange(rows, dtype=jnp.int32)
-    onehot = (
-        gathered[:, lines, :lines].reshape(1, tiles * lines) == mine.astype(jnp.float32)[:, None]
-    ).astype(jnp.float32)
-    sky = jnp.dot(
-        onehot,
-        gathered[:, :lines].reshape(tiles * lines, pixels),
-        precision=HIGH,
-        preferred_element_type=jnp.float32,
-    )
-
+    payload = jnp.concatenate([contribution, ids], axis=0)
     base = bins // CHUNKS
     bounds = [0]
     for c in range(CHUNKS):
@@ -130,8 +131,22 @@
             s = wave - c
             if 0 <= s < groups - 1:
                 arrived = lax.ppermute(pieces[c], "species", [(s, s + 1)])
+                if wave == 0:
+                    payload, arrived = lax.optimization_barrier((payload, arrived))
                 pieces[c] = pieces[c] + scales[c] * arrived
     carried = jnp.concatenate(pieces, axis=0)
+    gathered = gather_all(payload, "space")
+    mine = lax.axis_index("space") * rows + jnp.arange(rows, dtype=jnp.int32)
+    onehot = (
+        gathered[:, lines, :lines].reshape(1, tiles * lines) == mine.astype(jnp.float32)[:, None]
+    ).astype(jnp.float32)
+    sky = jnp.dot(
+        onehot,
+        gathered[:, :lines].reshape(tiles * lines, pixels),
+        precision=HIGH,
+        preferred_element_type=jnp.float32,
+    )
+
     return (carried[None], sky)
 
 

time: 98.9 us -> 98.3 us (level)
  the two profiles are of different devices: /device:TPU:26 before, /device:TPU:28 now
where the time goes in v3:
time: 98.3 us; the launch traced here: 97.9 us
  waiting for transfers between devices  61.1 us (62%)
  starting transfers between devices  23.8 us (24%)
  other arithmetic  5.66 us (6%)
  matrix products  3.36 us (3%)
  local copies, waits for them, and re-layouts  2.78 us (3%)
  between operations  1.15 us (1%)
    ppermute x12, waiting for transfers between devices, body(): arrived = lax.ppermute(pieces[c], 'species', [(s, s + 1)])  30.5 us
    ppermute x2, waiting for transfers between devices, padded_2(): lax.ppermute(head, axis, [((i + 1) % count, i) for i in range(ends)])  15.1 us
    ppermute x12, starting transfers between devices, body(): arrived = lax.ppermute(pieces[c], 'species', [(s, s + 1)])  10.6 us
    ppermute x2, waiting for transfers between devices, body(): lax.ppermute(everyone, 'species', [(i, i ^ span) for i in range(groups)])  6.36 us
    ppermute x2, waiting for transfers between devices, padded_2(): lax.ppermute(tail, axis, [(i, (i + 1) % count) for i in range(ends)])  5.04 us
    ppermute x2, starting transfers between devices, padded_2(): lax.ppermute(head, axis, [((i + 1) % count, i) for i in range(ends)])  4.7 us
    ppermute x2, starting transfers between devices, padded_2(): lax.ppermute(tail, axis, [(i, (i + 1) % count) for i in range(ends)])  4.33 us
    ppermute x3, waiting for transfers between devices, gather_all(): other = lax.ppermute(held, axis, [(i, i ^ span) for i in range(count)])  4.22 us
  transfers between devices with their start and end apart: 21, of which 12 were waited for; matrix products, arithmetic and copies ran while one was open for 5% of the time, Pallas kernels for 0%

profile of v3, /device:TPU:28, one launch (start us, length us, event | category | flops | bytes accessed | tf_op | source)
XLA Modules:
  0.0 97.9 jit_solution(7996735586984374828)
XLA Ops:
  0.7 1.4 %fusion.45 = (f32[32,1,32,128]{3,2,1,0:T(8,128)S(1)}, f32[32,1,32,128]{3,2,1,0:T(8,128)S(1)}) fusion(f32[32,2,32,128]{3,2,1,0:T(8,128)} %bitcast.112), kind=kLoop, calls=%fused_computation.104 | loop fusion | bytes 2097152 | tf_op jit(solution)/shard_map/slice | solution.py:16
  2.1 2.8 %collective-permute-start = (f32[32,1,32,128]{3,2,1,0:T(8,128)S(1)}, f32[32,1,32,128]{3,2,1,0:T(8,128)S(1)}, u32[]{:S(2)}, u32[]{:S(2)}) collective-permute-start(f32[32,1,32,128]{3,2,1,0:T(8,128)S(1)} %get-tuple-element.50), channel_id=1, source_target_pairs={{1,0},{2,1},{3,2},{4,3},{5,4},{6,5},{7,6},{9,8},{10,9},{11,10},{12... | collective-permute-start | bytes 1572872 | tf_op jit(solution)/shard_map/ppermute | solution.py:22
  4.8 1.9 %collective-permute-start.1 = (f32[32,1,32,128]{3,2,1,0:T(8,128)S(1)}, f32[32,1,32,128]{3,2,1,0:T(8,128)S(1)}, u32[]{:S(2)}, u32[]{:S(2)}) collective-permute-start(f32[32,1,32,128]{3,2,1,0:T(8,128)S(1)} %get-tuple-element.51), channel_id=1, source_target_pairs={{0,1},{1,2},{2,3},{3,4},{4,5},{5,6},{6,7},{8,9},{9,10},{10,11},{11... | collective-permute-start | bytes 1572872 | tf_op jit(solution)/shard_map/ppermute | solution.py:20
  6.8 8.3 %collective-permute-done = f32[32,1,32,128]{3,2,1,0:T(8,128)S(1)} collective-permute-done((f32[32,1,32,128]{3,2,1,0:T(8,128)S(1)}, f32[32,1,32,128]{3,2,1,0:T(8,128)S(1)}, u32[]{:S(2)}, u32[]{:S(2)}) %collective-permute-start) | collective-permute-done | bytes 524320 | tf_op jit(solution)/shard_map/ppermute | solution.py:22
  15.1 3.1 %collective-permute-done.1 = f32[32,1,32,128]{3,2,1,0:T(8,128)S(1)} collective-permute-done((f32[32,1,32,128]{3,2,1,0:T(8,128)S(1)}, f32[32,1,32,128]{3,2,1,0:T(8,128)S(1)}, u32[]{:S(2)}, u32[]{:S(2)}) %collective-permute-start.1) | collective-permute-done | bytes 524320 | tf_op jit(solution)/shard_map/ppermute | solution.py:20
  18.2 0.8 fusion.12
  19.1 1.9 %collective-permute-start.2 = (f32[32,1,32,128]{3,2,1,0:T(8,128)S(1)}, f32[32,1,32,128]{3,2,1,0:T(8,128)S(1)}, u32[]{:S(2)}, u32[]{:S(2)}) collective-permute-start(f32[32,1,32,128]{3,2,1,0:T(8,128)S(1)} %get-tuple-element.48), channel_id=1, source_target_pairs={{1,0},{2,1},{3,2},{4,3},{5,4},{6,5},{7,6},{9,8},{10,9},{11,10},{12... | collective-permute-start | bytes 1572872 | tf_op jit(solution)/shard_map/ppermute | solution.py:22
  21.0 2.4 %collective-permute-start.3 = (f32[32,1,32,128]{3,2,1,0:T(8,128)S(1)}, f32[32,1,32,128]{3,2,1,0:T(8,128)S(1)}, u32[]{:S(2)}, u32[]{:S(2)}) collective-permute-start(f32[32,1,32,128]{3,2,1,0:T(8,128)S(1)} %get-tuple-element.49), channel_id=1, source_target_pairs={{0,1},{1,2},{2,3},{3,4},{4,5},{5,6},{6,7},{8,9},{9,10},{10,11},{11... | collective-permute-start | bytes 1572872 | tf_op jit(solution)/shard_map/ppermute | solution.py:20
  23.7 6.7 %collective-permute-done.2 = f32[32,1,32,128]{3,2,1,0:T(8,128)S(1)} collective-permute-done((f32[32,1,32,128]{3,2,1,0:T(8,128)S(1)}, f32[32,1,32,128]{3,2,1,0:T(8,128)S(1)}, u32[]{:S(2)}, u32[]{:S(2)}) %collective-permute-start.2) | collective-permute-done | bytes 524320 | tf_op jit(solution)/shard_map/ppermute | solution.py:22
  30.4 2.0 %collective-permute-done.3 = f32[32,1,32,128]{3,2,1,0:T(8,128)S(1)} collective-permute-done((f32[32,1,32,128]{3,2,1,0:T(8,128)S(1)}, f32[32,1,32,128]{3,2,1,0:T(8,128)S(1)}, u32[]{:S(2)}, u32[]{:S(2)}) %collective-permute-start.3) | collective-permute-done | bytes 524320 | tf_op jit(solution)/shard_map/ppermute | solution.py:20
  32.4 0.8 fusion.13
  33.2 1.7 %convolution_bitcast_fusion = f32[4,8,64,128]{3,1,2,0:T(8,128)S(1)} fusion(f32[4,8,64,128]{3,2,1,0:T(8,128)S(1)} %bitcast.114, f32[1,32,32]{2,1,0:T(8,128)S(1)} %copy-done.3), kind=kOutput, calls=%fused_computation.10 | convolution fusion | flops 100663296 | bytes 2101248 | tf_op jit(solution)/shard_map/dot_general | solution.py:79
  37.4 2.8 %collective-permute-done.4 = f32[1,34,64]{2,1,0:T(8,128)S(1)} collective-permute-done((f32[1,34,64]{2,1,0:T(8,128)S(1)}, f32[1,34,64]{2,1,0:T(8,128)S(1)}, u32[]{:S(2)}, u32[]{:S(2)}) %collective-permute-start.4) | collective-permute-done | bytes 8736 | tf_op jit(solution)/shard_map/ppermute | solution.py:96
  41.9 3.6 %collective-permute-done.5 = f32[2,34,64]{2,1,0:T(8,128)S(1)} collective-permute-done((f32[2,34,64]{2,1,0:T(8,128)S(1)}, f32[2,34,64]{2,1,0:T(8,128)S(1)}, u32[]{:S(2)}, u32[]{:S(2)}) %collective-permute-start.5) | collective-permute-done | bytes 17440 | tf_op jit(solution)/shard_map/ppermute | solution.py:96
  46.6 1.1 %collective-permute-done.18 = f32[1,9,128]{2,1,0:T(8,128)S(1)} collective-permute-done((f32[1,9,128]{2,1,0:T(8,128)S(1)}, f32[1,9,128]{2,1,0:T(8,128)S(1)}, u32[]{:S(2)}, u32[]{:S(2)}) %collective-permute-start.18) | collective-permute-done | bytes 4640 | tf_op jit(solution)/shard_map/ppermute | solution.py:44
  47.7 3.2 %collective-permute-start.19 = (f32[2,9,128]{2,1,0:T(8,128)S(1)}, f32[2,9,128]{2,1,0:T(8,128)S(1)}, u32[]{:S(2)}, u32[]{:S(2)}) collective-permute-start(f32[2,9,128]{2,1,0:T(8,128)S(1)} %maximum_select_fusion.4), channel_id=1, source_target_pairs={{0,2},{1,3},{2,0},{3,1},{4,6},{5,7},{6,4},{7,5},{8,10},{9,11},{10,... | collective-permute-start | bytes 27656 | tf_op jit(solution)/shard_map/ppermute | solution.py:44
  51.0 0.7 collective-permute-start.9
  51.7 0.7 collective-permute-start.12
  52.4 0.7 collective-permute-start.15
  53.9 3.1 %collective-permute-done.20 = f32[4,9,128]{2,1,0:T(8,128)S(1)} collective-permute-done((f32[4,9,128]{2,1,0:T(8,128)S(1)}, f32[4,9,128]{2,1,0:T(8,128)S(1)}, u32[]{:S(2)}, u32[]{:S(2)}) %collective-permute-start.20) | collective-permute-done | bytes 18464 | tf_op jit(solution)/shard_map/ppermute | solution.py:44
  57.2 0.8 fusion.30
  58.9 0.7 collective-permute-start.13
  59.7 1.3 %collective-permute-start.8 = (f32[5,2,32,128]{3,2,1,0:T(8,128)S(1)}, f32[5,2,32,128]{3,2,1,0:T(8,128)S(1)}, u32[]{:S(2)}, u32[]{:S(2)}) collective-permute-start(f32[5,2,32,128]{3,2,1,0:T(8,128)S(1)} %multiply_add_fusion.10), channel_id=1, source_target_pairs={{16,24},{17,25},{18,26},{19,27},{20,28},{21,29},{22,30},{23,31}} | collective-permute-start | bytes 491528 | tf_op jit(solution)/shard_map/ppermute | solution.py:133
  61.1 0.7 collective-permute-start.16
  61.9 1.3 %collective-permute-start.11 = (f32[7,2,32,128]{3,2,1,0:T(8,128)S(1)}, f32[7,2,32,128]{3,2,1,0:T(8,128)S(1)}, u32[]{:S(2)}, u32[]{:S(2)}) collective-permute-start(f32[7,2,32,128]{3,2,1,0:T(8,128)S(1)} %multiply_add_fusion.7), channel_id=1, source_target_pairs={{16,24},{17,25},{18,26},{19,27},{20,28},{21,29},{22,30},{23,31}} | collective-permute-start | bytes 688136 | tf_op jit(solution)/shard_map/ppermute | solution.py:133
  63.2 7.6 %collective-permute-done.8 = f32[5,2,32,128]{3,2,1,0:T(8,128)S(1)} collective-permute-done((f32[5,2,32,128]{3,2,1,0:T(8,128)S(1)}, f32[5,2,32,128]{3,2,1,0:T(8,128)S(1)}, u32[]{:S(2)}, u32[]{:S(2)}) %collective-permute-start.8) | collective-permute-done | bytes 163872 | tf_op jit(solution)/shard_map/ppermute | solution.py:133
  71.0 1.3 %collective-permute-start.14 = (f32[9,2,32,128]{3,2,1,0:T(8,128)S(1)}, f32[9,2,32,128]{3,2,1,0:T(8,128)S(1)}, u32[]{:S(2)}, u32[]{:S(2)}) collective-permute-start(f32[9,2,32,128]{3,2,1,0:T(8,128)S(1)} %multiply_add_fusion.4), channel_id=1, source_target_pairs={{16,24},{17,25},{18,26},{19,27},{20,28},{21,29},{22,30},{23,31}} | collective-permute-start | bytes 884744 | tf_op jit(solution)/shard_map/ppermute | solution.py:133
  72.4 1.3 %collective-permute-start.17 = (f32[11,2,32,128]{3,2,1,0:T(8,128)S(1)}, f32[11,2,32,128]{3,2,1,0:T(8,128)S(1)}, u32[]{:S(2)}, u32[]{:S(2)}) collective-permute-start(f32[11,2,32,128]{3,2,1,0:T(8,128)S(1)} %multiply_add_fusion.1), channel_id=1, source_target_pairs={{16,24},{17,25},{18,26},{19,27},{20,28},{21,29},{22,30},{23,31}} | collective-permute-start | bytes 1081352 | tf_op jit(solution)/shard_map/ppermute | solution.py:133
  73.7 3.5 %collective-permute-done.11 = f32[7,2,32,128]{3,2,1,0:T(8,128)S(1)} collective-permute-done((f32[7,2,32,128]{3,2,1,0:T(8,128)S(1)}, f32[7,2,32,128]{3,2,1,0:T(8,128)S(1)}, u32[]{:S(2)}, u32[]{:S(2)}) %collective-permute-start.11) | collective-permute-done | bytes 229408 | tf_op jit(solution)/shard_map/ppermute | solution.py:133
  77.3 8.0 %collective-permute-done.14 = f32[9,2,32,128]{3,2,1,0:T(8,128)S(1)} collective-permute-done((f32[9,2,32,128]{3,2,1,0:T(8,128)S(1)}, f32[9,2,32,128]{3,2,1,0:T(8,128)S(1)}, u32[]{:S(2)}, u32[]{:S(2)}) %collective-permute-start.14) | collective-permute-done | bytes 294944 | tf_op jit(solution)/shard_map/ppermute | solution.py:133
  85.4 11.3 %collective-permute-done.17 = f32[11,2,32,128]{3,2,1,0:T(8,128)S(1)} collective-permute-done((f32[11,2,32,128]{3,2,1,0:T(8,128)S(1)}, f32[11,2,32,128]{3,2,1,0:T(8,128)S(1)}, u32[]{:S(2)}, u32[]{:S(2)}) %collective-permute-start.17) | collective-permute-done | bytes 360480 | tf_op jit(solution)/shard_map/ppermute | solution.py:133
  96.8 1.1 %maximum_bitcast_fusion = f32[1,32,2,32,128]{4,3,2,1,0:T(8,128)} fusion(f32[11,2,32,128]{3,2,1,0:T(8,128)S(1)} %multiply_add_fusion, f32[9,2,32,128]{3,2,1,0:T(8,128)S(1)} %multiply_add_fusion.3, f32[7,2,32,128]{3,2,1,0:T(8,128)S(1)} %multiply_add_fusion.6, f32[5,2,32,128]{3,2,1,0:T(8,128)S(1)} %multiply_add_fusion.9), kind=kLoop, calls=%fused_computation.47 | loop fusion | flops 786432 | bytes 2097152 | tf_op jit(solution)/shard_map/broadcast_in_dim | solution.py:150
  (79 shorter events, 8.4 us)
Async XLA Ops:
  0.6 45.7 %copy-start = (bf16[1,8,64,128]{3,2,1,0:T(8,128)(2,1)S(1)}, bf16[1,8,64,128]{3,2,1,0:T(8,128)(2,1)}, u32[]{:S(2)}) copy-start(bf16[1,8,64,128]{3,2,1,0:T(8,128)(2,1)} %param.22) | copy-start | bytes 393220
  0.6 17.5 %copy-start.1 = (f32[1,32,2,32,128]{4,3,2,1,0:T(8,128)S(1)}, f32[1,32,2,32,128]{4,3,2,1,0:T(8,128)}, u32[]{:S(2)}) copy-start(f32[1,32,2,32,128]{4,3,2,1,0:T(8,128)} %param.15) | copy-start | bytes 3145732
  0.7 17.5 %copy-start.2 = (f32[2,32,128]{2,1,0:T(8,128)S(1)}, f32[2,32,128]{2,1,0:T(8,128)}, u32[]{:S(2)}) copy-start(f32[2,32,128]{2,1,0:T(8,128)} %param.16) | copy-start | bytes 98308
  0.7 17.5 %copy-start.4 = (f32[1,32]{1,0:T(1,128)S(1)}, f32[1,32]{1,0:T(1,128)}, u32[]{:S(2)}) copy-start(f32[1,32]{1,0:T(1,128)} %param.17) | copy-start | bytes 388
  2.1 13.0 %collective-permute-start = (f32[32,1,32,128]{3,2,1,0:T(8,128)S(1)}, f32[32,1,32,128]{3,2,1,0:T(8,128)S(1)}, u32[]{:S(2)}, u32[]{:S(2)}) collective-permute-start(f32[32,1,32,128]{3,2,1,0:T(8,128)S(1)} %get-tuple-element.50), channel_id=1, source_target_pairs={{1,0},{2,1},{3,2},{4,3},{5,4},{6,5},{7,6},{9,8},{10,9},{11,10},{12... | collective-permute-start | bytes 1572872 | tf_op jit(solution)/shard_map/ppermute | solution.py:22
  4.8 13.3 %collective-permute-start.1 = (f32[32,1,32,128]{3,2,1,0:T(8,128)S(1)}, f32[32,1,32,128]{3,2,1,0:T(8,128)S(1)}, u32[]{:S(2)}, u32[]{:S(2)}) collective-permute-start(f32[32,1,32,128]{3,2,1,0:T(8,128)S(1)} %get-tuple-element.51), channel_id=1, source_target_pairs={{0,1},{1,2},{2,3},{3,4},{4,5},{5,6},{6,7},{8,9},{9,10},{10,11},{11... | collective-permute-start | bytes 1572872 | tf_op jit(solution)/shard_map/ppermute | solution.py:20
  19.0 4.5 %copy-start.7 = (f32[1,32]{1,0:T(1,128)S(1)}, f32[1,32]{1,0:T(1,128)}, u32[]{:S(2)}) copy-start(f32[1,32]{1,0:T(1,128)} %param.19) | copy-start | bytes 388
  19.0 4.5 %copy-start.6 = (f32[1,32]{1,0:T(1,128)S(1)}, f32[1,32]{1,0:T(1,128)}, u32[]{:S(2)}) copy-start(f32[1,32]{1,0:T(1,128)} %param.21) | copy-start | bytes 388
  19.1 11.4 %collective-permute-start.2 = (f32[32,1,32,128]{3,2,1,0:T(8,128)S(1)}, f32[32,1,32,128]{3,2,1,0:T(8,128)S(1)}, u32[]{:S(2)}, u32[]{:S(2)}) collective-permute-start(f32[32,1,32,128]{3,2,1,0:T(8,128)S(1)} %get-tuple-element.48), channel_id=1, source_target_pairs={{1,0},{2,1},{3,2},{4,3},{5,4},{6,5},{7,6},{9,8},{10,9},{11,10},{12... | collective-permute-start | bytes 1572872 | tf_op jit(solution)/shard_map/ppermute | solution.py:22
  21.0 11.4 %collective-permute-start.3 = (f32[32,1,32,128]{3,2,1,0:T(8,128)S(1)}, f32[32,1,32,128]{3,2,1,0:T(8,128)S(1)}, u32[]{:S(2)}, u32[]{:S(2)}) collective-permute-start(f32[32,1,32,128]{3,2,1,0:T(8,128)S(1)} %get-tuple-element.49), channel_id=1, source_target_pairs={{0,1},{1,2},{2,3},{3,4},{4,5},{5,6},{6,7},{8,9},{9,10},{10,11},{11... | collective-permute-start | bytes 1572872 | tf_op jit(solution)/shard_map/ppermute | solution.py:20
  23.7 9.5 %copy-start.3 = (f32[1,32,32]{2,1,0:T(8,128)S(1)}, f32[1,32,32]{2,1,0:T(8,128)}, u32[]{:S(2)}) copy-start(f32[1,32,32]{2,1,0:T(8,128)} %param.18) | copy-start | bytes 12292
  34.9 0.7 copy-start.5
  35.5 5.0 %copy-start.8 = (s32[1,8]{1,0:T(1,128)S(1)}, s32[1,8]{1,0:T(1,128)}, u32[]{:S(2)}) copy-start(s32[1,8]{1,0:T(1,128)} %param.23) | copy-start | bytes 100
  36.1 4.0 %collective-permute-start.4 = (f32[1,34,64]{2,1,0:T(8,128)S(1)}, f32[1,34,64]{2,1,0:T(8,128)S(1)}, u32[]{:S(2)}, u32[]{:S(2)}) collective-permute-start(f32[1,34,64]{2,1,0:T(8,128)S(1)} %maximum_bitcast_fusion.1), channel_id=1, source_target_pairs={{0,8},{8,0},{16,24},{24,16},{1,9},{9,1},{17,25},{25,17},{2,10},{10... | collective-permute-start | bytes 26120 | tf_op jit(solution)/shard_map/ppermute | solution.py:96
  40.2 5.3 %collective-permute-start.5 = (f32[2,34,64]{2,1,0:T(8,128)S(1)}, f32[2,34,64]{2,1,0:T(8,128)S(1)}, u32[]{:S(2)}, u32[]{:S(2)}) collective-permute-start(f32[2,34,64]{2,1,0:T(8,128)S(1)} %maximum_select_fusion.2), channel_id=1, source_target_pairs={{0,16},{8,24},{16,0},{24,8},{1,17},{9,25},{17,1},{25,9},{2,18},{10... | collective-permute-start | bytes 52232 | tf_op jit(solution)/shard_map/ppermute | solution.py:96
  41.2 5.2 %collective-permute-start.6 = (f32[5,2,32,128]{3,2,1,0:T(8,128)S(1)}, f32[5,2,32,128]{3,2,1,0:T(8,128)S(1)}, u32[]{:S(2)}, u32[]{:S(2)}) collective-permute-start(f32[5,2,32,128]{3,2,1,0:T(8,128)S(1)} %slice.186), channel_id=1, source_target_pairs={{0,8},{1,9},{2,10},{3,11},{4,12},{5,13},{6,14},{7,15}} | collective-permute-start | bytes 491528 | tf_op jit(solution)/shard_map/ppermute | solution.py:133
  46.5 1.2 %collective-permute-start.18 = (f32[1,9,128]{2,1,0:T(8,128)S(1)}, f32[1,9,128]{2,1,0:T(8,128)S(1)}, u32[]{:S(2)}, u32[]{:S(2)}) collective-permute-start(f32[1,9,128]{2,1,0:T(8,128)S(1)} %bitcast.115), channel_id=1, source_target_pairs={{0,1},{1,0},{2,3},{3,2},{4,5},{5,4},{6,7},{7,6},{8,9},{9,8},{10,11... | collective-permute-start | bytes 13832 | tf_op jit(solution)/shard_map/ppermute | solution.py:44
  47.7 5.3 %collective-permute-start.19 = (f32[2,9,128]{2,1,0:T(8,128)S(1)}, f32[2,9,128]{2,1,0:T(8,128)S(1)}, u32[]{:S(2)}, u32[]{:S(2)}) collective-permute-start(f32[2,9,128]{2,1,0:T(8,128)S(1)} %maximum_select_fusion.4), channel_id=1, source_target_pairs={{0,2},{1,3},{2,0},{3,1},{4,6},{5,7},{6,4},{7,5},{8,10},{9,11},{10,... | collective-permute-start | bytes 27656 | tf_op jit(solution)/shard_map/ppermute | solution.py:44
  51.0 7.0 %collective-permute-start.9 = (f32[7,2,32,128]{3,2,1,0:T(8,128)S(1)}, f32[7,2,32,128]{3,2,1,0:T(8,128)S(1)}, u32[]{:S(2)}, u32[]{:S(2)}) collective-permute-start(f32[7,2,32,128]{3,2,1,0:T(8,128)S(1)} %slice.199), channel_id=1, source_target_pairs={{0,8},{1,9},{2,10},{3,11},{4,12},{5,13},{6,14},{7,15}} | collective-permute-start | bytes 688136 | tf_op jit(solution)/shard_map/ppermute | solution.py:133
  51.7 7.1 %collective-permute-start.12 = (f32[9,2,32,128]{3,2,1,0:T(8,128)S(1)}, f32[9,2,32,128]{3,2,1,0:T(8,128)S(1)}, u32[]{:S(2)}, u32[]{:S(2)}) collective-permute-start(f32[9,2,32,128]{3,2,1,0:T(8,128)S(1)} %slice.201), channel_id=1, source_target_pairs={{0,8},{1,9},{2,10},{3,11},{4,12},{5,13},{6,14},{7,15}} | collective-permute-start | bytes 884744 | tf_op jit(solution)/shard_map/ppermute | solution.py:133
  52.4 8.6 %collective-permute-start.15 = (f32[11,2,32,128]{3,2,1,0:T(8,128)S(1)}, f32[11,2,32,128]{3,2,1,0:T(8,128)S(1)}, u32[]{:S(2)}, u32[]{:S(2)}) collective-permute-start(f32[11,2,32,128]{3,2,1,0:T(8,128)S(1)} %slice.203), channel_id=1, source_target_pairs={{0,8},{1,9},{2,10},{3,11},{4,12},{5,13},{6,14},{7,15}} | collective-permute-start | bytes 1081352 | tf_op jit(solution)/shard_map/ppermute | solution.py:133
  53.1 4.0 %collective-permute-start.20 = (f32[4,9,128]{2,1,0:T(8,128)S(1)}, f32[4,9,128]{2,1,0:T(8,128)S(1)}, u32[]{:S(2)}, u32[]{:S(2)}) collective-permute-start(f32[4,9,128]{2,1,0:T(8,128)S(1)} %maximum_select_fusion.3), channel_id=1, source_target_pairs={{0,4},{1,5},{2,6},{3,7},{4,0},{5,1},{6,2},{7,3},{8,12},{9,13},{10,... | collective-permute-start | bytes 55304 | tf_op jit(solution)/shard_map/ppermute | solution.py:44
  53.2 6.3 %collective-permute-start.7 = (f32[5,2,32,128]{3,2,1,0:T(8,128)S(1)}, f32[5,2,32,128]{3,2,1,0:T(8,128)S(1)}, u32[]{:S(2)}, u32[]{:S(2)}) collective-permute-start(f32[5,2,32,128]{3,2,1,0:T(8,128)S(1)} %multiply_add_fusion.11), channel_id=1, source_target_pairs={{8,16},{9,17},{10,18},{11,19},{12,20},{13,21},{14,22},{15,23}} | collective-permute-start | bytes 491528 | tf_op jit(solution)/shard_map/ppermute | solution.py:133
  58.1 3.7 %collective-permute-start.10 = (f32[7,2,32,128]{3,2,1,0:T(8,128)S(1)}, f32[7,2,32,128]{3,2,1,0:T(8,128)S(1)}, u32[]{:S(2)}, u32[]{:S(2)}) collective-permute-start(f32[7,2,32,128]{3,2,1,0:T(8,128)S(1)} %multiply_add_fusion.8), channel_id=1, source_target_pairs={{8,16},{9,17},{10,18},{11,19},{12,20},{13,21},{14,22},{15,23}} | collective-permute-start | bytes 688136 | tf_op jit(solution)/shard_map/ppermute | solution.py:133
  58.9 12.0 %collective-permute-start.13 = (f32[9,2,32,128]{3,2,1,0:T(8,128)S(1)}, f32[9,2,32,128]{3,2,1,0:T(8,128)S(1)}, u32[]{:S(2)}, u32[]{:S(2)}) collective-permute-start(f32[9,2,32,128]{3,2,1,0:T(8,128)S(1)} %multiply_add_fusion.5), channel_id=1, source_target_pairs={{8,16},{9,17},{10,18},{11,19},{12,20},{13,21},{14,22},{15,23}} | collective-permute-start | bytes 884744 | tf_op jit(solution)/shard_map/ppermute | solution.py:133
  59.7 11.1 %collective-permute-start.8 = (f32[5,2,32,128]{3,2,1,0:T(8,128)S(1)}, f32[5,2,32,128]{3,2,1,0:T(8,128)S(1)}, u32[]{:S(2)}, u32[]{:S(2)}) collective-permute-start(f32[5,2,32,128]{3,2,1,0:T(8,128)S(1)} %multiply_add_fusion.10), channel_id=1, source_target_pairs={{16,24},{17,25},{18,26},{19,27},{20,28},{21,29},{22,30},{23,31}} | collective-permute-start | bytes 491528 | tf_op jit(solution)/shard_map/ppermute | solution.py:133
  61.1 11.2 %collective-permute-start.16 = (f32[11,2,32,128]{3,2,1,0:T(8,128)S(1)}, f32[11,2,32,128]{3,2,1,0:T(8,128)S(1)}, u32[]{:S(2)}, u32[]{:S(2)}) collective-permute-start(f32[11,2,32,128]{3,2,1,0:T(8,128)S(1)} %multiply_add_fusion.2), channel_id=1, source_target_pairs={{8,16},{9,17},{10,18},{11,19},{12,20},{13,21},{14,22},{15,23}} | collective-permute-start | bytes 1081352 | tf_op jit(solution)/shard_map/ppermute | solution.py:133
  61.9 15.3 %collective-permute-start.11 = (f32[7,2,32,128]{3,2,1,0:T(8,128)S(1)}, f32[7,2,32,128]{3,2,1,0:T(8,128)S(1)}, u32[]{:S(2)}, u32[]{:S(2)}) collective-permute-start(f32[7,2,32,128]{3,2,1,0:T(8,128)S(1)} %multiply_add_fusion.7), channel_id=1, source_target_pairs={{16,24},{17,25},{18,26},{19,27},{20,28},{21,29},{22,30},{23,31}} | collective-permute-start | bytes 688136 | tf_op jit(solution)/shard_map/ppermute | solution.py:133
  71.0 14.4 %collective-permute-start.14 = (f32[9,2,32,128]{3,2,1,0:T(8,128)S(1)}, f32[9,2,32,128]{3,2,1,0:T(8,128)S(1)}, u32[]{:S(2)}, u32[]{:S(2)}) collective-permute-start(f32[9,2,32,128]{3,2,1,0:T(8,128)S(1)} %multiply_add_fusion.4), channel_id=1, source_target_pairs={{16,24},{17,25},{18,26},{19,27},{20,28},{21,29},{22,30},{23,31}} | collective-permute-start | bytes 884744 | tf_op jit(solution)/shard_map/ppermute | solution.py:133
  72.4 24.3 %collective-permute-start.17 = (f32[11,2,32,128]{3,2,1,0:T(8,128)S(1)}, f32[11,2,32,128]{3,2,1,0:T(8,128)S(1)}, u32[]{:S(2)}, u32[]{:S(2)}) collective-permute-start(f32[11,2,32,128]{3,2,1,0:T(8,128)S(1)} %multiply_add_fusion.1), channel_id=1, source_target_pairs={{16,24},{17,25},{18,26},{19,27},{20,28},{21,29},{22,30},{23,31}} | collective-permute-start | bytes 1081352 | tf_op jit(solution)/shard_map/ppermute | solution.py:133

commit v4 on v3

--- a/solution.py
+++ b/solution.py
@@ -72,10 +72,20 @@
     depth = field.shape[3]
     rate = diff_rate[0][:, None, None, None]
     factor = rate * space_factor[None]
+    halo = SUBSTEPS
+    count = lax.axis_size("space")
+    mine = jnp.concatenate([field, space_factor[None]], axis=0)
+    from_left = lax.ppermute(
+        mine[:, mine.shape[1] - halo:], "space", [(i, i + 1) for i in range(count - 1)]
+    )
+    from_right = lax.ppermute(mine[:, :halo], "space", [(i + 1, i) for i in range(count - 1)])
+    wide = jnp.concatenate([from_left[:bins], field, from_right[:bins]], axis=1)
+    wide_factor = rate * jnp.concatenate([from_left[bins], space_factor, from_right[bins]], axis=0)[None]
     for step in range(SUBSTEPS):
-        wider = padded_2(field, (("space", 1),), 1)
-        beside = wider[:, 2:] + wider[:, :-2] + cross_sum(field)
-        field = field + factor * (beside - 6.0 * field)
+        inner = wide[:, 1:-1]
+        beside = wide[:, 2:] + wide[:, :-2] + cross_sum(inner)
+        wide = inner + wide_factor[:, 1 + step:wide_factor.shape[1] - 1 - step] * (beside - 6.0 * inner)
+    field = wide
     solved = jnp.dot(
         loss_inverse[0],
         field.reshape(bins, -1),

time: 98.3 us -> 97.2 us (0.989)
  the two profiles are of different devices: /device:TPU:28 before, /device:TPU:26 now
where the time goes in v4:
time: 97.2 us; the launch traced here: 96.2 us
  waiting for transfers between devices  64 us (66%)
  starting transfers between devices  17.2 us (18%)
  other arithmetic  8.83 us (9%)
  matrix products  3.35 us (3%)
  local copies, waits for them, and re-layouts  1.6 us (2%)
  between operations  1.19 us (1%)
    ppermute x12, waiting for transfers between devices, body(): arrived = lax.ppermute(pieces[c], 'species', [(s, s + 1)])  30.5 us
    ppermute x1, waiting for transfers between devices, body(): lax.ppermute(mine[:, mine.shape[1] - halo:], 'space', [(i, i + 1) for i i...  10.6 us
    ppermute x12, starting transfers between devices, body(): arrived = lax.ppermute(pieces[c], 'species', [(s, s + 1)])  10.6 us
    ppermute x1, waiting for transfers between devices, body(): lax.ppermute(mine[:, :halo], 'space', [(i + 1, i) for i in range(count -...  10.5 us
    ppermute x2, waiting for transfers between devices, body(): lax.ppermute(everyone, 'species', [(i, i ^ span) for i in range(groups)])  6.68 us
    ppermute x3, waiting for transfers between devices, gather_all(): other = lax.ppermute(held, axis, [(i, i ^ span) for i in range(count)])  5.7 us
    ppermute x1, starting transfers between devices, body(): lax.ppermute(mine[:, :halo], 'space', [(i + 1, i) for i in range(count -...  3.64 us
    add x2, other arithmetic, body(): inner + wide_factor[:, 1 + step:wide_factor.shape[1] - 1 - step] * (besid...  2.71 us
  transfers between devices with their start and end apart: 19, of which 11 were waited for; matrix products, arithmetic and copies ran while one was open for 5% of the time, Pallas kernels for 0%

profile of v4, /device:TPU:26, one launch (start us, length us, event | category | flops | bytes accessed | tf_op | source)
XLA Modules:
  0.0 96.2 jit_solution(15167437206044815547)
XLA Ops:
  0.7 1.4 %pad_maximum_fusion.2 = f32[33,2,32,128]{3,2,1,0:T(8,128)S(1)} fusion(f32[1,2,32,128]{3,2,1,0:T(8,128)} %bitcast.121, f32[32,2,32,128]{3,2,1,0:T(8,128)} %bitcast.116), kind=kLoop, calls=%fused_computation.36 | loop fusion | flops 270336 | bytes 2162688 | tf_op jit(solution)/shard_map/concatenate | solution.py:77
  2.0 1.9 %collective-permute-start = (f32[33,2,32,128]{3,2,1,0:T(8,128)S(1)}, f32[33,2,32,128]{3,2,1,0:T(8,128)S(1)}, u32[]{:S(2)}, u32[]{:S(2)}) collective-permute-start(f32[33,2,32,128]{3,2,1,0:T(8,128)S(1)} %pad_maximum_fusion.2), channel_id=1, source_target_pairs={{0,1},{1,2},{2,3},{3,4},{4,5},{5,6},{6,7},{8,9},{9,10},{10,11},{11... | collective-permute-start | bytes 3244040 | tf_op jit(solution)/shard_map/ppermute | solution.py:78
  4.0 3.6 %collective-permute-start.1 = (f32[33,2,32,128]{3,2,1,0:T(8,128)S(1)}, f32[33,2,32,128]{3,2,1,0:T(8,128)S(1)}, u32[]{:S(2)}, u32[]{:S(2)}) collective-permute-start(f32[33,2,32,128]{3,2,1,0:T(8,128)S(1)} %pad_maximum_fusion.2), channel_id=1, source_target_pairs={{1,0},{2,1},{3,2},{4,3},{5,4},{6,5},{7,6},{9,8},{10,9},{11,10},{12... | collective-permute-start | bytes 3244040 | tf_op jit(solution)/shard_map/ppermute | solution.py:81
  7.9 10.6 %collective-permute-done = f32[33,2,32,128]{3,2,1,0:T(8,128)S(1)} collective-permute-done((f32[33,2,32,128]{3,2,1,0:T(8,128)S(1)}, f32[33,2,32,128]{3,2,1,0:T(8,128)S(1)}, u32[]{:S(2)}, u32[]{:S(2)}) %collective-permute-start) | collective-permute-done | bytes 1081376 | tf_op jit(solution)/shard_map/ppermute | solution.py:78
  18.6 10.5 %collective-permute-done.1 = f32[33,2,32,128]{3,2,1,0:T(8,128)S(1)} collective-permute-done((f32[33,2,32,128]{3,2,1,0:T(8,128)S(1)}, f32[33,2,32,128]{3,2,1,0:T(8,128)S(1)}, u32[]{:S(2)}, u32[]{:S(2)}) %collective-permute-start.1) | collective-permute-done | bytes 1081376 | tf_op jit(solution)/shard_map/ppermute | solution.py:81
  30.4 2.0 %fusion.6 = f32[32,4,32,128]{3,2,1,0:T(8,128)S(1)} fusion(f32[32,4,32,128]{3,2,1,0:T(8,128)S(1)} %pad_maximum_fusion, f32[32,6,32,128]{3,2,1,0:T(8,128)S(1)} %broadcast_multiply_fusion, f32[32,2,32,128]{3,2,1,0:T(8,128)S(1)} %slice.216, f32[32,2,32,128]{3,2,1,0:T(8,128)S(1)} %bitcast.118, f32[32,2,32,128]{3,2,1,0:T(8,128)S(1)} %slice.215), kind=kLoop, calls=%fused_computation.14 | loop fusion | flops 5767168 | bytes 9437184 | tf_op jit(solution)/shard_map/add | solution.py:87
  32.5 0.7 fusion.25
  33.2 1.7 %convolution_bitcast_fusion = f32[4,8,64,128]{3,1,2,0:T(8,128)S(1)} fusion(f32[4,8,64,128]{3,2,1,0:T(8,128)S(1)} %bitcast.119, f32[1,32,32]{2,1,0:T(8,128)S(1)} %copy-done.3), kind=kOutput, calls=%fused_computation.19 | convolution fusion | flops 100663296 | bytes 2101248 | tf_op jit(solution)/shard_map/dot_general | solution.py:89
  37.0 2.6 %collective-permute-done.2 = f32[1,34,64]{2,1,0:T(8,128)S(1)} collective-permute-done((f32[1,34,64]{2,1,0:T(8,128)S(1)}, f32[1,34,64]{2,1,0:T(8,128)S(1)}, u32[]{:S(2)}, u32[]{:S(2)}) %collective-permute-start.2) | collective-permute-done | bytes 8736 | tf_op jit(solution)/shard_map/ppermute | solution.py:106
  40.0 0.6 broadcast_select_fusion
  40.7 0.7 collective-permute-start.4
  41.4 4.1 %collective-permute-done.3 = f32[2,34,64]{2,1,0:T(8,128)S(1)} collective-permute-done((f32[2,34,64]{2,1,0:T(8,128)S(1)}, f32[2,34,64]{2,1,0:T(8,128)S(1)}, u32[]{:S(2)}, u32[]{:S(2)}) %collective-permute-start.3) | collective-permute-done | bytes 17440 | tf_op jit(solution)/shard_map/ppermute | solution.py:106
  46.6 1.0 %collective-permute-done.16 = f32[1,9,128]{2,1,0:T(8,128)S(1)} collective-permute-done((f32[1,9,128]{2,1,0:T(8,128)S(1)}, f32[1,9,128]{2,1,0:T(8,128)S(1)}, u32[]{:S(2)}, u32[]{:S(2)}) %collective-permute-start.16) | collective-permute-done | bytes 4640 | tf_op jit(solution)/shard_map/ppermute | solution.py:44
  47.8 0.7 collective-permute-start.7
  48.5 0.7 collective-permute-start.10
  49.1 0.7 collective-permute-start.13
  49.8 1.6 %collective-permute-done.17 = f32[2,9,128]{2,1,0:T(8,128)S(1)} collective-permute-done((f32[2,9,128]{2,1,0:T(8,128)S(1)}, f32[2,9,128]{2,1,0:T(8,128)S(1)}, u32[]{:S(2)}, u32[]{:S(2)}) %collective-permute-start.17) | collective-permute-done | bytes 9248 | tf_op jit(solution)/shard_map/ppermute | solution.py:44
  51.5 0.7 collective-permute-start.5
  52.2 3.1 %collective-permute-done.18 = f32[4,9,128]{2,1,0:T(8,128)S(1)} collective-permute-done((f32[4,9,128]{2,1,0:T(8,128)S(1)}, f32[4,9,128]{2,1,0:T(8,128)S(1)}, u32[]{:S(2)}, u32[]{:S(2)}) %collective-permute-start.18) | collective-permute-done | bytes 18464 | tf_op jit(solution)/shard_map/ppermute | solution.py:44
  55.4 0.8 fusion.30
  56.3 0.7 collective-permute-start.8
  57.1 0.7 collective-permute-start.11
  57.9 1.3 %collective-permute-start.6 = (f32[5,2,32,128]{3,2,1,0:T(8,128)S(1)}, f32[5,2,32,128]{3,2,1,0:T(8,128)S(1)}, u32[]{:S(2)}, u32[]{:S(2)}) collective-permute-start(f32[5,2,32,128]{3,2,1,0:T(8,128)S(1)} %multiply_add_fusion.10), channel_id=1, source_target_pairs={{16,24},{17,25},{18,26},{19,27},{20,28},{21,29},{22,30},{23,31}} | collective-permute-start | bytes 491528 | tf_op jit(solution)/shard_map/ppermute | solution.py:143
  59.3 0.7 collective-permute-start.14
  60.1 1.3 %collective-permute-start.9 = (f32[7,2,32,128]{3,2,1,0:T(8,128)S(1)}, f32[7,2,32,128]{3,2,1,0:T(8,128)S(1)}, u32[]{:S(2)}, u32[]{:S(2)}) collective-permute-start(f32[7,2,32,128]{3,2,1,0:T(8,128)S(1)} %multiply_add_fusion.7), channel_id=1, source_target_pairs={{16,24},{17,25},{18,26},{19,27},{20,28},{21,29},{22,30},{23,31}} | collective-permute-start | bytes 688136 | tf_op jit(solution)/shard_map/ppermute | solution.py:143
  61.4 7.0 %collective-permute-done.6 = f32[5,2,32,128]{3,2,1,0:T(8,128)S(1)} collective-permute-done((f32[5,2,32,128]{3,2,1,0:T(8,128)S(1)}, f32[5,2,32,128]{3,2,1,0:T(8,128)S(1)}, u32[]{:S(2)}, u32[]{:S(2)}) %collective-permute-start.6) | collective-permute-done | bytes 163872 | tf_op jit(solution)/shard_map/ppermute | solution.py:143
  68.6 1.3 %collective-permute-start.12 = (f32[9,2,32,128]{3,2,1,0:T(8,128)S(1)}, f32[9,2,32,128]{3,2,1,0:T(8,128)S(1)}, u32[]{:S(2)}, u32[]{:S(2)}) collective-permute-start(f32[9,2,32,128]{3,2,1,0:T(8,128)S(1)} %multiply_add_fusion.4), channel_id=1, source_target_pairs={{16,24},{17,25},{18,26},{19,27},{20,28},{21,29},{22,30},{23,31}} | collective-permute-start | bytes 884744 | tf_op jit(solution)/shard_map/ppermute | solution.py:143
  70.0 1.3 %collective-permute-start.15 = (f32[11,2,32,128]{3,2,1,0:T(8,128)S(1)}, f32[11,2,32,128]{3,2,1,0:T(8,128)S(1)}, u32[]{:S(2)}, u32[]{:S(2)}) collective-permute-start(f32[11,2,32,128]{3,2,1,0:T(8,128)S(1)} %multiply_add_fusion.1), channel_id=1, source_target_pairs={{16,24},{17,25},{18,26},{19,27},{20,28},{21,29},{22,30},{23,31}} | collective-permute-start | bytes 1081352 | tf_op jit(solution)/shard_map/ppermute | solution.py:143
  71.3 3.5 %collective-permute-done.9 = f32[7,2,32,128]{3,2,1,0:T(8,128)S(1)} collective-permute-done((f32[7,2,32,128]{3,2,1,0:T(8,128)S(1)}, f32[7,2,32,128]{3,2,1,0:T(8,128)S(1)}, u32[]{:S(2)}, u32[]{:S(2)}) %collective-permute-start.9) | collective-permute-done | bytes 229408 | tf_op jit(solution)/shard_map/ppermute | solution.py:143
  75.0 8.7 %collective-permute-done.12 = f32[9,2,32,128]{3,2,1,0:T(8,128)S(1)} collective-permute-done((f32[9,2,32,128]{3,2,1,0:T(8,128)S(1)}, f32[9,2,32,128]{3,2,1,0:T(8,128)S(1)}, u32[]{:S(2)}, u32[]{:S(2)}) %collective-permute-start.12) | collective-permute-done | bytes 294944 | tf_op jit(solution)/shard_map/ppermute | solution.py:143
  83.8 11.2 %collective-permute-done.15 = f32[11,2,32,128]{3,2,1,0:T(8,128)S(1)} collective-permute-done((f32[11,2,32,128]{3,2,1,0:T(8,128)S(1)}, f32[11,2,32,128]{3,2,1,0:T(8,128)S(1)}, u32[]{:S(2)}, u32[]{:S(2)}) %collective-permute-start.15) | collective-permute-done | bytes 360480 | tf_op jit(solution)/shard_map/ppermute | solution.py:143
  95.1 1.1 %maximum_bitcast_fusion = f32[1,32,2,32,128]{4,3,2,1,0:T(8,128)} fusion(f32[11,2,32,128]{3,2,1,0:T(8,128)S(1)} %multiply_add_fusion, f32[9,2,32,128]{3,2,1,0:T(8,128)S(1)} %multiply_add_fusion.3, f32[7,2,32,128]{3,2,1,0:T(8,128)S(1)} %multiply_add_fusion.6, f32[5,2,32,128]{3,2,1,0:T(8,128)S(1)} %multiply_add_fusion.9), kind=kLoop, calls=%fused_computation.47 | loop fusion | flops 786432 | bytes 2097152 | tf_op jit(solution)/shard_map/broadcast_in_dim | solution.py:160
  (82 shorter events, 6.6 us)
Async XLA Ops:
  0.6 45.6 %copy-start = (bf16[1,8,64,128]{3,2,1,0:T(8,128)(2,1)S(1)}, bf16[1,8,64,128]{3,2,1,0:T(8,128)(2,1)}, u32[]{:S(2)}) copy-start(bf16[1,8,64,128]{3,2,1,0:T(8,128)(2,1)} %param.22) | copy-start | bytes 393220
  0.6 7.0 %copy-start.6 = (f32[1,32]{1,0:T(1,128)S(1)}, f32[1,32]{1,0:T(1,128)}, u32[]{:S(2)}) copy-start(f32[1,32]{1,0:T(1,128)} %param.19) | copy-start | bytes 388
  0.7 7.0 %copy-start.5 = (f32[1,32]{1,0:T(1,128)S(1)}, f32[1,32]{1,0:T(1,128)}, u32[]{:S(2)}) copy-start(f32[1,32]{1,0:T(1,128)} %param.21) | copy-start | bytes 388
  2.0 16.5 %collective-permute-start = (f32[33,2,32,128]{3,2,1,0:T(8,128)S(1)}, f32[33,2,32,128]{3,2,1,0:T(8,128)S(1)}, u32[]{:S(2)}, u32[]{:S(2)}) collective-permute-start(f32[33,2,32,128]{3,2,1,0:T(8,128)S(1)} %pad_maximum_fusion.2), channel_id=1, source_target_pairs={{0,1},{1,2},{2,3},{3,4},{4,5},{5,6},{6,7},{8,9},{9,10},{10,11},{11... | collective-permute-start | bytes 3244040 | tf_op jit(solution)/shard_map/ppermute | solution.py:78
  4.0 25.1 %collective-permute-start.1 = (f32[33,2,32,128]{3,2,1,0:T(8,128)S(1)}, f32[33,2,32,128]{3,2,1,0:T(8,128)S(1)}, u32[]{:S(2)}, u32[]{:S(2)}) collective-permute-start(f32[33,2,32,128]{3,2,1,0:T(8,128)S(1)} %pad_maximum_fusion.2), channel_id=1, source_target_pairs={{1,0},{2,1},{3,2},{4,3},{5,4},{6,5},{7,6},{9,8},{10,9},{11,10},{12... | collective-permute-start | bytes 3244040 | tf_op jit(solution)/shard_map/ppermute | solution.py:81
  7.9 21.3 %copy-start.1 = (f32[1,32,2,32,128]{4,3,2,1,0:T(8,128)S(1)}, f32[1,32,2,32,128]{4,3,2,1,0:T(8,128)}, u32[]{:S(2)}) copy-start(f32[1,32,2,32,128]{4,3,2,1,0:T(8,128)} %param.15) | copy-start | bytes 3145732
  29.2 0.8 copy-start.2
  29.2 0.8 copy-start.7
  32.5 0.8 copy-start.3
  33.2 1.9 %copy-start.4 = (f32[1,32]{1,0:T(1,128)S(1)}, f32[1,32]{1,0:T(1,128)}, u32[]{:S(2)}) copy-start(f32[1,32]{1,0:T(1,128)} %param.20) | copy-start | bytes 388
  34.9 5.1 %copy-start.8 = (s32[1,8]{1,0:T(1,128)S(1)}, s32[1,8]{1,0:T(1,128)}, u32[]{:S(2)}) copy-start(s32[1,8]{1,0:T(1,128)} %param.23) | copy-start | bytes 100
  35.7 3.8 %collective-permute-start.2 = (f32[1,34,64]{2,1,0:T(8,128)S(1)}, f32[1,34,64]{2,1,0:T(8,128)S(1)}, u32[]{:S(2)}, u32[]{:S(2)}) collective-permute-start(f32[1,34,64]{2,1,0:T(8,128)S(1)} %maximum_bitcast_fusion.1), channel_id=1, source_target_pairs={{0,8},{8,0},{16,24},{24,16},{1,9},{9,1},{17,25},{25,17},{2,10},{10... | collective-permute-start | bytes 26120 | tf_op jit(solution)/shard_map/ppermute | solution.py:106
  39.6 5.8 %collective-permute-start.3 = (f32[2,34,64]{2,1,0:T(8,128)S(1)}, f32[2,34,64]{2,1,0:T(8,128)S(1)}, u32[]{:S(2)}, u32[]{:S(2)}) collective-permute-start(f32[2,34,64]{2,1,0:T(8,128)S(1)} %maximum_select_fusion.2), channel_id=1, source_target_pairs={{0,16},{8,24},{16,0},{24,8},{1,17},{9,25},{17,1},{25,9},{2,18},{10... | collective-permute-start | bytes 52232 | tf_op jit(solution)/shard_map/ppermute | solution.py:106
  40.7 5.7 %collective-permute-start.4 = (f32[5,2,32,128]{3,2,1,0:T(8,128)S(1)}, f32[5,2,32,128]{3,2,1,0:T(8,128)S(1)}, u32[]{:S(2)}, u32[]{:S(2)}) collective-permute-start(f32[5,2,32,128]{3,2,1,0:T(8,128)S(1)} %slice.194), channel_id=1, source_target_pairs={{0,8},{1,9},{2,10},{3,11},{4,12},{5,13},{6,14},{7,15}} | collective-permute-start | bytes 491528 | tf_op jit(solution)/shard_map/ppermute | solution.py:143
  46.4 1.2 %collective-permute-start.16 = (f32[1,9,128]{2,1,0:T(8,128)S(1)}, f32[1,9,128]{2,1,0:T(8,128)S(1)}, u32[]{:S(2)}, u32[]{:S(2)}) collective-permute-start(f32[1,9,128]{2,1,0:T(8,128)S(1)} %bitcast.122), channel_id=1, source_target_pairs={{0,1},{1,0},{2,3},{3,2},{4,5},{5,4},{6,7},{7,6},{8,9},{9,8},{10,11... | collective-permute-start | bytes 13832 | tf_op jit(solution)/shard_map/ppermute | solution.py:44
  47.7 3.7 %collective-permute-start.17 = (f32[2,9,128]{2,1,0:T(8,128)S(1)}, f32[2,9,128]{2,1,0:T(8,128)S(1)}, u32[]{:S(2)}, u32[]{:S(2)}) collective-permute-start(f32[2,9,128]{2,1,0:T(8,128)S(1)} %maximum_select_fusion.4), channel_id=1, source_target_pairs={{0,2},{1,3},{2,0},{3,1},{4,6},{5,7},{6,4},{7,5},{8,10},{9,11},{10,... | collective-permute-start | bytes 27656 | tf_op jit(solution)/shard_map/ppermute | solution.py:44
  47.8 8.5 %collective-permute-start.7 = (f32[7,2,32,128]{3,2,1,0:T(8,128)S(1)}, f32[7,2,32,128]{3,2,1,0:T(8,128)S(1)}, u32[]{:S(2)}, u32[]{:S(2)}) collective-permute-start(f32[7,2,32,128]{3,2,1,0:T(8,128)S(1)} %slice.207), channel_id=1, source_target_pairs={{0,8},{1,9},{2,10},{3,11},{4,12},{5,13},{6,14},{7,15}} | collective-permute-start | bytes 688136 | tf_op jit(solution)/shard_map/ppermute | solution.py:143
  48.5 8.6 %collective-permute-start.10 = (f32[9,2,32,128]{3,2,1,0:T(8,128)S(1)}, f32[9,2,32,128]{3,2,1,0:T(8,128)S(1)}, u32[]{:S(2)}, u32[]{:S(2)}) collective-permute-start(f32[9,2,32,128]{3,2,1,0:T(8,128)S(1)} %slice.209), channel_id=1, source_target_pairs={{0,8},{1,9},{2,10},{3,11},{4,12},{5,13},{6,14},{7,15}} | collective-permute-start | bytes 884744 | tf_op jit(solution)/shard_map/ppermute | solution.py:143
  49.1 10.1 %collective-permute-start.13 = (f32[11,2,32,128]{3,2,1,0:T(8,128)S(1)}, f32[11,2,32,128]{3,2,1,0:T(8,128)S(1)}, u32[]{:S(2)}, u32[]{:S(2)}) collective-permute-start(f32[11,2,32,128]{3,2,1,0:T(8,128)S(1)} %slice.211), channel_id=1, source_target_pairs={{0,8},{1,9},{2,10},{3,11},{4,12},{5,13},{6,14},{7,15}} | collective-permute-start | bytes 1081352 | tf_op jit(solution)/shard_map/ppermute | solution.py:143
  51.4 3.9 %collective-permute-start.18 = (f32[4,9,128]{2,1,0:T(8,128)S(1)}, f32[4,9,128]{2,1,0:T(8,128)S(1)}, u32[]{:S(2)}, u32[]{:S(2)}) collective-permute-start(f32[4,9,128]{2,1,0:T(8,128)S(1)} %maximum_select_fusion.3), channel_id=1, source_target_pairs={{0,4},{1,5},{2,6},{3,7},{4,0},{5,1},{6,2},{7,3},{8,12},{9,13},{10,... | collective-permute-start | bytes 55304 | tf_op jit(solution)/shard_map/ppermute | solution.py:44
  51.5 6.3 %collective-permute-start.5 = (f32[5,2,32,128]{3,2,1,0:T(8,128)S(1)}, f32[5,2,32,128]{3,2,1,0:T(8,128)S(1)}, u32[]{:S(2)}, u32[]{:S(2)}) collective-permute-start(f32[5,2,32,128]{3,2,1,0:T(8,128)S(1)} %multiply_add_fusion.11), channel_id=1, source_target_pairs={{8,16},{9,17},{10,18},{11,19},{12,20},{13,21},{14,22},{15,23}} | collective-permute-start | bytes 491528 | tf_op jit(solution)/shard_map/ppermute | solution.py:143
  56.3 3.7 %collective-permute-start.8 = (f32[7,2,32,128]{3,2,1,0:T(8,128)S(1)}, f32[7,2,32,128]{3,2,1,0:T(8,128)S(1)}, u32[]{:S(2)}, u32[]{:S(2)}) collective-permute-start(f32[7,2,32,128]{3,2,1,0:T(8,128)S(1)} %multiply_add_fusion.8), channel_id=1, source_target_pairs={{8,16},{9,17},{10,18},{11,19},{12,20},{13,21},{14,22},{15,23}} | collective-permute-start | bytes 688136 | tf_op jit(solution)/shard_map/ppermute | solution.py:143
  57.1 11.4 %collective-permute-start.11 = (f32[9,2,32,128]{3,2,1,0:T(8,128)S(1)}, f32[9,2,32,128]{3,2,1,0:T(8,128)S(1)}, u32[]{:S(2)}, u32[]{:S(2)}) collective-permute-start(f32[9,2,32,128]{3,2,1,0:T(8,128)S(1)} %multiply_add_fusion.5), channel_id=1, source_target_pairs={{8,16},{9,17},{10,18},{11,19},{12,20},{13,21},{14,22},{15,23}} | collective-permute-start | bytes 884744 | tf_op jit(solution)/shard_map/ppermute | solution.py:143
  57.9 10.5 %collective-permute-start.6 = (f32[5,2,32,128]{3,2,1,0:T(8,128)S(1)}, f32[5,2,32,128]{3,2,1,0:T(8,128)S(1)}, u32[]{:S(2)}, u32[]{:S(2)}) collective-permute-start(f32[5,2,32,128]{3,2,1,0:T(8,128)S(1)} %multiply_add_fusion.10), channel_id=1, source_target_pairs={{16,24},{17,25},{18,26},{19,27},{20,28},{21,29},{22,30},{23,31}} | collective-permute-start | bytes 491528 | tf_op jit(solution)/shard_map/ppermute | solution.py:143
  59.3 10.6 %collective-permute-start.14 = (f32[11,2,32,128]{3,2,1,0:T(8,128)S(1)}, f32[11,2,32,128]{3,2,1,0:T(8,128)S(1)}, u32[]{:S(2)}, u32[]{:S(2)}) collective-permute-start(f32[11,2,32,128]{3,2,1,0:T(8,128)S(1)} %multiply_add_fusion.2), channel_id=1, source_target_pairs={{8,16},{9,17},{10,18},{11,19},{12,20},{13,21},{14,22},{15,23}} | collective-permute-start | bytes 1081352 | tf_op jit(solution)/shard_map/ppermute | solution.py:143
  60.1 14.7 %collective-permute-start.9 = (f32[7,2,32,128]{3,2,1,0:T(8,128)S(1)}, f32[7,2,32,128]{3,2,1,0:T(8,128)S(1)}, u32[]{:S(2)}, u32[]{:S(2)}) collective-permute-start(f32[7,2,32,128]{3,2,1,0:T(8,128)S(1)} %multiply_add_fusion.7), channel_id=1, source_target_pairs={{16,24},{17,25},{18,26},{19,27},{20,28},{21,29},{22,30},{23,31}} | collective-permute-start | bytes 688136 | tf_op jit(solution)/shard_map/ppermute | solution.py:143
  68.6 15.0 %collective-permute-start.12 = (f32[9,2,32,128]{3,2,1,0:T(8,128)S(1)}, f32[9,2,32,128]{3,2,1,0:T(8,128)S(1)}, u32[]{:S(2)}, u32[]{:S(2)}) collective-permute-start(f32[9,2,32,128]{3,2,1,0:T(8,128)S(1)} %multiply_add_fusion.4), channel_id=1, source_target_pairs={{16,24},{17,25},{18,26},{19,27},{20,28},{21,29},{22,30},{23,31}} | collective-permute-start | bytes 884744 | tf_op jit(solution)/shard_map/ppermute | solution.py:143
  70.0 25.0 %collective-permute-start.15 = (f32[11,2,32,128]{3,2,1,0:T(8,128)S(1)}, f32[11,2,32,128]{3,2,1,0:T(8,128)S(1)}, u32[]{:S(2)}, u32[]{:S(2)}) collective-permute-start(f32[11,2,32,128]{3,2,1,0:T(8,128)S(1)} %multiply_add_fusion.1), channel_id=1, source_target_pairs={{16,24},{17,25},{18,26},{19,27},{20,28},{21,29},{22,30},{23,31}} | collective-permute-start | bytes 1081352 | tf_op jit(solution)/shard_map/ppermute | solution.py:143

commit v5 on v3

--- a/solution.py
+++ b/solution.py
@@ -71,31 +71,65 @@
     bins = field.shape[0]
     depth = field.shape[3]
     rate = diff_rate[0][:, None, None, None]
-    factor = rate * space_factor[None]
-    for step in range(SUBSTEPS):
-        wider = padded_2(field, (("space", 1),), 1)
-        beside = wider[:, 2:] + wider[:, :-2] + cross_sum(field)
-        field = field + factor * (beside - 6.0 * field)
-    solved = jnp.dot(
-        loss_inverse[0],
-        field.reshape(bins, -1),
-        precision=HIGH,
-        preferred_element_type=jnp.float32,
-    ).reshape(field.shape)
     chain = chain_yield[0]
-    own_part = survival[0][:, None, None, None] * solved
+    halo = SUBSTEPS
+    count = lax.axis_size("space")
+    right_pairs = [(i, i + 1) for i in range(count - 1)]
+    left_pairs = [(i + 1, i) for i in range(count - 1)]
+    layers = field.shape[1]
+    factor_left = lax.ppermute(space_factor[layers - halo:], "space", right_pairs)
+    factor_right = lax.ppermute(space_factor[:halo], "space", left_pairs)
+    wide_space = jnp.concatenate([factor_left, space_factor, factor_right], axis=0)[None]
 
+    base = bins // CHUNKS
+    sizes = [base + 2 * c - (CHUNKS - 1) for c in range(CHUNKS)]
+    sizes[-1] += bins - sum(sizes)
+    tops = [bins]
+    for size in sizes:
+        tops.append(tops[-1] - size)
+    spans = [(tops[c + 1], tops[c]) for c in range(CHUNKS)]
+
+    diffused = []
+    pieces = []
+    scales = []
+    for low, high in spans:
+        block = field[low:high]
+        from_left = lax.ppermute(block[:, layers - halo:], "space", right_pairs)
+        from_right = lax.ppermute(block[:, :halo], "space", left_pairs)
+        wide = jnp.concatenate([from_left, block, from_right], axis=1)
+        wide_factor = rate[low:high] * wide_space
+        for step in range(SUBSTEPS):
+            inner = wide[:, 1:-1]
+            beside = wide[:, 2:] + wide[:, :-2] + cross_sum(inner)
+            wide = inner + wide_factor[:, 1 + step:wide_factor.shape[1] - 1 - step] * (beside - 6.0 * inner)
+        diffused.insert(0, wide)
+        above = jnp.concatenate(diffused, axis=0) if len(diffused) > 1 else wide
+        solved = jnp.dot(
+            loss_inverse[0, low:high, low:],
+            above.reshape(bins - low, -1),
+            precision=HIGH,
+            preferred_element_type=jnp.float32,
+        ).reshape(wide.shape)
+        pieces.append(survival[0, low:high][:, None, None, None] * solved)
+        scales.append(chain[low:high][:, None, None, None])
+    own_part = jnp.concatenate(pieces[::-1], axis=0)
+
+    for c in range(CHUNKS):
+        arrived = lax.ppermute(pieces[c], "species", [(0, 1)])
+        pieces[c] = pieces[c] + scales[c] * arrived
+        if c == CHUNKS - 2:
+            early = pieces[:CHUNKS - 1]
     own_columns = jnp.sum(own_part, axis=3).reshape(bins, -1)
     cols = own_columns.shape[1]
     extra = jnp.zeros((2, cols), jnp.float32).at[0, :bins].set(chain).at[1, :bins].set(gamma_yield[0])
     packed = jnp.concatenate([own_columns, extra], axis=0)
+    packed, early = lax.optimization_barrier((packed, early))
+    pieces[:CHUNKS - 1] = early
     me_g = lax.axis_index("species")
     everyone = packed[None]
     span = 1
     while span < groups:
         other = lax.ppermute(everyone, "species", [(i, i ^ span) for i in range(groups)])
-        if span == 1:
-            own_part, other = lax.optimization_barrier((own_part, other))
         low = (me_g & span) == 0
         everyone = jnp.where(
             low,
@@ -119,22 +153,13 @@
     lines, pixels = contribution.shape
     ids = jnp.zeros((1, pixels), jnp.float32).at[0, :lines].set(sky_blocks[0].astype(jnp.float32))
     payload = jnp.concatenate([contribution, ids], axis=0)
-    base = bins // CHUNKS
-    bounds = [0]
-    for c in range(CHUNKS):
-        bounds.append(bounds[-1] + base + 2 * c - (CHUNKS - 1))
-    bounds[-1] = bins
-    pieces = [own_part[bounds[c]:bounds[c + 1]] for c in range(CHUNKS)]
-    scales = [chain[bounds[c]:bounds[c + 1]][:, None, None, None] for c in range(CHUNKS)]
     for wave in range(CHUNKS + groups - 2):
         for c in range(CHUNKS):
             s = wave - c
-            if 0 <= s < groups - 1:
+            if 1 <= s < groups - 1:
                 arrived = lax.ppermute(pieces[c], "species", [(s, s + 1)])
-                if wave == 0:
-                    payload, arrived = lax.optimization_barrier((payload, arrived))
                 pieces[c] = pieces[c] + scales[c] * arrived
-    carried = jnp.concatenate(pieces, axis=0)
+    carried = jnp.concatenate(pieces[::-1], axis=0)
     gathered = gather_all(payload, "space")
     mine = lax.axis_index("space") * rows + jnp.arange(rows, dtype=jnp.int32)
     onehot = (

time: 98.3 us -> 118 us (1.20)
  the two profiles are of different devices: /device:TPU:28 before, /device:TPU:26 now
where the time goes in v5:
time: 118 us; the launch traced here: 117 us
  starting transfers between devices  51.5 us (44%)
  waiting for transfers between devices  43.7 us (37%)
  local copies, waits for them, and re-layouts  7.83 us (7%)
  other arithmetic  7.65 us (6%)
  matrix products  4.5 us (4%)
  between operations  1.55 us (1%)
    ppermute x8, waiting for transfers between devices, body(): arrived = lax.ppermute(pieces[c], 'species', [(s, s + 1)])  33.3 us
    ppermute x4, starting transfers between devices, body(): from_left = lax.ppermute(block[:, layers - halo:], 'space', right_pairs)  12.7 us
    ppermute x4, starting transfers between devices, body(): from_right = lax.ppermute(block[:, :halo], 'space', left_pairs)  10.4 us
    ppermute x2, starting transfers between devices, body(): lax.ppermute(everyone, 'species', [(i, i ^ span) for i in range(groups)])  9.59 us
    ppermute x8, starting transfers between devices, body(): arrived = lax.ppermute(pieces[c], 'species', [(s, s + 1)])  7.88 us
    ppermute x3, waiting for transfers between devices, gather_all(): other = lax.ppermute(held, axis, [(i, i ^ span) for i in range(count)])  4.87 us
    ppermute x2, waiting for transfers between devices, body(): lax.ppermute(everyone, 'species', [(i, i ^ span) for i in range(groups)])  4.14 us
    slice x4, local copies, waits for them, and re-layouts, body(): block = field[low:high]  3.94 us
  transfers between devices with their start and end apart: 27, of which 9 were waited for; matrix products, arithmetic and copies ran while one was open for 14% of the time, Pallas kernels for 0%

profile of v5, /device:TPU:26, one launch (start us, length us, event | category | flops | bytes accessed | tf_op | source)
XLA Modules:
  0.0 116.8 jit_solution(17851468930172881532)
XLA Ops:
  0.7 1.0 slice_bitcast_fusion.3
  1.7 1.9 %collective-permute-start.8 = (f32[5,2,32,128]{3,2,1,0:T(8,128)S(1)}, f32[5,2,32,128]{3,2,1,0:T(8,128)S(1)}, u32[]{:S(2)}, u32[]{:S(2)}) collective-permute-start(f32[5,2,32,128]{3,2,1,0:T(8,128)S(1)} %slice_bitcast_fusion.3), channel_id=1, source_target_pairs={{0,1},{1,2},{2,3},{3,4},{4,5},{5,6},{6,7},{8,9},{9,10},{10,11},{11... | collective-permute-start | bytes 491528 | tf_op jit(solution)/shard_map/ppermute | solution.py:97
  3.6 3.6 %collective-permute-start.9 = (f32[5,2,32,128]{3,2,1,0:T(8,128)S(1)}, f32[5,2,32,128]{3,2,1,0:T(8,128)S(1)}, u32[]{:S(2)}, u32[]{:S(2)}) collective-permute-start(f32[5,2,32,128]{3,2,1,0:T(8,128)S(1)} %slice_bitcast_fusion.3), channel_id=1, source_target_pairs={{1,0},{2,1},{3,2},{4,3},{5,4},{6,5},{7,6},{9,8},{10,9},{11,10},{12... | collective-permute-start | bytes 491528 | tf_op jit(solution)/shard_map/ppermute | solution.py:98
  7.3 1.9 %collective-permute-start.2 = (f32[2,32,128]{2,1,0:T(8,128)}, f32[2,32,128]{2,1,0:T(8,128)S(1)}, u32[]{:S(2)}, u32[]{:S(2)}) collective-permute-start(f32[2,32,128]{2,1,0:T(8,128)} %param.16), channel_id=1, source_target_pairs={{0,1},{1,2},{2,3},{3,4},{4,5},{5,6},{6,7},{8,9},{9,10},{10,11},{11... | collective-permute-start | bytes 98312 | tf_op jit(solution)/shard_map/ppermute | solution.py:80
  9.2 3.6 %collective-permute-start.3 = (f32[2,32,128]{2,1,0:T(8,128)}, f32[2,32,128]{2,1,0:T(8,128)S(1)}, u32[]{:S(2)}, u32[]{:S(2)}) collective-permute-start(f32[2,32,128]{2,1,0:T(8,128)} %param.16), channel_id=1, source_target_pairs={{1,0},{2,1},{3,2},{4,3},{5,4},{6,5},{7,6},{9,8},{10,9},{11,10},{12... | collective-permute-start | bytes 98312 | tf_op jit(solution)/shard_map/ppermute | solution.py:81
  12.9 1.0 slice_bitcast_fusion.2
  13.8 2.7 %collective-permute-start.6 = (f32[7,2,32,128]{3,2,1,0:T(8,128)S(1)}, f32[7,2,32,128]{3,2,1,0:T(8,128)S(1)}, u32[]{:S(2)}, u32[]{:S(2)}) collective-permute-start(f32[7,2,32,128]{3,2,1,0:T(8,128)S(1)} %slice_bitcast_fusion.2), channel_id=1, source_target_pairs={{0,1},{1,2},{2,3},{3,4},{4,5},{5,6},{6,7},{8,9},{9,10},{10,11},{11... | collective-permute-start | bytes 688136 | tf_op jit(solution)/shard_map/ppermute | solution.py:97
  18.0 1.0 slice_bitcast_fusion.1
  19.0 1.0 slice_bitcast_fusion
  20.7 2.9 %collective-permute-start.7 = (f32[7,2,32,128]{3,2,1,0:T(8,128)S(1)}, f32[7,2,32,128]{3,2,1,0:T(8,128)S(1)}, u32[]{:S(2)}, u32[]{:S(2)}) collective-permute-start(f32[7,2,32,128]{3,2,1,0:T(8,128)S(1)} %slice_bitcast_fusion.2), channel_id=1, source_target_pairs={{1,0},{2,1},{3,2},{4,3},{5,4},{6,5},{7,6},{9,8},{10,9},{11,10},{12... | collective-permute-start | bytes 688136 | tf_op jit(solution)/shard_map/ppermute | solution.py:98
  23.6 3.6 %collective-permute-start.4 = (f32[9,2,32,128]{3,2,1,0:T(8,128)S(1)}, f32[9,2,32,128]{3,2,1,0:T(8,128)S(1)}, u32[]{:S(2)}, u32[]{:S(2)}) collective-permute-start(f32[9,2,32,128]{3,2,1,0:T(8,128)S(1)} %slice_bitcast_fusion.1), channel_id=1, source_target_pairs={{0,1},{1,2},{2,3},{3,4},{4,5},{5,6},{6,7},{8,9},{9,10},{10,11},{11... | collective-permute-start | bytes 884744 | tf_op jit(solution)/shard_map/ppermute | solution.py:97
  27.8 2.0 %collective-permute-start.5 = (f32[9,2,32,128]{3,2,1,0:T(8,128)S(1)}, f32[9,2,32,128]{3,2,1,0:T(8,128)S(1)}, u32[]{:S(2)}, u32[]{:S(2)}) collective-permute-start(f32[9,2,32,128]{3,2,1,0:T(8,128)S(1)} %slice_bitcast_fusion.1), channel_id=1, source_target_pairs={{1,0},{2,1},{3,2},{4,3},{5,4},{6,5},{7,6},{9,8},{10,9},{11,10},{12... | collective-permute-start | bytes 884744 | tf_op jit(solution)/shard_map/ppermute | solution.py:98
  29.8 4.5 %collective-permute-start = (f32[11,2,32,128]{3,2,1,0:T(8,128)S(1)}, f32[11,2,32,128]{3,2,1,0:T(8,128)S(1)}, u32[]{:S(2)}, u32[]{:S(2)}) collective-permute-start(f32[11,2,32,128]{3,2,1,0:T(8,128)S(1)} %slice_bitcast_fusion), channel_id=1, source_target_pairs={{0,1},{1,2},{2,3},{3,4},{4,5},{5,6},{6,7},{8,9},{9,10},{10,11},{11... | collective-permute-start | bytes 1081352 | tf_op jit(solution)/shard_map/ppermute | solution.py:97
  35.7 1.9 %collective-permute-start.1 = (f32[11,2,32,128]{3,2,1,0:T(8,128)S(1)}, f32[11,2,32,128]{3,2,1,0:T(8,128)S(1)}, u32[]{:S(2)}, u32[]{:S(2)}) collective-permute-start(f32[11,2,32,128]{3,2,1,0:T(8,128)S(1)} %slice_bitcast_fusion), channel_id=1, source_target_pairs={{1,0},{2,1},{3,2},{4,3},{5,4},{6,5},{7,6},{9,8},{10,9},{11,10},{12... | collective-permute-start | bytes 1081352 | tf_op jit(solution)/shard_map/ppermute | solution.py:98
  43.7 1.4 %collective-permute-done.1 = f32[11,2,32,128]{3,2,1,0:T(8,128)S(1)} collective-permute-done((f32[11,2,32,128]{3,2,1,0:T(8,128)S(1)}, f32[11,2,32,128]{3,2,1,0:T(8,128)S(1)}, u32[]{:S(2)}, u32[]{:S(2)}) %collective-permute-start.1) | collective-permute-done | bytes 360480 | tf_op jit(solution)/shard_map/ppermute | solution.py:98
  46.0 1.3 %fusion.12 = f32[8192,11]{0,1:T(8,128)S(1)} fusion(f32[4,8,64,128]{3,2,1,0:T(8,128)S(1)} %bitcast.172, f32[1,32,32]{2,1,0:T(8,128)S(1)} %copy-done.1), kind=kOutput, calls=%fused_computation.42 | convolution fusion | flops 34603008 | bytes 1417216 | tf_op jit(solution)/shard_map/dot_general | solution.py:107
  49.4 2.7 %collective-permute-done.22 = f32[1,34,64]{2,1,0:T(8,128)S(1)} collective-permute-done((f32[1,34,64]{2,1,0:T(8,128)S(1)}, f32[1,34,64]{2,1,0:T(8,128)S(1)}, u32[]{:S(2)}, u32[]{:S(2)}) %collective-permute-start.22) | collective-permute-done | bytes 8736 | tf_op jit(solution)/shard_map/ppermute | solution.py:132
  52.1 9.1 %collective-permute-start.23 = (f32[2,34,64]{2,1,0:T(8,128)S(1)}, f32[2,34,64]{2,1,0:T(8,128)S(1)}, u32[]{:S(2)}, u32[]{:S(2)}) collective-permute-start(f32[2,34,64]{2,1,0:T(8,128)S(1)} %maximum_select_fusion.2), channel_id=1, source_target_pairs={{0,16},{8,24},{16,0},{24,8},{1,17},{9,25},{17,1},{25,9},{2,18},{10... | collective-permute-start | bytes 52232 | tf_op jit(solution)/shard_map/ppermute | solution.py:132
  61.9 1.4 %collective-permute-done.23 = f32[2,34,64]{2,1,0:T(8,128)S(1)} collective-permute-done((f32[2,34,64]{2,1,0:T(8,128)S(1)}, f32[2,34,64]{2,1,0:T(8,128)S(1)}, u32[]{:S(2)}, u32[]{:S(2)}) %collective-permute-start.23) | collective-permute-done | bytes 17440 | tf_op jit(solution)/shard_map/ppermute | solution.py:132
  64.4 1.2 collective-permute-done.24
  65.6 3.7 %collective-permute-done.25 = f32[2,9,128]{2,1,0:T(8,128)S(1)} collective-permute-done((f32[2,9,128]{2,1,0:T(8,128)S(1)}, f32[2,9,128]{2,1,0:T(8,128)S(1)}, u32[]{:S(2)}, u32[]{:S(2)}) %collective-permute-start.25) | collective-permute-done | bytes 9248 | tf_op jit(solution)/shard_map/ppermute | solution.py:44
  69.3 2.6 %collective-permute-start.26 = (f32[4,9,128]{2,1,0:T(8,128)S(1)}, f32[4,9,128]{2,1,0:T(8,128)S(1)}, u32[]{:S(2)}, u32[]{:S(2)}) collective-permute-start(f32[4,9,128]{2,1,0:T(8,128)S(1)} %maximum_select_fusion.3), channel_id=1, source_target_pairs={{0,4},{1,5},{2,6},{3,7},{4,0},{5,1},{6,2},{7,3},{8,12},{9,13},{10,... | collective-permute-start | bytes 55304 | tf_op jit(solution)/shard_map/ppermute | solution.py:44
  74.8 0.8 fusion.75
  76.5 1.3 %collective-permute-start.21 = (f32[5,2,32,128]{3,2,1,0:T(8,128)S(1)}, f32[5,2,32,128]{3,2,1,0:T(8,128)S(1)}, u32[]{:S(2)}, u32[]{:S(2)}) collective-permute-start(f32[5,2,32,128]{3,2,1,0:T(8,128)S(1)} %multiply_add_fusion.10), channel_id=1, source_target_pairs={{16,24},{17,25},{18,26},{19,27},{20,28},{21,29},{22,30},{23,31}} | collective-permute-start | bytes 491528 | tf_op jit(solution)/shard_map/ppermute | solution.py:160
  77.9 1.3 %collective-permute-start.19 = (f32[7,2,32,128]{3,2,1,0:T(8,128)S(1)}, f32[7,2,32,128]{3,2,1,0:T(8,128)S(1)}, u32[]{:S(2)}, u32[]{:S(2)}) collective-permute-start(f32[7,2,32,128]{3,2,1,0:T(8,128)S(1)} %multiply_add_fusion.7), channel_id=1, source_target_pairs={{16,24},{17,25},{18,26},{19,27},{20,28},{21,29},{22,30},{23,31}} | collective-permute-start | bytes 688136 | tf_op jit(solution)/shard_map/ppermute | solution.py:160
  79.3 1.3 %collective-permute-start.17 = (f32[9,2,32,128]{3,2,1,0:T(8,128)S(1)}, f32[9,2,32,128]{3,2,1,0:T(8,128)S(1)}, u32[]{:S(2)}, u32[]{:S(2)}) collective-permute-start(f32[9,2,32,128]{3,2,1,0:T(8,128)S(1)} %multiply_add_fusion.4), channel_id=1, source_target_pairs={{16,24},{17,25},{18,26},{19,27},{20,28},{21,29},{22,30},{23,31}} | collective-permute-start | bytes 884744 | tf_op jit(solution)/shard_map/ppermute | solution.py:160
  80.6 20.2 %collective-permute-done.21 = f32[5,2,32,128]{3,2,1,0:T(8,128)S(1)} collective-permute-done((f32[5,2,32,128]{3,2,1,0:T(8,128)S(1)}, f32[5,2,32,128]{3,2,1,0:T(8,128)S(1)}, u32[]{:S(2)}, u32[]{:S(2)}) %collective-permute-start.21) | collective-permute-done | bytes 163872 | tf_op jit(solution)/shard_map/ppermute | solution.py:160
  101.0 1.3 %collective-permute-start.12 = (f32[11,2,32,128]{3,2,1,0:T(8,128)S(1)}, f32[11,2,32,128]{3,2,1,0:T(8,128)S(1)}, u32[]{:S(2)}, u32[]{:S(2)}) collective-permute-start(f32[11,2,32,128]{3,2,1,0:T(8,128)S(1)} %multiply_add_fusion.1), channel_id=1, source_target_pairs={{16,24},{17,25},{18,26},{19,27},{20,28},{21,29},{22,30},{23,31}} | collective-permute-start | bytes 1081352 | tf_op jit(solution)/shard_map/ppermute | solution.py:160
  102.3 3.4 %collective-permute-done.19 = f32[7,2,32,128]{3,2,1,0:T(8,128)S(1)} collective-permute-done((f32[7,2,32,128]{3,2,1,0:T(8,128)S(1)}, f32[7,2,32,128]{3,2,1,0:T(8,128)S(1)}, u32[]{:S(2)}, u32[]{:S(2)}) %collective-permute-start.19) | collective-permute-done | bytes 229408 | tf_op jit(solution)/shard_map/ppermute | solution.py:160
  105.8 6.0 %collective-permute-done.17 = f32[9,2,32,128]{3,2,1,0:T(8,128)S(1)} collective-permute-done((f32[9,2,32,128]{3,2,1,0:T(8,128)S(1)}, f32[9,2,32,128]{3,2,1,0:T(8,128)S(1)}, u32[]{:S(2)}, u32[]{:S(2)}) %collective-permute-start.17) | collective-permute-done | bytes 294944 | tf_op jit(solution)/shard_map/ppermute | solution.py:160
  111.9 3.8 %collective-permute-done.12 = f32[11,2,32,128]{3,2,1,0:T(8,128)S(1)} collective-permute-done((f32[11,2,32,128]{3,2,1,0:T(8,128)S(1)}, f32[11,2,32,128]{3,2,1,0:T(8,128)S(1)}, u32[]{:S(2)}, u32[]{:S(2)}) %collective-permute-start.12) | collective-permute-done | bytes 360480 | tf_op jit(solution)/shard_map/ppermute | solution.py:160
  115.8 1.0 maximum_bitcast_fusion
  (135 shorter events, 18.9 us)
Async XLA Ops:
  0.6 63.5 %copy-start = (bf16[1,8,64,128]{3,2,1,0:T(8,128)(2,1)S(1)}, bf16[1,8,64,128]{3,2,1,0:T(8,128)(2,1)}, u32[]{:S(2)}) copy-start(bf16[1,8,64,128]{3,2,1,0:T(8,128)(2,1)} %param.22) | copy-start | bytes 393220
  0.6 22.9 %copy-start.2 = (f32[2,32,128]{2,1,0:T(8,128)S(1)}, f32[2,32,128]{2,1,0:T(8,128)}, u32[]{:S(2)}) copy-start(f32[2,32,128]{2,1,0:T(8,128)} %param.16) | copy-start | bytes 98308
  0.7 19.4 %copy-start.6 = (f32[1,32]{1,0:T(1,128)S(1)}, f32[1,32]{1,0:T(1,128)}, u32[]{:S(2)}) copy-start(f32[1,32]{1,0:T(1,128)} %param.20) | copy-start | bytes 388
  0.7 19.6 %copy-start.4 = (f32[1,32]{1,0:T(1,128)S(1)}, f32[1,32]{1,0:T(1,128)}, u32[]{:S(2)}) copy-start(f32[1,32]{1,0:T(1,128)} %param.19) | copy-start | bytes 388
  0.7 19.8 %copy-start.3 = (f32[1,32]{1,0:T(1,128)S(1)}, f32[1,32]{1,0:T(1,128)}, u32[]{:S(2)}) copy-start(f32[1,32]{1,0:T(1,128)} %param.21) | copy-start | bytes 388
  1.7 26.1 %collective-permute-start.8 = (f32[5,2,32,128]{3,2,1,0:T(8,128)S(1)}, f32[5,2,32,128]{3,2,1,0:T(8,128)S(1)}, u32[]{:S(2)}, u32[]{:S(2)}) collective-permute-start(f32[5,2,32,128]{3,2,1,0:T(8,128)S(1)} %slice_bitcast_fusion.3), channel_id=1, source_target_pairs={{0,1},{1,2},{2,3},{3,4},{4,5},{5,6},{6,7},{8,9},{9,10},{10,11},{11... | collective-permute-start | bytes 491528 | tf_op jit(solution)/shard_map/ppermute | solution.py:97
  3.6 26.2 %collective-permute-start.9 = (f32[5,2,32,128]{3,2,1,0:T(8,128)S(1)}, f32[5,2,32,128]{3,2,1,0:T(8,128)S(1)}, u32[]{:S(2)}, u32[]{:S(2)}) collective-permute-start(f32[5,2,32,128]{3,2,1,0:T(8,128)S(1)} %slice_bitcast_fusion.3), channel_id=1, source_target_pairs={{1,0},{2,1},{3,2},{4,3},{5,4},{6,5},{7,6},{9,8},{10,9},{11,10},{12... | collective-permute-start | bytes 491528 | tf_op jit(solution)/shard_map/ppermute | solution.py:98
  7.3 13.4 %collective-permute-start.2 = (f32[2,32,128]{2,1,0:T(8,128)}, f32[2,32,128]{2,1,0:T(8,128)S(1)}, u32[]{:S(2)}, u32[]{:S(2)}) collective-permute-start(f32[2,32,128]{2,1,0:T(8,128)} %param.16), channel_id=1, source_target_pairs={{0,1},{1,2},{2,3},{3,4},{4,5},{5,6},{6,7},{8,9},{9,10},{10,11},{11... | collective-permute-start | bytes 98312 | tf_op jit(solution)/shard_map/ppermute | solution.py:80
  9.2 14.4 %collective-permute-start.3 = (f32[2,32,128]{2,1,0:T(8,128)}, f32[2,32,128]{2,1,0:T(8,128)S(1)}, u32[]{:S(2)}, u32[]{:S(2)}) collective-permute-start(f32[2,32,128]{2,1,0:T(8,128)} %param.16), channel_id=1, source_target_pairs={{1,0},{2,1},{3,2},{4,3},{5,4},{6,5},{7,6},{9,8},{10,9},{11,10},{12... | collective-permute-start | bytes 98312 | tf_op jit(solution)/shard_map/ppermute | solution.py:81
  13.8 21.8 %collective-permute-start.6 = (f32[7,2,32,128]{3,2,1,0:T(8,128)S(1)}, f32[7,2,32,128]{3,2,1,0:T(8,128)S(1)}, u32[]{:S(2)}, u32[]{:S(2)}) collective-permute-start(f32[7,2,32,128]{3,2,1,0:T(8,128)S(1)} %slice_bitcast_fusion.2), channel_id=1, source_target_pairs={{0,1},{1,2},{2,3},{3,4},{4,5},{5,6},{6,7},{8,9},{9,10},{10,11},{11... | collective-permute-start | bytes 688136 | tf_op jit(solution)/shard_map/ppermute | solution.py:97
  20.7 16.9 %collective-permute-start.7 = (f32[7,2,32,128]{3,2,1,0:T(8,128)S(1)}, f32[7,2,32,128]{3,2,1,0:T(8,128)S(1)}, u32[]{:S(2)}, u32[]{:S(2)}) collective-permute-start(f32[7,2,32,128]{3,2,1,0:T(8,128)S(1)} %slice_bitcast_fusion.2), channel_id=1, source_target_pairs={{1,0},{2,1},{3,2},{4,3},{5,4},{6,5},{7,6},{9,8},{10,9},{11,10},{12... | collective-permute-start | bytes 688136 | tf_op jit(solution)/shard_map/ppermute | solution.py:98
  23.6 16.3 %collective-permute-start.4 = (f32[9,2,32,128]{3,2,1,0:T(8,128)S(1)}, f32[9,2,32,128]{3,2,1,0:T(8,128)S(1)}, u32[]{:S(2)}, u32[]{:S(2)}) collective-permute-start(f32[9,2,32,128]{3,2,1,0:T(8,128)S(1)} %slice_bitcast_fusion.1), channel_id=1, source_target_pairs={{0,1},{1,2},{2,3},{3,4},{4,5},{5,6},{6,7},{8,9},{9,10},{10,11},{11... | collective-permute-start | bytes 884744 | tf_op jit(solution)/shard_map/ppermute | solution.py:97
  27.8 12.8 %collective-permute-start.5 = (f32[9,2,32,128]{3,2,1,0:T(8,128)S(1)}, f32[9,2,32,128]{3,2,1,0:T(8,128)S(1)}, u32[]{:S(2)}, u32[]{:S(2)}) collective-permute-start(f32[9,2,32,128]{3,2,1,0:T(8,128)S(1)} %slice_bitcast_fusion.1), channel_id=1, source_target_pairs={{1,0},{2,1},{3,2},{4,3},{5,4},{6,5},{7,6},{9,8},{10,9},{11,10},{12... | collective-permute-start | bytes 884744 | tf_op jit(solution)/shard_map/ppermute | solution.py:98
  29.8 13.8 %collective-permute-start = (f32[11,2,32,128]{3,2,1,0:T(8,128)S(1)}, f32[11,2,32,128]{3,2,1,0:T(8,128)S(1)}, u32[]{:S(2)}, u32[]{:S(2)}) collective-permute-start(f32[11,2,32,128]{3,2,1,0:T(8,128)S(1)} %slice_bitcast_fusion), channel_id=1, source_target_pairs={{0,1},{1,2},{2,3},{3,4},{4,5},{5,6},{6,7},{8,9},{9,10},{10,11},{11... | collective-permute-start | bytes 1081352 | tf_op jit(solution)/shard_map/ppermute | solution.py:97
  35.7 9.4 %collective-permute-start.1 = (f32[11,2,32,128]{3,2,1,0:T(8,128)S(1)}, f32[11,2,32,128]{3,2,1,0:T(8,128)S(1)}, u32[]{:S(2)}, u32[]{:S(2)}) collective-permute-start(f32[11,2,32,128]{3,2,1,0:T(8,128)S(1)} %slice_bitcast_fusion), channel_id=1, source_target_pairs={{1,0},{2,1},{3,2},{4,3},{5,4},{6,5},{7,6},{9,8},{10,9},{11,10},{12... | collective-permute-start | bytes 1081352 | tf_op jit(solution)/shard_map/ppermute | solution.py:98
  37.6 5.9 %collective-permute-start.13 = (f32[5,2,32,128]{3,2,1,0:T(8,128)S(1)}, f32[5,2,32,128]{3,2,1,0:T(8,128)S(1)}, u32[]{:S(2)}, u32[]{:S(2)}) collective-permute-start(f32[5,2,32,128]{3,2,1,0:T(8,128)S(1)} %broadcast_multiply_fusion.7), channel_id=1, source_target_pairs={{0,8},{1,9},{2,10},{3,11},{4,12},{5,13},{6,14},{7,15}} | collective-permute-start | bytes 491528 | tf_op jit(solution)/shard_map/ppermute | solution.py:118
  39.9 8.1 %collective-permute-start.14 = (f32[7,2,32,128]{3,2,1,0:T(8,128)S(1)}, f32[7,2,32,128]{3,2,1,0:T(8,128)S(1)}, u32[]{:S(2)}, u32[]{:S(2)}) collective-permute-start(f32[7,2,32,128]{3,2,1,0:T(8,128)S(1)} %broadcast_multiply_fusion.6), channel_id=1, source_target_pairs={{0,8},{1,9},{2,10},{3,11},{4,12},{5,13},{6,14},{7,15}} | collective-permute-start | bytes 688136 | tf_op jit(solution)/shard_map/ppermute | solution.py:118
  42.9 5.3 %collective-permute-start.15 = (f32[9,2,32,128]{3,2,1,0:T(8,128)S(1)}, f32[9,2,32,128]{3,2,1,0:T(8,128)S(1)}, u32[]{:S(2)}, u32[]{:S(2)}) collective-permute-start(f32[9,2,32,128]{3,2,1,0:T(8,128)S(1)} %broadcast_multiply_fusion.5), channel_id=1, source_target_pairs={{0,8},{1,9},{2,10},{3,11},{4,12},{5,13},{6,14},{7,15}} | collective-permute-start | bytes 884744 | tf_op jit(solution)/shard_map/ppermute | solution.py:118
  48.3 3.8 %collective-permute-start.22 = (f32[1,34,64]{2,1,0:T(8,128)S(1)}, f32[1,34,64]{2,1,0:T(8,128)S(1)}, u32[]{:S(2)}, u32[]{:S(2)}) collective-permute-start(f32[1,34,64]{2,1,0:T(8,128)S(1)} %bitcast.191), channel_id=1, source_target_pairs={{0,8},{8,0},{16,24},{24,16},{1,9},{9,1},{17,25},{25,17},{2,10},{10... | collective-permute-start | bytes 26120 | tf_op jit(solution)/shard_map/ppermute | solution.py:132
  52.1 11.2 %collective-permute-start.23 = (f32[2,34,64]{2,1,0:T(8,128)S(1)}, f32[2,34,64]{2,1,0:T(8,128)S(1)}, u32[]{:S(2)}, u32[]{:S(2)}) collective-permute-start(f32[2,34,64]{2,1,0:T(8,128)S(1)} %maximum_select_fusion.2), channel_id=1, source_target_pairs={{0,16},{8,24},{16,0},{24,8},{1,17},{9,25},{17,1},{25,9},{2,18},{10... | collective-permute-start | bytes 52232 | tf_op jit(solution)/shard_map/ppermute | solution.py:132
  64.3 1.2 %collective-permute-start.24 = (f32[1,9,128]{2,1,0:T(8,128)S(1)}, f32[1,9,128]{2,1,0:T(8,128)S(1)}, u32[]{:S(2)}, u32[]{:S(2)}) collective-permute-start(f32[1,9,128]{2,1,0:T(8,128)S(1)} %fusion.86), channel_id=1, source_target_pairs={{0,1},{1,0},{2,3},{3,2},{4,5},{5,4},{6,7},{7,6},{8,9},{9,8},{10,11... | collective-permute-start | bytes 13832 | tf_op jit(solution)/shard_map/ppermute | solution.py:44
  65.5 3.7 %collective-permute-start.25 = (f32[2,9,128]{2,1,0:T(8,128)S(1)}, f32[2,9,128]{2,1,0:T(8,128)S(1)}, u32[]{:S(2)}, u32[]{:S(2)}) collective-permute-start(f32[2,9,128]{2,1,0:T(8,128)S(1)} %maximum_select_fusion.4), channel_id=1, source_target_pairs={{0,2},{1,3},{2,0},{3,1},{4,6},{5,7},{6,4},{7,5},{8,10},{9,11},{10,... | collective-permute-start | bytes 27656 | tf_op jit(solution)/shard_map/ppermute | solution.py:44
  69.3 5.4 %collective-permute-start.26 = (f32[4,9,128]{2,1,0:T(8,128)S(1)}, f32[4,9,128]{2,1,0:T(8,128)S(1)}, u32[]{:S(2)}, u32[]{:S(2)}) collective-permute-start(f32[4,9,128]{2,1,0:T(8,128)S(1)} %maximum_select_fusion.3), channel_id=1, source_target_pairs={{0,4},{1,5},{2,6},{3,7},{4,0},{5,1},{6,2},{7,3},{8,12},{9,13},{10,... | collective-permute-start | bytes 55304 | tf_op jit(solution)/shard_map/ppermute | solution.py:44
  71.9 3.7 %collective-permute-start.10 = (f32[11,2,32,128]{3,2,1,0:T(8,128)S(1)}, f32[11,2,32,128]{3,2,1,0:T(8,128)S(1)}, u32[]{:S(2)}, u32[]{:S(2)}) collective-permute-start(f32[11,2,32,128]{3,2,1,0:T(8,128)S(1)} %broadcast_multiply_fusion.4), channel_id=1, source_target_pairs={{0,8},{1,9},{2,10},{3,11},{4,12},{5,13},{6,14},{7,15}} | collective-permute-start | bytes 1081352 | tf_op jit(solution)/shard_map/ppermute | solution.py:118
  72.6 6.6 %collective-permute-start.16 = (f32[9,2,32,128]{3,2,1,0:T(8,128)S(1)}, f32[9,2,32,128]{3,2,1,0:T(8,128)S(1)}, u32[]{:S(2)}, u32[]{:S(2)}) collective-permute-start(f32[9,2,32,128]{3,2,1,0:T(8,128)S(1)} %multiply_add_fusion.5), channel_id=1, source_target_pairs={{8,16},{9,17},{10,18},{11,19},{12,20},{13,21},{14,22},{15,23}} | collective-permute-start | bytes 884744 | tf_op jit(solution)/shard_map/ppermute | solution.py:160
  73.3 4.5 %collective-permute-start.18 = (f32[7,2,32,128]{3,2,1,0:T(8,128)S(1)}, f32[7,2,32,128]{3,2,1,0:T(8,128)S(1)}, u32[]{:S(2)}, u32[]{:S(2)}) collective-permute-start(f32[7,2,32,128]{3,2,1,0:T(8,128)S(1)} %multiply_add_fusion.8), channel_id=1, source_target_pairs={{8,16},{9,17},{10,18},{11,19},{12,20},{13,21},{14,22},{15,23}} | collective-permute-start | bytes 688136 | tf_op jit(solution)/shard_map/ppermute | solution.py:160
  74.0 2.4 %collective-permute-start.20 = (f32[5,2,32,128]{3,2,1,0:T(8,128)S(1)}, f32[5,2,32,128]{3,2,1,0:T(8,128)S(1)}, u32[]{:S(2)}, u32[]{:S(2)}) collective-permute-start(f32[5,2,32,128]{3,2,1,0:T(8,128)S(1)} %multiply_add_fusion.11), channel_id=1, source_target_pairs={{8,16},{9,17},{10,18},{11,19},{12,20},{13,21},{14,22},{15,23}} | collective-permute-start | bytes 491528 | tf_op jit(solution)/shard_map/ppermute | solution.py:160
  75.7 25.2 %collective-permute-start.11 = (f32[11,2,32,128]{3,2,1,0:T(8,128)S(1)}, f32[11,2,32,128]{3,2,1,0:T(8,128)S(1)}, u32[]{:S(2)}, u32[]{:S(2)}) collective-permute-start(f32[11,2,32,128]{3,2,1,0:T(8,128)S(1)} %multiply_add_fusion.2), channel_id=1, source_target_pairs={{8,16},{9,17},{10,18},{11,19},{12,20},{13,21},{14,22},{15,23}} | collective-permute-start | bytes 1081352 | tf_op jit(solution)/shard_map/ppermute | solution.py:160
  76.5 24.3 %collective-permute-start.21 = (f32[5,2,32,128]{3,2,1,0:T(8,128)S(1)}, f32[5,2,32,128]{3,2,1,0:T(8,128)S(1)}, u32[]{:S(2)}, u32[]{:S(2)}) collective-permute-start(f32[5,2,32,128]{3,2,1,0:T(8,128)S(1)} %multiply_add_fusion.10), channel_id=1, source_target_pairs={{16,24},{17,25},{18,26},{19,27},{20,28},{21,29},{22,30},{23,31}} | collective-permute-start | bytes 491528 | tf_op jit(solution)/shard_map/ppermute | solution.py:160
  77.9 27.8 %collective-permute-start.19 = (f32[7,2,32,128]{3,2,1,0:T(8,128)S(1)}, f32[7,2,32,128]{3,2,1,0:T(8,128)S(1)}, u32[]{:S(2)}, u32[]{:S(2)}) collective-permute-start(f32[7,2,32,128]{3,2,1,0:T(8,128)S(1)} %multiply_add_fusion.7), channel_id=1, source_target_pairs={{16,24},{17,25},{18,26},{19,27},{20,28},{21,29},{22,30},{23,31}} | collective-permute-start | bytes 688136 | tf_op jit(solution)/shard_map/ppermute | solution.py:160
  79.3 32.5 %collective-permute-start.17 = (f32[9,2,32,128]{3,2,1,0:T(8,128)S(1)}, f32[9,2,32,128]{3,2,1,0:T(8,128)S(1)}, u32[]{:S(2)}, u32[]{:S(2)}) collective-permute-start(f32[9,2,32,128]{3,2,1,0:T(8,128)S(1)} %multiply_add_fusion.4), channel_id=1, source_target_pairs={{16,24},{17,25},{18,26},{19,27},{20,28},{21,29},{22,30},{23,31}} | collective-permute-start | bytes 884744 | tf_op jit(solution)/shard_map/ppermute | solution.py:160
  101.0 14.6 %collective-permute-start.12 = (f32[11,2,32,128]{3,2,1,0:T(8,128)S(1)}, f32[11,2,32,128]{3,2,1,0:T(8,128)S(1)}, u32[]{:S(2)}, u32[]{:S(2)}) collective-permute-start(f32[11,2,32,128]{3,2,1,0:T(8,128)S(1)} %multiply_add_fusion.1), channel_id=1, source_target_pairs={{16,24},{17,25},{18,26},{19,27},{20,28},{21,29},{22,30},{23,31}} | collective-permute-start | bytes 1081352 | tf_op jit(solution)/shard_map/ppermute | solution.py:160
  (3 other events, 32.3 us)

commit v6 on v4

--- a/solution.py
+++ b/solution.py
@@ -132,7 +132,7 @@
     base = bins // CHUNKS
     bounds = [0]
     for c in range(CHUNKS):
-        bounds.append(bounds[-1] + base + 2 * c - (CHUNKS - 1))
+        bounds.append(bounds[-1] + base + (CHUNKS - 1) - 2 * c)
     bounds[-1] = bins
     pieces = [own_part[bounds[c]:bounds[c + 1]] for c in range(CHUNKS)]
     scales = [chain[bounds[c]:bounds[c + 1]][:, None, None, None] for c in range(CHUNKS)]

time: 97.2 us -> 105 us (1.080)
  waiting for transfers between devices: 64 us -> 72.7 us
    ppermute x12, waiting for transfers between devices: 30.5 us -> 41.4 us  [body(): arrived = lax.ppermute(pieces[c], 'species', [(s, s + 1)])]
    ppermute x2, waiting for transfers between devices: 6.68 us -> 5.24 us  [body(): lax.ppermute(everyone, 'species', [(i, i ^ span) for i in range(groups)])]
  transfers between devices with their start and end apart: 19 -> 19, of which waited for: 11 -> 11; matrix products, arithmetic and copies ran while one was open for 5% -> 4% of each run, Pallas kernels for 0% -> 0%
where the time goes in v6:
time: 105 us
  waiting for transfers between devices  72.7 us (69%)
  starting transfers between devices  17.2 us (16%)
  other arithmetic  8.8 us (8%)
  matrix products  3.35 us (3%)
  local copies, waits for them, and re-layouts  1.6 us (2%)
  between operations  1.17 us (1%)
    ppermute x12, waiting for transfers between devices, body(): arrived = lax.ppermute(pieces[c], 'species', [(s, s + 1)])  41.4 us
    ppermute x12, starting transfers between devices, body(): arrived = lax.ppermute(pieces[c], 'species', [(s, s + 1)])  10.6 us
    ppermute x1, waiting for transfers between devices, body(): lax.ppermute(mine[:, :halo], 'space', [(i + 1, i) for i in range(count -...  10.5 us
    ppermute x1, waiting for transfers between devices, body(): lax.ppermute(mine[:, mine.shape[1] - halo:], 'space', [(i, i + 1) for i i...  9.83 us
    ppermute x3, waiting for transfers between devices, gather_all(): other = lax.ppermute(held, axis, [(i, i ^ span) for i in range(count)])  5.73 us
    ppermute x2, waiting for transfers between devices, body(): lax.ppermute(everyone, 'species', [(i, i ^ span) for i in range(groups)])  5.24 us
    ppermute x1, starting transfers between devices, body(): lax.ppermute(mine[:, :halo], 'space', [(i + 1, i) for i in range(count -...  3.64 us
    add x2, other arithmetic, body(): inner + wide_factor[:, 1 + step:wide_factor.shape[1] - 1 - step] * (besid...  2.71 us
  transfers between devices with their start and end apart: 19, of which 11 were waited for; matrix products, arithmetic and copies ran while one was open for 4% of the time, Pallas kernels for 0%

profile of v6, /device:TPU:26, one launch (start us, length us, event | category | flops | bytes accessed | tf_op | source)
XLA Modules:
  0.0 104.8 jit_solution(13265559348620239303)
XLA Ops:
  0.7 1.4 %pad_maximum_fusion.2 = f32[33,2,32,128]{3,2,1,0:T(8,128)S(1)} fusion(f32[1,2,32,128]{3,2,1,0:T(8,128)} %bitcast.121, f32[32,2,32,128]{3,2,1,0:T(8,128)} %bitcast.116), kind=kLoop, calls=%fused_computation.36 | loop fusion | flops 270336 | bytes 2162688 | tf_op jit(solution)/shard_map/concatenate | solution.py:77
  2.0 1.9 %collective-permute-start = (f32[33,2,32,128]{3,2,1,0:T(8,128)S(1)}, f32[33,2,32,128]{3,2,1,0:T(8,128)S(1)}, u32[]{:S(2)}, u32[]{:S(2)}) collective-permute-start(f32[33,2,32,128]{3,2,1,0:T(8,128)S(1)} %pad_maximum_fusion.2), channel_id=1, source_target_pairs={{0,1},{1,2},{2,3},{3,4},{4,5},{5,6},{6,7},{8,9},{9,10},{10,11},{11... | collective-permute-start | bytes 3244040 | tf_op jit(solution)/shard_map/ppermute | solution.py:78
  4.0 3.6 %collective-permute-start.1 = (f32[33,2,32,128]{3,2,1,0:T(8,128)S(1)}, f32[33,2,32,128]{3,2,1,0:T(8,128)S(1)}, u32[]{:S(2)}, u32[]{:S(2)}) collective-permute-start(f32[33,2,32,128]{3,2,1,0:T(8,128)S(1)} %pad_maximum_fusion.2), channel_id=1, source_target_pairs={{1,0},{2,1},{3,2},{4,3},{5,4},{6,5},{7,6},{9,8},{10,9},{11,10},{12... | collective-permute-start | bytes 3244040 | tf_op jit(solution)/shard_map/ppermute | solution.py:81
  7.8 0.6 compare_reduce_fusion
  8.7 9.8 %collective-permute-done = f32[33,2,32,128]{3,2,1,0:T(8,128)S(1)} collective-permute-done((f32[33,2,32,128]{3,2,1,0:T(8,128)S(1)}, f32[33,2,32,128]{3,2,1,0:T(8,128)S(1)}, u32[]{:S(2)}, u32[]{:S(2)}) %collective-permute-start) | collective-permute-done | bytes 1081376 | tf_op jit(solution)/shard_map/ppermute | solution.py:78
  18.6 10.5 %collective-permute-done.1 = f32[33,2,32,128]{3,2,1,0:T(8,128)S(1)} collective-permute-done((f32[33,2,32,128]{3,2,1,0:T(8,128)S(1)}, f32[33,2,32,128]{3,2,1,0:T(8,128)S(1)}, u32[]{:S(2)}, u32[]{:S(2)}) %collective-permute-start.1) | collective-permute-done | bytes 1081376 | tf_op jit(solution)/shard_map/ppermute | solution.py:81
  30.4 2.0 %fusion.6 = f32[32,4,32,128]{3,2,1,0:T(8,128)S(1)} fusion(f32[32,4,32,128]{3,2,1,0:T(8,128)S(1)} %pad_maximum_fusion, f32[32,6,32,128]{3,2,1,0:T(8,128)S(1)} %broadcast_multiply_fusion, f32[32,2,32,128]{3,2,1,0:T(8,128)S(1)} %slice.216, f32[32,2,32,128]{3,2,1,0:T(8,128)S(1)} %bitcast.118, f32[32,2,32,128]{3,2,1,0:T(8,128)S(1)} %slice.215), kind=kLoop, calls=%fused_computation.14 | loop fusion | flops 5767168 | bytes 9437184 | tf_op jit(solution)/shard_map/add | solution.py:87
  32.5 0.7 fusion.25
  33.2 1.7 %convolution_bitcast_fusion = f32[4,8,64,128]{3,1,2,0:T(8,128)S(1)} fusion(f32[4,8,64,128]{3,2,1,0:T(8,128)S(1)} %bitcast.119, f32[1,32,32]{2,1,0:T(8,128)S(1)} %copy-done.3), kind=kOutput, calls=%fused_computation.19 | convolution fusion | flops 100663296 | bytes 2101248 | tf_op jit(solution)/shard_map/dot_general | solution.py:89
  36.2 0.6 broadcast_select_fusion
  36.9 2.7 %collective-permute-done.2 = f32[1,34,64]{2,1,0:T(8,128)S(1)} collective-permute-done((f32[1,34,64]{2,1,0:T(8,128)S(1)}, f32[1,34,64]{2,1,0:T(8,128)S(1)}, u32[]{:S(2)}, u32[]{:S(2)}) %collective-permute-start.2) | collective-permute-done | bytes 8736 | tf_op jit(solution)/shard_map/ppermute | solution.py:106
  40.1 0.7 collective-permute-start.4
  40.8 0.7 collective-permute-start.7
  41.5 0.7 collective-permute-start.10
  42.2 0.7 collective-permute-start.13
  42.8 2.6 %collective-permute-done.3 = f32[2,34,64]{2,1,0:T(8,128)S(1)} collective-permute-done((f32[2,34,64]{2,1,0:T(8,128)S(1)}, f32[2,34,64]{2,1,0:T(8,128)S(1)}, u32[]{:S(2)}, u32[]{:S(2)}) %collective-permute-start.3) | collective-permute-done | bytes 17440 | tf_op jit(solution)/shard_map/ppermute | solution.py:106
  46.5 0.7 collective-permute-start.14
  47.3 0.7 collective-permute-start.11
  48.2 0.7 collective-permute-start.8
  49.3 1.3 %collective-permute-start.15 = (f32[5,2,32,128]{3,2,1,0:T(8,128)S(1)}, f32[5,2,32,128]{3,2,1,0:T(8,128)S(1)}, u32[]{:S(2)}, u32[]{:S(2)}) collective-permute-start(f32[5,2,32,128]{3,2,1,0:T(8,128)S(1)} %multiply_add_fusion.10), channel_id=1, source_target_pairs={{16,24},{17,25},{18,26},{19,27},{20,28},{21,29},{22,30},{23,31}} | collective-permute-start | bytes 491528 | tf_op jit(solution)/shard_map/ppermute | solution.py:143
  50.6 2.3 %collective-permute-done.17 = f32[2,9,128]{2,1,0:T(8,128)S(1)} collective-permute-done((f32[2,9,128]{2,1,0:T(8,128)S(1)}, f32[2,9,128]{2,1,0:T(8,128)S(1)}, u32[]{:S(2)}, u32[]{:S(2)}) %collective-permute-start.17) | collective-permute-done | bytes 9248 | tf_op jit(solution)/shard_map/ppermute | solution.py:44
  53.1 0.7 collective-permute-start.5
  53.8 3.1 %collective-permute-done.18 = f32[4,9,128]{2,1,0:T(8,128)S(1)} collective-permute-done((f32[4,9,128]{2,1,0:T(8,128)S(1)}, f32[4,9,128]{2,1,0:T(8,128)S(1)}, u32[]{:S(2)}, u32[]{:S(2)}) %collective-permute-start.18) | collective-permute-done | bytes 18464 | tf_op jit(solution)/shard_map/ppermute | solution.py:44
  57.0 0.8 fusion.30
  57.9 1.3 %collective-permute-start.12 = (f32[7,2,32,128]{3,2,1,0:T(8,128)S(1)}, f32[7,2,32,128]{3,2,1,0:T(8,128)S(1)}, u32[]{:S(2)}, u32[]{:S(2)}) collective-permute-start(f32[7,2,32,128]{3,2,1,0:T(8,128)S(1)} %multiply_add_fusion.7), channel_id=1, source_target_pairs={{16,24},{17,25},{18,26},{19,27},{20,28},{21,29},{22,30},{23,31}} | collective-permute-start | bytes 688136 | tf_op jit(solution)/shard_map/ppermute | solution.py:143
  59.2 22.4 %collective-permute-done.15 = f32[5,2,32,128]{3,2,1,0:T(8,128)S(1)} collective-permute-done((f32[5,2,32,128]{3,2,1,0:T(8,128)S(1)}, f32[5,2,32,128]{3,2,1,0:T(8,128)S(1)}, u32[]{:S(2)}, u32[]{:S(2)}) %collective-permute-start.15) | collective-permute-done | bytes 163872 | tf_op jit(solution)/shard_map/ppermute | solution.py:143
  81.8 1.3 %collective-permute-start.9 = (f32[9,2,32,128]{3,2,1,0:T(8,128)S(1)}, f32[9,2,32,128]{3,2,1,0:T(8,128)S(1)}, u32[]{:S(2)}, u32[]{:S(2)}) collective-permute-start(f32[9,2,32,128]{3,2,1,0:T(8,128)S(1)} %multiply_add_fusion.4), channel_id=1, source_target_pairs={{16,24},{17,25},{18,26},{19,27},{20,28},{21,29},{22,30},{23,31}} | collective-permute-start | bytes 884744 | tf_op jit(solution)/shard_map/ppermute | solution.py:143
  83.3 1.3 %collective-permute-start.6 = (f32[11,2,32,128]{3,2,1,0:T(8,128)S(1)}, f32[11,2,32,128]{3,2,1,0:T(8,128)S(1)}, u32[]{:S(2)}, u32[]{:S(2)}) collective-permute-start(f32[11,2,32,128]{3,2,1,0:T(8,128)S(1)} %multiply_add_fusion.1), channel_id=1, source_target_pairs={{16,24},{17,25},{18,26},{19,27},{20,28},{21,29},{22,30},{23,31}} | collective-permute-start | bytes 1081352 | tf_op jit(solution)/shard_map/ppermute | solution.py:143
  84.6 4.5 %collective-permute-done.12 = f32[7,2,32,128]{3,2,1,0:T(8,128)S(1)} collective-permute-done((f32[7,2,32,128]{3,2,1,0:T(8,128)S(1)}, f32[7,2,32,128]{3,2,1,0:T(8,128)S(1)}, u32[]{:S(2)}, u32[]{:S(2)}) %collective-permute-start.12) | collective-permute-done | bytes 229408 | tf_op jit(solution)/shard_map/ppermute | solution.py:143
  89.2 5.8 %collective-permute-done.9 = f32[9,2,32,128]{3,2,1,0:T(8,128)S(1)} collective-permute-done((f32[9,2,32,128]{3,2,1,0:T(8,128)S(1)}, f32[9,2,32,128]{3,2,1,0:T(8,128)S(1)}, u32[]{:S(2)}, u32[]{:S(2)}) %collective-permute-start.9) | collective-permute-done | bytes 294944 | tf_op jit(solution)/shard_map/ppermute | solution.py:143
  95.1 8.6 %collective-permute-done.6 = f32[11,2,32,128]{3,2,1,0:T(8,128)S(1)} collective-permute-done((f32[11,2,32,128]{3,2,1,0:T(8,128)S(1)}, f32[11,2,32,128]{3,2,1,0:T(8,128)S(1)}, u32[]{:S(2)}, u32[]{:S(2)}) %collective-permute-start.6) | collective-permute-done | bytes 360480 | tf_op jit(solution)/shard_map/ppermute | solution.py:143
  103.8 1.0 %maximum_bitcast_fusion = f32[1,32,2,32,128]{4,3,2,1,0:T(8,128)} fusion(f32[5,2,32,128]{3,2,1,0:T(8,128)S(1)} %multiply_add_fusion.9, f32[7,2,32,128]{3,2,1,0:T(8,128)S(1)} %multiply_add_fusion.6, f32[9,2,32,128]{3,2,1,0:T(8,128)S(1)} %multiply_add_fusion.3, f32[11,2,32,128]{3,2,1,0:T(8,128)S(1)} %multiply_add_fusion), kind=kLoop, calls=%fused_computation.47 | loop fusion | flops 786432 | bytes 2097152 | tf_op jit(solution)/shard_map/broadcast_in_dim | solution.py:160
  (82 shorter events, 6.2 us)
Async XLA Ops:
  0.6 45.6 %copy-start = (bf16[1,8,64,128]{3,2,1,0:T(8,128)(2,1)S(1)}, bf16[1,8,64,128]{3,2,1,0:T(8,128)(2,1)}, u32[]{:S(2)}) copy-start(bf16[1,8,64,128]{3,2,1,0:T(8,128)(2,1)} %param.22) | copy-start | bytes 393220
  0.6 7.0 %copy-start.6 = (f32[1,32]{1,0:T(1,128)S(1)}, f32[1,32]{1,0:T(1,128)}, u32[]{:S(2)}) copy-start(f32[1,32]{1,0:T(1,128)} %param.19) | copy-start | bytes 388
  0.7 7.0 %copy-start.5 = (f32[1,32]{1,0:T(1,128)S(1)}, f32[1,32]{1,0:T(1,128)}, u32[]{:S(2)}) copy-start(f32[1,32]{1,0:T(1,128)} %param.21) | copy-start | bytes 388
  2.0 16.5 %collective-permute-start = (f32[33,2,32,128]{3,2,1,0:T(8,128)S(1)}, f32[33,2,32,128]{3,2,1,0:T(8,128)S(1)}, u32[]{:S(2)}, u32[]{:S(2)}) collective-permute-start(f32[33,2,32,128]{3,2,1,0:T(8,128)S(1)} %pad_maximum_fusion.2), channel_id=1, source_target_pairs={{0,1},{1,2},{2,3},{3,4},{4,5},{5,6},{6,7},{8,9},{9,10},{10,11},{11... | collective-permute-start | bytes 3244040 | tf_op jit(solution)/shard_map/ppermute | solution.py:78
  4.0 25.1 %collective-permute-start.1 = (f32[33,2,32,128]{3,2,1,0:T(8,128)S(1)}, f32[33,2,32,128]{3,2,1,0:T(8,128)S(1)}, u32[]{:S(2)}, u32[]{:S(2)}) collective-permute-start(f32[33,2,32,128]{3,2,1,0:T(8,128)S(1)} %pad_maximum_fusion.2), channel_id=1, source_target_pairs={{1,0},{2,1},{3,2},{4,3},{5,4},{6,5},{7,6},{9,8},{10,9},{11,10},{12... | collective-permute-start | bytes 3244040 | tf_op jit(solution)/shard_map/ppermute | solution.py:81
  8.7 20.5 %copy-start.1 = (f32[1,32,2,32,128]{4,3,2,1,0:T(8,128)S(1)}, f32[1,32,2,32,128]{4,3,2,1,0:T(8,128)}, u32[]{:S(2)}) copy-start(f32[1,32,2,32,128]{4,3,2,1,0:T(8,128)} %param.15) | copy-start | bytes 3145732
  29.2 0.8 copy-start.2
  29.2 0.8 copy-start.7
  32.5 0.8 copy-start.3
  33.2 1.9 %copy-start.4 = (f32[1,32]{1,0:T(1,128)S(1)}, f32[1,32]{1,0:T(1,128)}, u32[]{:S(2)}) copy-start(f32[1,32]{1,0:T(1,128)} %param.20) | copy-start | bytes 388
  34.9 1.3 %copy-start.8 = (s32[1,8]{1,0:T(1,128)S(1)}, s32[1,8]{1,0:T(1,128)}, u32[]{:S(2)}) copy-start(s32[1,8]{1,0:T(1,128)} %param.23) | copy-start | bytes 100
  35.7 3.8 %collective-permute-start.2 = (f32[1,34,64]{2,1,0:T(8,128)S(1)}, f32[1,34,64]{2,1,0:T(8,128)S(1)}, u32[]{:S(2)}, u32[]{:S(2)}) collective-permute-start(f32[1,34,64]{2,1,0:T(8,128)S(1)} %maximum_bitcast_fusion.1), channel_id=1, source_target_pairs={{0,8},{8,0},{16,24},{24,16},{1,9},{9,1},{17,25},{25,17},{2,10},{10... | collective-permute-start | bytes 26120 | tf_op jit(solution)/shard_map/ppermute | solution.py:106
  39.6 5.8 %collective-permute-start.3 = (f32[2,34,64]{2,1,0:T(8,128)S(1)}, f32[2,34,64]{2,1,0:T(8,128)S(1)}, u32[]{:S(2)}, u32[]{:S(2)}) collective-permute-start(f32[2,34,64]{2,1,0:T(8,128)S(1)} %maximum_select_fusion.2), channel_id=1, source_target_pairs={{0,16},{8,24},{16,0},{24,8},{1,17},{9,25},{17,1},{25,9},{2,18},{10... | collective-permute-start | bytes 52232 | tf_op jit(solution)/shard_map/ppermute | solution.py:106
  40.1 7.9 %collective-permute-start.4 = (f32[11,2,32,128]{3,2,1,0:T(8,128)S(1)}, f32[11,2,32,128]{3,2,1,0:T(8,128)S(1)}, u32[]{:S(2)}, u32[]{:S(2)}) collective-permute-start(f32[11,2,32,128]{3,2,1,0:T(8,128)S(1)} %slice.194), channel_id=1, source_target_pairs={{0,8},{1,9},{2,10},{3,11},{4,12},{5,13},{6,14},{7,15}} | collective-permute-start | bytes 1081352 | tf_op jit(solution)/shard_map/ppermute | solution.py:143
  40.8 7.3 %collective-permute-start.7 = (f32[9,2,32,128]{3,2,1,0:T(8,128)S(1)}, f32[9,2,32,128]{3,2,1,0:T(8,128)S(1)}, u32[]{:S(2)}, u32[]{:S(2)}) collective-permute-start(f32[9,2,32,128]{3,2,1,0:T(8,128)S(1)} %slice.207), channel_id=1, source_target_pairs={{0,8},{1,9},{2,10},{3,11},{4,12},{5,13},{6,14},{7,15}} | collective-permute-start | bytes 884744 | tf_op jit(solution)/shard_map/ppermute | solution.py:143
  41.5 5.7 %collective-permute-start.10 = (f32[7,2,32,128]{3,2,1,0:T(8,128)S(1)}, f32[7,2,32,128]{3,2,1,0:T(8,128)S(1)}, u32[]{:S(2)}, u32[]{:S(2)}) collective-permute-start(f32[7,2,32,128]{3,2,1,0:T(8,128)S(1)} %slice.209), channel_id=1, source_target_pairs={{0,8},{1,9},{2,10},{3,11},{4,12},{5,13},{6,14},{7,15}} | collective-permute-start | bytes 688136 | tf_op jit(solution)/shard_map/ppermute | solution.py:143
  42.2 4.2 %collective-permute-start.13 = (f32[5,2,32,128]{3,2,1,0:T(8,128)S(1)}, f32[5,2,32,128]{3,2,1,0:T(8,128)S(1)}, u32[]{:S(2)}, u32[]{:S(2)}) collective-permute-start(f32[5,2,32,128]{3,2,1,0:T(8,128)S(1)} %slice.211), channel_id=1, source_target_pairs={{0,8},{1,9},{2,10},{3,11},{4,12},{5,13},{6,14},{7,15}} | collective-permute-start | bytes 491528 | tf_op jit(solution)/shard_map/ppermute | solution.py:143
  46.5 2.7 %collective-permute-start.14 = (f32[5,2,32,128]{3,2,1,0:T(8,128)S(1)}, f32[5,2,32,128]{3,2,1,0:T(8,128)S(1)}, u32[]{:S(2)}, u32[]{:S(2)}) collective-permute-start(f32[5,2,32,128]{3,2,1,0:T(8,128)S(1)} %multiply_add_fusion.11), channel_id=1, source_target_pairs={{8,16},{9,17},{10,18},{11,19},{12,20},{13,21},{14,22},{15,23}} | collective-permute-start | bytes 491528 | tf_op jit(solution)/shard_map/ppermute | solution.py:143
  47.3 10.5 %collective-permute-start.11 = (f32[7,2,32,128]{3,2,1,0:T(8,128)S(1)}, f32[7,2,32,128]{3,2,1,0:T(8,128)S(1)}, u32[]{:S(2)}, u32[]{:S(2)}) collective-permute-start(f32[7,2,32,128]{3,2,1,0:T(8,128)S(1)} %multiply_add_fusion.8), channel_id=1, source_target_pairs={{8,16},{9,17},{10,18},{11,19},{12,20},{13,21},{14,22},{15,23}} | collective-permute-start | bytes 688136 | tf_op jit(solution)/shard_map/ppermute | solution.py:143
  48.0 1.2 %collective-permute-start.16 = (f32[1,9,128]{2,1,0:T(8,128)S(1)}, f32[1,9,128]{2,1,0:T(8,128)S(1)}, u32[]{:S(2)}, u32[]{:S(2)}) collective-permute-start(f32[1,9,128]{2,1,0:T(8,128)S(1)} %bitcast.122), channel_id=1, source_target_pairs={{0,1},{1,0},{2,3},{3,2},{4,5},{5,4},{6,7},{7,6},{8,9},{9,8},{10,11... | collective-permute-start | bytes 13832 | tf_op jit(solution)/shard_map/ppermute | solution.py:44
  48.2 33.5 %collective-permute-start.8 = (f32[9,2,32,128]{3,2,1,0:T(8,128)S(1)}, f32[9,2,32,128]{3,2,1,0:T(8,128)S(1)}, u32[]{:S(2)}, u32[]{:S(2)}) collective-permute-start(f32[9,2,32,128]{3,2,1,0:T(8,128)S(1)} %multiply_add_fusion.5), channel_id=1, source_target_pairs={{8,16},{9,17},{10,18},{11,19},{12,20},{13,21},{14,22},{15,23}} | collective-permute-start | bytes 884744 | tf_op jit(solution)/shard_map/ppermute | solution.py:143
  49.2 3.7 %collective-permute-start.17 = (f32[2,9,128]{2,1,0:T(8,128)S(1)}, f32[2,9,128]{2,1,0:T(8,128)S(1)}, u32[]{:S(2)}, u32[]{:S(2)}) collective-permute-start(f32[2,9,128]{2,1,0:T(8,128)S(1)} %maximum_select_fusion.4), channel_id=1, source_target_pairs={{0,2},{1,3},{2,0},{3,1},{4,6},{5,7},{6,4},{7,5},{8,10},{9,11},{10,... | collective-permute-start | bytes 27656 | tf_op jit(solution)/shard_map/ppermute | solution.py:44
  49.3 32.3 %collective-permute-start.15 = (f32[5,2,32,128]{3,2,1,0:T(8,128)S(1)}, f32[5,2,32,128]{3,2,1,0:T(8,128)S(1)}, u32[]{:S(2)}, u32[]{:S(2)}) collective-permute-start(f32[5,2,32,128]{3,2,1,0:T(8,128)S(1)} %multiply_add_fusion.10), channel_id=1, source_target_pairs={{16,24},{17,25},{18,26},{19,27},{20,28},{21,29},{22,30},{23,31}} | collective-permute-start | bytes 491528 | tf_op jit(solution)/shard_map/ppermute | solution.py:143
  53.0 3.9 %collective-permute-start.18 = (f32[4,9,128]{2,1,0:T(8,128)S(1)}, f32[4,9,128]{2,1,0:T(8,128)S(1)}, u32[]{:S(2)}, u32[]{:S(2)}) collective-permute-start(f32[4,9,128]{2,1,0:T(8,128)S(1)} %maximum_select_fusion.3), channel_id=1, source_target_pairs={{0,4},{1,5},{2,6},{3,7},{4,0},{5,1},{6,2},{7,3},{8,12},{9,13},{10,... | collective-permute-start | bytes 55304 | tf_op jit(solution)/shard_map/ppermute | solution.py:44
  53.1 30.0 %collective-permute-start.5 = (f32[11,2,32,128]{3,2,1,0:T(8,128)S(1)}, f32[11,2,32,128]{3,2,1,0:T(8,128)S(1)}, u32[]{:S(2)}, u32[]{:S(2)}) collective-permute-start(f32[11,2,32,128]{3,2,1,0:T(8,128)S(1)} %multiply_add_fusion.2), channel_id=1, source_target_pairs={{8,16},{9,17},{10,18},{11,19},{12,20},{13,21},{14,22},{15,23}} | collective-permute-start | bytes 1081352 | tf_op jit(solution)/shard_map/ppermute | solution.py:143
  57.9 31.2 %collective-permute-start.12 = (f32[7,2,32,128]{3,2,1,0:T(8,128)S(1)}, f32[7,2,32,128]{3,2,1,0:T(8,128)S(1)}, u32[]{:S(2)}, u32[]{:S(2)}) collective-permute-start(f32[7,2,32,128]{3,2,1,0:T(8,128)S(1)} %multiply_add_fusion.7), channel_id=1, source_target_pairs={{16,24},{17,25},{18,26},{19,27},{20,28},{21,29},{22,30},{23,31}} | collective-permute-start | bytes 688136 | tf_op jit(solution)/shard_map/ppermute | solution.py:143
  81.8 13.2 %collective-permute-start.9 = (f32[9,2,32,128]{3,2,1,0:T(8,128)S(1)}, f32[9,2,32,128]{3,2,1,0:T(8,128)S(1)}, u32[]{:S(2)}, u32[]{:S(2)}) collective-permute-start(f32[9,2,32,128]{3,2,1,0:T(8,128)S(1)} %multiply_add_fusion.4), channel_id=1, source_target_pairs={{16,24},{17,25},{18,26},{19,27},{20,28},{21,29},{22,30},{23,31}} | collective-permute-start | bytes 884744 | tf_op jit(solution)/shard_map/ppermute | solution.py:143
  83.3 20.4 %collective-permute-start.6 = (f32[11,2,32,128]{3,2,1,0:T(8,128)S(1)}, f32[11,2,32,128]{3,2,1,0:T(8,128)S(1)}, u32[]{:S(2)}, u32[]{:S(2)}) collective-permute-start(f32[11,2,32,128]{3,2,1,0:T(8,128)S(1)} %multiply_add_fusion.1), channel_id=1, source_target_pairs={{16,24},{17,25},{18,26},{19,27},{20,28},{21,29},{22,30},{23,31}} | collective-permute-start | bytes 1081352 | tf_op jit(solution)/shard_map/ppermute | solution.py:143

commit v7 on v4

--- a/solution.py
+++ b/solution.py
@@ -141,7 +141,7 @@
             s = wave - c
             if 0 <= s < groups - 1:
                 arrived = lax.ppermute(pieces[c], "species", [(s, s + 1)])
-                if wave == 0:
+                if s == 0 and c == CHUNKS - 1:
                     payload, arrived = lax.optimization_barrier((payload, arrived))
                 pieces[c] = pieces[c] + scales[c] * arrived
     carried = jnp.concatenate(pieces, axis=0)

time: 97.2 us -> 96.9 us (level)
    ppermute x12, waiting for transfers between devices: 30.5 us -> 33 us  [body(): arrived = lax.ppermute(pieces[c], 'species', [(s, s + 1)])]
    ppermute x2, waiting for transfers between devices: 6.68 us -> 5.24 us  [body(): lax.ppermute(everyone, 'species', [(i, i ^ span) for i in range(groups)])]
where the time goes in v7:
time: 96.9 us; the launch traced here: 96.4 us
  waiting for transfers between devices  64.3 us (66%)
  starting transfers between devices  17.2 us (18%)
  other arithmetic  8.84 us (9%)
  matrix products  3.35 us (3%)
  local copies, waits for them, and re-layouts  1.6 us (2%)
  between operations  1.17 us (1%)
    ppermute x12, waiting for transfers between devices, body(): arrived = lax.ppermute(pieces[c], 'species', [(s, s + 1)])  33 us
    ppermute x12, starting transfers between devices, body(): arrived = lax.ppermute(pieces[c], 'species', [(s, s + 1)])  10.6 us
    ppermute x1, waiting for transfers between devices, body(): lax.ppermute(mine[:, :halo], 'space', [(i + 1, i) for i in range(count -...  10.5 us
    ppermute x1, waiting for transfers between devices, body(): lax.ppermute(mine[:, mine.shape[1] - halo:], 'space', [(i, i + 1) for i i...  9.83 us
    ppermute x3, waiting for transfers between devices, gather_all(): other = lax.ppermute(held, axis, [(i, i ^ span) for i in range(count)])  5.73 us
    ppermute x2, waiting for transfers between devices, body(): lax.ppermute(everyone, 'species', [(i, i ^ span) for i in range(groups)])  5.24 us
    ppermute x1, starting transfers between devices, body(): lax.ppermute(mine[:, :halo], 'space', [(i + 1, i) for i in range(count -...  3.64 us
    add x2, other arithmetic, body(): inner + wide_factor[:, 1 + step:wide_factor.shape[1] - 1 - step] * (besid...  2.71 us
  transfers between devices with their start and end apart: 19, of which 11 were waited for; matrix products, arithmetic and copies ran while one was open for 5% of the time, Pallas kernels for 0%

profile of v7, /device:TPU:26, one launch (start us, length us, event | category | flops | bytes accessed | tf_op | source)
XLA Modules:
  0.0 96.4 jit_solution(299647390948934784)
XLA Ops:
  0.7 1.4 %pad_maximum_fusion.2 = f32[33,2,32,128]{3,2,1,0:T(8,128)S(1)} fusion(f32[1,2,32,128]{3,2,1,0:T(8,128)} %bitcast.121, f32[32,2,32,128]{3,2,1,0:T(8,128)} %bitcast.116), kind=kLoop, calls=%fused_computation.36 | loop fusion | flops 270336 | bytes 2162688 | tf_op jit(solution)/shard_map/concatenate | solution.py:77
  2.0 1.9 %collective-permute-start = (f32[33,2,32,128]{3,2,1,0:T(8,128)S(1)}, f32[33,2,32,128]{3,2,1,0:T(8,128)S(1)}, u32[]{:S(2)}, u32[]{:S(2)}) collective-permute-start(f32[33,2,32,128]{3,2,1,0:T(8,128)S(1)} %pad_maximum_fusion.2), channel_id=1, source_target_pairs={{0,1},{1,2},{2,3},{3,4},{4,5},{5,6},{6,7},{8,9},{9,10},{10,11},{11... | collective-permute-start | bytes 3244040 | tf_op jit(solution)/shard_map/ppermute | solution.py:78
  4.0 3.6 %collective-permute-start.1 = (f32[33,2,32,128]{3,2,1,0:T(8,128)S(1)}, f32[33,2,32,128]{3,2,1,0:T(8,128)S(1)}, u32[]{:S(2)}, u32[]{:S(2)}) collective-permute-start(f32[33,2,32,128]{3,2,1,0:T(8,128)S(1)} %pad_maximum_fusion.2), channel_id=1, source_target_pairs={{1,0},{2,1},{3,2},{4,3},{5,4},{6,5},{7,6},{9,8},{10,9},{11,10},{12... | collective-permute-start | bytes 3244040 | tf_op jit(solution)/shard_map/ppermute | solution.py:81
  7.8 0.6 compare_reduce_fusion
  8.7 9.8 %collective-permute-done = f32[33,2,32,128]{3,2,1,0:T(8,128)S(1)} collective-permute-done((f32[33,2,32,128]{3,2,1,0:T(8,128)S(1)}, f32[33,2,32,128]{3,2,1,0:T(8,128)S(1)}, u32[]{:S(2)}, u32[]{:S(2)}) %collective-permute-start) | collective-permute-done | bytes 1081376 | tf_op jit(solution)/shard_map/ppermute | solution.py:78
  18.6 10.5 %collective-permute-done.1 = f32[33,2,32,128]{3,2,1,0:T(8,128)S(1)} collective-permute-done((f32[33,2,32,128]{3,2,1,0:T(8,128)S(1)}, f32[33,2,32,128]{3,2,1,0:T(8,128)S(1)}, u32[]{:S(2)}, u32[]{:S(2)}) %collective-permute-start.1) | collective-permute-done | bytes 1081376 | tf_op jit(solution)/shard_map/ppermute | solution.py:81
  30.4 2.0 %fusion.6 = f32[32,4,32,128]{3,2,1,0:T(8,128)S(1)} fusion(f32[32,4,32,128]{3,2,1,0:T(8,128)S(1)} %pad_maximum_fusion, f32[32,6,32,128]{3,2,1,0:T(8,128)S(1)} %broadcast_multiply_fusion, f32[32,2,32,128]{3,2,1,0:T(8,128)S(1)} %slice.216, f32[32,2,32,128]{3,2,1,0:T(8,128)S(1)} %bitcast.118, f32[32,2,32,128]{3,2,1,0:T(8,128)S(1)} %slice.215), kind=kLoop, calls=%fused_computation.14 | loop fusion | flops 5767168 | bytes 9437184 | tf_op jit(solution)/shard_map/add | solution.py:87
  32.5 0.7 fusion.25
  33.2 1.7 %convolution_bitcast_fusion = f32[4,8,64,128]{3,1,2,0:T(8,128)S(1)} fusion(f32[4,8,64,128]{3,2,1,0:T(8,128)S(1)} %bitcast.119, f32[1,32,32]{2,1,0:T(8,128)S(1)} %copy-done.3), kind=kOutput, calls=%fused_computation.19 | convolution fusion | flops 100663296 | bytes 2101248 | tf_op jit(solution)/shard_map/dot_general | solution.py:89
  36.2 0.6 broadcast_select_fusion
  36.9 2.7 %collective-permute-done.2 = f32[1,34,64]{2,1,0:T(8,128)S(1)} collective-permute-done((f32[1,34,64]{2,1,0:T(8,128)S(1)}, f32[1,34,64]{2,1,0:T(8,128)S(1)}, u32[]{:S(2)}, u32[]{:S(2)}) %collective-permute-start.2) | collective-permute-done | bytes 8736 | tf_op jit(solution)/shard_map/ppermute | solution.py:106
  40.1 0.7 collective-permute-start.13
  40.8 0.7 collective-permute-start.3
  41.5 0.7 collective-permute-start.6
  42.1 0.7 collective-permute-start.9
  42.8 2.6 %collective-permute-done.12 = f32[2,34,64]{2,1,0:T(8,128)S(1)} collective-permute-done((f32[2,34,64]{2,1,0:T(8,128)S(1)}, f32[2,34,64]{2,1,0:T(8,128)S(1)}, u32[]{:S(2)}, u32[]{:S(2)}) %collective-permute-start.12) | collective-permute-done | bytes 17440 | tf_op jit(solution)/shard_map/ppermute | solution.py:106
  46.5 0.7 collective-permute-start.4
  47.3 0.7 collective-permute-start.7
  48.2 0.7 collective-permute-start.10
  49.3 1.3 %collective-permute-start.5 = (f32[5,2,32,128]{3,2,1,0:T(8,128)S(1)}, f32[5,2,32,128]{3,2,1,0:T(8,128)S(1)}, u32[]{:S(2)}, u32[]{:S(2)}) collective-permute-start(f32[5,2,32,128]{3,2,1,0:T(8,128)S(1)} %multiply_add_fusion.10), channel_id=1, source_target_pairs={{16,24},{17,25},{18,26},{19,27},{20,28},{21,29},{22,30},{23,31}} | collective-permute-start | bytes 491528 | tf_op jit(solution)/shard_map/ppermute | solution.py:143
  50.6 2.3 %collective-permute-done.17 = f32[2,9,128]{2,1,0:T(8,128)S(1)} collective-permute-done((f32[2,9,128]{2,1,0:T(8,128)S(1)}, f32[2,9,128]{2,1,0:T(8,128)S(1)}, u32[]{:S(2)}, u32[]{:S(2)}) %collective-permute-start.17) | collective-permute-done | bytes 9248 | tf_op jit(solution)/shard_map/ppermute | solution.py:44
  53.1 0.7 collective-permute-start.14
  53.8 3.1 %collective-permute-done.18 = f32[4,9,128]{2,1,0:T(8,128)S(1)} collective-permute-done((f32[4,9,128]{2,1,0:T(8,128)S(1)}, f32[4,9,128]{2,1,0:T(8,128)S(1)}, u32[]{:S(2)}, u32[]{:S(2)}) %collective-permute-start.18) | collective-permute-done | bytes 18464 | tf_op jit(solution)/shard_map/ppermute | solution.py:44
  57.0 0.8 fusion.30
  57.9 1.3 %collective-permute-start.8 = (f32[7,2,32,128]{3,2,1,0:T(8,128)S(1)}, f32[7,2,32,128]{3,2,1,0:T(8,128)S(1)}, u32[]{:S(2)}, u32[]{:S(2)}) collective-permute-start(f32[7,2,32,128]{3,2,1,0:T(8,128)S(1)} %multiply_add_fusion.7), channel_id=1, source_target_pairs={{16,24},{17,25},{18,26},{19,27},{20,28},{21,29},{22,30},{23,31}} | collective-permute-start | bytes 688136 | tf_op jit(solution)/shard_map/ppermute | solution.py:143
  59.2 10.0 %collective-permute-done.5 = f32[5,2,32,128]{3,2,1,0:T(8,128)S(1)} collective-permute-done((f32[5,2,32,128]{3,2,1,0:T(8,128)S(1)}, f32[5,2,32,128]{3,2,1,0:T(8,128)S(1)}, u32[]{:S(2)}, u32[]{:S(2)}) %collective-permute-start.5) | collective-permute-done | bytes 163872 | tf_op jit(solution)/shard_map/ppermute | solution.py:143
  69.4 1.3 %collective-permute-start.11 = (f32[9,2,32,128]{3,2,1,0:T(8,128)S(1)}, f32[9,2,32,128]{3,2,1,0:T(8,128)S(1)}, u32[]{:S(2)}, u32[]{:S(2)}) collective-permute-start(f32[9,2,32,128]{3,2,1,0:T(8,128)S(1)} %multiply_add_fusion.4), channel_id=1, source_target_pairs={{16,24},{17,25},{18,26},{19,27},{20,28},{21,29},{22,30},{23,31}} | collective-permute-start | bytes 884744 | tf_op jit(solution)/shard_map/ppermute | solution.py:143
  70.8 1.3 %collective-permute-start.15 = (f32[11,2,32,128]{3,2,1,0:T(8,128)S(1)}, f32[11,2,32,128]{3,2,1,0:T(8,128)S(1)}, u32[]{:S(2)}, u32[]{:S(2)}) collective-permute-start(f32[11,2,32,128]{3,2,1,0:T(8,128)S(1)} %multiply_add_fusion.1), channel_id=1, source_target_pairs={{16,24},{17,25},{18,26},{19,27},{20,28},{21,29},{22,30},{23,31}} | collective-permute-start | bytes 1081352 | tf_op jit(solution)/shard_map/ppermute | solution.py:143
  72.1 4.2 %collective-permute-done.8 = f32[7,2,32,128]{3,2,1,0:T(8,128)S(1)} collective-permute-done((f32[7,2,32,128]{3,2,1,0:T(8,128)S(1)}, f32[7,2,32,128]{3,2,1,0:T(8,128)S(1)}, u32[]{:S(2)}, u32[]{:S(2)}) %collective-permute-start.8) | collective-permute-done | bytes 229408 | tf_op jit(solution)/shard_map/ppermute | solution.py:143
  76.4 9.7 %collective-permute-done.11 = f32[9,2,32,128]{3,2,1,0:T(8,128)S(1)} collective-permute-done((f32[9,2,32,128]{3,2,1,0:T(8,128)S(1)}, f32[9,2,32,128]{3,2,1,0:T(8,128)S(1)}, u32[]{:S(2)}, u32[]{:S(2)}) %collective-permute-start.11) | collective-permute-done | bytes 294944 | tf_op jit(solution)/shard_map/ppermute | solution.py:143
  86.2 9.0 %collective-permute-done.15 = f32[11,2,32,128]{3,2,1,0:T(8,128)S(1)} collective-permute-done((f32[11,2,32,128]{3,2,1,0:T(8,128)S(1)}, f32[11,2,32,128]{3,2,1,0:T(8,128)S(1)}, u32[]{:S(2)}, u32[]{:S(2)}) %collective-permute-start.15) | collective-permute-done | bytes 360480 | tf_op jit(solution)/shard_map/ppermute | solution.py:143
  95.4 1.1 %maximum_bitcast_fusion = f32[1,32,2,32,128]{4,3,2,1,0:T(8,128)} fusion(f32[11,2,32,128]{3,2,1,0:T(8,128)S(1)} %multiply_add_fusion, f32[9,2,32,128]{3,2,1,0:T(8,128)S(1)} %multiply_add_fusion.3, f32[7,2,32,128]{3,2,1,0:T(8,128)S(1)} %multiply_add_fusion.6, f32[5,2,32,128]{3,2,1,0:T(8,128)S(1)} %multiply_add_fusion.9), kind=kLoop, calls=%fused_computation.47 | loop fusion | flops 786432 | bytes 2097152 | tf_op jit(solution)/shard_map/broadcast_in_dim | solution.py:160
  (82 shorter events, 6.2 us)
Async XLA Ops:
  0.6 45.6 %copy-start = (bf16[1,8,64,128]{3,2,1,0:T(8,128)(2,1)S(1)}, bf16[1,8,64,128]{3,2,1,0:T(8,128)(2,1)}, u32[]{:S(2)}) copy-start(bf16[1,8,64,128]{3,2,1,0:T(8,128)(2,1)} %param.22) | copy-start | bytes 393220
  0.6 7.0 %copy-start.6 = (f32[1,32]{1,0:T(1,128)S(1)}, f32[1,32]{1,0:T(1,128)}, u32[]{:S(2)}) copy-start(f32[1,32]{1,0:T(1,128)} %param.19) | copy-start | bytes 388
  0.7 7.0 %copy-start.5 = (f32[1,32]{1,0:T(1,128)S(1)}, f32[1,32]{1,0:T(1,128)}, u32[]{:S(2)}) copy-start(f32[1,32]{1,0:T(1,128)} %param.21) | copy-start | bytes 388
  2.0 16.5 %collective-permute-start = (f32[33,2,32,128]{3,2,1,0:T(8,128)S(1)}, f32[33,2,32,128]{3,2,1,0:T(8,128)S(1)}, u32[]{:S(2)}, u32[]{:S(2)}) collective-permute-start(f32[33,2,32,128]{3,2,1,0:T(8,128)S(1)} %pad_maximum_fusion.2), channel_id=1, source_target_pairs={{0,1},{1,2},{2,3},{3,4},{4,5},{5,6},{6,7},{8,9},{9,10},{10,11},{11... | collective-permute-start | bytes 3244040 | tf_op jit(solution)/shard_map/ppermute | solution.py:78
  4.0 25.1 %collective-permute-start.1 = (f32[33,2,32,128]{3,2,1,0:T(8,128)S(1)}, f32[33,2,32,128]{3,2,1,0:T(8,128)S(1)}, u32[]{:S(2)}, u32[]{:S(2)}) collective-permute-start(f32[33,2,32,128]{3,2,1,0:T(8,128)S(1)} %pad_maximum_fusion.2), channel_id=1, source_target_pairs={{1,0},{2,1},{3,2},{4,3},{5,4},{6,5},{7,6},{9,8},{10,9},{11,10},{12... | collective-permute-start | bytes 3244040 | tf_op jit(solution)/shard_map/ppermute | solution.py:81
  8.7 20.5 %copy-start.1 = (f32[1,32,2,32,128]{4,3,2,1,0:T(8,128)S(1)}, f32[1,32,2,32,128]{4,3,2,1,0:T(8,128)}, u32[]{:S(2)}) copy-start(f32[1,32,2,32,128]{4,3,2,1,0:T(8,128)} %param.15) | copy-start | bytes 3145732
  29.2 0.8 copy-start.2
  29.2 0.8 copy-start.7
  32.5 0.8 copy-start.3
  33.2 1.9 %copy-start.4 = (f32[1,32]{1,0:T(1,128)S(1)}, f32[1,32]{1,0:T(1,128)}, u32[]{:S(2)}) copy-start(f32[1,32]{1,0:T(1,128)} %param.20) | copy-start | bytes 388
  34.9 1.3 %copy-start.8 = (s32[1,8]{1,0:T(1,128)S(1)}, s32[1,8]{1,0:T(1,128)}, u32[]{:S(2)}) copy-start(s32[1,8]{1,0:T(1,128)} %param.23) | copy-start | bytes 100
  35.7 3.8 %collective-permute-start.2 = (f32[1,34,64]{2,1,0:T(8,128)S(1)}, f32[1,34,64]{2,1,0:T(8,128)S(1)}, u32[]{:S(2)}, u32[]{:S(2)}) collective-permute-start(f32[1,34,64]{2,1,0:T(8,128)S(1)} %maximum_bitcast_fusion.1), channel_id=1, source_target_pairs={{0,8},{8,0},{16,24},{24,16},{1,9},{9,1},{17,25},{25,17},{2,10},{10... | collective-permute-start | bytes 26120 | tf_op jit(solution)/shard_map/ppermute | solution.py:106
  39.6 5.8 %collective-permute-start.12 = (f32[2,34,64]{2,1,0:T(8,128)S(1)}, f32[2,34,64]{2,1,0:T(8,128)S(1)}, u32[]{:S(2)}, u32[]{:S(2)}) collective-permute-start(f32[2,34,64]{2,1,0:T(8,128)S(1)} %maximum_select_fusion.2), channel_id=1, source_target_pairs={{0,16},{8,24},{16,0},{24,8},{1,17},{9,25},{17,1},{25,9},{2,18},{10... | collective-permute-start | bytes 52232 | tf_op jit(solution)/shard_map/ppermute | solution.py:106
  40.1 7.9 %collective-permute-start.13 = (f32[11,2,32,128]{3,2,1,0:T(8,128)S(1)}, f32[11,2,32,128]{3,2,1,0:T(8,128)S(1)}, u32[]{:S(2)}, u32[]{:S(2)}) collective-permute-start(f32[11,2,32,128]{3,2,1,0:T(8,128)S(1)} %slice.200), channel_id=1, source_target_pairs={{0,8},{1,9},{2,10},{3,11},{4,12},{5,13},{6,14},{7,15}} | collective-permute-start | bytes 1081352 | tf_op jit(solution)/shard_map/ppermute | solution.py:143
  40.8 5.6 %collective-permute-start.3 = (f32[5,2,32,128]{3,2,1,0:T(8,128)S(1)}, f32[5,2,32,128]{3,2,1,0:T(8,128)S(1)}, u32[]{:S(2)}, u32[]{:S(2)}) collective-permute-start(f32[5,2,32,128]{3,2,1,0:T(8,128)S(1)} %slice.194), channel_id=1, source_target_pairs={{0,8},{1,9},{2,10},{3,11},{4,12},{5,13},{6,14},{7,15}} | collective-permute-start | bytes 491528 | tf_op jit(solution)/shard_map/ppermute | solution.py:143
  41.5 5.7 %collective-permute-start.6 = (f32[7,2,32,128]{3,2,1,0:T(8,128)S(1)}, f32[7,2,32,128]{3,2,1,0:T(8,128)S(1)}, u32[]{:S(2)}, u32[]{:S(2)}) collective-permute-start(f32[7,2,32,128]{3,2,1,0:T(8,128)S(1)} %slice.196), channel_id=1, source_target_pairs={{0,8},{1,9},{2,10},{3,11},{4,12},{5,13},{6,14},{7,15}} | collective-permute-start | bytes 688136 | tf_op jit(solution)/shard_map/ppermute | solution.py:143
  42.1 6.0 %collective-permute-start.9 = (f32[9,2,32,128]{3,2,1,0:T(8,128)S(1)}, f32[9,2,32,128]{3,2,1,0:T(8,128)S(1)}, u32[]{:S(2)}, u32[]{:S(2)}) collective-permute-start(f32[9,2,32,128]{3,2,1,0:T(8,128)S(1)} %slice.198), channel_id=1, source_target_pairs={{0,8},{1,9},{2,10},{3,11},{4,12},{5,13},{6,14},{7,15}} | collective-permute-start | bytes 884744 | tf_op jit(solution)/shard_map/ppermute | solution.py:143
  46.5 2.7 %collective-permute-start.4 = (f32[5,2,32,128]{3,2,1,0:T(8,128)S(1)}, f32[5,2,32,128]{3,2,1,0:T(8,128)S(1)}, u32[]{:S(2)}, u32[]{:S(2)}) collective-permute-start(f32[5,2,32,128]{3,2,1,0:T(8,128)S(1)} %multiply_add_fusion.11), channel_id=1, source_target_pairs={{8,16},{9,17},{10,18},{11,19},{12,20},{13,21},{14,22},{15,23}} | collective-permute-start | bytes 491528 | tf_op jit(solution)/shard_map/ppermute | solution.py:143
  47.3 10.5 %collective-permute-start.7 = (f32[7,2,32,128]{3,2,1,0:T(8,128)S(1)}, f32[7,2,32,128]{3,2,1,0:T(8,128)S(1)}, u32[]{:S(2)}, u32[]{:S(2)}) collective-permute-start(f32[7,2,32,128]{3,2,1,0:T(8,128)S(1)} %multiply_add_fusion.8), channel_id=1, source_target_pairs={{8,16},{9,17},{10,18},{11,19},{12,20},{13,21},{14,22},{15,23}} | collective-permute-start | bytes 688136 | tf_op jit(solution)/shard_map/ppermute | solution.py:143
  48.0 1.2 %collective-permute-start.16 = (f32[1,9,128]{2,1,0:T(8,128)S(1)}, f32[1,9,128]{2,1,0:T(8,128)S(1)}, u32[]{:S(2)}, u32[]{:S(2)}) collective-permute-start(f32[1,9,128]{2,1,0:T(8,128)S(1)} %bitcast.122), channel_id=1, source_target_pairs={{0,1},{1,0},{2,3},{3,2},{4,5},{5,4},{6,7},{7,6},{8,9},{9,8},{10,11... | collective-permute-start | bytes 13832 | tf_op jit(solution)/shard_map/ppermute | solution.py:44
  48.2 21.1 %collective-permute-start.10 = (f32[9,2,32,128]{3,2,1,0:T(8,128)S(1)}, f32[9,2,32,128]{3,2,1,0:T(8,128)S(1)}, u32[]{:S(2)}, u32[]{:S(2)}) collective-permute-start(f32[9,2,32,128]{3,2,1,0:T(8,128)S(1)} %multiply_add_fusion.5), channel_id=1, source_target_pairs={{8,16},{9,17},{10,18},{11,19},{12,20},{13,21},{14,22},{15,23}} | collective-permute-start | bytes 884744 | tf_op jit(solution)/shard_map/ppermute | solution.py:143
  49.2 3.7 %collective-permute-start.17 = (f32[2,9,128]{2,1,0:T(8,128)S(1)}, f32[2,9,128]{2,1,0:T(8,128)S(1)}, u32[]{:S(2)}, u32[]{:S(2)}) collective-permute-start(f32[2,9,128]{2,1,0:T(8,128)S(1)} %maximum_select_fusion.4), channel_id=1, source_target_pairs={{0,2},{1,3},{2,0},{3,1},{4,6},{5,7},{6,4},{7,5},{8,10},{9,11},{10,... | collective-permute-start | bytes 27656 | tf_op jit(solution)/shard_map/ppermute | solution.py:44
  49.3 19.9 %collective-permute-start.5 = (f32[5,2,32,128]{3,2,1,0:T(8,128)S(1)}, f32[5,2,32,128]{3,2,1,0:T(8,128)S(1)}, u32[]{:S(2)}, u32[]{:S(2)}) collective-permute-start(f32[5,2,32,128]{3,2,1,0:T(8,128)S(1)} %multiply_add_fusion.10), channel_id=1, source_target_pairs={{16,24},{17,25},{18,26},{19,27},{20,28},{21,29},{22,30},{23,31}} | collective-permute-start | bytes 491528 | tf_op jit(solution)/shard_map/ppermute | solution.py:143
  53.0 3.9 %collective-permute-start.18 = (f32[4,9,128]{2,1,0:T(8,128)S(1)}, f32[4,9,128]{2,1,0:T(8,128)S(1)}, u32[]{:S(2)}, u32[]{:S(2)}) collective-permute-start(f32[4,9,128]{2,1,0:T(8,128)S(1)} %maximum_select_fusion.3), channel_id=1, source_target_pairs={{0,4},{1,5},{2,6},{3,7},{4,0},{5,1},{6,2},{7,3},{8,12},{9,13},{10,... | collective-permute-start | bytes 55304 | tf_op jit(solution)/shard_map/ppermute | solution.py:44
  53.1 17.6 %collective-permute-start.14 = (f32[11,2,32,128]{3,2,1,0:T(8,128)S(1)}, f32[11,2,32,128]{3,2,1,0:T(8,128)S(1)}, u32[]{:S(2)}, u32[]{:S(2)}) collective-permute-start(f32[11,2,32,128]{3,2,1,0:T(8,128)S(1)} %multiply_add_fusion.2), channel_id=1, source_target_pairs={{8,16},{9,17},{10,18},{11,19},{12,20},{13,21},{14,22},{15,23}} | collective-permute-start | bytes 1081352 | tf_op jit(solution)/shard_map/ppermute | solution.py:143
  57.9 18.4 %collective-permute-start.8 = (f32[7,2,32,128]{3,2,1,0:T(8,128)S(1)}, f32[7,2,32,128]{3,2,1,0:T(8,128)S(1)}, u32[]{:S(2)}, u32[]{:S(2)}) collective-permute-start(f32[7,2,32,128]{3,2,1,0:T(8,128)S(1)} %multiply_add_fusion.7), channel_id=1, source_target_pairs={{16,24},{17,25},{18,26},{19,27},{20,28},{21,29},{22,30},{23,31}} | collective-permute-start | bytes 688136 | tf_op jit(solution)/shard_map/ppermute | solution.py:143
  69.4 16.7 %collective-permute-start.11 = (f32[9,2,32,128]{3,2,1,0:T(8,128)S(1)}, f32[9,2,32,128]{3,2,1,0:T(8,128)S(1)}, u32[]{:S(2)}, u32[]{:S(2)}) collective-permute-start(f32[9,2,32,128]{3,2,1,0:T(8,128)S(1)} %multiply_add_fusion.4), channel_id=1, source_target_pairs={{16,24},{17,25},{18,26},{19,27},{20,28},{21,29},{22,30},{23,31}} | collective-permute-start | bytes 884744 | tf_op jit(solution)/shard_map/ppermute | solution.py:143
  70.8 24.4 %collective-permute-start.15 = (f32[11,2,32,128]{3,2,1,0:T(8,128)S(1)}, f32[11,2,32,128]{3,2,1,0:T(8,128)S(1)}, u32[]{:S(2)}, u32[]{:S(2)}) collective-permute-start(f32[11,2,32,128]{3,2,1,0:T(8,128)S(1)} %multiply_add_fusion.1), channel_id=1, source_target_pairs={{16,24},{17,25},{18,26},{19,27},{20,28},{21,29},{22,30},{23,31}} | collective-permute-start | bytes 1081352 | tf_op jit(solution)/shard_map/ppermute | solution.py:143

commit v8 on v7

--- a/solution.py
+++ b/solution.py
@@ -129,22 +129,23 @@
     lines, pixels = contribution.shape
     ids = jnp.zeros((1, pixels), jnp.float32).at[0, :lines].set(sky_blocks[0].astype(jnp.float32))
     payload = jnp.concatenate([contribution, ids], axis=0)
-    base = bins // CHUNKS
-    bounds = [0]
-    for c in range(CHUNKS):
-        bounds.append(bounds[-1] + base + 2 * c - (CHUNKS - 1))
-    bounds[-1] = bins
-    pieces = [own_part[bounds[c]:bounds[c + 1]] for c in range(CHUNKS)]
-    scales = [chain[bounds[c]:bounds[c + 1]][:, None, None, None] for c in range(CHUNKS)]
+    size = bins // CHUNKS
+    stack = own_part.reshape((CHUNKS, size) + own_part.shape[1:])
+    yields = chain.reshape(CHUNKS, size)[:, :, None, None, None]
+    pairs = [(g, g + 1) for g in range(groups - 1)]
     for wave in range(CHUNKS + groups - 2):
-        for c in range(CHUNKS):
-            s = wave - c
-            if 0 <= s < groups - 1:
-                arrived = lax.ppermute(pieces[c], "species", [(s, s + 1)])
-                if s == 0 and c == CHUNKS - 1:
-                    payload, arrived = lax.optimization_barrier((payload, arrived))
-                pieces[c] = pieces[c] + scales[c] * arrived
-    carried = jnp.concatenate(pieces, axis=0)
+        sent = lax.dynamic_index_in_dim(stack, jnp.clip(wave - me_g, 0, CHUNKS - 1), 0, keepdims=False)
+        arrived = lax.ppermute(sent, "species", pairs)
+        if wave == 0:
+            payload, arrived = lax.optimization_barrier((payload, arrived))
+        slot = wave - me_g + 1
+        valid = (me_g >= 1) & (slot >= 0) & (slot < CHUNKS)
+        slot = jnp.clip(slot, 0, CHUNKS - 1)
+        current = lax.dynamic_index_in_dim(stack, slot, 0, keepdims=False)
+        scale = lax.dynamic_index_in_dim(yields, slot, 0, keepdims=False)
+        updated = jnp.where(valid, current + scale * arrived, current)
+        stack = lax.dynamic_update_index_in_dim(stack, updated, slot, 0)
+    carried = stack.reshape(own_part.shape)
     gathered = gather_all(payload, "space")
     mine = lax.axis_index("space") * rows + jnp.arange(rows, dtype=jnp.int32)
     onehot = (

time: 96.9 us -> 101 us (1.042)
  the two profiles are of different devices: /device:TPU:26 before, /device:TPU:12 now
where the time goes in v8:
time: 101 us; the launch traced here: 100 us
  waiting for transfers between devices  62.9 us (62%)
  starting transfers between devices  21.8 us (22%)
  other arithmetic  7.9 us (8%)
  matrix products  3.35 us (3%)
  local copies, waits for them, and re-layouts  3.1 us (3%)
  between operations  1.2 us (1%)
    ppermute x6, waiting for transfers between devices, body(): arrived = lax.ppermute(sent, 'species', pairs)  36.5 us
    ppermute x1, waiting for transfers between devices, body(): lax.ppermute(mine[:, mine.shape[1] - halo:], 'space', [(i, i + 1) for i i...  16.9 us
    ppermute x6, starting transfers between devices, body(): arrived = lax.ppermute(sent, 'species', pairs)  12.1 us
    ppermute x3, waiting for transfers between devices, gather_all(): other = lax.ppermute(held, axis, [(i, i ^ span) for i in range(count)])  5 us
    ppermute x1, starting transfers between devices, body(): lax.ppermute(mine[:, :halo], 'space', [(i + 1, i) for i in range(count -...  4.54 us
    ppermute x2, waiting for transfers between devices, body(): lax.ppermute(everyone, 'species', [(i, i ^ span) for i in range(groups)])  3.63 us
    ppermute x2, starting transfers between devices, body(): lax.ppermute(everyone, 'species', [(i, i ^ span) for i in range(groups)])  3.17 us
    add x2, other arithmetic, body(): inner + wide_factor[:, 1 + step:wide_factor.shape[1] - 1 - step] * (besid...  2.71 us
  transfers between devices with their start and end apart: 13, of which 12 were waited for; matrix products, arithmetic and copies ran while one was open for 5% of the time, Pallas kernels for 0%

profile of v8, /device:TPU:12, one launch (start us, length us, event | category | flops | bytes accessed | tf_op | source)
XLA Modules:
  0.0 100.3 jit_solution(18086259340448185289)
XLA Ops:
  0.7 1.4 %pad_maximum_fusion.2 = f32[33,2,32,128]{3,2,1,0:T(8,128)S(1)} fusion(f32[1,2,32,128]{3,2,1,0:T(8,128)} %bitcast.176, f32[32,2,32,128]{3,2,1,0:T(8,128)} %bitcast.171), kind=kLoop, calls=%fused_computation.36 | loop fusion | flops 270336 | bytes 2162688 | tf_op jit(solution)/shard_map/concatenate | solution.py:77
  2.0 1.9 %collective-permute-start = (f32[33,2,32,128]{3,2,1,0:T(8,128)S(1)}, f32[33,2,32,128]{3,2,1,0:T(8,128)S(1)}, u32[]{:S(2)}, u32[]{:S(2)}) collective-permute-start(f32[33,2,32,128]{3,2,1,0:T(8,128)S(1)} %pad_maximum_fusion.2), channel_id=1, source_target_pairs={{0,1},{1,2},{2,3},{3,4},{4,5},{5,6},{6,7},{8,9},{9,10},{10,11},{11... | collective-permute-start | bytes 3244040 | tf_op jit(solution)/shard_map/ppermute | solution.py:78
  4.0 4.5 %collective-permute-start.1 = (f32[33,2,32,128]{3,2,1,0:T(8,128)S(1)}, f32[33,2,32,128]{3,2,1,0:T(8,128)S(1)}, u32[]{:S(2)}, u32[]{:S(2)}) collective-permute-start(f32[33,2,32,128]{3,2,1,0:T(8,128)S(1)} %pad_maximum_fusion.2), channel_id=1, source_target_pairs={{1,0},{2,1},{3,2},{4,3},{5,4},{6,5},{7,6},{9,8},{10,9},{11,10},{12... | collective-permute-start | bytes 3244040 | tf_op jit(solution)/shard_map/ppermute | solution.py:81
  8.6 0.5 broadcast.126
  9.1 0.7 reduce.19
  9.9 0.6 compare_reduce_fusion
  10.6 0.6 broadcast_select_fusion
  11.2 16.9 %collective-permute-done = f32[33,2,32,128]{3,2,1,0:T(8,128)S(1)} collective-permute-done((f32[33,2,32,128]{3,2,1,0:T(8,128)S(1)}, f32[33,2,32,128]{3,2,1,0:T(8,128)S(1)}, u32[]{:S(2)}, u32[]{:S(2)}) %collective-permute-start) | collective-permute-done | bytes 1081376 | tf_op jit(solution)/shard_map/ppermute | solution.py:78
  28.3 0.9 collective-permute-done.1
  30.4 2.0 %fusion.6 = f32[32,4,32,128]{3,2,1,0:T(8,128)S(1)} fusion(f32[32,4,32,128]{3,2,1,0:T(8,128)S(1)} %pad_maximum_fusion, f32[32,6,32,128]{3,2,1,0:T(8,128)S(1)} %broadcast_multiply_fusion, f32[32,2,32,128]{3,2,1,0:T(8,128)S(1)} %slice.180, f32[32,2,32,128]{3,2,1,0:T(8,128)S(1)} %bitcast.173, f32[32,2,32,128]{3,2,1,0:T(8,128)S(1)} %slice.179), kind=kLoop, calls=%fused_computation.14 | loop fusion | flops 5767168 | bytes 9437184 | tf_op jit(solution)/shard_map/add | solution.py:87
  32.5 0.7 fusion.25
  33.2 1.7 %convolution_bitcast_fusion = f32[4,8,64,128]{3,1,2,0:T(8,128)S(1)} fusion(f32[4,8,64,128]{3,2,1,0:T(8,128)S(1)} %bitcast.174, f32[1,32,32]{2,1,0:T(8,128)S(1)} %copy-done.4), kind=kOutput, calls=%fused_computation.19 | convolution fusion | flops 100663296 | bytes 2101248 | tf_op jit(solution)/shard_map/dot_general | solution.py:89
  35.1 0.5 fusion.61
  35.7 0.5 collective-permute-start.2
  36.3 3.3 %collective-permute-done.2 = f32[1,34,64]{2,1,0:T(8,128)S(1)} collective-permute-done((f32[1,34,64]{2,1,0:T(8,128)S(1)}, f32[1,34,64]{2,1,0:T(8,128)S(1)}, u32[]{:S(2)}, u32[]{:S(2)}) %collective-permute-start.2) | collective-permute-done | bytes 8736 | tf_op jit(solution)/shard_map/ppermute | solution.py:106
  39.6 2.7 %collective-permute-start.3 = (f32[2,34,64]{2,1,0:T(8,128)S(1)}, f32[2,34,64]{2,1,0:T(8,128)S(1)}, u32[]{:S(2)}, u32[]{:S(2)}) collective-permute-start(f32[2,34,64]{2,1,0:T(8,128)S(1)} %maximum_select_fusion.2), channel_id=1, source_target_pairs={{0,16},{8,24},{16,0},{24,8},{1,17},{9,25},{17,1},{25,9},{2,18},{10... | collective-permute-start | bytes 52232 | tf_op jit(solution)/shard_map/ppermute | solution.py:106
  42.3 1.9 %collective-permute-start.4 = (f32[8,2,32,128]{3,2,1,0:T(8,128)S(1)}, f32[8,2,32,128]{3,2,1,0:T(8,128)S(1)}, u32[]{:S(2)}, u32[]{:S(2)}) collective-permute-start(f32[8,2,32,128]{3,2,1,0:T(8,128)S(1)} %get-tuple-element.58), channel_id=1, source_target_pairs={{0,8},{8,16},{16,24},{1,9},{9,17},{17,25},{2,10},{10,18},{18,26},{... | collective-permute-start | bytes 786440 | tf_op jit(solution)/shard_map/ppermute | solution.py:138
  45.5 6.0 %collective-permute-done.4 = f32[8,2,32,128]{3,2,1,0:T(8,128)S(1)} collective-permute-done((f32[8,2,32,128]{3,2,1,0:T(8,128)S(1)}, f32[8,2,32,128]{3,2,1,0:T(8,128)S(1)}, u32[]{:S(2)}, u32[]{:S(2)}) %collective-permute-start.4) | collective-permute-done | bytes 262176 | tf_op jit(solution)/shard_map/ppermute | solution.py:138
  51.7 1.9 %collective-permute-start.5 = (f32[8,2,32,128]{3,2,1,0:T(8,128)S(1)}, f32[8,2,32,128]{3,2,1,0:T(8,128)S(1)}, u32[]{:S(2)}, u32[]{:S(2)}) collective-permute-start(f32[8,2,32,128]{3,2,1,0:T(8,128)S(1)} %get-tuple-element.56), channel_id=1, source_target_pairs={{0,8},{8,16},{16,24},{1,9},{9,17},{17,25},{2,10},{10,18},{18,26},{... | collective-permute-start | bytes 786440 | tf_op jit(solution)/shard_map/ppermute | solution.py:138
  53.7 8.5 %collective-permute-done.5 = f32[8,2,32,128]{3,2,1,0:T(8,128)S(1)} collective-permute-done((f32[8,2,32,128]{3,2,1,0:T(8,128)S(1)}, f32[8,2,32,128]{3,2,1,0:T(8,128)S(1)}, u32[]{:S(2)}, u32[]{:S(2)}) %collective-permute-start.5) | collective-permute-done | bytes 262176 | tf_op jit(solution)/shard_map/ppermute | solution.py:138
  62.4 1.9 %collective-permute-start.6 = (f32[8,2,32,128]{3,2,1,0:T(8,128)S(1)}, f32[8,2,32,128]{3,2,1,0:T(8,128)S(1)}, u32[]{:S(2)}, u32[]{:S(2)}) collective-permute-start(f32[8,2,32,128]{3,2,1,0:T(8,128)S(1)} %get-tuple-element.54), channel_id=1, source_target_pairs={{0,8},{8,16},{16,24},{1,9},{9,17},{17,25},{2,10},{10,18},{18,26},{... | collective-permute-start | bytes 786440 | tf_op jit(solution)/shard_map/ppermute | solution.py:138
  64.3 8.6 %collective-permute-done.6 = f32[8,2,32,128]{3,2,1,0:T(8,128)S(1)} collective-permute-done((f32[8,2,32,128]{3,2,1,0:T(8,128)S(1)}, f32[8,2,32,128]{3,2,1,0:T(8,128)S(1)}, u32[]{:S(2)}, u32[]{:S(2)}) %collective-permute-start.6) | collective-permute-done | bytes 262176 | tf_op jit(solution)/shard_map/ppermute | solution.py:138
  73.1 2.2 %collective-permute-start.7 = (f32[8,2,32,128]{3,2,1,0:T(8,128)S(1)}, f32[8,2,32,128]{3,2,1,0:T(8,128)S(1)}, u32[]{:S(2)}, u32[]{:S(2)}) collective-permute-start(f32[8,2,32,128]{3,2,1,0:T(8,128)S(1)} %get-tuple-element.52), channel_id=1, source_target_pairs={{0,8},{8,16},{16,24},{1,9},{9,17},{17,25},{2,10},{10,18},{18,26},{... | collective-permute-start | bytes 786440 | tf_op jit(solution)/shard_map/ppermute | solution.py:138
  75.3 1.1 %collective-permute-done.10 = f32[1,9,128]{2,1,0:T(8,128)S(1)} collective-permute-done((f32[1,9,128]{2,1,0:T(8,128)S(1)}, f32[1,9,128]{2,1,0:T(8,128)S(1)}, u32[]{:S(2)}, u32[]{:S(2)}) %collective-permute-start.10) | collective-permute-done | bytes 4640 | tf_op jit(solution)/shard_map/ppermute | solution.py:44
  76.5 4.8 %collective-permute-done.7 = f32[8,2,32,128]{3,2,1,0:T(8,128)S(1)} collective-permute-done((f32[8,2,32,128]{3,2,1,0:T(8,128)S(1)}, f32[8,2,32,128]{3,2,1,0:T(8,128)S(1)}, u32[]{:S(2)}, u32[]{:S(2)}) %collective-permute-start.7) | collective-permute-done | bytes 262176 | tf_op jit(solution)/shard_map/ppermute | solution.py:138
  81.5 2.2 %collective-permute-start.8 = (f32[8,2,32,128]{3,2,1,0:T(8,128)S(1)}, f32[8,2,32,128]{3,2,1,0:T(8,128)S(1)}, u32[]{:S(2)}, u32[]{:S(2)}) collective-permute-start(f32[8,2,32,128]{3,2,1,0:T(8,128)S(1)} %get-tuple-element.50), channel_id=1, source_target_pairs={{0,8},{8,16},{16,24},{1,9},{9,17},{17,25},{2,10},{10,18},{18,26},{... | collective-permute-start | bytes 786440 | tf_op jit(solution)/shard_map/ppermute | solution.py:138
  83.8 3.9 %collective-permute-done.12 = f32[4,9,128]{2,1,0:T(8,128)S(1)} collective-permute-done((f32[4,9,128]{2,1,0:T(8,128)S(1)}, f32[4,9,128]{2,1,0:T(8,128)S(1)}, u32[]{:S(2)}, u32[]{:S(2)}) %collective-permute-start.12) | collective-permute-done | bytes 18464 | tf_op jit(solution)/shard_map/ppermute | solution.py:44
  87.7 3.1 %collective-permute-done.8 = f32[8,2,32,128]{3,2,1,0:T(8,128)S(1)} collective-permute-done((f32[8,2,32,128]{3,2,1,0:T(8,128)S(1)}, f32[8,2,32,128]{3,2,1,0:T(8,128)S(1)}, u32[]{:S(2)}, u32[]{:S(2)}) %collective-permute-start.8) | collective-permute-done | bytes 262176 | tf_op jit(solution)/shard_map/ppermute | solution.py:138
  91.0 1.9 %collective-permute-start.9 = (f32[8,2,32,128]{3,2,1,0:T(8,128)S(1)}, f32[8,2,32,128]{3,2,1,0:T(8,128)S(1)}, u32[]{:S(2)}, u32[]{:S(2)}) collective-permute-start(f32[8,2,32,128]{3,2,1,0:T(8,128)S(1)} %get-tuple-element.48), channel_id=1, source_target_pairs={{0,8},{8,16},{16,24},{1,9},{9,17},{17,25},{2,10},{10,18},{18,26},{... | collective-permute-start | bytes 786440 | tf_op jit(solution)/shard_map/ppermute | solution.py:138
  93.0 0.8 fusion.42
  93.8 5.4 %collective-permute-done.9 = f32[8,2,32,128]{3,2,1,0:T(8,128)S(1)} collective-permute-done((f32[8,2,32,128]{3,2,1,0:T(8,128)S(1)}, f32[8,2,32,128]{3,2,1,0:T(8,128)S(1)}, u32[]{:S(2)}, u32[]{:S(2)}) %collective-permute-start.9) | collective-permute-done | bytes 262176 | tf_op jit(solution)/shard_map/ppermute | solution.py:138
  99.4 1.0 copy-done.1
  (67 shorter events, 4.4 us)
Async XLA Ops:
  0.6 44.7 %copy-start = (bf16[1,8,64,128]{3,2,1,0:T(8,128)(2,1)S(1)}, bf16[1,8,64,128]{3,2,1,0:T(8,128)(2,1)}, u32[]{:S(2)}) copy-start(bf16[1,8,64,128]{3,2,1,0:T(8,128)(2,1)} %param.22) | copy-start | bytes 393220
  0.6 7.9 %copy-start.6 = (f32[1,32]{1,0:T(1,128)S(1)}, f32[1,32]{1,0:T(1,128)}, u32[]{:S(2)}) copy-start(f32[1,32]{1,0:T(1,128)} %param.19) | copy-start | bytes 388
  0.7 9.2 %copy-start.7 = (f32[1,32]{1,0:T(1,128)S(1)}, f32[1,32]{1,0:T(1,128)}, u32[]{:S(2)}) copy-start(f32[1,32]{1,0:T(1,128)} %param.21) | copy-start | bytes 388
  0.7 9.9 %copy-start.9 = (s32[1,8]{1,0:T(1,128)S(1)}, s32[1,8]{1,0:T(1,128)}, u32[]{:S(2)}) copy-start(s32[1,8]{1,0:T(1,128)} %param.23) | copy-start | bytes 100
  2.0 26.1 %collective-permute-start = (f32[33,2,32,128]{3,2,1,0:T(8,128)S(1)}, f32[33,2,32,128]{3,2,1,0:T(8,128)S(1)}, u32[]{:S(2)}, u32[]{:S(2)}) collective-permute-start(f32[33,2,32,128]{3,2,1,0:T(8,128)S(1)} %pad_maximum_fusion.2), channel_id=1, source_target_pairs={{0,1},{1,2},{2,3},{3,4},{4,5},{5,6},{6,7},{8,9},{9,10},{10,11},{11... | collective-permute-start | bytes 3244040 | tf_op jit(solution)/shard_map/ppermute | solution.py:78
  4.0 25.1 %collective-permute-start.1 = (f32[33,2,32,128]{3,2,1,0:T(8,128)S(1)}, f32[33,2,32,128]{3,2,1,0:T(8,128)S(1)}, u32[]{:S(2)}, u32[]{:S(2)}) collective-permute-start(f32[33,2,32,128]{3,2,1,0:T(8,128)S(1)} %pad_maximum_fusion.2), channel_id=1, source_target_pairs={{1,0},{2,1},{3,2},{4,3},{5,4},{6,5},{7,6},{9,8},{10,9},{11,10},{12... | collective-permute-start | bytes 3244040 | tf_op jit(solution)/shard_map/ppermute | solution.py:81
  11.2 17.9 %copy-start.2 = (f32[1,32,2,32,128]{4,3,2,1,0:T(8,128)S(1)}, f32[1,32,2,32,128]{4,3,2,1,0:T(8,128)}, u32[]{:S(2)}) copy-start(f32[1,32,2,32,128]{4,3,2,1,0:T(8,128)} %param.15) | copy-start | bytes 3145732
  29.2 0.8 copy-start.3
  29.2 0.8 copy-start.8
  32.5 0.8 copy-start.4
  33.2 1.9 %copy-start.5 = (f32[1,32]{1,0:T(1,128)S(1)}, f32[1,32]{1,0:T(1,128)}, u32[]{:S(2)}) copy-start(f32[1,32]{1,0:T(1,128)} %param.20) | copy-start | bytes 388
  35.7 3.8 %collective-permute-start.2 = (f32[1,34,64]{2,1,0:T(8,128)S(1)}, f32[1,34,64]{2,1,0:T(8,128)S(1)}, u32[]{:S(2)}, u32[]{:S(2)}) collective-permute-start(f32[1,34,64]{2,1,0:T(8,128)S(1)} %maximum_bitcast_fusion), channel_id=1, source_target_pairs={{0,8},{8,0},{16,24},{24,16},{1,9},{9,1},{17,25},{25,17},{2,10},{10... | collective-permute-start | bytes 26120 | tf_op jit(solution)/shard_map/ppermute | solution.py:106
  39.6 5.0 %collective-permute-start.3 = (f32[2,34,64]{2,1,0:T(8,128)S(1)}, f32[2,34,64]{2,1,0:T(8,128)S(1)}, u32[]{:S(2)}, u32[]{:S(2)}) collective-permute-start(f32[2,34,64]{2,1,0:T(8,128)S(1)} %maximum_select_fusion.2), channel_id=1, source_target_pairs={{0,16},{8,24},{16,0},{24,8},{1,17},{9,25},{17,1},{25,9},{2,18},{10... | collective-permute-start | bytes 52232 | tf_op jit(solution)/shard_map/ppermute | solution.py:106
  42.3 9.3 %collective-permute-start.4 = (f32[8,2,32,128]{3,2,1,0:T(8,128)S(1)}, f32[8,2,32,128]{3,2,1,0:T(8,128)S(1)}, u32[]{:S(2)}, u32[]{:S(2)}) collective-permute-start(f32[8,2,32,128]{3,2,1,0:T(8,128)S(1)} %get-tuple-element.58), channel_id=1, source_target_pairs={{0,8},{8,16},{16,24},{1,9},{9,17},{17,25},{2,10},{10,18},{18,26},{... | collective-permute-start | bytes 786440 | tf_op jit(solution)/shard_map/ppermute | solution.py:138
  51.7 10.5 %collective-permute-start.5 = (f32[8,2,32,128]{3,2,1,0:T(8,128)S(1)}, f32[8,2,32,128]{3,2,1,0:T(8,128)S(1)}, u32[]{:S(2)}, u32[]{:S(2)}) collective-permute-start(f32[8,2,32,128]{3,2,1,0:T(8,128)S(1)} %get-tuple-element.56), channel_id=1, source_target_pairs={{0,8},{8,16},{16,24},{1,9},{9,17},{17,25},{2,10},{10,18},{18,26},{... | collective-permute-start | bytes 786440 | tf_op jit(solution)/shard_map/ppermute | solution.py:138
  62.4 10.5 %collective-permute-start.6 = (f32[8,2,32,128]{3,2,1,0:T(8,128)S(1)}, f32[8,2,32,128]{3,2,1,0:T(8,128)S(1)}, u32[]{:S(2)}, u32[]{:S(2)}) collective-permute-start(f32[8,2,32,128]{3,2,1,0:T(8,128)S(1)} %get-tuple-element.54), channel_id=1, source_target_pairs={{0,8},{8,16},{16,24},{1,9},{9,17},{17,25},{2,10},{10,18},{18,26},{... | collective-permute-start | bytes 786440 | tf_op jit(solution)/shard_map/ppermute | solution.py:138
  73.1 8.3 %collective-permute-start.7 = (f32[8,2,32,128]{3,2,1,0:T(8,128)S(1)}, f32[8,2,32,128]{3,2,1,0:T(8,128)S(1)}, u32[]{:S(2)}, u32[]{:S(2)}) collective-permute-start(f32[8,2,32,128]{3,2,1,0:T(8,128)S(1)} %get-tuple-element.52), channel_id=1, source_target_pairs={{0,8},{8,16},{16,24},{1,9},{9,17},{17,25},{2,10},{10,18},{18,26},{... | collective-permute-start | bytes 786440 | tf_op jit(solution)/shard_map/ppermute | solution.py:138
  75.3 1.2 %collective-permute-start.10 = (f32[1,9,128]{2,1,0:T(8,128)S(1)}, f32[1,9,128]{2,1,0:T(8,128)S(1)}, u32[]{:S(2)}, u32[]{:S(2)}) collective-permute-start(f32[1,9,128]{2,1,0:T(8,128)S(1)} %bitcast.177), channel_id=1, source_target_pairs={{0,1},{1,0},{2,3},{3,2},{4,5},{5,4},{6,7},{7,6},{8,9},{9,8},{10,11... | collective-permute-start | bytes 13832 | tf_op jit(solution)/shard_map/ppermute | solution.py:44
  76.5 7.2 %collective-permute-start.11 = (f32[2,9,128]{2,1,0:T(8,128)S(1)}, f32[2,9,128]{2,1,0:T(8,128)S(1)}, u32[]{:S(2)}, u32[]{:S(2)}) collective-permute-start(f32[2,9,128]{2,1,0:T(8,128)S(1)} %maximum_select_fusion.4), channel_id=1, source_target_pairs={{0,2},{1,3},{2,0},{3,1},{4,6},{5,7},{6,4},{7,5},{8,10},{9,11},{10,... | collective-permute-start | bytes 27656 | tf_op jit(solution)/shard_map/ppermute | solution.py:44
  81.5 9.3 %collective-permute-start.8 = (f32[8,2,32,128]{3,2,1,0:T(8,128)S(1)}, f32[8,2,32,128]{3,2,1,0:T(8,128)S(1)}, u32[]{:S(2)}, u32[]{:S(2)}) collective-permute-start(f32[8,2,32,128]{3,2,1,0:T(8,128)S(1)} %get-tuple-element.50), channel_id=1, source_target_pairs={{0,8},{8,16},{16,24},{1,9},{9,17},{17,25},{2,10},{10,18},{18,26},{... | collective-permute-start | bytes 786440 | tf_op jit(solution)/shard_map/ppermute | solution.py:138
  83.7 4.0 %collective-permute-start.12 = (f32[4,9,128]{2,1,0:T(8,128)S(1)}, f32[4,9,128]{2,1,0:T(8,128)S(1)}, u32[]{:S(2)}, u32[]{:S(2)}) collective-permute-start(f32[4,9,128]{2,1,0:T(8,128)S(1)} %maximum_select_fusion.3), channel_id=1, source_target_pairs={{0,4},{1,5},{2,6},{3,7},{4,0},{5,1},{6,2},{7,3},{8,12},{9,13},{10,... | collective-permute-start | bytes 55304 | tf_op jit(solution)/shard_map/ppermute | solution.py:44
  91.0 8.3 %collective-permute-start.9 = (f32[8,2,32,128]{3,2,1,0:T(8,128)S(1)}, f32[8,2,32,128]{3,2,1,0:T(8,128)S(1)}, u32[]{:S(2)}, u32[]{:S(2)}) collective-permute-start(f32[8,2,32,128]{3,2,1,0:T(8,128)S(1)} %get-tuple-element.48), channel_id=1, source_target_pairs={{0,8},{8,16},{16,24},{1,9},{9,17},{17,25},{2,10},{10,18},{18,26},{... | collective-permute-start | bytes 786440 | tf_op jit(solution)/shard_map/ppermute | solution.py:138
  99.4 1.0 copy-start.1

commit v9 on v7

--- a/solution.py
+++ b/solution.py
@@ -99,13 +99,29 @@
     cols = own_columns.shape[1]
     extra = jnp.zeros((2, cols), jnp.float32).at[0, :bins].set(chain).at[1, :bins].set(gamma_yield[0])
     packed = jnp.concatenate([own_columns, extra], axis=0)
+    me_chain = lax.axis_index("species")
+    size = bins // CHUNKS
+    stack = own_part.reshape((CHUNKS, size) + own_part.shape[1:])
+    yields = chain.reshape(CHUNKS, size)[:, :, None, None, None]
+    pairs = [(g, g + 1) for g in range(groups - 1)]
+    for wave in range(CHUNKS + groups - 2):
+        sent = lax.dynamic_index_in_dim(stack, jnp.clip(wave - me_chain, 0, CHUNKS - 1), 0, keepdims=False)
+        arrived = lax.ppermute(sent, "species", pairs)
+        if wave == 0:
+            packed, arrived = lax.optimization_barrier((packed, arrived))
+        slot = wave - me_chain + 1
+        valid = (me_chain >= 1) & (slot >= 0) & (slot < CHUNKS)
+        slot = jnp.clip(slot, 0, CHUNKS - 1)
+        current = lax.dynamic_index_in_dim(stack, slot, 0, keepdims=False)
+        scale = lax.dynamic_index_in_dim(yields, slot, 0, keepdims=False)
+        updated = jnp.where(valid, current + scale * arrived, current)
+        stack = lax.dynamic_update_index_in_dim(stack, updated, slot, 0)
+    carried = stack.reshape(own_part.shape)
     me_g = lax.axis_index("species")
     everyone = packed[None]
     span = 1
     while span < groups:
         other = lax.ppermute(everyone, "species", [(i, i ^ span) for i in range(groups)])
-        if span == 1:
-            own_part, other = lax.optimization_barrier((own_part, other))
         low = (me_g & span) == 0
         everyone = jnp.where(
             low,
@@ -129,22 +145,6 @@
     lines, pixels = contribution.shape
     ids = jnp.zeros((1, pixels), jnp.float32).at[0, :lines].set(sky_blocks[0].astype(jnp.float32))
     payload = jnp.concatenate([contribution, ids], axis=0)
-    base = bins // CHUNKS
-    bounds = [0]
-    for c in range(CHUNKS):
-        bounds.append(bounds[-1] + base + 2 * c - (CHUNKS - 1))
-    bounds[-1] = bins
-    pieces = [own_part[bounds[c]:bounds[c + 1]] for c in range(CHUNKS)]
-    scales = [chain[bounds[c]:bounds[c + 1]][:, None, None, None] for c in range(CHUNKS)]
-    for wave in range(CHUNKS + groups - 2):
-        for c in range(CHUNKS):
-            s = wave - c
-            if 0 <= s < groups - 1:
-                arrived = lax.ppermute(pieces[c], "species", [(s, s + 1)])
-                if s == 0 and c == CHUNKS - 1:
-                    payload, arrived = lax.optimization_barrier((payload, arrived))
-                pieces[c] = pieces[c] + scales[c] * arrived
-    carried = jnp.concatenate(pieces, axis=0)
     gathered = gather_all(payload, "space")
     mine = lax.axis_index("space") * rows + jnp.arange(rows, dtype=jnp.int32)
     onehot = (

time: 96.9 us -> 99.3 us (1.025)
  the two profiles are of different devices: /device:TPU:26 before, /device:TPU:12 now
where the time goes in v9:
time: 99.3 us; the launch traced here: 98.8 us
  waiting for transfers between devices  59.1 us (60%)
  starting transfers between devices  23.2 us (23%)
  other arithmetic  8.71 us (9%)
  local copies, waits for them, and re-layouts  3.35 us (3%)
  matrix products  3.33 us (3%)
  between operations  1.17 us (1%)
    ppermute x6, waiting for transfers between devices, body(): arrived = lax.ppermute(sent, 'species', pairs)  33.2 us
    ppermute x1, waiting for transfers between devices, body(): lax.ppermute(mine[:, mine.shape[1] - halo:], 'space', [(i, i + 1) for i i...  16.1 us
    ppermute x6, starting transfers between devices, body(): arrived = lax.ppermute(sent, 'species', pairs)  13.8 us
    ppermute x3, waiting for transfers between devices, gather_all(): other = lax.ppermute(held, axis, [(i, i ^ span) for i in range(count)])  5 us
    ppermute x1, starting transfers between devices, body(): lax.ppermute(mine[:, :halo], 'space', [(i + 1, i) for i in range(count -...  4.54 us
    ppermute x2, waiting for transfers between devices, body(): lax.ppermute(everyone, 'species', [(i, i ^ span) for i in range(groups)])  3.85 us
    ppermute x2, starting transfers between devices, body(): lax.ppermute(everyone, 'species', [(i, i ^ span) for i in range(groups)])  2.83 us
    add x2, other arithmetic, body(): inner + wide_factor[:, 1 + step:wide_factor.shape[1] - 1 - step] * (besid...  2.71 us
  transfers between devices with their start and end apart: 13, of which 12 were waited for; matrix products, arithmetic and copies ran while one was open for 6% of the time, Pallas kernels for 0%

profile of v9, /device:TPU:12, one launch (start us, length us, event | category | flops | bytes accessed | tf_op | source)
XLA Modules:
  0.0 98.8 jit_solution(14997715864044117709)
XLA Ops:
  0.7 1.4 %pad_maximum_fusion.2 = f32[33,2,32,128]{3,2,1,0:T(8,128)S(1)} fusion(f32[1,2,32,128]{3,2,1,0:T(8,128)} %bitcast.176, f32[32,2,32,128]{3,2,1,0:T(8,128)} %bitcast.168), kind=kLoop, calls=%fused_computation.35 | loop fusion | flops 270336 | bytes 2162688 | tf_op jit(solution)/shard_map/concatenate | solution.py:77
  2.1 1.9 %collective-permute-start = (f32[33,2,32,128]{3,2,1,0:T(8,128)S(1)}, f32[33,2,32,128]{3,2,1,0:T(8,128)S(1)}, u32[]{:S(2)}, u32[]{:S(2)}) collective-permute-start(f32[33,2,32,128]{3,2,1,0:T(8,128)S(1)} %pad_maximum_fusion.2), channel_id=1, source_target_pairs={{0,1},{1,2},{2,3},{3,4},{4,5},{5,6},{6,7},{8,9},{9,10},{10,11},{11... | collective-permute-start | bytes 3244040 | tf_op jit(solution)/shard_map/ppermute | solution.py:78
  4.0 4.5 %collective-permute-start.1 = (f32[33,2,32,128]{3,2,1,0:T(8,128)S(1)}, f32[33,2,32,128]{3,2,1,0:T(8,128)S(1)}, u32[]{:S(2)}, u32[]{:S(2)}) collective-permute-start(f32[33,2,32,128]{3,2,1,0:T(8,128)S(1)} %pad_maximum_fusion.2), channel_id=1, source_target_pairs={{1,0},{2,1},{3,2},{4,3},{5,4},{6,5},{7,6},{9,8},{10,9},{11,10},{12... | collective-permute-start | bytes 3244040 | tf_op jit(solution)/shard_map/ppermute | solution.py:81
  8.6 0.5 broadcast.130
  9.1 0.7 reduce.22
  9.8 0.7 reduce.23
  10.8 0.6 compare_reduce_fusion
  11.4 0.7 broadcast_select_fusion
  12.1 16.1 %collective-permute-done = f32[33,2,32,128]{3,2,1,0:T(8,128)S(1)} collective-permute-done((f32[33,2,32,128]{3,2,1,0:T(8,128)S(1)}, f32[33,2,32,128]{3,2,1,0:T(8,128)S(1)}, u32[]{:S(2)}, u32[]{:S(2)}) %collective-permute-start) | collective-permute-done | bytes 1081376 | tf_op jit(solution)/shard_map/ppermute | solution.py:78
  28.3 0.9 collective-permute-done.1
  29.5 0.5 copy-done.2
  30.4 2.0 %fusion.6 = f32[32,4,32,128]{3,2,1,0:T(8,128)S(1)} fusion(f32[32,4,32,128]{3,2,1,0:T(8,128)S(1)} %pad_maximum_fusion, f32[32,6,32,128]{3,2,1,0:T(8,128)S(1)} %broadcast_multiply_fusion, f32[32,2,32,128]{3,2,1,0:T(8,128)S(1)} %slice.180, f32[32,2,32,128]{3,2,1,0:T(8,128)S(1)} %bitcast.170, f32[32,2,32,128]{3,2,1,0:T(8,128)S(1)} %slice.179), kind=kLoop, calls=%fused_computation.14 | loop fusion | flops 5767168 | bytes 9437184 | tf_op jit(solution)/shard_map/add | solution.py:87
  32.5 0.7 fusion.25
  33.3 1.7 %fusion.26 = f32[8192,32]{0,1:T(8,128)S(1)} fusion(f32[4,8,64,128]{3,2,1,0:T(8,128)S(1)} %bitcast.173, f32[1,32,32]{2,1,0:T(8,128)S(1)} %copy-done.3), kind=kOutput, calls=%fused_computation.43 | convolution fusion | flops 100663296 | bytes 2101248 | tf_op jit(solution)/shard_map/dot_general | solution.py:89
  35.1 3.5 %collective-permute-start.2 = (f32[8,2,32,128]{3,0,2,1:T(8,128)S(1)}, f32[8,2,32,128]{3,0,2,1:T(8,128)S(1)}, u32[]{:S(2)}, u32[]{:S(2)}) collective-permute-start(f32[8,2,32,128]{3,0,2,1:T(8,128)S(1)} %get-tuple-element.52), channel_id=1, source_target_pairs={{0,8},{8,16},{16,24},{1,9},{9,17},{17,25},{2,10},{10,18},{18,26},{... | collective-permute-start | bytes 786440 | tf_op jit(solution)/shard_map/ppermute | solution.py:109
  39.4 4.2 %collective-permute-done.2 = f32[8,2,32,128]{3,0,2,1:T(8,128)S(1)} collective-permute-done((f32[8,2,32,128]{3,0,2,1:T(8,128)S(1)}, f32[8,2,32,128]{3,0,2,1:T(8,128)S(1)}, u32[]{:S(2)}, u32[]{:S(2)}) %collective-permute-start.2) | collective-permute-done | bytes 262176 | tf_op jit(solution)/shard_map/ppermute | solution.py:109
  43.7 3.7 %collective-permute-done.8 = f32[1,34,64]{2,1,0:T(8,128)S(1)} collective-permute-done((f32[1,34,64]{2,1,0:T(8,128)S(1)}, f32[1,34,64]{2,1,0:T(8,128)S(1)}, u32[]{:S(2)}, u32[]{:S(2)}) %collective-permute-start.8) | collective-permute-done | bytes 8736 | tf_op jit(solution)/shard_map/ppermute | solution.py:124
  47.4 2.8 %collective-permute-start.9 = (f32[2,34,64]{2,1,0:T(8,128)S(1)}, f32[2,34,64]{2,1,0:T(8,128)S(1)}, u32[]{:S(2)}, u32[]{:S(2)}) collective-permute-start(f32[2,34,64]{2,1,0:T(8,128)S(1)} %maximum_select_fusion.2), channel_id=1, source_target_pairs={{0,16},{8,24},{16,0},{24,8},{1,17},{9,25},{17,1},{25,9},{2,18},{10... | collective-permute-start | bytes 52232 | tf_op jit(solution)/shard_map/ppermute | solution.py:124
  50.3 1.9 %collective-permute-start.3 = (f32[8,2,32,128]{3,0,2,1:T(8,128)S(1)}, f32[8,2,32,128]{3,0,2,1:T(8,128)S(1)}, u32[]{:S(2)}, u32[]{:S(2)}) collective-permute-start(f32[8,2,32,128]{3,0,2,1:T(8,128)S(1)} %get-tuple-element.50), channel_id=1, source_target_pairs={{0,8},{8,16},{16,24},{1,9},{9,17},{17,25},{2,10},{10,18},{18,26},{... | collective-permute-start | bytes 786440 | tf_op jit(solution)/shard_map/ppermute | solution.py:109
  52.9 8.2 %collective-permute-done.3 = f32[8,2,32,128]{3,0,2,1:T(8,128)S(1)} collective-permute-done((f32[8,2,32,128]{3,0,2,1:T(8,128)S(1)}, f32[8,2,32,128]{3,0,2,1:T(8,128)S(1)}, u32[]{:S(2)}, u32[]{:S(2)}) %collective-permute-start.3) | collective-permute-done | bytes 262176 | tf_op jit(solution)/shard_map/ppermute | solution.py:109
  61.2 1.9 %collective-permute-start.4 = (f32[8,2,32,128]{3,0,2,1:T(8,128)S(1)}, f32[8,2,32,128]{3,0,2,1:T(8,128)S(1)}, u32[]{:S(2)}, u32[]{:S(2)}) collective-permute-start(f32[8,2,32,128]{3,0,2,1:T(8,128)S(1)} %get-tuple-element.48), channel_id=1, source_target_pairs={{0,8},{8,16},{16,24},{1,9},{9,17},{17,25},{2,10},{10,18},{18,26},{... | collective-permute-start | bytes 786440 | tf_op jit(solution)/shard_map/ppermute | solution.py:109
  63.4 8.0 %collective-permute-done.4 = f32[8,2,32,128]{3,0,2,1:T(8,128)S(1)} collective-permute-done((f32[8,2,32,128]{3,0,2,1:T(8,128)S(1)}, f32[8,2,32,128]{3,0,2,1:T(8,128)S(1)}, u32[]{:S(2)}, u32[]{:S(2)}) %collective-permute-start.4) | collective-permute-done | bytes 262176 | tf_op jit(solution)/shard_map/ppermute | solution.py:109
  71.6 2.2 %collective-permute-start.5 = (f32[8,2,32,128]{3,0,2,1:T(8,128)S(1)}, f32[8,2,32,128]{3,0,2,1:T(8,128)S(1)}, u32[]{:S(2)}, u32[]{:S(2)}) collective-permute-start(f32[8,2,32,128]{3,0,2,1:T(8,128)S(1)} %get-tuple-element.46), channel_id=1, source_target_pairs={{0,8},{8,16},{16,24},{1,9},{9,17},{17,25},{2,10},{10,18},{18,26},{... | collective-permute-start | bytes 786440 | tf_op jit(solution)/shard_map/ppermute | solution.py:109
  74.1 1.1 %collective-permute-done.10 = f32[1,9,128]{2,1,0:T(8,128)S(1)} collective-permute-done((f32[1,9,128]{2,1,0:T(8,128)S(1)}, f32[1,9,128]{2,1,0:T(8,128)S(1)}, u32[]{:S(2)}, u32[]{:S(2)}) %collective-permute-start.10) | collective-permute-done | bytes 4640 | tf_op jit(solution)/shard_map/ppermute | solution.py:44
  75.2 4.6 %collective-permute-done.5 = f32[8,2,32,128]{3,0,2,1:T(8,128)S(1)} collective-permute-done((f32[8,2,32,128]{3,0,2,1:T(8,128)S(1)}, f32[8,2,32,128]{3,0,2,1:T(8,128)S(1)}, u32[]{:S(2)}, u32[]{:S(2)}) %collective-permute-start.5) | collective-permute-done | bytes 262176 | tf_op jit(solution)/shard_map/ppermute | solution.py:109
  80.0 2.2 %collective-permute-start.6 = (f32[8,2,32,128]{3,0,2,1:T(8,128)S(1)}, f32[8,2,32,128]{3,0,2,1:T(8,128)S(1)}, u32[]{:S(2)}, u32[]{:S(2)}) collective-permute-start(f32[8,2,32,128]{3,0,2,1:T(8,128)S(1)} %get-tuple-element.44), channel_id=1, source_target_pairs={{0,8},{8,16},{16,24},{1,9},{9,17},{17,25},{2,10},{10,18},{18,26},{... | collective-permute-start | bytes 786440 | tf_op jit(solution)/shard_map/ppermute | solution.py:109
  82.4 3.9 %collective-permute-done.12 = f32[4,9,128]{2,1,0:T(8,128)S(1)} collective-permute-done((f32[4,9,128]{2,1,0:T(8,128)S(1)}, f32[4,9,128]{2,1,0:T(8,128)S(1)}, u32[]{:S(2)}, u32[]{:S(2)}) %collective-permute-start.12) | collective-permute-done | bytes 18464 | tf_op jit(solution)/shard_map/ppermute | solution.py:44
  86.2 2.9 %collective-permute-done.6 = f32[8,2,32,128]{3,0,2,1:T(8,128)S(1)} collective-permute-done((f32[8,2,32,128]{3,0,2,1:T(8,128)S(1)}, f32[8,2,32,128]{3,0,2,1:T(8,128)S(1)}, u32[]{:S(2)}, u32[]{:S(2)}) %collective-permute-start.6) | collective-permute-done | bytes 262176 | tf_op jit(solution)/shard_map/ppermute | solution.py:109
  89.3 2.1 %collective-permute-start.7 = (f32[8,2,32,128]{3,0,2,1:T(8,128)S(1)}, f32[8,2,32,128]{3,0,2,1:T(8,128)S(1)}, u32[]{:S(2)}, u32[]{:S(2)}) collective-permute-start(f32[8,2,32,128]{3,0,2,1:T(8,128)S(1)} %get-tuple-element.42), channel_id=1, source_target_pairs={{0,8},{8,16},{16,24},{1,9},{9,17},{17,25},{2,10},{10,18},{18,26},{... | collective-permute-start | bytes 786440 | tf_op jit(solution)/shard_map/ppermute | solution.py:109
  91.5 0.8 fusion.43
  92.3 5.3 %collective-permute-done.7 = f32[8,2,32,128]{3,0,2,1:T(8,128)S(1)} collective-permute-done((f32[8,2,32,128]{3,0,2,1:T(8,128)S(1)}, f32[8,2,32,128]{3,0,2,1:T(8,128)S(1)}, u32[]{:S(2)}, u32[]{:S(2)}) %collective-permute-start.7) | collective-permute-done | bytes 262176 | tf_op jit(solution)/shard_map/ppermute | solution.py:109
  97.7 1.2 %copy.12 = f32[4,8,2,32,128]{4,3,2,1,0:T(8,128)} copy(f32[4,8,2,32,128]{4,1,3,2,0:T(8,128)S(1)} %fusion.40) | data formatting | bytes 2097152 | tf_op jit(solution)/shard_map/jit(dynamic_update_index_in_dim)/dynamic_update_slice | solution.py:118
  (69 shorter events, 4.4 us)
Async XLA Ops:
  0.6 73.2 %copy-start = (bf16[1,8,64,128]{3,2,1,0:T(8,128)(2,1)S(1)}, bf16[1,8,64,128]{3,2,1,0:T(8,128)(2,1)}, u32[]{:S(2)}) copy-start(bf16[1,8,64,128]{3,2,1,0:T(8,128)(2,1)} %param.22) | copy-start | bytes 393220
  0.6 8.4 %copy-start.4 = (f32[1,32]{1,0:T(1,128)S(1)}, f32[1,32]{1,0:T(1,128)}, u32[]{:S(2)}) copy-start(f32[1,32]{1,0:T(1,128)} %param.20) | copy-start | bytes 388
  0.7 9.2 %copy-start.5 = (f32[1,32]{1,0:T(1,128)S(1)}, f32[1,32]{1,0:T(1,128)}, u32[]{:S(2)}) copy-start(f32[1,32]{1,0:T(1,128)} %param.19) | copy-start | bytes 388
  0.7 10.0 %copy-start.6 = (f32[1,32]{1,0:T(1,128)S(1)}, f32[1,32]{1,0:T(1,128)}, u32[]{:S(2)}) copy-start(f32[1,32]{1,0:T(1,128)} %param.21) | copy-start | bytes 388
  0.7 10.7 %copy-start.8 = (s32[1,8]{1,0:T(1,128)S(1)}, s32[1,8]{1,0:T(1,128)}, u32[]{:S(2)}) copy-start(s32[1,8]{1,0:T(1,128)} %param.23) | copy-start | bytes 100
  2.1 26.1 %collective-permute-start = (f32[33,2,32,128]{3,2,1,0:T(8,128)S(1)}, f32[33,2,32,128]{3,2,1,0:T(8,128)S(1)}, u32[]{:S(2)}, u32[]{:S(2)}) collective-permute-start(f32[33,2,32,128]{3,2,1,0:T(8,128)S(1)} %pad_maximum_fusion.2), channel_id=1, source_target_pairs={{0,1},{1,2},{2,3},{3,4},{4,5},{5,6},{6,7},{8,9},{9,10},{10,11},{11... | collective-permute-start | bytes 3244040 | tf_op jit(solution)/shard_map/ppermute | solution.py:78
  4.0 25.1 %collective-permute-start.1 = (f32[33,2,32,128]{3,2,1,0:T(8,128)S(1)}, f32[33,2,32,128]{3,2,1,0:T(8,128)S(1)}, u32[]{:S(2)}, u32[]{:S(2)}) collective-permute-start(f32[33,2,32,128]{3,2,1,0:T(8,128)S(1)} %pad_maximum_fusion.2), channel_id=1, source_target_pairs={{1,0},{2,1},{3,2},{4,3},{5,4},{6,5},{7,6},{9,8},{10,9},{11,10},{12... | collective-permute-start | bytes 3244040 | tf_op jit(solution)/shard_map/ppermute | solution.py:81
  12.1 17.1 %copy-start.1 = (f32[1,32,2,32,128]{4,3,2,1,0:T(8,128)S(1)}, f32[1,32,2,32,128]{4,3,2,1,0:T(8,128)}, u32[]{:S(2)}) copy-start(f32[1,32,2,32,128]{4,3,2,1,0:T(8,128)} %param.15) | copy-start | bytes 3145732
  29.2 0.8 copy-start.2
  29.2 0.8 copy-start.7
  32.5 0.8 copy-start.3
  35.1 8.5 %collective-permute-start.2 = (f32[8,2,32,128]{3,0,2,1:T(8,128)S(1)}, f32[8,2,32,128]{3,0,2,1:T(8,128)S(1)}, u32[]{:S(2)}, u32[]{:S(2)}) collective-permute-start(f32[8,2,32,128]{3,0,2,1:T(8,128)S(1)} %get-tuple-element.52), channel_id=1, source_target_pairs={{0,8},{8,16},{16,24},{1,9},{9,17},{17,25},{2,10},{10,18},{18,26},{... | collective-permute-start | bytes 786440 | tf_op jit(solution)/shard_map/ppermute | solution.py:109
  43.6 3.8 %collective-permute-start.8 = (f32[1,34,64]{2,1,0:T(8,128)S(1)}, f32[1,34,64]{2,1,0:T(8,128)S(1)}, u32[]{:S(2)}, u32[]{:S(2)}) collective-permute-start(f32[1,34,64]{2,1,0:T(8,128)S(1)} %bitcast.177), channel_id=1, source_target_pairs={{0,8},{8,0},{16,24},{24,16},{1,9},{9,1},{17,25},{25,17},{2,10},{10... | collective-permute-start | bytes 26120 | tf_op jit(solution)/shard_map/ppermute | solution.py:124
  47.4 5.0 %collective-permute-start.9 = (f32[2,34,64]{2,1,0:T(8,128)S(1)}, f32[2,34,64]{2,1,0:T(8,128)S(1)}, u32[]{:S(2)}, u32[]{:S(2)}) collective-permute-start(f32[2,34,64]{2,1,0:T(8,128)S(1)} %maximum_select_fusion.2), channel_id=1, source_target_pairs={{0,16},{8,24},{16,0},{24,8},{1,17},{9,25},{17,1},{25,9},{2,18},{10... | collective-permute-start | bytes 52232 | tf_op jit(solution)/shard_map/ppermute | solution.py:124
  50.3 10.8 %collective-permute-start.3 = (f32[8,2,32,128]{3,0,2,1:T(8,128)S(1)}, f32[8,2,32,128]{3,0,2,1:T(8,128)S(1)}, u32[]{:S(2)}, u32[]{:S(2)}) collective-permute-start(f32[8,2,32,128]{3,0,2,1:T(8,128)S(1)} %get-tuple-element.50), channel_id=1, source_target_pairs={{0,8},{8,16},{16,24},{1,9},{9,17},{17,25},{2,10},{10,18},{18,26},{... | collective-permute-start | bytes 786440 | tf_op jit(solution)/shard_map/ppermute | solution.py:109
  61.2 10.2 %collective-permute-start.4 = (f32[8,2,32,128]{3,0,2,1:T(8,128)S(1)}, f32[8,2,32,128]{3,0,2,1:T(8,128)S(1)}, u32[]{:S(2)}, u32[]{:S(2)}) collective-permute-start(f32[8,2,32,128]{3,0,2,1:T(8,128)S(1)} %get-tuple-element.48), channel_id=1, source_target_pairs={{0,8},{8,16},{16,24},{1,9},{9,17},{17,25},{2,10},{10,18},{18,26},{... | collective-permute-start | bytes 786440 | tf_op jit(solution)/shard_map/ppermute | solution.py:109
  71.6 8.3 %collective-permute-start.5 = (f32[8,2,32,128]{3,0,2,1:T(8,128)S(1)}, f32[8,2,32,128]{3,0,2,1:T(8,128)S(1)}, u32[]{:S(2)}, u32[]{:S(2)}) collective-permute-start(f32[8,2,32,128]{3,0,2,1:T(8,128)S(1)} %get-tuple-element.46), channel_id=1, source_target_pairs={{0,8},{8,16},{16,24},{1,9},{9,17},{17,25},{2,10},{10,18},{18,26},{... | collective-permute-start | bytes 786440 | tf_op jit(solution)/shard_map/ppermute | solution.py:109
  74.0 1.2 %collective-permute-start.10 = (f32[1,9,128]{2,1,0:T(8,128)S(1)}, f32[1,9,128]{2,1,0:T(8,128)S(1)}, u32[]{:S(2)}, u32[]{:S(2)}) collective-permute-start(f32[1,9,128]{2,1,0:T(8,128)S(1)} %fusion.55), channel_id=1, source_target_pairs={{0,1},{1,0},{2,3},{3,2},{4,5},{5,4},{6,7},{7,6},{8,9},{9,8},{10,11... | collective-permute-start | bytes 13832 | tf_op jit(solution)/shard_map/ppermute | solution.py:44
  75.2 7.0 %collective-permute-start.11 = (f32[2,9,128]{2,1,0:T(8,128)S(1)}, f32[2,9,128]{2,1,0:T(8,128)S(1)}, u32[]{:S(2)}, u32[]{:S(2)}) collective-permute-start(f32[2,9,128]{2,1,0:T(8,128)S(1)} %maximum_select_fusion.4), channel_id=1, source_target_pairs={{0,2},{1,3},{2,0},{3,1},{4,6},{5,7},{6,4},{7,5},{8,10},{9,11},{10,... | collective-permute-start | bytes 27656 | tf_op jit(solution)/shard_map/ppermute | solution.py:44
  80.0 9.1 %collective-permute-start.6 = (f32[8,2,32,128]{3,0,2,1:T(8,128)S(1)}, f32[8,2,32,128]{3,0,2,1:T(8,128)S(1)}, u32[]{:S(2)}, u32[]{:S(2)}) collective-permute-start(f32[8,2,32,128]{3,0,2,1:T(8,128)S(1)} %get-tuple-element.44), channel_id=1, source_target_pairs={{0,8},{8,16},{16,24},{1,9},{9,17},{17,25},{2,10},{10,18},{18,26},{... | collective-permute-start | bytes 786440 | tf_op jit(solution)/shard_map/ppermute | solution.py:109
  82.3 4.0 %collective-permute-start.12 = (f32[4,9,128]{2,1,0:T(8,128)S(1)}, f32[4,9,128]{2,1,0:T(8,128)S(1)}, u32[]{:S(2)}, u32[]{:S(2)}) collective-permute-start(f32[4,9,128]{2,1,0:T(8,128)S(1)} %maximum_select_fusion.3), channel_id=1, source_target_pairs={{0,4},{1,5},{2,6},{3,7},{4,0},{5,1},{6,2},{7,3},{8,12},{9,13},{10,... | collective-permute-start | bytes 55304 | tf_op jit(solution)/shard_map/ppermute | solution.py:44
  89.3 8.3 %collective-permute-start.7 = (f32[8,2,32,128]{3,0,2,1:T(8,128)S(1)}, f32[8,2,32,128]{3,0,2,1:T(8,128)S(1)}, u32[]{:S(2)}, u32[]{:S(2)}) collective-permute-start(f32[8,2,32,128]{3,0,2,1:T(8,128)S(1)} %get-tuple-element.42), channel_id=1, source_target_pairs={{0,8},{8,16},{16,24},{1,9},{9,17},{17,25},{2,10},{10,18},{18,26},{... | collective-permute-start | bytes 786440 | tf_op jit(solution)/shard_map/ppermute | solution.py:109

commit v10 on v9

--- a/solution.py
+++ b/solution.py
@@ -145,7 +145,8 @@
     lines, pixels = contribution.shape
     ids = jnp.zeros((1, pixels), jnp.float32).at[0, :lines].set(sky_blocks[0].astype(jnp.float32))
     payload = jnp.concatenate([contribution, ids], axis=0)
-    gathered = gather_all(payload, "space")
+    big = jnp.zeros((256, payload.shape[1]), jnp.float32).at[:payload.shape[0]].set(payload)
+    gathered = lax.all_gather(big, "space")[:, :payload.shape[0]]
     mine = lax.axis_index("space") * rows + jnp.arange(rows, dtype=jnp.int32)
     onehot = (
         gathered[:, lines, :lines].reshape(1, tiles * lines) == mine.astype(jnp.float32)[:, None]

time: 99.3 us -> 116 us (1.17)
  between operations: 1.17 us -> 14.5 us
  local copies, waits for them, and re-layouts: 3.35 us -> 4.77 us
    ppermute x3 -> x0, waiting for transfers between devices: 5 us -> none  [gather_all(): other = lax.ppermute(held, axis, [(i, i ^ span) for i in range(count)])]
    ppermute x6, waiting for transfers between devices: 33.2 us -> 38 us  [body(): arrived = lax.ppermute(sent, 'species', pairs)]
  transfers between devices with their start and end apart: 13 -> 11, of which waited for: 12 -> 10; matrix products, arithmetic and copies ran while one was open for 6% -> 7% of each run, Pallas kernels for 0% -> 0%
where the time goes in v10:
time: 116 us; the launch traced here: 115 us
  waiting for transfers between devices  58.8 us (51%)
  starting transfers between devices  24.2 us (21%)
  between operations  14.5 us (12%)
  other arithmetic  8.65 us (7%)
  local copies, waits for them, and re-layouts  4.77 us (4%)
  matrix products  4.1 us (4%)
    ppermute x6, waiting for transfers between devices, body(): arrived = lax.ppermute(sent, 'species', pairs)  38 us
    ppermute x1, waiting for transfers between devices, body(): lax.ppermute(mine[:, mine.shape[1] - halo:], 'space', [(i, i + 1) for i i...  16.1 us
    ppermute x6, starting transfers between devices, body(): arrived = lax.ppermute(sent, 'species', pairs)  14.9 us
    ppermute x1, starting transfers between devices, body(): lax.ppermute(mine[:, :halo], 'space', [(i + 1, i) for i in range(count -...  4.54 us
    ppermute x2, waiting for transfers between devices, body(): lax.ppermute(everyone, 'species', [(i, i ^ span) for i in range(groups)])  3.85 us
    ppermute x2, starting transfers between devices, body(): lax.ppermute(everyone, 'species', [(i, i ^ span) for i in range(groups)])  2.82 us
    add x2, other arithmetic, body(): inner + wide_factor[:, 1 + step:wide_factor.shape[1] - 1 - step] * (besid...  2.71 us
  transfers between devices with their start and end apart: 11, of which 10 were waited for; matrix products, arithmetic and copies ran while one was open for 7% of the time, Pallas kernels for 0%

profile of v10, /device:TPU:12, one launch (start us, length us, event | category | flops | bytes accessed | tf_op | source)
XLA Modules:
  0.0 115.1 jit_solution(15039310187587911616)
XLA Ops:
  7.3 1.4 %pad_maximum_fusion.2 = f32[33,2,32,128]{3,2,1,0:T(8,128)S(1)} fusion(f32[1,2,32,128]{3,2,1,0:T(8,128)} %bitcast.176, f32[32,2,32,128]{3,2,1,0:T(8,128)} %bitcast.168), kind=kLoop, calls=%fused_computation.35 | loop fusion | flops 270336 | bytes 2162688 | tf_op jit(solution)/shard_map/concatenate | solution.py:77
  8.6 1.9 %collective-permute-start = (f32[33,2,32,128]{3,2,1,0:T(8,128)S(1)}, f32[33,2,32,128]{3,2,1,0:T(8,128)S(1)}, u32[]{:S(2)}, u32[]{:S(2)}) collective-permute-start(f32[33,2,32,128]{3,2,1,0:T(8,128)S(1)} %pad_maximum_fusion.2), channel_id=1, source_target_pairs={{0,1},{1,2},{2,3},{3,4},{4,5},{5,6},{6,7},{8,9},{9,10},{10,11},{11... | collective-permute-start | bytes 3244040 | tf_op jit(solution)/shard_map/ppermute | solution.py:78
  10.6 4.5 %collective-permute-start.1 = (f32[33,2,32,128]{3,2,1,0:T(8,128)S(1)}, f32[33,2,32,128]{3,2,1,0:T(8,128)S(1)}, u32[]{:S(2)}, u32[]{:S(2)}) collective-permute-start(f32[33,2,32,128]{3,2,1,0:T(8,128)S(1)} %pad_maximum_fusion.2), channel_id=1, source_target_pairs={{1,0},{2,1},{3,2},{4,3},{5,4},{6,5},{7,6},{9,8},{10,9},{11,10},{12... | collective-permute-start | bytes 3244040 | tf_op jit(solution)/shard_map/ppermute | solution.py:81
  15.1 0.5 broadcast.151
  15.6 0.7 reduce.24
  16.4 0.7 reduce.25
  17.3 0.6 compare_reduce_fusion
  18.0 0.7 broadcast_select_fusion
  18.6 16.1 %collective-permute-done = f32[33,2,32,128]{3,2,1,0:T(8,128)S(1)} collective-permute-done((f32[33,2,32,128]{3,2,1,0:T(8,128)S(1)}, f32[33,2,32,128]{3,2,1,0:T(8,128)S(1)}, u32[]{:S(2)}, u32[]{:S(2)}) %collective-permute-start) | collective-permute-done | bytes 1081376 | tf_op jit(solution)/shard_map/ppermute | solution.py:78
  34.8 0.9 collective-permute-done.1
  36.0 0.5 copy-done.2
  37.0 2.0 %fusion.6 = f32[32,4,32,128]{3,2,1,0:T(8,128)S(1)} fusion(f32[32,4,32,128]{3,2,1,0:T(8,128)S(1)} %pad_maximum_fusion, f32[32,6,32,128]{3,2,1,0:T(8,128)S(1)} %broadcast_multiply_fusion, f32[32,2,32,128]{3,2,1,0:T(8,128)S(1)} %slice.199, f32[32,2,32,128]{3,2,1,0:T(8,128)S(1)} %bitcast.170, f32[32,2,32,128]{3,2,1,0:T(8,128)S(1)} %slice.198), kind=kLoop, calls=%fused_computation.14 | loop fusion | flops 5767168 | bytes 9437184 | tf_op jit(solution)/shard_map/add | solution.py:87
  39.1 0.7 fusion.25
  39.8 1.7 %fusion.26 = f32[8192,32]{0,1:T(8,128)S(1)} fusion(f32[4,8,64,128]{3,2,1,0:T(8,128)S(1)} %bitcast.173, f32[1,32,32]{2,1,0:T(8,128)S(1)} %copy-done.3), kind=kOutput, calls=%fused_computation.43 | convolution fusion | flops 100663296 | bytes 2101248 | tf_op jit(solution)/shard_map/dot_general | solution.py:89
  41.7 3.5 %collective-permute-start.2 = (f32[8,2,32,128]{3,0,2,1:T(8,128)S(1)}, f32[8,2,32,128]{3,0,2,1:T(8,128)S(1)}, u32[]{:S(2)}, u32[]{:S(2)}) collective-permute-start(f32[8,2,32,128]{3,0,2,1:T(8,128)S(1)} %get-tuple-element.64), channel_id=1, source_target_pairs={{0,8},{8,16},{16,24},{1,9},{9,17},{17,25},{2,10},{10,18},{18,26},{... | collective-permute-start | bytes 786440 | tf_op jit(solution)/shard_map/ppermute | solution.py:109
  46.0 4.2 %collective-permute-done.2 = f32[8,2,32,128]{3,0,2,1:T(8,128)S(1)} collective-permute-done((f32[8,2,32,128]{3,0,2,1:T(8,128)S(1)}, f32[8,2,32,128]{3,0,2,1:T(8,128)S(1)}, u32[]{:S(2)}, u32[]{:S(2)}) %collective-permute-start.2) | collective-permute-done | bytes 262176 | tf_op jit(solution)/shard_map/ppermute | solution.py:109
  50.3 3.7 %collective-permute-done.8 = f32[1,34,64]{2,1,0:T(8,128)S(1)} collective-permute-done((f32[1,34,64]{2,1,0:T(8,128)S(1)}, f32[1,34,64]{2,1,0:T(8,128)S(1)}, u32[]{:S(2)}, u32[]{:S(2)}) %collective-permute-start.8) | collective-permute-done | bytes 8736 | tf_op jit(solution)/shard_map/ppermute | solution.py:124
  54.0 2.8 %collective-permute-start.9 = (f32[2,34,64]{2,1,0:T(8,128)S(1)}, f32[2,34,64]{2,1,0:T(8,128)S(1)}, u32[]{:S(2)}, u32[]{:S(2)}) collective-permute-start(f32[2,34,64]{2,1,0:T(8,128)S(1)} %maximum_select_fusion.1), channel_id=1, source_target_pairs={{0,16},{8,24},{16,0},{24,8},{1,17},{9,25},{17,1},{25,9},{2,18},{10... | collective-permute-start | bytes 52232 | tf_op jit(solution)/shard_map/ppermute | solution.py:124
  56.8 1.9 %collective-permute-start.3 = (f32[8,2,32,128]{3,0,2,1:T(8,128)S(1)}, f32[8,2,32,128]{3,0,2,1:T(8,128)S(1)}, u32[]{:S(2)}, u32[]{:S(2)}) collective-permute-start(f32[8,2,32,128]{3,0,2,1:T(8,128)S(1)} %get-tuple-element.62), channel_id=1, source_target_pairs={{0,8},{8,16},{16,24},{1,9},{9,17},{17,25},{2,10},{10,18},{18,26},{... | collective-permute-start | bytes 786440 | tf_op jit(solution)/shard_map/ppermute | solution.py:109
  59.7 7.9 %collective-permute-done.3 = f32[8,2,32,128]{3,0,2,1:T(8,128)S(1)} collective-permute-done((f32[8,2,32,128]{3,0,2,1:T(8,128)S(1)}, f32[8,2,32,128]{3,0,2,1:T(8,128)S(1)}, u32[]{:S(2)}, u32[]{:S(2)}) %collective-permute-start.3) | collective-permute-done | bytes 262176 | tf_op jit(solution)/shard_map/ppermute | solution.py:109
  67.8 1.9 %collective-permute-start.4 = (f32[8,2,32,128]{3,0,2,1:T(8,128)S(1)}, f32[8,2,32,128]{3,0,2,1:T(8,128)S(1)}, u32[]{:S(2)}, u32[]{:S(2)}) collective-permute-start(f32[8,2,32,128]{3,0,2,1:T(8,128)S(1)} %get-tuple-element.60), channel_id=1, source_target_pairs={{0,8},{8,16},{16,24},{1,9},{9,17},{17,25},{2,10},{10,18},{18,26},{... | collective-permute-start | bytes 786440 | tf_op jit(solution)/shard_map/ppermute | solution.py:109
  69.9 0.7 scatter.19
  70.6 7.4 %collective-permute-done.4 = f32[8,2,32,128]{3,0,2,1:T(8,128)S(1)} collective-permute-done((f32[8,2,32,128]{3,0,2,1:T(8,128)S(1)}, f32[8,2,32,128]{3,0,2,1:T(8,128)S(1)}, u32[]{:S(2)}, u32[]{:S(2)}) %collective-permute-start.4) | collective-permute-done | bytes 262176 | tf_op jit(solution)/shard_map/ppermute | solution.py:109
  78.1 2.2 %collective-permute-start.5 = (f32[8,2,32,128]{3,0,2,1:T(8,128)S(1)}, f32[8,2,32,128]{3,0,2,1:T(8,128)S(1)}, u32[]{:S(2)}, u32[]{:S(2)}) collective-permute-start(f32[8,2,32,128]{3,0,2,1:T(8,128)S(1)} %get-tuple-element.58), channel_id=1, source_target_pairs={{0,8},{8,16},{16,24},{1,9},{9,17},{17,25},{2,10},{10,18},{18,26},{... | collective-permute-start | bytes 786440 | tf_op jit(solution)/shard_map/ppermute | solution.py:109
  80.4 7.2 %collective-permute-done.5 = f32[8,2,32,128]{3,0,2,1:T(8,128)S(1)} collective-permute-done((f32[8,2,32,128]{3,0,2,1:T(8,128)S(1)}, f32[8,2,32,128]{3,0,2,1:T(8,128)S(1)}, u32[]{:S(2)}, u32[]{:S(2)}) %collective-permute-start.5) | collective-permute-done | bytes 262176 | tf_op jit(solution)/shard_map/ppermute | solution.py:109
  87.7 2.5 %collective-permute-start.6 = (f32[8,2,32,128]{3,0,2,1:T(8,128)S(1)}, f32[8,2,32,128]{3,0,2,1:T(8,128)S(1)}, u32[]{:S(2)}, u32[]{:S(2)}) collective-permute-start(f32[8,2,32,128]{3,0,2,1:T(8,128)S(1)} %get-tuple-element.56), channel_id=1, source_target_pairs={{0,8},{8,16},{16,24},{1,9},{9,17},{17,25},{2,10},{10,18},{18,26},{... | collective-permute-start | bytes 786440 | tf_op jit(solution)/shard_map/ppermute | solution.py:109
  90.2 5.9 %collective-permute-done.6 = f32[8,2,32,128]{3,0,2,1:T(8,128)S(1)} collective-permute-done((f32[8,2,32,128]{3,0,2,1:T(8,128)S(1)}, f32[8,2,32,128]{3,0,2,1:T(8,128)S(1)}, u32[]{:S(2)}, u32[]{:S(2)}) %collective-permute-start.6) | collective-permute-done | bytes 262176 | tf_op jit(solution)/shard_map/ppermute | solution.py:109
  96.3 2.9 %collective-permute-start.7 = (f32[8,2,32,128]{3,0,2,1:T(8,128)S(1)}, f32[8,2,32,128]{3,0,2,1:T(8,128)S(1)}, u32[]{:S(2)}, u32[]{:S(2)}) collective-permute-start(f32[8,2,32,128]{3,0,2,1:T(8,128)S(1)} %get-tuple-element.54), channel_id=1, source_target_pairs={{0,8},{8,16},{16,24},{1,9},{9,17},{17,25},{2,10},{10,18},{18,26},{... | collective-permute-start | bytes 786440 | tf_op jit(solution)/shard_map/ppermute | solution.py:109
  99.2 5.4 %collective-permute-done.7 = f32[8,2,32,128]{3,0,2,1:T(8,128)S(1)} collective-permute-done((f32[8,2,32,128]{3,0,2,1:T(8,128)S(1)}, f32[8,2,32,128]{3,0,2,1:T(8,128)S(1)}, u32[]{:S(2)}, u32[]{:S(2)}) %collective-permute-start.7) | collective-permute-done | bytes 262176 | tf_op jit(solution)/shard_map/ppermute | solution.py:109
  104.7 1.2 %copy.13 = f32[4,8,2,32,128]{4,3,2,1,0:T(8,128)} copy(f32[4,8,2,32,128]{4,1,3,2,0:T(8,128)S(1)} %fusion.40) | data formatting | bytes 2097152 | tf_op jit(solution)/shard_map/jit(dynamic_update_index_in_dim)/dynamic_update_slice | solution.py:118
  105.9 0.8 slice_reduce_fusion
  106.7 1.6 %fusion.43 = f32[48,128]{1,0:T(8,128)} fusion(f32[8,256,128]{2,1,0:T(8,128)} %all-gather.2.cloned.1.call-done, f32[64]{0:T(128)S(1)} %eq.23, f32[48]{0:T(128)S(1)} %add_convert_fusion), kind=kOutput, calls=%fused_computation.79 | convolution fusion | flops 4721664 | bytes 57792 | tf_op jit(solution)/shard_map/dot_general | solution.py:154
  (64 shorter events, 4.2 us)
Async XLA Ops:
  7.2 62.5 %copy-start = (bf16[1,8,64,128]{3,2,1,0:T(8,128)(2,1)S(1)}, bf16[1,8,64,128]{3,2,1,0:T(8,128)(2,1)}, u32[]{:S(2)}) copy-start(bf16[1,8,64,128]{3,2,1,0:T(8,128)(2,1)} %param.24) | copy-start | bytes 393220
  7.2 8.5 %copy-start.4 = (f32[1,32]{1,0:T(1,128)S(1)}, f32[1,32]{1,0:T(1,128)}, u32[]{:S(2)}) copy-start(f32[1,32]{1,0:T(1,128)} %param.22) | copy-start | bytes 388
  7.2 9.2 %copy-start.5 = (f32[1,32]{1,0:T(1,128)S(1)}, f32[1,32]{1,0:T(1,128)}, u32[]{:S(2)}) copy-start(f32[1,32]{1,0:T(1,128)} %param.21) | copy-start | bytes 388
  7.2 10.0 %copy-start.6 = (f32[1,32]{1,0:T(1,128)S(1)}, f32[1,32]{1,0:T(1,128)}, u32[]{:S(2)}) copy-start(f32[1,32]{1,0:T(1,128)} %param.23) | copy-start | bytes 388
  7.2 10.8 %copy-start.8 = (s32[1,8]{1,0:T(1,128)S(1)}, s32[1,8]{1,0:T(1,128)}, u32[]{:S(2)}) copy-start(s32[1,8]{1,0:T(1,128)} %param.25) | copy-start | bytes 100
  7.2 98.6 %all-gather.2.cloned.1.call-start = ((), (), s32[]{:S(2)}) async-start(), calls=%async_computation | async-start | bytes 1179648 | tf_op jit(solution)/shard_map/all_gather | solution.py:149
  8.6 26.1 %collective-permute-start = (f32[33,2,32,128]{3,2,1,0:T(8,128)S(1)}, f32[33,2,32,128]{3,2,1,0:T(8,128)S(1)}, u32[]{:S(2)}, u32[]{:S(2)}) collective-permute-start(f32[33,2,32,128]{3,2,1,0:T(8,128)S(1)} %pad_maximum_fusion.2), channel_id=1, source_target_pairs={{0,1},{1,2},{2,3},{3,4},{4,5},{5,6},{6,7},{8,9},{9,10},{10,11},{11... | collective-permute-start | bytes 3244040 | tf_op jit(solution)/shard_map/ppermute | solution.py:78
  10.6 25.1 %collective-permute-start.1 = (f32[33,2,32,128]{3,2,1,0:T(8,128)S(1)}, f32[33,2,32,128]{3,2,1,0:T(8,128)S(1)}, u32[]{:S(2)}, u32[]{:S(2)}) collective-permute-start(f32[33,2,32,128]{3,2,1,0:T(8,128)S(1)} %pad_maximum_fusion.2), channel_id=1, source_target_pairs={{1,0},{2,1},{3,2},{4,3},{5,4},{6,5},{7,6},{9,8},{10,9},{11,10},{12... | collective-permute-start | bytes 3244040 | tf_op jit(solution)/shard_map/ppermute | solution.py:81
  18.6 17.1 %copy-start.1 = (f32[1,32,2,32,128]{4,3,2,1,0:T(8,128)S(1)}, f32[1,32,2,32,128]{4,3,2,1,0:T(8,128)}, u32[]{:S(2)}) copy-start(f32[1,32,2,32,128]{4,3,2,1,0:T(8,128)} %param.17) | copy-start | bytes 3145732
  35.8 0.8 copy-start.2
  35.8 0.8 copy-start.7
  39.0 0.8 copy-start.3
  41.7 8.5 %collective-permute-start.2 = (f32[8,2,32,128]{3,0,2,1:T(8,128)S(1)}, f32[8,2,32,128]{3,0,2,1:T(8,128)S(1)}, u32[]{:S(2)}, u32[]{:S(2)}) collective-permute-start(f32[8,2,32,128]{3,0,2,1:T(8,128)S(1)} %get-tuple-element.64), channel_id=1, source_target_pairs={{0,8},{8,16},{16,24},{1,9},{9,17},{17,25},{2,10},{10,18},{18,26},{... | collective-permute-start | bytes 786440 | tf_op jit(solution)/shard_map/ppermute | solution.py:109
  50.2 3.8 %collective-permute-start.8 = (f32[1,34,64]{2,1,0:T(8,128)S(1)}, f32[1,34,64]{2,1,0:T(8,128)S(1)}, u32[]{:S(2)}, u32[]{:S(2)}) collective-permute-start(f32[1,34,64]{2,1,0:T(8,128)S(1)} %bitcast.177), channel_id=1, source_target_pairs={{0,8},{8,0},{16,24},{24,16},{1,9},{9,1},{17,25},{25,17},{2,10},{10... | collective-permute-start | bytes 26120 | tf_op jit(solution)/shard_map/ppermute | solution.py:124
  54.0 5.0 %collective-permute-start.9 = (f32[2,34,64]{2,1,0:T(8,128)S(1)}, f32[2,34,64]{2,1,0:T(8,128)S(1)}, u32[]{:S(2)}, u32[]{:S(2)}) collective-permute-start(f32[2,34,64]{2,1,0:T(8,128)S(1)} %maximum_select_fusion.1), channel_id=1, source_target_pairs={{0,16},{8,24},{16,0},{24,8},{1,17},{9,25},{17,1},{25,9},{2,18},{10... | collective-permute-start | bytes 52232 | tf_op jit(solution)/shard_map/ppermute | solution.py:124
  56.8 10.8 %collective-permute-start.3 = (f32[8,2,32,128]{3,0,2,1:T(8,128)S(1)}, f32[8,2,32,128]{3,0,2,1:T(8,128)S(1)}, u32[]{:S(2)}, u32[]{:S(2)}) collective-permute-start(f32[8,2,32,128]{3,0,2,1:T(8,128)S(1)} %get-tuple-element.62), channel_id=1, source_target_pairs={{0,8},{8,16},{16,24},{1,9},{9,17},{17,25},{2,10},{10,18},{18,26},{... | collective-permute-start | bytes 786440 | tf_op jit(solution)/shard_map/ppermute | solution.py:109
  67.8 10.2 %collective-permute-start.4 = (f32[8,2,32,128]{3,0,2,1:T(8,128)S(1)}, f32[8,2,32,128]{3,0,2,1:T(8,128)S(1)}, u32[]{:S(2)}, u32[]{:S(2)}) collective-permute-start(f32[8,2,32,128]{3,0,2,1:T(8,128)S(1)} %get-tuple-element.60), channel_id=1, source_target_pairs={{0,8},{8,16},{16,24},{1,9},{9,17},{17,25},{2,10},{10,18},{18,26},{... | collective-permute-start | bytes 786440 | tf_op jit(solution)/shard_map/ppermute | solution.py:109
  78.1 9.4 %collective-permute-start.5 = (f32[8,2,32,128]{3,0,2,1:T(8,128)S(1)}, f32[8,2,32,128]{3,0,2,1:T(8,128)S(1)}, u32[]{:S(2)}, u32[]{:S(2)}) collective-permute-start(f32[8,2,32,128]{3,0,2,1:T(8,128)S(1)} %get-tuple-element.58), channel_id=1, source_target_pairs={{0,8},{8,16},{16,24},{1,9},{9,17},{17,25},{2,10},{10,18},{18,26},{... | collective-permute-start | bytes 786440 | tf_op jit(solution)/shard_map/ppermute | solution.py:109
  87.7 8.5 %collective-permute-start.6 = (f32[8,2,32,128]{3,0,2,1:T(8,128)S(1)}, f32[8,2,32,128]{3,0,2,1:T(8,128)S(1)}, u32[]{:S(2)}, u32[]{:S(2)}) collective-permute-start(f32[8,2,32,128]{3,0,2,1:T(8,128)S(1)} %get-tuple-element.56), channel_id=1, source_target_pairs={{0,8},{8,16},{16,24},{1,9},{9,17},{17,25},{2,10},{10,18},{18,26},{... | collective-permute-start | bytes 786440 | tf_op jit(solution)/shard_map/ppermute | solution.py:109
  96.3 8.3 %collective-permute-start.7 = (f32[8,2,32,128]{3,0,2,1:T(8,128)S(1)}, f32[8,2,32,128]{3,0,2,1:T(8,128)S(1)}, u32[]{:S(2)}, u32[]{:S(2)}) collective-permute-start(f32[8,2,32,128]{3,0,2,1:T(8,128)S(1)} %get-tuple-element.54), channel_id=1, source_target_pairs={{0,8},{8,16},{16,24},{1,9},{9,17},{17,25},{2,10},{10,18},{18,26},{... | collective-permute-start | bytes 786440 | tf_op jit(solution)/shard_map/ppermute | solution.py:109
Sparse Core Ops, SparseCore 0:
  70.7 22.4 all-gather.1

commit v11 on v7

--- a/solution.py
+++ b/solution.py
@@ -35,21 +35,14 @@
 
 def gather_all(block, axis):
     count = lax.axis_size(axis)
-    if count & (count - 1):
-        return lax.all_gather(block, axis)
     me = lax.axis_index(axis)
-    held = block[None]
-    span = 1
-    while span < count:
-        other = lax.ppermute(held, axis, [(i, i ^ span) for i in range(count)])
-        low = (me & span) == 0
-        held = jnp.where(
-            low,
-            jnp.concatenate([held, other], axis=0),
-            jnp.concatenate([other, held], axis=0),
-        )
-        span *= 2
-    return held
+    by_shift = [block] + [
+        lax.ppermute(block, axis, [(i, (i + d) % count) for i in range(count)])
+        for d in range(1, count)
+    ]
+    stacked = jnp.stack(by_shift)
+    order = (me - jnp.arange(count)) % count
+    return jnp.take(stacked, order, axis=0)
 
 
 def body(
@@ -99,20 +92,7 @@
     cols = own_columns.shape[1]
     extra = jnp.zeros((2, cols), jnp.float32).at[0, :bins].set(chain).at[1, :bins].set(gamma_yield[0])
     packed = jnp.concatenate([own_columns, extra], axis=0)
-    me_g = lax.axis_index("species")
-    everyone = packed[None]
-    span = 1
-    while span < groups:
-        other = lax.ppermute(everyone, "species", [(i, i ^ span) for i in range(groups)])
-        if span == 1:
-            own_part, other = lax.optimization_barrier((own_part, other))
-        low = (me_g & span) == 0
-        everyone = jnp.where(
-            low,
-            jnp.concatenate([everyone, other], axis=0),
-            jnp.concatenate([other, everyone], axis=0),
-        )
-        span *= 2
+    everyone = gather_all(packed, "species")
     sums = everyone[0, :bins]
     total = jnp.zeros((cols,), jnp.float32)
     for group in range(groups):

time: 96.9 us -> 103 us (1.063)
  starting transfers between devices: 17.2 us -> 24.5 us
  waiting for transfers between devices: 64.3 us -> 61.1 us
  local copies, waits for them, and re-layouts: 1.6 us -> 2.73 us
  other arithmetic: 8.84 us -> 9.94 us
    ppermute x5 -> x10, starting transfers between devices: 1.07 us -> 8.42 us  [gather_all(): lax.ppermute(block, axis, [(i, (i + d) % count) for i in range(count)])]
    ppermute x5 -> x10, waiting for transfers between devices: 11 us -> 8.34 us  [gather_all(): lax.ppermute(block, axis, [(i, (i + d) % count) for i in range(count)])]
    gather x0 -> x2, local copies, waits for them, and re-layouts: none -> 1.11 us  [gather_all(): return jnp.take(stacked, order, axis=0)]
  transfers between devices with their start and end apart: 19 -> 24, of which waited for: 11 -> 14; matrix products, arithmetic and copies ran while one was open for 5% -> 7% of each run, Pallas kernels for 0% -> 0%
where the time goes in v11:
time: 103 us
  waiting for transfers between devices  61.1 us (59%)
  starting transfers between devices  24.5 us (24%)
  other arithmetic  9.94 us (10%)
  matrix products  3.35 us (3%)
  local copies, waits for them, and re-layouts  2.73 us (3%)
  between operations  1.25 us (1%)
    ppermute x12, waiting for transfers between devices, body(): arrived = lax.ppermute(pieces[c], 'species', [(s, s + 1)])  33.2 us
    ppermute x12, starting transfers between devices, body(): arrived = lax.ppermute(pieces[c], 'species', [(s, s + 1)])  10.6 us
    ppermute x1, waiting for transfers between devices, body(): lax.ppermute(mine[:, :halo], 'space', [(i + 1, i) for i in range(count -...  10.5 us
    ppermute x1, waiting for transfers between devices, body(): lax.ppermute(mine[:, mine.shape[1] - halo:], 'space', [(i, i + 1) for i i...  9.05 us
    ppermute x10, starting transfers between devices, gather_all(): lax.ppermute(block, axis, [(i, (i + d) % count) for i in range(count)])  8.42 us
    ppermute x10, waiting for transfers between devices, gather_all(): lax.ppermute(block, axis, [(i, (i + d) % count) for i in range(count)])  8.34 us
    ppermute x1, starting transfers between devices, body(): lax.ppermute(mine[:, :halo], 'space', [(i + 1, i) for i in range(count -...  3.64 us
    add x2, other arithmetic, body(): inner + wide_factor[:, 1 + step:wide_factor.shape[1] - 1 - step] * (besid...  2.71 us
  transfers between devices with their start and end apart: 24, of which 14 were waited for; matrix products, arithmetic and copies ran while one was open for 7% of the time, Pallas kernels for 0%

profile of v11, /device:TPU:26, one launch (start us, length us, event | category | flops | bytes accessed | tf_op | source)
XLA Modules:
  0.0 102.9 jit_solution(6525631275630950950)
XLA Ops:
  0.7 1.4 %pad_maximum_fusion.2 = f32[33,2,32,128]{3,2,1,0:T(8,128)S(1)} fusion(f32[1,2,32,128]{3,2,1,0:T(8,128)} %bitcast.143, f32[32,2,32,128]{3,2,1,0:T(8,128)} %bitcast.138), kind=kLoop, calls=%fused_computation.38 | loop fusion | flops 270336 | bytes 2162688 | tf_op jit(solution)/shard_map/concatenate | solution.py:70
  2.0 1.9 %collective-permute-start = (f32[33,2,32,128]{3,2,1,0:T(8,128)S(1)}, f32[33,2,32,128]{3,2,1,0:T(8,128)S(1)}, u32[]{:S(2)}, u32[]{:S(2)}) collective-permute-start(f32[33,2,32,128]{3,2,1,0:T(8,128)S(1)} %pad_maximum_fusion.2), channel_id=1, source_target_pairs={{0,1},{1,2},{2,3},{3,4},{4,5},{5,6},{6,7},{8,9},{9,10},{10,11},{11... | collective-permute-start | bytes 3244040 | tf_op jit(solution)/shard_map/ppermute | solution.py:71
  4.0 3.6 %collective-permute-start.1 = (f32[33,2,32,128]{3,2,1,0:T(8,128)S(1)}, f32[33,2,32,128]{3,2,1,0:T(8,128)S(1)}, u32[]{:S(2)}, u32[]{:S(2)}) collective-permute-start(f32[33,2,32,128]{3,2,1,0:T(8,128)S(1)} %pad_maximum_fusion.2), channel_id=1, source_target_pairs={{1,0},{2,1},{3,2},{4,3},{5,4},{6,5},{7,6},{9,8},{10,9},{11,10},{12... | collective-permute-start | bytes 3244040 | tf_op jit(solution)/shard_map/ppermute | solution.py:74
  9.5 9.1 %collective-permute-done = f32[33,2,32,128]{3,2,1,0:T(8,128)S(1)} collective-permute-done((f32[33,2,32,128]{3,2,1,0:T(8,128)S(1)}, f32[33,2,32,128]{3,2,1,0:T(8,128)S(1)}, u32[]{:S(2)}, u32[]{:S(2)}) %collective-permute-start) | collective-permute-done | bytes 1081376 | tf_op jit(solution)/shard_map/ppermute | solution.py:71
  18.6 10.5 %collective-permute-done.1 = f32[33,2,32,128]{3,2,1,0:T(8,128)S(1)} collective-permute-done((f32[33,2,32,128]{3,2,1,0:T(8,128)S(1)}, f32[33,2,32,128]{3,2,1,0:T(8,128)S(1)}, u32[]{:S(2)}, u32[]{:S(2)}) %collective-permute-start.1) | collective-permute-done | bytes 1081376 | tf_op jit(solution)/shard_map/ppermute | solution.py:74
  30.4 2.0 %fusion.6 = f32[32,4,32,128]{3,2,1,0:T(8,128)S(1)} fusion(f32[32,4,32,128]{3,2,1,0:T(8,128)S(1)} %pad_maximum_fusion, f32[32,6,32,128]{3,2,1,0:T(8,128)S(1)} %broadcast_multiply_fusion, f32[32,2,32,128]{3,2,1,0:T(8,128)S(1)} %slice.220, f32[32,2,32,128]{3,2,1,0:T(8,128)S(1)} %bitcast.140, f32[32,2,32,128]{3,2,1,0:T(8,128)S(1)} %slice.219), kind=kLoop, calls=%fused_computation.16 | loop fusion | flops 5767168 | bytes 9437184 | tf_op jit(solution)/shard_map/add | solution.py:80
  32.5 0.7 fusion.25
  33.2 1.7 %convolution_bitcast_fusion = f32[4,8,64,128]{3,1,2,0:T(8,128)S(1)} fusion(f32[4,8,64,128]{3,2,1,0:T(8,128)S(1)} %bitcast.141, f32[1,32,32]{2,1,0:T(8,128)S(1)} %copy-done.3), kind=kOutput, calls=%fused_computation.21 | convolution fusion | flops 100663296 | bytes 2101248 | tf_op jit(solution)/shard_map/dot_general | solution.py:82
  36.0 1.7 %collective-permute-start.12 = (f32[34,64]{1,0:T(8,128)S(1)}, f32[34,64]{1,0:T(8,128)S(1)}, u32[]{:S(2)}, u32[]{:S(2)}) collective-permute-start(f32[34,64]{1,0:T(8,128)S(1)} %get-tuple-element.48), channel_id=1, source_target_pairs={{0,16},{8,24},{16,0},{24,8},{1,17},{9,25},{17,1},{25,9},{2,18},{10... | collective-permute-start | bytes 26120 | tf_op jit(solution)/shard_map/ppermute | solution.py:40
  38.2 0.7 collective-permute-start.14
  41.4 1.9 %collective-permute-done.13 = f32[34,64]{1,0:T(8,128)S(1)} collective-permute-done((f32[34,64]{1,0:T(8,128)S(1)}, f32[34,64]{1,0:T(8,128)S(1)}, u32[]{:S(2)}, u32[]{:S(2)}) %collective-permute-start.13) | collective-permute-done | bytes 8736 | tf_op jit(solution)/shard_map/ppermute | solution.py:40
  46.6 0.7 collective-permute-start.9
  47.4 1.3 %collective-permute-start.4 = (f32[5,2,32,128]{3,2,1,0:T(8,128)S(1)}, f32[5,2,32,128]{3,2,1,0:T(8,128)}, u32[]{:S(2)}, u32[]{:S(2)}) collective-permute-start(f32[5,2,32,128]{3,2,1,0:T(8,128)S(1)} %multiply_add_fusion.10), channel_id=1, source_target_pairs={{16,24},{17,25},{18,26},{19,27},{20,28},{21,29},{22,30},{23,31}} | collective-permute-start | bytes 491528 | tf_op jit(solution)/shard_map/ppermute | solution.py:123
  49.0 1.7 %collective-permute-start.18 = (f32[9,128]{1,0:T(8,128)S(1)}, f32[9,128]{1,0:T(8,128)S(1)}, u32[]{:S(2)}, u32[]{:S(2)}) collective-permute-start(f32[9,128]{1,0:T(8,128)S(1)} %select_maximum_fusion), channel_id=1, source_target_pairs={{0,2},{1,3},{2,4},{3,5},{4,6},{5,7},{6,0},{7,1},{8,10},{9,11},{10,... | collective-permute-start | bytes 13832 | tf_op jit(solution)/shard_map/ppermute | solution.py:40
  50.7 1.1 %collective-permute-done.17 = f32[9,128]{1,0:T(8,128)S(1)} collective-permute-done((f32[9,128]{1,0:T(8,128)S(1)}, f32[9,128]{1,0:T(8,128)S(1)}, u32[]{:S(2)}, u32[]{:S(2)}) %collective-permute-start.17) | collective-permute-done | bytes 4640 | tf_op jit(solution)/shard_map/ppermute | solution.py:40
  51.8 0.9 collective-permute-done.18
  52.7 0.9 collective-permute-start.20
  53.6 1.3 %collective-permute-done.19 = f32[9,128]{1,0:T(8,128)S(1)} collective-permute-done((f32[9,128]{1,0:T(8,128)S(1)}, f32[9,128]{1,0:T(8,128)S(1)}, u32[]{:S(2)}, u32[]{:S(2)}) %collective-permute-start.19) | collective-permute-done | bytes 4640 | tf_op jit(solution)/shard_map/ppermute | solution.py:40
  54.9 1.2 %collective-permute-start.21 = (f32[9,128]{1,0:T(8,128)S(1)}, f32[9,128]{1,0:T(8,128)S(1)}, u32[]{:S(2)}, u32[]{:S(2)}) collective-permute-start(f32[9,128]{1,0:T(8,128)S(1)} %select_maximum_fusion), channel_id=1, source_target_pairs={{0,5},{1,6},{2,7},{3,0},{4,1},{5,2},{6,3},{7,4},{8,13},{9,14},{10,... | collective-permute-start | bytes 13832 | tf_op jit(solution)/shard_map/ppermute | solution.py:40
  56.3 1.6 %collective-permute-start.22 = (f32[9,128]{1,0:T(8,128)S(1)}, f32[9,128]{1,0:T(8,128)S(1)}, u32[]{:S(2)}, u32[]{:S(2)}) collective-permute-start(f32[9,128]{1,0:T(8,128)S(1)} %select_maximum_fusion), channel_id=1, source_target_pairs={{0,6},{1,7},{2,0},{3,1},{4,2},{5,3},{6,4},{7,5},{8,14},{9,15},{10,... | collective-permute-start | bytes 13832 | tf_op jit(solution)/shard_map/ppermute | solution.py:40
  57.9 0.9 collective-permute-done.21
  59.2 1.7 %collective-permute-done.22 = f32[9,128]{1,0:T(8,128)S(1)} collective-permute-done((f32[9,128]{1,0:T(8,128)S(1)}, f32[9,128]{1,0:T(8,128)S(1)}, u32[]{:S(2)}, u32[]{:S(2)}) %collective-permute-start.22) | collective-permute-done | bytes 4640 | tf_op jit(solution)/shard_map/ppermute | solution.py:40
  62.3 0.8 fusion.30
  63.2 1.3 %collective-permute-start.7 = (f32[7,2,32,128]{3,2,1,0:T(8,128)S(1)}, f32[7,2,32,128]{3,2,1,0:T(8,128)S(1)}, u32[]{:S(2)}, u32[]{:S(2)}) collective-permute-start(f32[7,2,32,128]{3,2,1,0:T(8,128)S(1)} %multiply_add_fusion.7), channel_id=1, source_target_pairs={{16,24},{17,25},{18,26},{19,27},{20,28},{21,29},{22,30},{23,31}} | collective-permute-start | bytes 688136 | tf_op jit(solution)/shard_map/ppermute | solution.py:123
  64.5 4.7 %collective-permute-done.4 = f32[5,2,32,128]{3,2,1,0:T(8,128)} collective-permute-done((f32[5,2,32,128]{3,2,1,0:T(8,128)S(1)}, f32[5,2,32,128]{3,2,1,0:T(8,128)}, u32[]{:S(2)}, u32[]{:S(2)}) %collective-permute-start.4) | collective-permute-done | bytes 163872 | tf_op jit(solution)/shard_map/ppermute | solution.py:123
  69.2 1.0 multiply_add_fusion.9
  70.3 1.3 %collective-permute-start.10 = (f32[9,2,32,128]{3,2,1,0:T(8,128)S(1)}, f32[9,2,32,128]{3,2,1,0:T(8,128)S(1)}, u32[]{:S(2)}, u32[]{:S(2)}) collective-permute-start(f32[9,2,32,128]{3,2,1,0:T(8,128)S(1)} %multiply_add_fusion.4), channel_id=1, source_target_pairs={{16,24},{17,25},{18,26},{19,27},{20,28},{21,29},{22,30},{23,31}} | collective-permute-start | bytes 884744 | tf_op jit(solution)/shard_map/ppermute | solution.py:123
  71.7 1.3 %collective-permute-start.16 = (f32[11,2,32,128]{3,2,1,0:T(8,128)S(1)}, f32[11,2,32,128]{3,2,1,0:T(8,128)S(1)}, u32[]{:S(2)}, u32[]{:S(2)}) collective-permute-start(f32[11,2,32,128]{3,2,1,0:T(8,128)S(1)} %multiply_add_fusion.1), channel_id=1, source_target_pairs={{16,24},{17,25},{18,26},{19,27},{20,28},{21,29},{22,30},{23,31}} | collective-permute-start | bytes 1081352 | tf_op jit(solution)/shard_map/ppermute | solution.py:123
  73.0 15.6 %collective-permute-done.7 = f32[7,2,32,128]{3,2,1,0:T(8,128)S(1)} collective-permute-done((f32[7,2,32,128]{3,2,1,0:T(8,128)S(1)}, f32[7,2,32,128]{3,2,1,0:T(8,128)S(1)}, u32[]{:S(2)}, u32[]{:S(2)}) %collective-permute-start.7) | collective-permute-done | bytes 229408 | tf_op jit(solution)/shard_map/ppermute | solution.py:123
  88.7 6.2 %collective-permute-done.10 = f32[9,2,32,128]{3,2,1,0:T(8,128)S(1)} collective-permute-done((f32[9,2,32,128]{3,2,1,0:T(8,128)S(1)}, f32[9,2,32,128]{3,2,1,0:T(8,128)S(1)}, u32[]{:S(2)}, u32[]{:S(2)}) %collective-permute-start.10) | collective-permute-done | bytes 294944 | tf_op jit(solution)/shard_map/ppermute | solution.py:123
  95.1 6.6 %collective-permute-done.16 = f32[11,2,32,128]{3,2,1,0:T(8,128)S(1)} collective-permute-done((f32[11,2,32,128]{3,2,1,0:T(8,128)S(1)}, f32[11,2,32,128]{3,2,1,0:T(8,128)S(1)}, u32[]{:S(2)}, u32[]{:S(2)}) %collective-permute-start.16) | collective-permute-done | bytes 360480 | tf_op jit(solution)/shard_map/ppermute | solution.py:123
  101.8 1.1 %maximum_bitcast_fusion = f32[1,32,2,32,128]{4,3,2,1,0:T(8,128)} fusion(f32[11,2,32,128]{3,2,1,0:T(8,128)S(1)} %multiply_add_fusion, f32[9,2,32,128]{3,2,1,0:T(8,128)S(1)} %multiply_add_fusion.3, f32[7,2,32,128]{3,2,1,0:T(8,128)S(1)} %multiply_add_fusion.6, f32[5,2,32,128]{3,2,1,0:T(8,128)S(1)} %multiply_add_fusion.9), kind=kLoop, calls=%fused_computation.49 | loop fusion | flops 786432 | bytes 2097152 | tf_op jit(solution)/shard_map/broadcast_in_dim | solution.py:140
  (106 shorter events, 13.3 us)
Async XLA Ops:
  0.6 44.1 %copy-start = (bf16[1,8,64,128]{3,2,1,0:T(8,128)(2,1)S(1)}, bf16[1,8,64,128]{3,2,1,0:T(8,128)(2,1)}, u32[]{:S(2)}) copy-start(bf16[1,8,64,128]{3,2,1,0:T(8,128)(2,1)} %param.22) | copy-start | bytes 393220
  0.6 7.7 %copy-start.6 = (f32[1,32]{1,0:T(1,128)S(1)}, f32[1,32]{1,0:T(1,128)}, u32[]{:S(2)}) copy-start(f32[1,32]{1,0:T(1,128)} %param.19) | copy-start | bytes 388
  0.7 7.7 %copy-start.5 = (f32[1,32]{1,0:T(1,128)S(1)}, f32[1,32]{1,0:T(1,128)}, u32[]{:S(2)}) copy-start(f32[1,32]{1,0:T(1,128)} %param.21) | copy-start | bytes 388
  0.7 8.1 %copy-start.8 = (s32[1,8]{1,0:T(1,128)S(1)}, s32[1,8]{1,0:T(1,128)}, u32[]{:S(2)}) copy-start(s32[1,8]{1,0:T(1,128)} %param.23) | copy-start | bytes 100
  2.0 16.5 %collective-permute-start = (f32[33,2,32,128]{3,2,1,0:T(8,128)S(1)}, f32[33,2,32,128]{3,2,1,0:T(8,128)S(1)}, u32[]{:S(2)}, u32[]{:S(2)}) collective-permute-start(f32[33,2,32,128]{3,2,1,0:T(8,128)S(1)} %pad_maximum_fusion.2), channel_id=1, source_target_pairs={{0,1},{1,2},{2,3},{3,4},{4,5},{5,6},{6,7},{8,9},{9,10},{10,11},{11... | collective-permute-start | bytes 3244040 | tf_op jit(solution)/shard_map/ppermute | solution.py:71
  4.0 25.1 %collective-permute-start.1 = (f32[33,2,32,128]{3,2,1,0:T(8,128)S(1)}, f32[33,2,32,128]{3,2,1,0:T(8,128)S(1)}, u32[]{:S(2)}, u32[]{:S(2)}) collective-permute-start(f32[33,2,32,128]{3,2,1,0:T(8,128)S(1)} %pad_maximum_fusion.2), channel_id=1, source_target_pairs={{1,0},{2,1},{3,2},{4,3},{5,4},{6,5},{7,6},{9,8},{10,9},{11,10},{12... | collective-permute-start | bytes 3244040 | tf_op jit(solution)/shard_map/ppermute | solution.py:74
  9.4 19.7 %copy-start.1 = (f32[1,32,2,32,128]{4,3,2,1,0:T(8,128)S(1)}, f32[1,32,2,32,128]{4,3,2,1,0:T(8,128)}, u32[]{:S(2)}) copy-start(f32[1,32,2,32,128]{4,3,2,1,0:T(8,128)} %param.15) | copy-start | bytes 3145732
  29.2 0.8 copy-start.2
  32.5 0.8 copy-start.3
  33.2 1.9 %copy-start.4 = (f32[1,32]{1,0:T(1,128)S(1)}, f32[1,32]{1,0:T(1,128)}, u32[]{:S(2)}) copy-start(f32[1,32]{1,0:T(1,128)} %param.20) | copy-start | bytes 388
  35.7 3.9 %collective-permute-start.11 = (f32[34,64]{1,0:T(8,128)S(1)}, f32[34,64]{1,0:T(8,128)S(1)}, u32[]{:S(2)}, u32[]{:S(2)}) collective-permute-start(f32[34,64]{1,0:T(8,128)S(1)} %get-tuple-element.48), channel_id=1, source_target_pairs={{0,8},{8,16},{16,24},{24,0},{1,9},{9,17},{17,25},{25,1},{2,10},{10... | collective-permute-start | bytes 26120 | tf_op jit(solution)/shard_map/ppermute | solution.py:40
  36.0 4.7 %collective-permute-start.12 = (f32[34,64]{1,0:T(8,128)S(1)}, f32[34,64]{1,0:T(8,128)S(1)}, u32[]{:S(2)}, u32[]{:S(2)}) collective-permute-start(f32[34,64]{1,0:T(8,128)S(1)} %get-tuple-element.48), channel_id=1, source_target_pairs={{0,16},{8,24},{16,0},{24,8},{1,17},{9,25},{17,1},{25,9},{2,18},{10... | collective-permute-start | bytes 26120 | tf_op jit(solution)/shard_map/ppermute | solution.py:40
  37.7 5.6 %collective-permute-start.13 = (f32[34,64]{1,0:T(8,128)S(1)}, f32[34,64]{1,0:T(8,128)S(1)}, u32[]{:S(2)}, u32[]{:S(2)}) collective-permute-start(f32[34,64]{1,0:T(8,128)S(1)} %get-tuple-element.48), channel_id=1, source_target_pairs={{0,24},{8,0},{16,8},{24,16},{1,25},{9,1},{17,9},{25,17},{2,26},{10... | collective-permute-start | bytes 26120 | tf_op jit(solution)/shard_map/ppermute | solution.py:40
  38.2 10.4 %collective-permute-start.14 = (f32[11,2,32,128]{3,2,1,0:T(8,128)S(1)}, f32[11,2,32,128]{3,2,1,0:T(8,128)S(1)}, u32[]{:S(2)}, u32[]{:S(2)}) collective-permute-start(f32[11,2,32,128]{3,2,1,0:T(8,128)S(1)} %slice.231), channel_id=1, source_target_pairs={{0,8},{1,9},{2,10},{3,11},{4,12},{5,13},{6,14},{7,15}} | collective-permute-start | bytes 1081352 | tf_op jit(solution)/shard_map/ppermute | solution.py:123
  38.9 6.0 %collective-permute-start.2 = (f32[5,2,32,128]{3,2,1,0:T(8,128)S(1)}, f32[5,2,32,128]{3,2,1,0:T(8,128)S(1)}, u32[]{:S(2)}, u32[]{:S(2)}) collective-permute-start(f32[5,2,32,128]{3,2,1,0:T(8,128)S(1)} %slice.228), channel_id=1, source_target_pairs={{0,8},{1,9},{2,10},{3,11},{4,12},{5,13},{6,14},{7,15}} | collective-permute-start | bytes 491528 | tf_op jit(solution)/shard_map/ppermute | solution.py:123
  39.6 6.0 %collective-permute-start.5 = (f32[7,2,32,128]{3,2,1,0:T(8,128)S(1)}, f32[7,2,32,128]{3,2,1,0:T(8,128)S(1)}, u32[]{:S(2)}, u32[]{:S(2)}) collective-permute-start(f32[7,2,32,128]{3,2,1,0:T(8,128)S(1)} %slice.229), channel_id=1, source_target_pairs={{0,8},{1,9},{2,10},{3,11},{4,12},{5,13},{6,14},{7,15}} | collective-permute-start | bytes 688136 | tf_op jit(solution)/shard_map/ppermute | solution.py:123
  40.7 5.8 %collective-permute-start.8 = (f32[9,2,32,128]{3,2,1,0:T(8,128)S(1)}, f32[9,2,32,128]{3,2,1,0:T(8,128)S(1)}, u32[]{:S(2)}, u32[]{:S(2)}) collective-permute-start(f32[9,2,32,128]{3,2,1,0:T(8,128)S(1)} %slice.230), channel_id=1, source_target_pairs={{0,8},{1,9},{2,10},{3,11},{4,12},{5,13},{6,14},{7,15}} | collective-permute-start | bytes 884744 | tf_op jit(solution)/shard_map/ppermute | solution.py:123
  45.0 2.3 %collective-permute-start.3 = (f32[5,2,32,128]{3,2,1,0:T(8,128)S(1)}, f32[5,2,32,128]{3,2,1,0:T(8,128)S(1)}, u32[]{:S(2)}, u32[]{:S(2)}) collective-permute-start(f32[5,2,32,128]{3,2,1,0:T(8,128)S(1)} %multiply_add_fusion.11), channel_id=1, source_target_pairs={{8,16},{9,17},{10,18},{11,19},{12,20},{13,21},{14,22},{15,23}} | collective-permute-start | bytes 491528 | tf_op jit(solution)/shard_map/ppermute | solution.py:123
  45.8 17.4 %collective-permute-start.6 = (f32[7,2,32,128]{3,2,1,0:T(8,128)S(1)}, f32[7,2,32,128]{3,2,1,0:T(8,128)S(1)}, u32[]{:S(2)}, u32[]{:S(2)}) collective-permute-start(f32[7,2,32,128]{3,2,1,0:T(8,128)S(1)} %multiply_add_fusion.8), channel_id=1, source_target_pairs={{8,16},{9,17},{10,18},{11,19},{12,20},{13,21},{14,22},{15,23}} | collective-permute-start | bytes 688136 | tf_op jit(solution)/shard_map/ppermute | solution.py:123
  46.6 23.6 %collective-permute-start.9 = (f32[9,2,32,128]{3,2,1,0:T(8,128)S(1)}, f32[9,2,32,128]{3,2,1,0:T(8,128)S(1)}, u32[]{:S(2)}, u32[]{:S(2)}) collective-permute-start(f32[9,2,32,128]{3,2,1,0:T(8,128)S(1)} %multiply_add_fusion.5), channel_id=1, source_target_pairs={{8,16},{9,17},{10,18},{11,19},{12,20},{13,21},{14,22},{15,23}} | collective-permute-start | bytes 884744 | tf_op jit(solution)/shard_map/ppermute | solution.py:123
  47.4 21.8 %collective-permute-start.4 = (f32[5,2,32,128]{3,2,1,0:T(8,128)S(1)}, f32[5,2,32,128]{3,2,1,0:T(8,128)}, u32[]{:S(2)}, u32[]{:S(2)}) collective-permute-start(f32[5,2,32,128]{3,2,1,0:T(8,128)S(1)} %multiply_add_fusion.10), channel_id=1, source_target_pairs={{16,24},{17,25},{18,26},{19,27},{20,28},{21,29},{22,30},{23,31}} | collective-permute-start | bytes 491528 | tf_op jit(solution)/shard_map/ppermute | solution.py:123
  48.7 3.1 %collective-permute-start.17 = (f32[9,128]{1,0:T(8,128)S(1)}, f32[9,128]{1,0:T(8,128)S(1)}, u32[]{:S(2)}, u32[]{:S(2)}) collective-permute-start(f32[9,128]{1,0:T(8,128)S(1)} %select_maximum_fusion), channel_id=1, source_target_pairs={{0,1},{1,2},{2,3},{3,4},{4,5},{5,6},{6,7},{7,0},{8,9},{9,10},{10,1... | collective-permute-start | bytes 13832 | tf_op jit(solution)/shard_map/ppermute | solution.py:40
  49.0 3.7 %collective-permute-start.18 = (f32[9,128]{1,0:T(8,128)S(1)}, f32[9,128]{1,0:T(8,128)S(1)}, u32[]{:S(2)}, u32[]{:S(2)}) collective-permute-start(f32[9,128]{1,0:T(8,128)S(1)} %select_maximum_fusion), channel_id=1, source_target_pairs={{0,2},{1,3},{2,4},{3,5},{4,6},{5,7},{6,0},{7,1},{8,10},{9,11},{10,... | collective-permute-start | bytes 13832 | tf_op jit(solution)/shard_map/ppermute | solution.py:40
  51.8 3.1 %collective-permute-start.19 = (f32[9,128]{1,0:T(8,128)S(1)}, f32[9,128]{1,0:T(8,128)S(1)}, u32[]{:S(2)}, u32[]{:S(2)}) collective-permute-start(f32[9,128]{1,0:T(8,128)S(1)} %select_maximum_fusion), channel_id=1, source_target_pairs={{0,3},{1,4},{2,5},{3,6},{4,7},{5,0},{6,1},{7,2},{8,11},{9,12},{10,... | collective-permute-start | bytes 13832 | tf_op jit(solution)/shard_map/ppermute | solution.py:40
  52.7 3.7 %collective-permute-start.20 = (f32[9,128]{1,0:T(8,128)S(1)}, f32[9,128]{1,0:T(8,128)S(1)}, u32[]{:S(2)}, u32[]{:S(2)}) collective-permute-start(f32[9,128]{1,0:T(8,128)S(1)} %select_maximum_fusion), channel_id=1, source_target_pairs={{0,4},{1,5},{2,6},{3,7},{4,0},{5,1},{6,2},{7,3},{8,12},{9,13},{10,... | collective-permute-start | bytes 13832 | tf_op jit(solution)/shard_map/ppermute | solution.py:40
  54.9 4.0 %collective-permute-start.21 = (f32[9,128]{1,0:T(8,128)S(1)}, f32[9,128]{1,0:T(8,128)S(1)}, u32[]{:S(2)}, u32[]{:S(2)}) collective-permute-start(f32[9,128]{1,0:T(8,128)S(1)} %select_maximum_fusion), channel_id=1, source_target_pairs={{0,5},{1,6},{2,7},{3,0},{4,1},{5,2},{6,3},{7,4},{8,13},{9,14},{10,... | collective-permute-start | bytes 13832 | tf_op jit(solution)/shard_map/ppermute | solution.py:40
  56.3 4.5 %collective-permute-start.22 = (f32[9,128]{1,0:T(8,128)S(1)}, f32[9,128]{1,0:T(8,128)S(1)}, u32[]{:S(2)}, u32[]{:S(2)}) collective-permute-start(f32[9,128]{1,0:T(8,128)S(1)} %select_maximum_fusion), channel_id=1, source_target_pairs={{0,6},{1,7},{2,0},{3,1},{4,2},{5,3},{6,4},{7,5},{8,14},{9,15},{10,... | collective-permute-start | bytes 13832 | tf_op jit(solution)/shard_map/ppermute | solution.py:40
  58.9 2.7 %collective-permute-start.23 = (f32[9,128]{1,0:T(8,128)S(1)}, f32[9,128]{1,0:T(8,128)S(1)}, u32[]{:S(2)}, u32[]{:S(2)}) collective-permute-start(f32[9,128]{1,0:T(8,128)S(1)} %select_maximum_fusion), channel_id=1, source_target_pairs={{0,7},{1,0},{2,1},{3,2},{4,3},{5,4},{6,5},{7,6},{8,15},{9,8},{10,9... | collective-permute-start | bytes 13832 | tf_op jit(solution)/shard_map/ppermute | solution.py:40
  60.9 10.7 %collective-permute-start.15 = (f32[11,2,32,128]{3,2,1,0:T(8,128)S(1)}, f32[11,2,32,128]{3,2,1,0:T(8,128)S(1)}, u32[]{:S(2)}, u32[]{:S(2)}) collective-permute-start(f32[11,2,32,128]{3,2,1,0:T(8,128)S(1)} %multiply_add_fusion.2), channel_id=1, source_target_pairs={{8,16},{9,17},{10,18},{11,19},{12,20},{13,21},{14,22},{15,23}} | collective-permute-start | bytes 1081352 | tf_op jit(solution)/shard_map/ppermute | solution.py:123
  63.2 25.4 %collective-permute-start.7 = (f32[7,2,32,128]{3,2,1,0:T(8,128)S(1)}, f32[7,2,32,128]{3,2,1,0:T(8,128)S(1)}, u32[]{:S(2)}, u32[]{:S(2)}) collective-permute-start(f32[7,2,32,128]{3,2,1,0:T(8,128)S(1)} %multiply_add_fusion.7), channel_id=1, source_target_pairs={{16,24},{17,25},{18,26},{19,27},{20,28},{21,29},{22,30},{23,31}} | collective-permute-start | bytes 688136 | tf_op jit(solution)/shard_map/ppermute | solution.py:123
  70.3 24.7 %collective-permute-start.10 = (f32[9,2,32,128]{3,2,1,0:T(8,128)S(1)}, f32[9,2,32,128]{3,2,1,0:T(8,128)S(1)}, u32[]{:S(2)}, u32[]{:S(2)}) collective-permute-start(f32[9,2,32,128]{3,2,1,0:T(8,128)S(1)} %multiply_add_fusion.4), channel_id=1, source_target_pairs={{16,24},{17,25},{18,26},{19,27},{20,28},{21,29},{22,30},{23,31}} | collective-permute-start | bytes 884744 | tf_op jit(solution)/shard_map/ppermute | solution.py:123
  71.7 30.0 %collective-permute-start.16 = (f32[11,2,32,128]{3,2,1,0:T(8,128)S(1)}, f32[11,2,32,128]{3,2,1,0:T(8,128)S(1)}, u32[]{:S(2)}, u32[]{:S(2)}) collective-permute-start(f32[11,2,32,128]{3,2,1,0:T(8,128)S(1)} %multiply_add_fusion.1), channel_id=1, source_target_pairs={{16,24},{17,25},{18,26},{19,27},{20,28},{21,29},{22,30},{23,31}} | collective-permute-start | bytes 1081352 | tf_op jit(solution)/shard_map/ppermute | solution.py:123
  (1 other events, 0.8 us)

commit v12 on v9

--- a/solution.py
+++ b/solution.py
@@ -99,24 +99,21 @@
     cols = own_columns.shape[1]
     extra = jnp.zeros((2, cols), jnp.float32).at[0, :bins].set(chain).at[1, :bins].set(gamma_yield[0])
     packed = jnp.concatenate([own_columns, extra], axis=0)
-    me_chain = lax.axis_index("species")
-    size = bins // CHUNKS
-    stack = own_part.reshape((CHUNKS, size) + own_part.shape[1:])
-    yields = chain.reshape(CHUNKS, size)[:, :, None, None, None]
-    pairs = [(g, g + 1) for g in range(groups - 1)]
+    base = bins // CHUNKS
+    bounds = [0]
+    for c in range(CHUNKS):
+        bounds.append(bounds[-1] + base + 2 * c - (CHUNKS - 1))
+    bounds[-1] = bins
+    pieces = [own_part[bounds[c]:bounds[c + 1]] for c in range(CHUNKS)]
+    scales = [chain[bounds[c]:bounds[c + 1]][:, None, None, None] for c in range(CHUNKS)]
     for wave in range(CHUNKS + groups - 2):
-        sent = lax.dynamic_index_in_dim(stack, jnp.clip(wave - me_chain, 0, CHUNKS - 1), 0, keepdims=False)
-        arrived = lax.ppermute(sent, "species", pairs)
-        if wave == 0:
-            packed, arrived = lax.optimization_barrier((packed, arrived))
-        slot = wave - me_chain + 1
-        valid = (me_chain >= 1) & (slot >= 0) & (slot < CHUNKS)
-        slot = jnp.clip(slot, 0, CHUNKS - 1)
-        current = lax.dynamic_index_in_dim(stack, slot, 0, keepdims=False)
-        scale = lax.dynamic_index_in_dim(yields, slot, 0, keepdims=False)
-        updated = jnp.where(valid, current + scale * arrived, current)
-        stack = lax.dynamic_update_index_in_dim(stack, updated, slot, 0)
-    carried = stack.reshape(own_part.shape)
+        for c in range(CHUNKS):
+            s = wave - c
+            if 0 <= s < groups - 1:
+                arrived = lax.ppermute(pieces[c], "species", [(s, s + 1)])
+                pieces[c] = pieces[c] + scales[c] * arrived
+    packed, pieces = lax.optimization_barrier((packed, pieces))
+    carried = jnp.concatenate(pieces, axis=0)
     me_g = lax.axis_index("species")
     everyone = packed[None]
     span = 1

time: 99.3 us -> 116 us (1.17)
  the two profiles are of different devices: /device:TPU:12 before, /device:TPU:26 now
where the time goes in v12:
time: 116 us; the launch traced here: 115 us
  waiting for transfers between devices  83.8 us (72%)
  starting transfers between devices  16.4 us (14%)
  other arithmetic  8.86 us (8%)
  matrix products  3.35 us (3%)
  local copies, waits for them, and re-layouts  1.66 us (1%)
  between operations  1.24 us (1%)
    ppermute x12, waiting for transfers between devices, body(): arrived = lax.ppermute(pieces[c], 'species', [(s, s + 1)])  47.6 us
    ppermute x1, waiting for transfers between devices, body(): lax.ppermute(mine[:, mine.shape[1] - halo:], 'space', [(i, i + 1) for i i...  10.7 us
    ppermute x12, starting transfers between devices, body(): arrived = lax.ppermute(pieces[c], 'species', [(s, s + 1)])  10.6 us
    ppermute x1, waiting for transfers between devices, body(): lax.ppermute(mine[:, :halo], 'space', [(i + 1, i) for i in range(count -...  10.5 us
    ppermute x3, waiting for transfers between devices, gather_all(): other = lax.ppermute(held, axis, [(i, i ^ span) for i in range(count)])  7.72 us
    ppermute x2, waiting for transfers between devices, body(): lax.ppermute(everyone, 'species', [(i, i ^ span) for i in range(groups)])  7.33 us
    ppermute x1, starting transfers between devices, body(): lax.ppermute(mine[:, :halo], 'space', [(i + 1, i) for i in range(count -...  3.64 us
    add x2, other arithmetic, body(): inner + wide_factor[:, 1 + step:wide_factor.shape[1] - 1 - step] * (besid...  2.71 us
  transfers between devices with their start and end apart: 19, of which 11 were waited for; matrix products, arithmetic and copies ran while one was open for 3% of the time, Pallas kernels for 0%

profile of v12, /device:TPU:26, one launch (start us, length us, event | category | flops | bytes accessed | tf_op | source)
XLA Modules:
  0.0 115.3 jit_solution(969538676783964030)
XLA Ops:
  0.7 1.4 %pad_maximum_fusion.2 = f32[33,2,32,128]{3,2,1,0:T(8,128)S(1)} fusion(f32[1,2,32,128]{3,2,1,0:T(8,128)} %bitcast.121, f32[32,2,32,128]{3,2,1,0:T(8,128)} %bitcast.116), kind=kLoop, calls=%fused_computation.36 | loop fusion | flops 270336 | bytes 2162688 | tf_op jit(solution)/shard_map/concatenate | solution.py:77
  2.1 1.9 %collective-permute-start = (f32[33,2,32,128]{3,2,1,0:T(8,128)S(1)}, f32[33,2,32,128]{3,2,1,0:T(8,128)S(1)}, u32[]{:S(2)}, u32[]{:S(2)}) collective-permute-start(f32[33,2,32,128]{3,2,1,0:T(8,128)S(1)} %pad_maximum_fusion.2), channel_id=1, source_target_pairs={{0,1},{1,2},{2,3},{3,4},{4,5},{5,6},{6,7},{8,9},{9,10},{10,11},{11... | collective-permute-start | bytes 3244040 | tf_op jit(solution)/shard_map/ppermute | solution.py:78
  4.0 3.6 %collective-permute-start.1 = (f32[33,2,32,128]{3,2,1,0:T(8,128)S(1)}, f32[33,2,32,128]{3,2,1,0:T(8,128)S(1)}, u32[]{:S(2)}, u32[]{:S(2)}) collective-permute-start(f32[33,2,32,128]{3,2,1,0:T(8,128)S(1)} %pad_maximum_fusion.2), channel_id=1, source_target_pairs={{1,0},{2,1},{3,2},{4,3},{5,4},{6,5},{7,6},{9,8},{10,9},{11,10},{12... | collective-permute-start | bytes 3244040 | tf_op jit(solution)/shard_map/ppermute | solution.py:81
  7.9 10.7 %collective-permute-done = f32[33,2,32,128]{3,2,1,0:T(8,128)S(1)} collective-permute-done((f32[33,2,32,128]{3,2,1,0:T(8,128)S(1)}, f32[33,2,32,128]{3,2,1,0:T(8,128)S(1)}, u32[]{:S(2)}, u32[]{:S(2)}) %collective-permute-start) | collective-permute-done | bytes 1081376 | tf_op jit(solution)/shard_map/ppermute | solution.py:78
  18.6 10.5 %collective-permute-done.1 = f32[33,2,32,128]{3,2,1,0:T(8,128)S(1)} collective-permute-done((f32[33,2,32,128]{3,2,1,0:T(8,128)S(1)}, f32[33,2,32,128]{3,2,1,0:T(8,128)S(1)}, u32[]{:S(2)}, u32[]{:S(2)}) %collective-permute-start.1) | collective-permute-done | bytes 1081376 | tf_op jit(solution)/shard_map/ppermute | solution.py:81
  30.5 2.0 %fusion.6 = f32[32,4,32,128]{3,2,1,0:T(8,128)S(1)} fusion(f32[32,4,32,128]{3,2,1,0:T(8,128)S(1)} %pad_maximum_fusion, f32[32,6,32,128]{3,2,1,0:T(8,128)S(1)} %broadcast_multiply_fusion, f32[32,2,32,128]{3,2,1,0:T(8,128)S(1)} %slice.216, f32[32,2,32,128]{3,2,1,0:T(8,128)S(1)} %bitcast.118, f32[32,2,32,128]{3,2,1,0:T(8,128)S(1)} %slice.215), kind=kLoop, calls=%fused_computation.14 | loop fusion | flops 5767168 | bytes 9437184 | tf_op jit(solution)/shard_map/add | solution.py:87
  32.5 0.7 fusion.25
  33.3 1.7 %convolution_bitcast_fusion = f32[4,8,64,128]{3,1,2,0:T(8,128)S(1)} fusion(f32[4,8,64,128]{3,2,1,0:T(8,128)S(1)} %bitcast.119, f32[1,32,32]{2,1,0:T(8,128)S(1)} %copy-done.3), kind=kOutput, calls=%fused_computation.19 | convolution fusion | flops 100663296 | bytes 2101248 | tf_op jit(solution)/shard_map/dot_general | solution.py:89
  35.7 0.7 collective-permute-start.2
  36.7 0.7 collective-permute-start.11
  37.4 0.7 collective-permute-start.8
  38.1 0.7 collective-permute-start.5
  38.9 0.7 collective-permute-start.3
  39.7 0.7 collective-permute-start.6
  40.5 0.7 collective-permute-start.9
  41.3 1.3 %collective-permute-start.4 = (f32[5,2,32,128]{3,2,1,0:T(8,128)S(1)}, f32[5,2,32,128]{3,2,1,0:T(8,128)S(1)}, u32[]{:S(2)}, u32[]{:S(2)}) collective-permute-start(f32[5,2,32,128]{3,2,1,0:T(8,128)S(1)} %multiply_add_fusion.10), channel_id=1, source_target_pairs={{16,24},{17,25},{18,26},{19,27},{20,28},{21,29},{22,30},{23,31}} | collective-permute-start | bytes 491528 | tf_op jit(solution)/shard_map/ppermute | solution.py:113
  42.7 0.7 collective-permute-start.12
  43.5 1.3 %collective-permute-start.7 = (f32[7,2,32,128]{3,2,1,0:T(8,128)S(1)}, f32[7,2,32,128]{3,2,1,0:T(8,128)S(1)}, u32[]{:S(2)}, u32[]{:S(2)}) collective-permute-start(f32[7,2,32,128]{3,2,1,0:T(8,128)S(1)} %multiply_add_fusion.7), channel_id=1, source_target_pairs={{16,24},{17,25},{18,26},{19,27},{20,28},{21,29},{22,30},{23,31}} | collective-permute-start | bytes 688136 | tf_op jit(solution)/shard_map/ppermute | solution.py:113
  44.8 11.8 %collective-permute-done.4 = f32[5,2,32,128]{3,2,1,0:T(8,128)S(1)} collective-permute-done((f32[5,2,32,128]{3,2,1,0:T(8,128)S(1)}, f32[5,2,32,128]{3,2,1,0:T(8,128)S(1)}, u32[]{:S(2)}, u32[]{:S(2)}) %collective-permute-start.4) | collective-permute-done | bytes 163872 | tf_op jit(solution)/shard_map/ppermute | solution.py:113
  56.8 1.3 %collective-permute-start.10 = (f32[9,2,32,128]{3,2,1,0:T(8,128)S(1)}, f32[9,2,32,128]{3,2,1,0:T(8,128)S(1)}, u32[]{:S(2)}, u32[]{:S(2)}) collective-permute-start(f32[9,2,32,128]{3,2,1,0:T(8,128)S(1)} %multiply_add_fusion.4), channel_id=1, source_target_pairs={{16,24},{17,25},{18,26},{19,27},{20,28},{21,29},{22,30},{23,31}} | collective-permute-start | bytes 884744 | tf_op jit(solution)/shard_map/ppermute | solution.py:113
  58.3 1.3 %collective-permute-start.13 = (f32[11,2,32,128]{3,2,1,0:T(8,128)S(1)}, f32[11,2,32,128]{3,2,1,0:T(8,128)S(1)}, u32[]{:S(2)}, u32[]{:S(2)}) collective-permute-start(f32[11,2,32,128]{3,2,1,0:T(8,128)S(1)} %multiply_add_fusion.1), channel_id=1, source_target_pairs={{16,24},{17,25},{18,26},{19,27},{20,28},{21,29},{22,30},{23,31}} | collective-permute-start | bytes 1081352 | tf_op jit(solution)/shard_map/ppermute | solution.py:113
  59.6 19.1 %collective-permute-done.7 = f32[7,2,32,128]{3,2,1,0:T(8,128)S(1)} collective-permute-done((f32[7,2,32,128]{3,2,1,0:T(8,128)S(1)}, f32[7,2,32,128]{3,2,1,0:T(8,128)S(1)}, u32[]{:S(2)}, u32[]{:S(2)}) %collective-permute-start.7) | collective-permute-done | bytes 229408 | tf_op jit(solution)/shard_map/ppermute | solution.py:113
  78.7 7.6 %collective-permute-done.10 = f32[9,2,32,128]{3,2,1,0:T(8,128)S(1)} collective-permute-done((f32[9,2,32,128]{3,2,1,0:T(8,128)S(1)}, f32[9,2,32,128]{3,2,1,0:T(8,128)S(1)}, u32[]{:S(2)}, u32[]{:S(2)}) %collective-permute-start.10) | collective-permute-done | bytes 294944 | tf_op jit(solution)/shard_map/ppermute | solution.py:113
  86.5 9.0 %collective-permute-done.13 = f32[11,2,32,128]{3,2,1,0:T(8,128)S(1)} collective-permute-done((f32[11,2,32,128]{3,2,1,0:T(8,128)S(1)}, f32[11,2,32,128]{3,2,1,0:T(8,128)S(1)}, u32[]{:S(2)}, u32[]{:S(2)}) %collective-permute-start.13) | collective-permute-done | bytes 360480 | tf_op jit(solution)/shard_map/ppermute | solution.py:113
  96.4 3.1 %collective-permute-done.14 = f32[1,34,64]{2,1,0:T(8,128)S(1)} collective-permute-done((f32[1,34,64]{2,1,0:T(8,128)S(1)}, f32[1,34,64]{2,1,0:T(8,128)S(1)}, u32[]{:S(2)}, u32[]{:S(2)}) %collective-permute-start.14) | collective-permute-done | bytes 8736 | tf_op jit(solution)/shard_map/ppermute | solution.py:121
  99.6 0.7 broadcast_select_fusion
  100.2 4.2 %collective-permute-done.15 = f32[2,34,64]{2,1,0:T(8,128)S(1)} collective-permute-done((f32[2,34,64]{2,1,0:T(8,128)S(1)}, f32[2,34,64]{2,1,0:T(8,128)S(1)}, u32[]{:S(2)}, u32[]{:S(2)}) %collective-permute-start.15) | collective-permute-done | bytes 17440 | tf_op jit(solution)/shard_map/ppermute | solution.py:121
  105.5 1.2 collective-permute-done.16
  106.7 3.7 %collective-permute-done.17 = f32[2,9,128]{2,1,0:T(8,128)S(1)} collective-permute-done((f32[2,9,128]{2,1,0:T(8,128)S(1)}, f32[2,9,128]{2,1,0:T(8,128)S(1)}, u32[]{:S(2)}, u32[]{:S(2)}) %collective-permute-start.17) | collective-permute-done | bytes 9248 | tf_op jit(solution)/shard_map/ppermute | solution.py:44
  110.4 1.0 maximum_bitcast_fusion
  111.5 2.9 %collective-permute-done.18 = f32[4,9,128]{2,1,0:T(8,128)S(1)} collective-permute-done((f32[4,9,128]{2,1,0:T(8,128)S(1)}, f32[4,9,128]{2,1,0:T(8,128)S(1)}, u32[]{:S(2)}, u32[]{:S(2)}) %collective-permute-start.18) | collective-permute-done | bytes 18464 | tf_op jit(solution)/shard_map/ppermute | solution.py:44
  114.5 0.8 fusion.30
  (82 shorter events, 5.8 us)
Async XLA Ops:
  0.6 104.6 %copy-start = (bf16[1,8,64,128]{3,2,1,0:T(8,128)(2,1)S(1)}, bf16[1,8,64,128]{3,2,1,0:T(8,128)(2,1)}, u32[]{:S(2)}) copy-start(bf16[1,8,64,128]{3,2,1,0:T(8,128)(2,1)} %param.22) | copy-start | bytes 393220
  0.6 7.0 %copy-start.5 = (f32[1,32]{1,0:T(1,128)S(1)}, f32[1,32]{1,0:T(1,128)}, u32[]{:S(2)}) copy-start(f32[1,32]{1,0:T(1,128)} %param.19) | copy-start | bytes 388
  2.1 16.5 %collective-permute-start = (f32[33,2,32,128]{3,2,1,0:T(8,128)S(1)}, f32[33,2,32,128]{3,2,1,0:T(8,128)S(1)}, u32[]{:S(2)}, u32[]{:S(2)}) collective-permute-start(f32[33,2,32,128]{3,2,1,0:T(8,128)S(1)} %pad_maximum_fusion.2), channel_id=1, source_target_pairs={{0,1},{1,2},{2,3},{3,4},{4,5},{5,6},{6,7},{8,9},{9,10},{10,11},{11... | collective-permute-start | bytes 3244040 | tf_op jit(solution)/shard_map/ppermute | solution.py:78
  4.0 25.1 %collective-permute-start.1 = (f32[33,2,32,128]{3,2,1,0:T(8,128)S(1)}, f32[33,2,32,128]{3,2,1,0:T(8,128)S(1)}, u32[]{:S(2)}, u32[]{:S(2)}) collective-permute-start(f32[33,2,32,128]{3,2,1,0:T(8,128)S(1)} %pad_maximum_fusion.2), channel_id=1, source_target_pairs={{1,0},{2,1},{3,2},{4,3},{5,4},{6,5},{7,6},{9,8},{10,9},{11,10},{12... | collective-permute-start | bytes 3244040 | tf_op jit(solution)/shard_map/ppermute | solution.py:81
  7.9 21.4 %copy-start.1 = (f32[1,32,2,32,128]{4,3,2,1,0:T(8,128)S(1)}, f32[1,32,2,32,128]{4,3,2,1,0:T(8,128)}, u32[]{:S(2)}) copy-start(f32[1,32,2,32,128]{4,3,2,1,0:T(8,128)} %param.15) | copy-start | bytes 3145732
  29.2 0.8 copy-start.2
  29.3 0.8 copy-start.7
  32.5 0.8 copy-start.3
  33.3 1.9 %copy-start.4 = (f32[1,32]{1,0:T(1,128)S(1)}, f32[1,32]{1,0:T(1,128)}, u32[]{:S(2)}) copy-start(f32[1,32]{1,0:T(1,128)} %param.20) | copy-start | bytes 388
  35.0 1.4 %copy-start.6 = (f32[1,32]{1,0:T(1,128)S(1)}, f32[1,32]{1,0:T(1,128)}, u32[]{:S(2)}) copy-start(f32[1,32]{1,0:T(1,128)} %param.21) | copy-start | bytes 388
  35.7 3.1 %collective-permute-start.2 = (f32[5,2,32,128]{3,2,1,0:T(8,128)S(1)}, f32[5,2,32,128]{3,2,1,0:T(8,128)S(1)}, u32[]{:S(2)}, u32[]{:S(2)}) collective-permute-start(f32[5,2,32,128]{3,2,1,0:T(8,128)S(1)} %slice.224), channel_id=1, source_target_pairs={{0,8},{1,9},{2,10},{3,11},{4,12},{5,13},{6,14},{7,15}} | collective-permute-start | bytes 491528 | tf_op jit(solution)/shard_map/ppermute | solution.py:113
  36.7 5.9 %collective-permute-start.11 = (f32[11,2,32,128]{3,2,1,0:T(8,128)S(1)}, f32[11,2,32,128]{3,2,1,0:T(8,128)S(1)}, u32[]{:S(2)}, u32[]{:S(2)}) collective-permute-start(f32[11,2,32,128]{3,2,1,0:T(8,128)S(1)} %slice.227), channel_id=1, source_target_pairs={{0,8},{1,9},{2,10},{3,11},{4,12},{5,13},{6,14},{7,15}} | collective-permute-start | bytes 1081352 | tf_op jit(solution)/shard_map/ppermute | solution.py:113
  37.4 3.0 %collective-permute-start.8 = (f32[9,2,32,128]{3,2,1,0:T(8,128)S(1)}, f32[9,2,32,128]{3,2,1,0:T(8,128)S(1)}, u32[]{:S(2)}, u32[]{:S(2)}) collective-permute-start(f32[9,2,32,128]{3,2,1,0:T(8,128)S(1)} %slice.226), channel_id=1, source_target_pairs={{0,8},{1,9},{2,10},{3,11},{4,12},{5,13},{6,14},{7,15}} | collective-permute-start | bytes 884744 | tf_op jit(solution)/shard_map/ppermute | solution.py:113
  38.1 1.6 %collective-permute-start.5 = (f32[7,2,32,128]{3,2,1,0:T(8,128)S(1)}, f32[7,2,32,128]{3,2,1,0:T(8,128)S(1)}, u32[]{:S(2)}, u32[]{:S(2)}) collective-permute-start(f32[7,2,32,128]{3,2,1,0:T(8,128)S(1)} %slice.225), channel_id=1, source_target_pairs={{0,8},{1,9},{2,10},{3,11},{4,12},{5,13},{6,14},{7,15}} | collective-permute-start | bytes 688136 | tf_op jit(solution)/shard_map/ppermute | solution.py:113
  38.9 2.3 %collective-permute-start.3 = (f32[5,2,32,128]{3,2,1,0:T(8,128)S(1)}, f32[5,2,32,128]{3,2,1,0:T(8,128)S(1)}, u32[]{:S(2)}, u32[]{:S(2)}) collective-permute-start(f32[5,2,32,128]{3,2,1,0:T(8,128)S(1)} %multiply_add_fusion.11), channel_id=1, source_target_pairs={{8,16},{9,17},{10,18},{11,19},{12,20},{13,21},{14,22},{15,23}} | collective-permute-start | bytes 491528 | tf_op jit(solution)/shard_map/ppermute | solution.py:113
  39.7 3.7 %collective-permute-start.6 = (f32[7,2,32,128]{3,2,1,0:T(8,128)S(1)}, f32[7,2,32,128]{3,2,1,0:T(8,128)S(1)}, u32[]{:S(2)}, u32[]{:S(2)}) collective-permute-start(f32[7,2,32,128]{3,2,1,0:T(8,128)S(1)} %multiply_add_fusion.8), channel_id=1, source_target_pairs={{8,16},{9,17},{10,18},{11,19},{12,20},{13,21},{14,22},{15,23}} | collective-permute-start | bytes 688136 | tf_op jit(solution)/shard_map/ppermute | solution.py:113
  40.5 16.2 %collective-permute-start.9 = (f32[9,2,32,128]{3,2,1,0:T(8,128)S(1)}, f32[9,2,32,128]{3,2,1,0:T(8,128)S(1)}, u32[]{:S(2)}, u32[]{:S(2)}) collective-permute-start(f32[9,2,32,128]{3,2,1,0:T(8,128)S(1)} %multiply_add_fusion.5), channel_id=1, source_target_pairs={{8,16},{9,17},{10,18},{11,19},{12,20},{13,21},{14,22},{15,23}} | collective-permute-start | bytes 884744 | tf_op jit(solution)/shard_map/ppermute | solution.py:113
  41.3 15.3 %collective-permute-start.4 = (f32[5,2,32,128]{3,2,1,0:T(8,128)S(1)}, f32[5,2,32,128]{3,2,1,0:T(8,128)S(1)}, u32[]{:S(2)}, u32[]{:S(2)}) collective-permute-start(f32[5,2,32,128]{3,2,1,0:T(8,128)S(1)} %multiply_add_fusion.10), channel_id=1, source_target_pairs={{16,24},{17,25},{18,26},{19,27},{20,28},{21,29},{22,30},{23,31}} | collective-permute-start | bytes 491528 | tf_op jit(solution)/shard_map/ppermute | solution.py:113
  42.7 15.4 %collective-permute-start.12 = (f32[11,2,32,128]{3,2,1,0:T(8,128)S(1)}, f32[11,2,32,128]{3,2,1,0:T(8,128)S(1)}, u32[]{:S(2)}, u32[]{:S(2)}) collective-permute-start(f32[11,2,32,128]{3,2,1,0:T(8,128)S(1)} %multiply_add_fusion.2), channel_id=1, source_target_pairs={{8,16},{9,17},{10,18},{11,19},{12,20},{13,21},{14,22},{15,23}} | collective-permute-start | bytes 1081352 | tf_op jit(solution)/shard_map/ppermute | solution.py:113
  43.5 35.1 %collective-permute-start.7 = (f32[7,2,32,128]{3,2,1,0:T(8,128)S(1)}, f32[7,2,32,128]{3,2,1,0:T(8,128)S(1)}, u32[]{:S(2)}, u32[]{:S(2)}) collective-permute-start(f32[7,2,32,128]{3,2,1,0:T(8,128)S(1)} %multiply_add_fusion.7), channel_id=1, source_target_pairs={{16,24},{17,25},{18,26},{19,27},{20,28},{21,29},{22,30},{23,31}} | collective-permute-start | bytes 688136 | tf_op jit(solution)/shard_map/ppermute | solution.py:113
  56.8 42.8 %copy-start.8 = (s32[1,8]{1,0:T(1,128)S(1)}, s32[1,8]{1,0:T(1,128)}, u32[]{:S(2)}) copy-start(s32[1,8]{1,0:T(1,128)} %param.23) | copy-start | bytes 100
  56.8 29.6 %collective-permute-start.10 = (f32[9,2,32,128]{3,2,1,0:T(8,128)S(1)}, f32[9,2,32,128]{3,2,1,0:T(8,128)S(1)}, u32[]{:S(2)}, u32[]{:S(2)}) collective-permute-start(f32[9,2,32,128]{3,2,1,0:T(8,128)S(1)} %multiply_add_fusion.4), channel_id=1, source_target_pairs={{16,24},{17,25},{18,26},{19,27},{20,28},{21,29},{22,30},{23,31}} | collective-permute-start | bytes 884744 | tf_op jit(solution)/shard_map/ppermute | solution.py:113
  58.3 37.3 %collective-permute-start.13 = (f32[11,2,32,128]{3,2,1,0:T(8,128)S(1)}, f32[11,2,32,128]{3,2,1,0:T(8,128)S(1)}, u32[]{:S(2)}, u32[]{:S(2)}) collective-permute-start(f32[11,2,32,128]{3,2,1,0:T(8,128)S(1)} %multiply_add_fusion.1), channel_id=1, source_target_pairs={{16,24},{17,25},{18,26},{19,27},{20,28},{21,29},{22,30},{23,31}} | collective-permute-start | bytes 1081352 | tf_op jit(solution)/shard_map/ppermute | solution.py:113
  95.6 3.8 %collective-permute-start.14 = (f32[1,34,64]{2,1,0:T(8,128)S(1)}, f32[1,34,64]{2,1,0:T(8,128)S(1)}, u32[]{:S(2)}, u32[]{:S(2)}) collective-permute-start(f32[1,34,64]{2,1,0:T(8,128)S(1)} %bitcast.122), channel_id=1, source_target_pairs={{0,8},{8,0},{16,24},{24,16},{1,9},{9,1},{17,25},{25,17},{2,10},{10... | collective-permute-start | bytes 26120 | tf_op jit(solution)/shard_map/ppermute | solution.py:121
  99.5 5.0 %collective-permute-start.15 = (f32[2,34,64]{2,1,0:T(8,128)S(1)}, f32[2,34,64]{2,1,0:T(8,128)S(1)}, u32[]{:S(2)}, u32[]{:S(2)}) collective-permute-start(f32[2,34,64]{2,1,0:T(8,128)S(1)} %maximum_select_fusion.2), channel_id=1, source_target_pairs={{0,16},{8,24},{16,0},{24,8},{1,17},{9,25},{17,1},{25,9},{2,18},{10... | collective-permute-start | bytes 52232 | tf_op jit(solution)/shard_map/ppermute | solution.py:121
  105.4 1.2 %collective-permute-start.16 = (f32[1,9,128]{2,1,0:T(8,128)S(1)}, f32[1,9,128]{2,1,0:T(8,128)S(1)}, u32[]{:S(2)}, u32[]{:S(2)}) collective-permute-start(f32[1,9,128]{2,1,0:T(8,128)S(1)} %fusion.42), channel_id=1, source_target_pairs={{0,1},{1,0},{2,3},{3,2},{4,5},{5,4},{6,7},{7,6},{8,9},{9,8},{10,11... | collective-permute-start | bytes 13832 | tf_op jit(solution)/shard_map/ppermute | solution.py:44
  106.7 3.7 %collective-permute-start.17 = (f32[2,9,128]{2,1,0:T(8,128)S(1)}, f32[2,9,128]{2,1,0:T(8,128)S(1)}, u32[]{:S(2)}, u32[]{:S(2)}) collective-permute-start(f32[2,9,128]{2,1,0:T(8,128)S(1)} %maximum_select_fusion.4), channel_id=1, source_target_pairs={{0,2},{1,3},{2,0},{3,1},{4,6},{5,7},{6,4},{7,5},{8,10},{9,11},{10,... | collective-permute-start | bytes 27656 | tf_op jit(solution)/shard_map/ppermute | solution.py:44
  110.4 3.9 %collective-permute-start.18 = (f32[4,9,128]{2,1,0:T(8,128)S(1)}, f32[4,9,128]{2,1,0:T(8,128)S(1)}, u32[]{:S(2)}, u32[]{:S(2)}) collective-permute-start(f32[4,9,128]{2,1,0:T(8,128)S(1)} %maximum_select_fusion.3), channel_id=1, source_target_pairs={{0,4},{1,5},{2,6},{3,7},{4,0},{5,1},{6,2},{7,3},{8,12},{9,13},{10,... | collective-permute-start | bytes 55304 | tf_op jit(solution)/shard_map/ppermute | solution.py:44

commit v13 on v7

--- a/solution.py
+++ b/solution.py
@@ -129,22 +129,27 @@
     lines, pixels = contribution.shape
     ids = jnp.zeros((1, pixels), jnp.float32).at[0, :lines].set(sky_blocks[0].astype(jnp.float32))
     payload = jnp.concatenate([contribution, ids], axis=0)
-    base = bins // CHUNKS
-    bounds = [0]
-    for c in range(CHUNKS):
-        bounds.append(bounds[-1] + base + 2 * c - (CHUNKS - 1))
-    bounds[-1] = bins
-    pieces = [own_part[bounds[c]:bounds[c + 1]] for c in range(CHUNKS)]
-    scales = [chain[bounds[c]:bounds[c + 1]][:, None, None, None] for c in range(CHUNKS)]
-    for wave in range(CHUNKS + groups - 2):
-        for c in range(CHUNKS):
-            s = wave - c
-            if 0 <= s < groups - 1:
-                arrived = lax.ppermute(pieces[c], "species", [(s, s + 1)])
-                if s == 0 and c == CHUNKS - 1:
-                    payload, arrived = lax.optimization_barrier((payload, arrived))
-                pieces[c] = pieces[c] + scales[c] * arrived
-    carried = jnp.concatenate(pieces, axis=0)
+    slabs = own_part.reshape((bins, own_part.shape[1], groups, -1) + own_part.shape[3:])
+    slabs = jnp.moveaxis(slabs, 2, 0)
+    me_s = lax.axis_index("species")
+    shifts = list(range(1, groups))
+    by_shift = [lax.dynamic_index_in_dim(slabs, me_s, 0, keepdims=False)]
+    for d in shifts:
+        outgoing = lax.dynamic_index_in_dim(slabs, (me_s + d) % groups, 0, keepdims=False)
+        by_shift.append(lax.ppermute(outgoing, "species", [(i, (i + d) % groups) for i in range(groups)]))
+    parts = jnp.take(jnp.stack(by_shift), (me_s - jnp.arange(groups)) % groups, axis=0)
+    running = parts[0]
+    results = [running]
+    for group in range(1, groups):
+        running = everyone[group, bins, :bins][:, None, None, None] * running + parts[group]
+        results.append(running)
+    results = jnp.stack(results)
+    back = [lax.dynamic_index_in_dim(results, me_s, 0, keepdims=False)]
+    for d in shifts:
+        outgoing = lax.dynamic_index_in_dim(results, (me_s + d) % groups, 0, keepdims=False)
+        back.append(lax.ppermute(outgoing, "species", [(i, (i + d) % groups) for i in range(groups)]))
+    mine_slabs = jnp.take(jnp.stack(back), (me_s - jnp.arange(groups)) % groups, axis=0)
+    carried = jnp.moveaxis(mine_slabs, 0, 2).reshape(own_part.shape)
     gathered = gather_all(payload, "space")
     mine = lax.axis_index("space") * rows + jnp.arange(rows, dtype=jnp.int32)
     onehot = (

time: 96.9 us -> 102 us (1.053)
  waiting for transfers between devices: 64.3 us -> 72.4 us
  starting transfers between devices: 17.2 us -> 12.9 us
  local copies, waits for them, and re-layouts: 1.6 us -> 2.79 us
    ppermute x12 -> x6, waiting for transfers between devices: 33 us -> 37.4 us  [body(): lax.ppermute(outgoing, 'species', [(i, (i + d) % groups) for i in range(g...]
    ppermute x12 -> x6, starting transfers between devices: 10.6 us -> 6.16 us  [body(): lax.ppermute(outgoing, 'species', [(i, (i + d) % groups) for i in range(g...]
    ppermute x2, waiting for transfers between devices: 5.24 us -> 8.73 us  [body(): lax.ppermute(everyone, 'species', [(i, i ^ span) for i in range(groups)])]
    another operation x2 -> x6, other arithmetic: 1.29 us -> 2.72 us
    gather x0 -> x2, local copies, waits for them, and re-layouts: none -> 1.24 us  [the longest x1 0.62 us: body(): jnp.take(jnp.stack(back), (me_s - jnp.arange(groups)) % groups, axis=0)]
    broadcast_in_dim x1, other arithmetic: 1.09 us -> 0.01 us  [gather_all(): held = block[None]]
  transfers between devices with their start and end apart: 19 -> 13, of which waited for: 11 -> 11; matrix products, arithmetic and copies ran while one was open for 5% -> 3% of each run, Pallas kernels for 0% -> 0%
where the time goes in v13:
time: 102 us; the launch traced here: 101 us
  waiting for transfers between devices  72.4 us (71%)
  starting transfers between devices  12.9 us (13%)
  other arithmetic  8.43 us (8%)
  matrix products  3.35 us (3%)
  local copies, waits for them, and re-layouts  2.79 us (3%)
  between operations  1.08 us (1%)
    ppermute x6, waiting for transfers between devices, body(): lax.ppermute(outgoing, 'species', [(i, (i + d) % groups) for i in range(g...  37.4 us
    ppermute x1, waiting for transfers between devices, body(): lax.ppermute(mine[:, :halo], 'space', [(i + 1, i) for i in range(count -...  10.5 us
    ppermute x1, waiting for transfers between devices, body(): lax.ppermute(mine[:, mine.shape[1] - halo:], 'space', [(i, i + 1) for i i...  9.37 us
    ppermute x2, waiting for transfers between devices, body(): lax.ppermute(everyone, 'species', [(i, i ^ span) for i in range(groups)])  8.73 us
    ppermute x3, waiting for transfers between devices, gather_all(): other = lax.ppermute(held, axis, [(i, i ^ span) for i in range(count)])  6.34 us
    ppermute x6, starting transfers between devices, body(): lax.ppermute(outgoing, 'species', [(i, (i + d) % groups) for i in range(g...  6.16 us
    ppermute x1, starting transfers between devices, body(): lax.ppermute(mine[:, :halo], 'space', [(i + 1, i) for i in range(count -...  3.64 us
    add x2, other arithmetic, body(): inner + wide_factor[:, 1 + step:wide_factor.shape[1] - 1 - step] * (besid...  2.71 us
  transfers between devices with their start and end apart: 13, of which 11 were waited for; matrix products, arithmetic and copies ran while one was open for 3% of the time, Pallas kernels for 0%

profile of v13, /device:TPU:26, one launch (start us, length us, event | category | flops | bytes accessed | tf_op | source)
XLA Modules:
  0.0 100.9 jit_solution(8703541579834156710)
XLA Ops:
  0.7 1.4 %pad_maximum_fusion.2 = f32[33,2,32,128]{3,2,1,0:T(8,128)S(1)} fusion(f32[1,2,32,128]{3,2,1,0:T(8,128)} %bitcast.145, f32[32,2,32,128]{3,2,1,0:T(8,128)} %bitcast.133), kind=kLoop, calls=%fused_computation.38 | loop fusion | flops 270336 | bytes 2162688 | tf_op jit(solution)/shard_map/concatenate | solution.py:77
  2.0 1.9 %collective-permute-start = (f32[33,2,32,128]{3,2,1,0:T(8,128)S(1)}, f32[33,2,32,128]{3,2,1,0:T(8,128)S(1)}, u32[]{:S(2)}, u32[]{:S(2)}) collective-permute-start(f32[33,2,32,128]{3,2,1,0:T(8,128)S(1)} %pad_maximum_fusion.2), channel_id=1, source_target_pairs={{0,1},{1,2},{2,3},{3,4},{4,5},{5,6},{6,7},{8,9},{9,10},{10,11},{11... | collective-permute-start | bytes 3244040 | tf_op jit(solution)/shard_map/ppermute | solution.py:78
  4.0 3.6 %collective-permute-start.1 = (f32[33,2,32,128]{3,2,1,0:T(8,128)S(1)}, f32[33,2,32,128]{3,2,1,0:T(8,128)S(1)}, u32[]{:S(2)}, u32[]{:S(2)}) collective-permute-start(f32[33,2,32,128]{3,2,1,0:T(8,128)S(1)} %pad_maximum_fusion.2), channel_id=1, source_target_pairs={{1,0},{2,1},{3,2},{4,3},{5,4},{6,5},{7,6},{9,8},{10,9},{11,10},{12... | collective-permute-start | bytes 3244040 | tf_op jit(solution)/shard_map/ppermute | solution.py:81
  7.8 0.6 compare_reduce_fusion
  8.5 0.6 broadcast_select_fusion.1
  9.1 9.4 %collective-permute-done = f32[33,2,32,128]{3,2,1,0:T(8,128)S(1)} collective-permute-done((f32[33,2,32,128]{3,2,1,0:T(8,128)S(1)}, f32[33,2,32,128]{3,2,1,0:T(8,128)S(1)}, u32[]{:S(2)}, u32[]{:S(2)}) %collective-permute-start) | collective-permute-done | bytes 1081376 | tf_op jit(solution)/shard_map/ppermute | solution.py:78
  18.6 10.5 %collective-permute-done.1 = f32[33,2,32,128]{3,2,1,0:T(8,128)S(1)} collective-permute-done((f32[33,2,32,128]{3,2,1,0:T(8,128)S(1)}, f32[33,2,32,128]{3,2,1,0:T(8,128)S(1)}, u32[]{:S(2)}, u32[]{:S(2)}) %collective-permute-start.1) | collective-permute-done | bytes 1081376 | tf_op jit(solution)/shard_map/ppermute | solution.py:81
  29.5 0.5 copy-done.2
  30.0 0.4 broadcast_multiply_fusion
  30.4 2.0 %fusion.6 = f32[32,4,32,128]{3,2,1,0:T(8,128)S(1)} fusion(f32[32,4,32,128]{3,2,1,0:T(8,128)S(1)} %pad_maximum_fusion, f32[32,6,32,128]{3,2,1,0:T(8,128)S(1)} %broadcast_multiply_fusion, f32[32,2,32,128]{3,2,1,0:T(8,128)S(1)} %slice.203, f32[32,2,32,128]{3,2,1,0:T(8,128)S(1)} %bitcast.135, f32[32,2,32,128]{3,2,1,0:T(8,128)S(1)} %slice.202), kind=kLoop, calls=%fused_computation.16 | loop fusion | flops 5767168 | bytes 9437184 | tf_op jit(solution)/shard_map/add | solution.py:87
  32.5 0.7 fusion.25
  33.2 1.7 %convolution_bitcast_fusion = f32[4,8,64,128]{3,1,2,0:T(8,128)S(1)} fusion(f32[4,8,64,128]{3,2,1,0:T(8,128)S(1)} %bitcast.137, f32[1,32,32]{2,1,0:T(8,128)S(1)} %copy-done.3), kind=kOutput, calls=%fused_computation.21 | convolution fusion | flops 100663296 | bytes 2101248 | tf_op jit(solution)/shard_map/dot_general | solution.py:89
  35.1 0.5 fusion.45
  35.7 0.5 collective-permute-start.2
  36.3 3.3 %collective-permute-done.2 = f32[1,34,64]{2,1,0:T(8,128)S(1)} collective-permute-done((f32[1,34,64]{2,1,0:T(8,128)S(1)}, f32[1,34,64]{2,1,0:T(8,128)S(1)}, u32[]{:S(2)}, u32[]{:S(2)}) %collective-permute-start.2) | collective-permute-done | bytes 8736 | tf_op jit(solution)/shard_map/ppermute | solution.py:106
  39.6 0.4 collective-permute-start.6
  40.0 5.4 %collective-permute-done.6 = f32[2,34,64]{2,1,0:T(8,128)S(1)} collective-permute-done((f32[2,34,64]{2,1,0:T(8,128)S(1)}, f32[2,34,64]{2,1,0:T(8,128)S(1)}, u32[]{:S(2)}, u32[]{:S(2)}) %collective-permute-start.6) | collective-permute-done | bytes 17440 | tf_op jit(solution)/shard_map/ppermute | solution.py:106
  46.6 1.0 %collective-permute-done.10 = f32[1,9,128]{2,1,0:T(8,128)S(1)} collective-permute-done((f32[1,9,128]{2,1,0:T(8,128)S(1)}, f32[1,9,128]{2,1,0:T(8,128)S(1)}, u32[]{:S(2)}, u32[]{:S(2)}) %collective-permute-start.10) | collective-permute-done | bytes 4640 | tf_op jit(solution)/shard_map/ppermute | solution.py:44
  47.9 1.2 %collective-permute-start.4 = (f32[32,2,8,128]{3,2,1,0:T(8,128)S(1)}, f32[32,2,8,128]{3,2,1,0:T(8,128)S(1)}, u32[]{:S(2)}, u32[]{:S(2)}) collective-permute-start(f32[32,2,8,128]{3,2,1,0:T(8,128)S(1)} %get-tuple-element.55), channel_id=1, source_target_pairs={{0,16},{8,24},{16,0},{24,8},{1,17},{9,25},{17,1},{25,9},{2,18},{10... | collective-permute-start | bytes 786440 | tf_op jit(solution)/shard_map/ppermute | solution.py:139
  49.1 0.8 collective-permute-start.5
  49.9 1.5 %collective-permute-done.11 = f32[2,9,128]{2,1,0:T(8,128)S(1)} collective-permute-done((f32[2,9,128]{2,1,0:T(8,128)S(1)}, f32[2,9,128]{2,1,0:T(8,128)S(1)}, u32[]{:S(2)}, u32[]{:S(2)}) %collective-permute-start.11) | collective-permute-done | bytes 9248 | tf_op jit(solution)/shard_map/ppermute | solution.py:44
  51.5 3.8 %collective-permute-done.12 = f32[4,9,128]{2,1,0:T(8,128)S(1)} collective-permute-done((f32[4,9,128]{2,1,0:T(8,128)S(1)}, f32[4,9,128]{2,1,0:T(8,128)S(1)}, u32[]{:S(2)}, u32[]{:S(2)}) %collective-permute-start.12) | collective-permute-done | bytes 18464 | tf_op jit(solution)/shard_map/ppermute | solution.py:44
  55.3 1.3 %collective-permute-done.3 = f32[32,2,8,128]{3,2,1,0:T(8,128)S(1)} collective-permute-done((f32[32,2,8,128]{3,2,1,0:T(8,128)S(1)}, f32[32,2,8,128]{3,2,1,0:T(8,128)S(1)}, u32[]{:S(2)}, u32[]{:S(2)}) %collective-permute-start.3) | collective-permute-done | bytes 262176 | tf_op jit(solution)/shard_map/ppermute | solution.py:139
  56.6 15.7 %collective-permute-done.4 = f32[32,2,8,128]{3,2,1,0:T(8,128)S(1)} collective-permute-done((f32[32,2,8,128]{3,2,1,0:T(8,128)S(1)}, f32[32,2,8,128]{3,2,1,0:T(8,128)S(1)}, u32[]{:S(2)}, u32[]{:S(2)}) %collective-permute-start.4) | collective-permute-done | bytes 262176 | tf_op jit(solution)/shard_map/ppermute | solution.py:139
  72.4 0.6 gather_fusion
  73.6 2.1 %collective-permute-start.8 = (f32[32,2,8,128]{3,2,1,0:T(8,128)S(1)}, f32[32,2,8,128]{3,2,1,0:T(8,128)S(1)}, u32[]{:S(2)}, u32[]{:S(2)}) collective-permute-start(f32[32,2,8,128]{3,2,1,0:T(8,128)S(1)} %get-tuple-element.50), channel_id=1, source_target_pairs={{0,16},{8,24},{16,0},{24,8},{1,17},{9,25},{17,1},{25,9},{2,18},{10... | collective-permute-start | bytes 786440 | tf_op jit(solution)/shard_map/ppermute | solution.py:150
  75.7 1.9 %collective-permute-start.9 = (f32[32,2,8,128]{3,2,1,0:T(8,128)S(1)}, f32[32,2,8,128]{3,2,1,0:T(8,128)S(1)}, u32[]{:S(2)}, u32[]{:S(2)}) collective-permute-start(f32[32,2,8,128]{3,2,1,0:T(8,128)S(1)} %get-tuple-element.49), channel_id=1, source_target_pairs={{0,24},{8,0},{16,8},{24,16},{1,25},{9,1},{17,9},{25,17},{2,26},{10... | collective-permute-start | bytes 786440 | tf_op jit(solution)/shard_map/ppermute | solution.py:150
  77.8 0.8 fusion.30
  78.6 2.6 %collective-permute-done.7 = f32[32,2,8,128]{3,2,1,0:T(8,128)S(1)} collective-permute-done((f32[32,2,8,128]{3,2,1,0:T(8,128)S(1)}, f32[32,2,8,128]{3,2,1,0:T(8,128)S(1)}, u32[]{:S(2)}, u32[]{:S(2)}) %collective-permute-start.7) | collective-permute-done | bytes 262176 | tf_op jit(solution)/shard_map/ppermute | solution.py:150
  81.2 17.8 %collective-permute-done.8 = f32[32,2,8,128]{3,2,1,0:T(8,128)S(1)} collective-permute-done((f32[32,2,8,128]{3,2,1,0:T(8,128)S(1)}, f32[32,2,8,128]{3,2,1,0:T(8,128)S(1)}, u32[]{:S(2)}, u32[]{:S(2)}) %collective-permute-start.8) | collective-permute-done | bytes 262176 | tf_op jit(solution)/shard_map/ppermute | solution.py:150
  99.1 0.6 gather_fusion.1
  99.7 1.2 %copy_bitcast_fusion = f32[1,32,2,32,128]{4,3,2,1,0:T(8,128)} fusion(f32[4,32,2,8,128]{4,3,2,1,0:T(8,128)S(1)} %gather_fusion.1, pred[4]{0:T(512)(128)(4,1)S(1)} %compare_and_fusion), kind=kLoop, calls=%fused_computation.52 | loop fusion | flops 262144 | bytes 2097156 | tf_op jit(solution)/shard_map/broadcast_in_dim;reshape | solution.py:165
  (62 shorter events, 3.2 us)
Async XLA Ops:
  0.6 45.6 %copy-start = (bf16[1,8,64,128]{3,2,1,0:T(8,128)(2,1)S(1)}, bf16[1,8,64,128]{3,2,1,0:T(8,128)(2,1)}, u32[]{:S(2)}) copy-start(bf16[1,8,64,128]{3,2,1,0:T(8,128)(2,1)} %param.24) | copy-start | bytes 393220
  0.6 7.0 %copy-start.5 = (f32[1,32]{1,0:T(1,128)S(1)}, f32[1,32]{1,0:T(1,128)}, u32[]{:S(2)}) copy-start(f32[1,32]{1,0:T(1,128)} %param.21) | copy-start | bytes 388
  0.7 7.0 %copy-start.6 = (f32[1,32]{1,0:T(1,128)S(1)}, f32[1,32]{1,0:T(1,128)}, u32[]{:S(2)}) copy-start(f32[1,32]{1,0:T(1,128)} %param.23) | copy-start | bytes 388
  0.7 7.8 %copy-start.8 = (s32[1,8]{1,0:T(1,128)S(1)}, s32[1,8]{1,0:T(1,128)}, u32[]{:S(2)}) copy-start(s32[1,8]{1,0:T(1,128)} %param.25) | copy-start | bytes 100
  2.0 16.5 %collective-permute-start = (f32[33,2,32,128]{3,2,1,0:T(8,128)S(1)}, f32[33,2,32,128]{3,2,1,0:T(8,128)S(1)}, u32[]{:S(2)}, u32[]{:S(2)}) collective-permute-start(f32[33,2,32,128]{3,2,1,0:T(8,128)S(1)} %pad_maximum_fusion.2), channel_id=1, source_target_pairs={{0,1},{1,2},{2,3},{3,4},{4,5},{5,6},{6,7},{8,9},{9,10},{10,11},{11... | collective-permute-start | bytes 3244040 | tf_op jit(solution)/shard_map/ppermute | solution.py:78
  4.0 25.1 %collective-permute-start.1 = (f32[33,2,32,128]{3,2,1,0:T(8,128)S(1)}, f32[33,2,32,128]{3,2,1,0:T(8,128)S(1)}, u32[]{:S(2)}, u32[]{:S(2)}) collective-permute-start(f32[33,2,32,128]{3,2,1,0:T(8,128)S(1)} %pad_maximum_fusion.2), channel_id=1, source_target_pairs={{1,0},{2,1},{3,2},{4,3},{5,4},{6,5},{7,6},{9,8},{10,9},{11,10},{12... | collective-permute-start | bytes 3244040 | tf_op jit(solution)/shard_map/ppermute | solution.py:81
  9.1 20.1 %copy-start.1 = (f32[1,32,2,32,128]{4,3,2,1,0:T(8,128)S(1)}, f32[1,32,2,32,128]{4,3,2,1,0:T(8,128)}, u32[]{:S(2)}) copy-start(f32[1,32,2,32,128]{4,3,2,1,0:T(8,128)} %param.17) | copy-start | bytes 3145732
  29.2 0.8 copy-start.2
  29.2 0.8 copy-start.7
  32.5 0.8 copy-start.3
  33.2 1.9 %copy-start.4 = (f32[1,32]{1,0:T(1,128)S(1)}, f32[1,32]{1,0:T(1,128)}, u32[]{:S(2)}) copy-start(f32[1,32]{1,0:T(1,128)} %param.22) | copy-start | bytes 388
  35.7 3.8 %collective-permute-start.2 = (f32[1,34,64]{2,1,0:T(8,128)S(1)}, f32[1,34,64]{2,1,0:T(8,128)S(1)}, u32[]{:S(2)}, u32[]{:S(2)}) collective-permute-start(f32[1,34,64]{2,1,0:T(8,128)S(1)} %maximum_bitcast_fusion), channel_id=1, source_target_pairs={{0,8},{8,0},{16,24},{24,16},{1,9},{9,1},{17,25},{25,17},{2,10},{10... | collective-permute-start | bytes 26120 | tf_op jit(solution)/shard_map/ppermute | solution.py:106
  39.6 5.8 %collective-permute-start.6 = (f32[2,34,64]{2,1,0:T(8,128)S(1)}, f32[2,34,64]{2,1,0:T(8,128)S(1)}, u32[]{:S(2)}, u32[]{:S(2)}) collective-permute-start(f32[2,34,64]{2,1,0:T(8,128)S(1)} %maximum_select_fusion.2), channel_id=1, source_target_pairs={{0,16},{8,24},{16,0},{24,8},{1,17},{9,25},{17,1},{25,9},{2,18},{10... | collective-permute-start | bytes 52232 | tf_op jit(solution)/shard_map/ppermute | solution.py:106
  46.4 1.2 %collective-permute-start.10 = (f32[1,9,128]{2,1,0:T(8,128)S(1)}, f32[1,9,128]{2,1,0:T(8,128)S(1)}, u32[]{:S(2)}, u32[]{:S(2)}) collective-permute-start(f32[1,9,128]{2,1,0:T(8,128)S(1)} %fusion.42), channel_id=1, source_target_pairs={{0,1},{1,0},{2,3},{3,2},{4,5},{5,4},{6,7},{7,6},{8,9},{9,8},{10,11... | collective-permute-start | bytes 13832 | tf_op jit(solution)/shard_map/ppermute | solution.py:44
  47.6 3.7 %collective-permute-start.11 = (f32[2,9,128]{2,1,0:T(8,128)S(1)}, f32[2,9,128]{2,1,0:T(8,128)S(1)}, u32[]{:S(2)}, u32[]{:S(2)}) collective-permute-start(f32[2,9,128]{2,1,0:T(8,128)S(1)} %maximum_select_fusion.4), channel_id=1, source_target_pairs={{0,2},{1,3},{2,0},{3,1},{4,6},{5,7},{6,4},{7,5},{8,10},{9,11},{10,... | collective-permute-start | bytes 27656 | tf_op jit(solution)/shard_map/ppermute | solution.py:44
  47.8 8.8 %collective-permute-start.3 = (f32[32,2,8,128]{3,2,1,0:T(8,128)S(1)}, f32[32,2,8,128]{3,2,1,0:T(8,128)S(1)}, u32[]{:S(2)}, u32[]{:S(2)}) collective-permute-start(f32[32,2,8,128]{3,2,1,0:T(8,128)S(1)} %get-tuple-element.56), channel_id=1, source_target_pairs={{0,8},{8,16},{16,24},{24,0},{1,9},{9,17},{17,25},{25,1},{2,10},{10... | collective-permute-start | bytes 786440 | tf_op jit(solution)/shard_map/ppermute | solution.py:139
  47.9 24.4 %collective-permute-start.4 = (f32[32,2,8,128]{3,2,1,0:T(8,128)S(1)}, f32[32,2,8,128]{3,2,1,0:T(8,128)S(1)}, u32[]{:S(2)}, u32[]{:S(2)}) collective-permute-start(f32[32,2,8,128]{3,2,1,0:T(8,128)S(1)} %get-tuple-element.55), channel_id=1, source_target_pairs={{0,16},{8,24},{16,0},{24,8},{1,17},{9,25},{17,1},{25,9},{2,18},{10... | collective-permute-start | bytes 786440 | tf_op jit(solution)/shard_map/ppermute | solution.py:139
  49.1 23.2 %collective-permute-start.5 = (f32[32,2,8,128]{3,2,1,0:T(8,128)S(1)}, f32[32,2,8,128]{3,2,1,0:T(8,128)S(1)}, u32[]{:S(2)}, u32[]{:S(2)}) collective-permute-start(f32[32,2,8,128]{3,2,1,0:T(8,128)S(1)} %get-tuple-element.54), channel_id=1, source_target_pairs={{0,24},{8,0},{16,8},{24,16},{1,25},{9,1},{17,9},{25,17},{2,26},{10... | collective-permute-start | bytes 786440 | tf_op jit(solution)/shard_map/ppermute | solution.py:139
  51.4 3.9 %collective-permute-start.12 = (f32[4,9,128]{2,1,0:T(8,128)S(1)}, f32[4,9,128]{2,1,0:T(8,128)S(1)}, u32[]{:S(2)}, u32[]{:S(2)}) collective-permute-start(f32[4,9,128]{2,1,0:T(8,128)S(1)} %maximum_select_fusion.3), channel_id=1, source_target_pairs={{0,4},{1,5},{2,6},{3,7},{4,0},{5,1},{6,2},{7,3},{8,12},{9,13},{10,... | collective-permute-start | bytes 55304 | tf_op jit(solution)/shard_map/ppermute | solution.py:44
  73.6 7.6 %collective-permute-start.7 = (f32[32,2,8,128]{3,2,1,0:T(8,128)S(1)}, f32[32,2,8,128]{3,2,1,0:T(8,128)S(1)}, u32[]{:S(2)}, u32[]{:S(2)}) collective-permute-start(f32[32,2,8,128]{3,2,1,0:T(8,128)S(1)} %get-tuple-element.51), channel_id=1, source_target_pairs={{0,8},{8,16},{16,24},{24,0},{1,9},{9,17},{17,25},{25,1},{2,10},{10... | collective-permute-start | bytes 786440 | tf_op jit(solution)/shard_map/ppermute | solution.py:150
  73.6 25.4 %collective-permute-start.8 = (f32[32,2,8,128]{3,2,1,0:T(8,128)S(1)}, f32[32,2,8,128]{3,2,1,0:T(8,128)S(1)}, u32[]{:S(2)}, u32[]{:S(2)}) collective-permute-start(f32[32,2,8,128]{3,2,1,0:T(8,128)S(1)} %get-tuple-element.50), channel_id=1, source_target_pairs={{0,16},{8,24},{16,0},{24,8},{1,17},{9,25},{17,1},{25,9},{2,18},{10... | collective-permute-start | bytes 786440 | tf_op jit(solution)/shard_map/ppermute | solution.py:150
  75.7 23.3 %collective-permute-start.9 = (f32[32,2,8,128]{3,2,1,0:T(8,128)S(1)}, f32[32,2,8,128]{3,2,1,0:T(8,128)S(1)}, u32[]{:S(2)}, u32[]{:S(2)}) collective-permute-start(f32[32,2,8,128]{3,2,1,0:T(8,128)S(1)} %get-tuple-element.49), channel_id=1, source_target_pairs={{0,24},{8,0},{16,8},{24,16},{1,25},{9,1},{17,9},{25,17},{2,26},{10... | collective-permute-start | bytes 786440 | tf_op jit(solution)/shard_map/ppermute | solution.py:150

commit v14 on v13

--- a/solution.py
+++ b/solution.py
@@ -67,6 +67,7 @@
     tiles = lax.axis_size("space")
     rows = NB // tiles
 
+    yields_all = gather_all(chain_yield[0], "species")
     field = density[0]
     bins = field.shape[0]
     depth = field.shape[3]
@@ -99,13 +100,21 @@
     cols = own_columns.shape[1]
     extra = jnp.zeros((2, cols), jnp.float32).at[0, :bins].set(chain).at[1, :bins].set(gamma_yield[0])
     packed = jnp.concatenate([own_columns, extra], axis=0)
+    slabs = own_part.reshape((bins, own_part.shape[1], groups, -1) + own_part.shape[3:])
+    slabs = jnp.moveaxis(slabs, 2, 0)
+    me_s = lax.axis_index("species")
+    shifts = list(range(1, groups))
+    by_shift = [lax.dynamic_index_in_dim(slabs, me_s, 0, keepdims=False)]
+    for d in shifts:
+        outgoing = lax.dynamic_index_in_dim(slabs, (me_s + d) % groups, 0, keepdims=False)
+        by_shift.append(lax.ppermute(outgoing, "species", [(i, (i + d) % groups) for i in range(groups)]))
+    packed, by_shift = lax.optimization_barrier((packed, by_shift))
+    parts = jnp.take(jnp.stack(by_shift), (me_s - jnp.arange(groups)) % groups, axis=0)
     me_g = lax.axis_index("species")
     everyone = packed[None]
     span = 1
     while span < groups:
         other = lax.ppermute(everyone, "species", [(i, i ^ span) for i in range(groups)])
-        if span == 1:
-            own_part, other = lax.optimization_barrier((own_part, other))
         low = (me_g & span) == 0
         everyone = jnp.where(
             low,
@@ -129,19 +138,10 @@
     lines, pixels = contribution.shape
     ids = jnp.zeros((1, pixels), jnp.float32).at[0, :lines].set(sky_blocks[0].astype(jnp.float32))
     payload = jnp.concatenate([contribution, ids], axis=0)
-    slabs = own_part.reshape((bins, own_part.shape[1], groups, -1) + own_part.shape[3:])
-    slabs = jnp.moveaxis(slabs, 2, 0)
-    me_s = lax.axis_index("species")
-    shifts = list(range(1, groups))
-    by_shift = [lax.dynamic_index_in_dim(slabs, me_s, 0, keepdims=False)]
-    for d in shifts:
-        outgoing = lax.dynamic_index_in_dim(slabs, (me_s + d) % groups, 0, keepdims=False)
-        by_shift.append(lax.ppermute(outgoing, "species", [(i, (i + d) % groups) for i in range(groups)]))
-    parts = jnp.take(jnp.stack(by_shift), (me_s - jnp.arange(groups)) % groups, axis=0)
     running = parts[0]
     results = [running]
     for group in range(1, groups):
-        running = everyone[group, bins, :bins][:, None, None, None] * running + parts[group]
+        running = yields_all[group][:, None, None, None] * running + parts[group]
         results.append(running)
     results = jnp.stack(results)
     back = [lax.dynamic_index_in_dim(results, me_s, 0, keepdims=False)]

time: 102 us -> 106 us (1.039)
  the two profiles are of different devices: /device:TPU:26 before, /device:TPU:0 now
where the time goes in v14:
time: 106 us
  starting transfers between devices  52.6 us (50%)
  waiting for transfers between devices  36.8 us (35%)
  other arithmetic  8.54 us (8%)
  local copies, waits for them, and re-layouts  3.76 us (4%)
  matrix products  3.35 us (3%)
    ppermute x6, waiting for transfers between devices, body(): lax.ppermute(outgoing, 'species', [(i, (i + d) % groups) for i in range(g...  28.1 us
    ppermute x5, starting transfers between devices, gather_all(): other = lax.ppermute(held, axis, [(i, i ^ span) for i in range(count)])  27.6 us
    ppermute x2, starting transfers between devices, body(): lax.ppermute(everyone, 'species', [(i, i ^ span) for i in range(groups)])  11 us
    ppermute x6, starting transfers between devices, body(): lax.ppermute(outgoing, 'species', [(i, (i + d) % groups) for i in range(g...  9.64 us
    ppermute x2, waiting for transfers between devices, body(): lax.ppermute(everyone, 'species', [(i, i ^ span) for i in range(groups)])  4.78 us
    ppermute x5, waiting for transfers between devices, gather_all(): other = lax.ppermute(held, axis, [(i, i ^ span) for i in range(count)])  3.87 us
    ppermute x1, starting transfers between devices, body(): lax.ppermute(mine[:, mine.shape[1] - halo:], 'space', [(i, i + 1) for i i...  3.1 us
    add x2, other arithmetic, body(): inner + wide_factor[:, 1 + step:wide_factor.shape[1] - 1 - step] * (besid...  2.71 us
  transfers between devices with their start and end apart: 15, of which 10 were waited for; matrix products, arithmetic and copies ran while one was open for 4% of the time, Pallas kernels for 0%

profile of v14, /device:TPU:0, one launch (start us, length us, event | category | flops | bytes accessed | tf_op | source)
XLA Modules:
  0.0 106.1 jit_solution(5710441533006442360)
XLA Ops:
  0.7 1.4 %pad_maximum_fusion.2 = f32[33,2,32,128]{3,2,1,0:T(8,128)S(1)} fusion(f32[1,2,32,128]{3,2,1,0:T(8,128)} %bitcast.154, f32[32,2,32,128]{3,2,1,0:T(8,128)} %bitcast.141), kind=kLoop, calls=%fused_computation.38 | loop fusion | flops 270336 | bytes 2162688 | tf_op jit(solution)/shard_map/concatenate | solution.py:78
  2.0 1.3 %collective-permute-start.1 = (f32[33,2,32,128]{3,2,1,0:T(8,128)S(1)}, f32[33,2,32,128]{3,2,1,0:T(8,128)S(1)}, u32[]{:S(2)}, u32[]{:S(2)}) collective-permute-start(f32[33,2,32,128]{3,2,1,0:T(8,128)S(1)} %pad_maximum_fusion.2), channel_id=1, source_target_pairs={{1,0},{2,1},{3,2},{4,3},{5,4},{6,5},{7,6},{9,8},{10,9},{11,10},{12... | collective-permute-start | bytes 3244040 | tf_op jit(solution)/shard_map/ppermute | solution.py:82
  3.3 3.1 %collective-permute-start = (f32[33,2,32,128]{3,2,1,0:T(8,128)S(1)}, f32[33,2,32,128]{3,2,1,0:T(8,128)S(1)}, u32[]{:S(2)}, u32[]{:S(2)}) collective-permute-start(f32[33,2,32,128]{3,2,1,0:T(8,128)S(1)} %pad_maximum_fusion.2), channel_id=1, source_target_pairs={{0,1},{1,2},{2,3},{3,4},{4,5},{5,6},{6,7},{8,9},{9,10},{10,11},{11... | collective-permute-start | bytes 3244040 | tf_op jit(solution)/shard_map/ppermute | solution.py:79
  6.5 3.1 %collective-permute-start.5 = (f32[1,32]{1,0:T(1,128)S(1)}, f32[1,32]{1,0:T(1,128)S(1)}, u32[]{:S(2)}, u32[]{:S(2)}) collective-permute-start(f32[1,32]{1,0:T(1,128)S(1)} %copy-done.5), channel_id=1, source_target_pairs={{0,8},{8,0},{16,24},{24,16},{1,9},{9,1},{17,25},{25,17},{2,10},{10... | collective-permute-start | bytes 392 | tf_op jit(solution)/shard_map/ppermute | solution.py:44
  9.5 0.6 compare_reduce_fusion
  10.3 0.7 broadcast_select_fusion.1
  11.1 3.1 %collective-permute-start.6 = (f32[2,32]{1,0:T(2,128)S(1)}, f32[2,32]{1,0:T(2,128)S(1)}, u32[]{:S(2)}, u32[]{:S(2)}) collective-permute-start(f32[2,32]{1,0:T(2,128)S(1)} %maximum_select_fusion.6), channel_id=1, source_target_pairs={{0,16},{8,24},{16,0},{24,8},{1,17},{9,25},{17,1},{25,9},{2,18},{10... | collective-permute-start | bytes 776 | tf_op jit(solution)/shard_map/ppermute | solution.py:44
  14.3 1.4 %collective-permute-done.6 = f32[2,32]{1,0:T(2,128)S(1)} collective-permute-done((f32[2,32]{1,0:T(2,128)S(1)}, f32[2,32]{1,0:T(2,128)S(1)}, u32[]{:S(2)}, u32[]{:S(2)}) %collective-permute-start.6) | collective-permute-done | bytes 288 | tf_op jit(solution)/shard_map/ppermute | solution.py:44
  15.9 1.0 copy-done.1
  18.2 2.0 %fusion.6 = f32[32,4,32,128]{3,2,1,0:T(8,128)S(1)} fusion(f32[32,4,32,128]{3,2,1,0:T(8,128)S(1)} %pad_maximum_fusion, f32[32,6,32,128]{3,2,1,0:T(8,128)S(1)} %broadcast_multiply_fusion, f32[32,2,32,128]{3,2,1,0:T(8,128)S(1)} %slice.212, f32[32,2,32,128]{3,2,1,0:T(8,128)S(1)} %bitcast.143, f32[32,2,32,128]{3,2,1,0:T(8,128)S(1)} %slice.211), kind=kLoop, calls=%fused_computation.16 | loop fusion | flops 5767168 | bytes 9437184 | tf_op jit(solution)/shard_map/add | solution.py:88
  20.3 0.7 fusion.25
  21.0 1.7 %convolution_bitcast_fusion = f32[4,8,64,128]{3,1,2,0:T(8,128)S(1)} fusion(f32[4,8,64,128]{3,2,1,0:T(8,128)S(1)} %bitcast.146, f32[1,32,32]{2,1,0:T(8,128)S(1)} %copy-done.3), kind=kOutput, calls=%fused_computation.21 | convolution fusion | flops 100663296 | bytes 2101248 | tf_op jit(solution)/shard_map/dot_general | solution.py:90
  23.2 2.0 %collective-permute-start.2 = (f32[32,2,8,128]{3,2,1,0:T(8,128)S(1)}, f32[32,2,8,128]{3,2,1,0:T(8,128)S(1)}, u32[]{:S(2)}, u32[]{:S(2)}) collective-permute-start(f32[32,2,8,128]{3,2,1,0:T(8,128)S(1)} %get-tuple-element.59), channel_id=1, source_target_pairs={{0,8},{8,16},{16,24},{24,0},{1,9},{9,17},{17,25},{25,1},{2,10},{10... | collective-permute-start | bytes 786440 | tf_op jit(solution)/shard_map/ppermute | solution.py:110
  25.2 2.6 %collective-permute-start.3 = (f32[32,2,8,128]{3,2,1,0:T(8,128)S(1)}, f32[32,2,8,128]{3,2,1,0:T(8,128)S(1)}, u32[]{:S(2)}, u32[]{:S(2)}) collective-permute-start(f32[32,2,8,128]{3,2,1,0:T(8,128)S(1)} %get-tuple-element.58), channel_id=1, source_target_pairs={{0,16},{8,24},{16,0},{24,8},{1,17},{9,25},{17,1},{25,9},{2,18},{10... | collective-permute-start | bytes 786440 | tf_op jit(solution)/shard_map/ppermute | solution.py:110
  27.8 1.3 %collective-permute-start.4 = (f32[32,2,8,128]{3,2,1,0:T(8,128)S(1)}, f32[32,2,8,128]{3,2,1,0:T(8,128)S(1)}, u32[]{:S(2)}, u32[]{:S(2)}) collective-permute-start(f32[32,2,8,128]{3,2,1,0:T(8,128)S(1)} %get-tuple-element.57), channel_id=1, source_target_pairs={{0,24},{8,0},{16,8},{24,16},{1,25},{9,1},{17,9},{25,17},{2,26},{10... | collective-permute-start | bytes 786440 | tf_op jit(solution)/shard_map/ppermute | solution.py:110
  29.7 2.0 %collective-permute-done.2 = f32[32,2,8,128]{3,2,1,0:T(8,128)S(1)} collective-permute-done((f32[32,2,8,128]{3,2,1,0:T(8,128)S(1)}, f32[32,2,8,128]{3,2,1,0:T(8,128)S(1)}, u32[]{:S(2)}, u32[]{:S(2)}) %collective-permute-start.2) | collective-permute-done | bytes 262176 | tf_op jit(solution)/shard_map/ppermute | solution.py:110
  31.7 5.5 %collective-permute-done.3 = f32[32,2,8,128]{3,2,1,0:T(8,128)S(1)} collective-permute-done((f32[32,2,8,128]{3,2,1,0:T(8,128)S(1)}, f32[32,2,8,128]{3,2,1,0:T(8,128)S(1)}, u32[]{:S(2)}, u32[]{:S(2)}) %collective-permute-start.3) | collective-permute-done | bytes 262176 | tf_op jit(solution)/shard_map/ppermute | solution.py:110
  37.2 9.9 %collective-permute-start.10 = (f32[1,34,64]{2,1,0:T(8,128)S(1)}, f32[1,34,64]{2,1,0:T(8,128)S(1)}, u32[]{:S(2)}, u32[]{:S(2)}) collective-permute-start(f32[1,34,64]{2,1,0:T(8,128)S(1)} %bitcast.155), channel_id=1, source_target_pairs={{0,8},{8,0},{16,24},{24,16},{1,9},{9,1},{17,25},{25,17},{2,10},{10... | collective-permute-start | bytes 26120 | tf_op jit(solution)/shard_map/ppermute | solution.py:117
  47.2 0.6 gather_fusion
  47.8 1.0 collective-permute-done.10
  48.9 1.1 %collective-permute-start.11 = (f32[2,34,64]{2,1,0:T(8,128)S(1)}, f32[2,34,64]{2,1,0:T(8,128)S(1)}, u32[]{:S(2)}, u32[]{:S(2)}) collective-permute-start(f32[2,34,64]{2,1,0:T(8,128)S(1)} %maximum_select_fusion.2), channel_id=1, source_target_pairs={{0,16},{8,24},{16,0},{24,8},{1,17},{9,25},{17,1},{25,9},{2,18},{10... | collective-permute-start | bytes 52232 | tf_op jit(solution)/shard_map/ppermute | solution.py:117
  50.1 3.7 %collective-permute-done.11 = f32[2,34,64]{2,1,0:T(8,128)S(1)} collective-permute-done((f32[2,34,64]{2,1,0:T(8,128)S(1)}, f32[2,34,64]{2,1,0:T(8,128)S(1)}, u32[]{:S(2)}, u32[]{:S(2)}) %collective-permute-start.11) | collective-permute-done | bytes 17440 | tf_op jit(solution)/shard_map/ppermute | solution.py:117
  54.8 2.5 %collective-permute-start.12 = (f32[1,9,128]{2,1,0:T(8,128)S(1)}, f32[1,9,128]{2,1,0:T(8,128)S(1)}, u32[]{:S(2)}, u32[]{:S(2)}) collective-permute-start(f32[1,9,128]{2,1,0:T(8,128)S(1)} %fusion.42), channel_id=1, source_target_pairs={{0,1},{1,0},{2,3},{3,2},{4,5},{5,4},{6,7},{7,6},{8,9},{9,8},{10,11... | collective-permute-start | bytes 13832 | tf_op jit(solution)/shard_map/ppermute | solution.py:44
  57.5 0.7 collective-permute-done.12
  58.2 12.9 %collective-permute-start.13 = (f32[2,9,128]{2,1,0:T(8,128)S(1)}, f32[2,9,128]{2,1,0:T(8,128)S(1)}, u32[]{:S(2)}, u32[]{:S(2)}) collective-permute-start(f32[2,9,128]{2,1,0:T(8,128)S(1)} %maximum_select_fusion.4), channel_id=1, source_target_pairs={{0,2},{1,3},{2,0},{3,1},{4,6},{5,7},{6,4},{7,5},{8,10},{9,11},{10,... | collective-permute-start | bytes 27656 | tf_op jit(solution)/shard_map/ppermute | solution.py:44
  71.2 1.6 %collective-permute-done.13 = f32[2,9,128]{2,1,0:T(8,128)S(1)} collective-permute-done((f32[2,9,128]{2,1,0:T(8,128)S(1)}, f32[2,9,128]{2,1,0:T(8,128)S(1)}, u32[]{:S(2)}, u32[]{:S(2)}) %collective-permute-start.13) | collective-permute-done | bytes 9248 | tf_op jit(solution)/shard_map/ppermute | solution.py:44
  72.9 5.9 %collective-permute-start.14 = (f32[4,9,128]{2,1,0:T(8,128)S(1)}, f32[4,9,128]{2,1,0:T(8,128)S(1)}, u32[]{:S(2)}, u32[]{:S(2)}) collective-permute-start(f32[4,9,128]{2,1,0:T(8,128)S(1)} %maximum_select_fusion.3), channel_id=1, source_target_pairs={{0,4},{1,5},{2,6},{3,7},{4,0},{5,1},{6,2},{7,3},{8,12},{9,13},{10,... | collective-permute-start | bytes 55304 | tf_op jit(solution)/shard_map/ppermute | solution.py:44
  78.9 3.1 %collective-permute-start.9 = (f32[32,2,8,128]{3,2,1,0:T(8,128)S(1)}, f32[32,2,8,128]{3,2,1,0:T(8,128)S(1)}, u32[]{:S(2)}, u32[]{:S(2)}) collective-permute-start(f32[32,2,8,128]{3,2,1,0:T(8,128)S(1)} %get-tuple-element.53), channel_id=1, source_target_pairs={{0,24},{8,0},{16,8},{24,16},{1,25},{9,1},{17,9},{25,17},{2,26},{10... | collective-permute-start | bytes 786440 | tf_op jit(solution)/shard_map/ppermute | solution.py:150
  82.7 0.8 fusion.30
  83.5 5.2 %collective-permute-done.9 = f32[32,2,8,128]{3,2,1,0:T(8,128)S(1)} collective-permute-done((f32[32,2,8,128]{3,2,1,0:T(8,128)S(1)}, f32[32,2,8,128]{3,2,1,0:T(8,128)S(1)}, u32[]{:S(2)}, u32[]{:S(2)}) %collective-permute-start.9) | collective-permute-done | bytes 262176 | tf_op jit(solution)/shard_map/ppermute | solution.py:150
  88.8 15.4 %collective-permute-done.8 = f32[32,2,8,128]{3,2,1,0:T(8,128)S(1)} collective-permute-done((f32[32,2,8,128]{3,2,1,0:T(8,128)S(1)}, f32[32,2,8,128]{3,2,1,0:T(8,128)S(1)}, u32[]{:S(2)}, u32[]{:S(2)}) %collective-permute-start.8) | collective-permute-done | bytes 262176 | tf_op jit(solution)/shard_map/ppermute | solution.py:150
  104.9 1.2 %copy_bitcast_fusion = f32[1,32,2,32,128]{4,3,2,1,0:T(8,128)} fusion(f32[4,32,2,8,128]{4,3,2,1,0:T(8,128)S(1)} %gather_fusion.1, pred[4]{0:T(512)(128)(4,1)S(1)} %compare_and_fusion), kind=kLoop, calls=%fused_computation.52 | loop fusion | flops 262144 | bytes 2097156 | tf_op jit(solution)/shard_map/broadcast_in_dim;reshape | solution.py:165
  (70 shorter events, 5.8 us)
Async XLA Ops:
  0.6 54.0 %copy-start = (bf16[1,8,64,128]{3,2,1,0:T(8,128)(2,1)S(1)}, bf16[1,8,64,128]{3,2,1,0:T(8,128)(2,1)}, u32[]{:S(2)}) copy-start(bf16[1,8,64,128]{3,2,1,0:T(8,128)(2,1)} %param.24) | copy-start | bytes 393220
  0.6 5.8 %copy-start.5 = (f32[1,32]{1,0:T(1,128)S(1)}, f32[1,32]{1,0:T(1,128)}, u32[]{:S(2)}) copy-start(f32[1,32]{1,0:T(1,128)} %param.21) | copy-start | bytes 388
  0.7 9.6 %copy-start.8 = (s32[1,8]{1,0:T(1,128)S(1)}, s32[1,8]{1,0:T(1,128)}, u32[]{:S(2)}) copy-start(s32[1,8]{1,0:T(1,128)} %param.25) | copy-start | bytes 100
  0.7 13.5 %copy-start.6 = (f32[1,32]{1,0:T(1,128)S(1)}, f32[1,32]{1,0:T(1,128)}, u32[]{:S(2)}) copy-start(f32[1,32]{1,0:T(1,128)} %param.23) | copy-start | bytes 388
  2.0 13.7 %collective-permute-start.1 = (f32[33,2,32,128]{3,2,1,0:T(8,128)S(1)}, f32[33,2,32,128]{3,2,1,0:T(8,128)S(1)}, u32[]{:S(2)}, u32[]{:S(2)}) collective-permute-start(f32[33,2,32,128]{3,2,1,0:T(8,128)S(1)} %pad_maximum_fusion.2), channel_id=1, source_target_pairs={{1,0},{2,1},{3,2},{4,3},{5,4},{6,5},{7,6},{9,8},{10,9},{11,10},{12... | collective-permute-start | bytes 3244040 | tf_op jit(solution)/shard_map/ppermute | solution.py:82
  3.3 12.5 %collective-permute-start = (f32[33,2,32,128]{3,2,1,0:T(8,128)S(1)}, f32[33,2,32,128]{3,2,1,0:T(8,128)S(1)}, u32[]{:S(2)}, u32[]{:S(2)}) collective-permute-start(f32[33,2,32,128]{3,2,1,0:T(8,128)S(1)} %pad_maximum_fusion.2), channel_id=1, source_target_pairs={{0,1},{1,2},{2,3},{3,4},{4,5},{5,6},{6,7},{8,9},{9,10},{10,11},{11... | collective-permute-start | bytes 3244040 | tf_op jit(solution)/shard_map/ppermute | solution.py:79
  6.5 4.6 %collective-permute-start.5 = (f32[1,32]{1,0:T(1,128)S(1)}, f32[1,32]{1,0:T(1,128)S(1)}, u32[]{:S(2)}, u32[]{:S(2)}) collective-permute-start(f32[1,32]{1,0:T(1,128)S(1)} %copy-done.5), channel_id=1, source_target_pairs={{0,8},{8,0},{16,24},{24,16},{1,9},{9,1},{17,25},{25,17},{2,10},{10... | collective-permute-start | bytes 392 | tf_op jit(solution)/shard_map/ppermute | solution.py:44
  11.1 4.6 %collective-permute-start.6 = (f32[2,32]{1,0:T(2,128)S(1)}, f32[2,32]{1,0:T(2,128)S(1)}, u32[]{:S(2)}, u32[]{:S(2)}) collective-permute-start(f32[2,32]{1,0:T(2,128)S(1)} %maximum_select_fusion.6), channel_id=1, source_target_pairs={{0,16},{8,24},{16,0},{24,8},{1,17},{9,25},{17,1},{25,9},{2,18},{10... | collective-permute-start | bytes 776 | tf_op jit(solution)/shard_map/ppermute | solution.py:44
  15.7 1.2 %copy-start.1 = (f32[1,32,2,32,128]{4,3,2,1,0:T(8,128)S(1)}, f32[1,32,2,32,128]{4,3,2,1,0:T(8,128)}, u32[]{:S(2)}) copy-start(f32[1,32,2,32,128]{4,3,2,1,0:T(8,128)} %param.17) | copy-start | bytes 3145732
  17.0 0.8 copy-start.2
  17.0 0.8 copy-start.7
  20.2 0.8 copy-start.3
  21.0 1.9 %copy-start.4 = (f32[1,32]{1,0:T(1,128)S(1)}, f32[1,32]{1,0:T(1,128)}, u32[]{:S(2)}) copy-start(f32[1,32]{1,0:T(1,128)} %param.22) | copy-start | bytes 388
  23.2 8.5 %collective-permute-start.2 = (f32[32,2,8,128]{3,2,1,0:T(8,128)S(1)}, f32[32,2,8,128]{3,2,1,0:T(8,128)S(1)}, u32[]{:S(2)}, u32[]{:S(2)}) collective-permute-start(f32[32,2,8,128]{3,2,1,0:T(8,128)S(1)} %get-tuple-element.59), channel_id=1, source_target_pairs={{0,8},{8,16},{16,24},{24,0},{1,9},{9,17},{17,25},{25,1},{2,10},{10... | collective-permute-start | bytes 786440 | tf_op jit(solution)/shard_map/ppermute | solution.py:110
  25.2 12.0 %collective-permute-start.3 = (f32[32,2,8,128]{3,2,1,0:T(8,128)S(1)}, f32[32,2,8,128]{3,2,1,0:T(8,128)S(1)}, u32[]{:S(2)}, u32[]{:S(2)}) collective-permute-start(f32[32,2,8,128]{3,2,1,0:T(8,128)S(1)} %get-tuple-element.58), channel_id=1, source_target_pairs={{0,16},{8,24},{16,0},{24,8},{1,17},{9,25},{17,1},{25,9},{2,18},{10... | collective-permute-start | bytes 786440 | tf_op jit(solution)/shard_map/ppermute | solution.py:110
  27.8 9.4 %collective-permute-start.4 = (f32[32,2,8,128]{3,2,1,0:T(8,128)S(1)}, f32[32,2,8,128]{3,2,1,0:T(8,128)S(1)}, u32[]{:S(2)}, u32[]{:S(2)}) collective-permute-start(f32[32,2,8,128]{3,2,1,0:T(8,128)S(1)} %get-tuple-element.57), channel_id=1, source_target_pairs={{0,24},{8,0},{16,8},{24,16},{1,25},{9,1},{17,9},{25,17},{2,26},{10... | collective-permute-start | bytes 786440 | tf_op jit(solution)/shard_map/ppermute | solution.py:110
  37.2 11.7 %collective-permute-start.10 = (f32[1,34,64]{2,1,0:T(8,128)S(1)}, f32[1,34,64]{2,1,0:T(8,128)S(1)}, u32[]{:S(2)}, u32[]{:S(2)}) collective-permute-start(f32[1,34,64]{2,1,0:T(8,128)S(1)} %bitcast.155), channel_id=1, source_target_pairs={{0,8},{8,0},{16,24},{24,16},{1,9},{9,1},{17,25},{25,17},{2,10},{10... | collective-permute-start | bytes 26120 | tf_op jit(solution)/shard_map/ppermute | solution.py:117
  48.9 5.0 %collective-permute-start.11 = (f32[2,34,64]{2,1,0:T(8,128)S(1)}, f32[2,34,64]{2,1,0:T(8,128)S(1)}, u32[]{:S(2)}, u32[]{:S(2)}) collective-permute-start(f32[2,34,64]{2,1,0:T(8,128)S(1)} %maximum_select_fusion.2), channel_id=1, source_target_pairs={{0,16},{8,24},{16,0},{24,8},{1,17},{9,25},{17,1},{25,9},{2,18},{10... | collective-permute-start | bytes 52232 | tf_op jit(solution)/shard_map/ppermute | solution.py:117
  54.8 3.4 %collective-permute-start.12 = (f32[1,9,128]{2,1,0:T(8,128)S(1)}, f32[1,9,128]{2,1,0:T(8,128)S(1)}, u32[]{:S(2)}, u32[]{:S(2)}) collective-permute-start(f32[1,9,128]{2,1,0:T(8,128)S(1)} %fusion.42), channel_id=1, source_target_pairs={{0,1},{1,0},{2,3},{3,2},{4,5},{5,4},{6,7},{7,6},{8,9},{9,8},{10,11... | collective-permute-start | bytes 13832 | tf_op jit(solution)/shard_map/ppermute | solution.py:44
  58.2 14.7 %collective-permute-start.13 = (f32[2,9,128]{2,1,0:T(8,128)S(1)}, f32[2,9,128]{2,1,0:T(8,128)S(1)}, u32[]{:S(2)}, u32[]{:S(2)}) collective-permute-start(f32[2,9,128]{2,1,0:T(8,128)S(1)} %maximum_select_fusion.4), channel_id=1, source_target_pairs={{0,2},{1,3},{2,0},{3,1},{4,6},{5,7},{6,4},{7,5},{8,10},{9,11},{10,... | collective-permute-start | bytes 27656 | tf_op jit(solution)/shard_map/ppermute | solution.py:44
  72.9 9.7 %collective-permute-start.14 = (f32[4,9,128]{2,1,0:T(8,128)S(1)}, f32[4,9,128]{2,1,0:T(8,128)S(1)}, u32[]{:S(2)}, u32[]{:S(2)}) collective-permute-start(f32[4,9,128]{2,1,0:T(8,128)S(1)} %maximum_select_fusion.3), channel_id=1, source_target_pairs={{0,4},{1,5},{2,6},{3,7},{4,0},{5,1},{6,2},{7,3},{8,12},{9,13},{10,... | collective-permute-start | bytes 55304 | tf_op jit(solution)/shard_map/ppermute | solution.py:44
  78.9 9.9 %collective-permute-start.9 = (f32[32,2,8,128]{3,2,1,0:T(8,128)S(1)}, f32[32,2,8,128]{3,2,1,0:T(8,128)S(1)}, u32[]{:S(2)}, u32[]{:S(2)}) collective-permute-start(f32[32,2,8,128]{3,2,1,0:T(8,128)S(1)} %get-tuple-element.53), channel_id=1, source_target_pairs={{0,24},{8,0},{16,8},{24,16},{1,25},{9,1},{17,9},{25,17},{2,26},{10... | collective-permute-start | bytes 786440 | tf_op jit(solution)/shard_map/ppermute | solution.py:150
  82.0 22.2 %collective-permute-start.8 = (f32[32,2,8,128]{3,2,1,0:T(8,128)S(1)}, f32[32,2,8,128]{3,2,1,0:T(8,128)S(1)}, u32[]{:S(2)}, u32[]{:S(2)}) collective-permute-start(f32[32,2,8,128]{3,2,1,0:T(8,128)S(1)} %get-tuple-element.54), channel_id=1, source_target_pairs={{0,16},{8,24},{16,0},{24,8},{1,17},{9,25},{17,1},{25,9},{2,18},{10... | collective-permute-start | bytes 786440 | tf_op jit(solution)/shard_map/ppermute | solution.py:150
  82.4 21.8 %collective-permute-start.7 = (f32[32,2,8,128]{3,2,1,0:T(8,128)S(1)}, f32[32,2,8,128]{3,2,1,0:T(8,128)S(1)}, u32[]{:S(2)}, u32[]{:S(2)}) collective-permute-start(f32[32,2,8,128]{3,2,1,0:T(8,128)S(1)} %get-tuple-element.55), channel_id=1, source_target_pairs={{0,8},{8,16},{16,24},{24,0},{1,9},{9,17},{17,25},{25,1},{2,10},{10... | collective-permute-start | bytes 786440 | tf_op jit(solution)/shard_map/ppermute | solution.py:150

commit v15 on v14

--- a/solution.py
+++ b/solution.py
@@ -104,24 +104,22 @@
     slabs = jnp.moveaxis(slabs, 2, 0)
     me_s = lax.axis_index("species")
     shifts = list(range(1, groups))
-    by_shift = [lax.dynamic_index_in_dim(slabs, me_s, 0, keepdims=False)]
+    flat_packed = packed.reshape(-1)
+    slab_shape = slabs.shape[1:]
+    slab_size = slabs[0].size
+
+    def message(index):
+        slab = lax.dynamic_index_in_dim(slabs, index, 0, keepdims=False)
+        return jnp.concatenate([slab.reshape(-1), flat_packed])
+
+    by_shift = [message(me_s)]
     for d in shifts:
-        outgoing = lax.dynamic_index_in_dim(slabs, (me_s + d) % groups, 0, keepdims=False)
-        by_shift.append(lax.ppermute(outgoing, "species", [(i, (i + d) % groups) for i in range(groups)]))
-    packed, by_shift = lax.optimization_barrier((packed, by_shift))
-    parts = jnp.take(jnp.stack(by_shift), (me_s - jnp.arange(groups)) % groups, axis=0)
-    me_g = lax.axis_index("species")
-    everyone = packed[None]
-    span = 1
-    while span < groups:
-        other = lax.ppermute(everyone, "species", [(i, i ^ span) for i in range(groups)])
-        low = (me_g & span) == 0
-        everyone = jnp.where(
-            low,
-            jnp.concatenate([everyone, other], axis=0),
-            jnp.concatenate([other, everyone], axis=0),
+        by_shift.append(
+            lax.ppermute(message((me_s + d) % groups), "species", [(i, (i + d) % groups) for i in range(groups)])
         )
-        span *= 2
+    landed = jnp.take(jnp.stack(by_shift), (me_s - jnp.arange(groups)) % groups, axis=0)
+    parts = landed[:, :slab_size].reshape((groups,) + slab_shape)
+    everyone = landed[:, slab_size:].reshape((groups,) + packed.shape)
     sums = everyone[0, :bins]
     total = jnp.zeros((cols,), jnp.float32)
     for group in range(groups):

time: 106 us -> 103 us (0.972)
  starting transfers between devices: 52.6 us -> 49.4 us
  waiting for transfers between devices: 36.8 us -> 34.3 us
  other arithmetic: 8.54 us -> 9.71 us
  local copies, waits for them, and re-layouts: 3.76 us -> 4.93 us
    ppermute x5, starting transfers between devices: 27.6 us -> 37.2 us  [gather_all(): other = lax.ppermute(held, axis, [(i, i ^ span) for i in range(count)])]
    ppermute x6 -> x3, waiting for transfers between devices: 28.1 us -> 19.1 us  [body(): lax.ppermute(outgoing, 'species', [(i, (i + d) % groups) for i in range(g...]
    ppermute x2 -> x3, waiting for transfers between devices: 4.78 us -> 12.9 us  [body(): lax.ppermute(message((me_s + d) % groups), 'species', [(i, (i + d) % grou...]
    ppermute x2 -> x3, starting transfers between devices: 11 us -> 3.1 us  [body(): lax.ppermute(message((me_s + d) % groups), 'species', [(i, (i + d) % grou...]
    ppermute x6 -> x3, starting transfers between devices: 9.64 us -> 4.67 us  [body(): lax.ppermute(outgoing, 'species', [(i, (i + d) % groups) for i in range(g...]
    ppermute x5, waiting for transfers between devices: 3.87 us -> 2.28 us  [gather_all(): other = lax.ppermute(held, axis, [(i, i ^ span) for i in range(count)])]
  transfers between devices with their start and end apart: 15 -> 13, of which waited for: 10 -> 6; matrix products, arithmetic and copies ran while one was open for 4% -> 10% of each run, Pallas kernels for 0% -> 0%
where the time goes in v15:
time: 103 us
  starting transfers between devices  49.4 us (48%)
  waiting for transfers between devices  34.3 us (33%)
  other arithmetic  9.71 us (9%)
  local copies, waits for them, and re-layouts  4.93 us (5%)
  matrix products  3.35 us (3%)
  between operations  1.11 us (1%)
    ppermute x5, starting transfers between devices, gather_all(): other = lax.ppermute(held, axis, [(i, i ^ span) for i in range(count)])  37.2 us
    ppermute x3, waiting for transfers between devices, body(): lax.ppermute(outgoing, 'species', [(i, (i + d) % groups) for i in range(g...  19.1 us
    ppermute x3, waiting for transfers between devices, body(): lax.ppermute(message((me_s + d) % groups), 'species', [(i, (i + d) % grou...  12.9 us
    ppermute x3, starting transfers between devices, body(): lax.ppermute(outgoing, 'species', [(i, (i + d) % groups) for i in range(g...  4.67 us
    ppermute x1, starting transfers between devices, body(): lax.ppermute(mine[:, mine.shape[1] - halo:], 'space', [(i, i + 1) for i i...  3.1 us
    ppermute x3, starting transfers between devices, body(): lax.ppermute(message((me_s + d) % groups), 'species', [(i, (i + d) % grou...  3.1 us
    add x2, other arithmetic, body(): inner + wide_factor[:, 1 + step:wide_factor.shape[1] - 1 - step] * (besid...  2.71 us
    ppermute x5, waiting for transfers between devices, gather_all(): other = lax.ppermute(held, axis, [(i, i ^ span) for i in range(count)])  2.28 us
  transfers between devices with their start and end apart: 13, of which 6 were waited for; matrix products, arithmetic and copies ran while one was open for 10% of the time, Pallas kernels for 0%

profile of v15, /device:TPU:0, one launch (start us, length us, event | category | flops | bytes accessed | tf_op | source)
XLA Modules:
  0.0 102.8 jit_solution(118463966282342025)
XLA Ops:
  0.7 1.4 %pad_maximum_fusion.3 = f32[33,2,32,128]{3,2,1,0:T(8,128)S(1)} fusion(f32[1,2,32,128]{3,2,1,0:T(8,128)} %bitcast.156, f32[32,2,32,128]{3,2,1,0:T(8,128)} %bitcast.138), kind=kLoop, calls=%fused_computation.39 | loop fusion | flops 270336 | bytes 2162688 | tf_op jit(solution)/shard_map/concatenate | solution.py:78
  2.0 1.3 %collective-permute-start.1 = (f32[33,2,32,128]{3,2,1,0:T(8,128)S(1)}, f32[33,2,32,128]{3,2,1,0:T(8,128)S(1)}, u32[]{:S(2)}, u32[]{:S(2)}) collective-permute-start(f32[33,2,32,128]{3,2,1,0:T(8,128)S(1)} %pad_maximum_fusion.3), channel_id=1, source_target_pairs={{1,0},{2,1},{3,2},{4,3},{5,4},{6,5},{7,6},{9,8},{10,9},{11,10},{12... | collective-permute-start | bytes 3244040 | tf_op jit(solution)/shard_map/ppermute | solution.py:82
  3.3 3.1 %collective-permute-start = (f32[33,2,32,128]{3,2,1,0:T(8,128)S(1)}, f32[33,2,32,128]{3,2,1,0:T(8,128)S(1)}, u32[]{:S(2)}, u32[]{:S(2)}) collective-permute-start(f32[33,2,32,128]{3,2,1,0:T(8,128)S(1)} %pad_maximum_fusion.3), channel_id=1, source_target_pairs={{0,1},{1,2},{2,3},{3,4},{4,5},{5,6},{6,7},{8,9},{9,10},{10,11},{11... | collective-permute-start | bytes 3244040 | tf_op jit(solution)/shard_map/ppermute | solution.py:79
  6.5 3.1 %collective-permute-start.5 = (f32[1,32]{1,0:T(1,128)S(1)}, f32[1,32]{1,0:T(1,128)S(1)}, u32[]{:S(2)}, u32[]{:S(2)}) collective-permute-start(f32[1,32]{1,0:T(1,128)S(1)} %copy-done.5), channel_id=1, source_target_pairs={{0,8},{8,0},{16,24},{24,16},{1,9},{9,1},{17,25},{25,17},{2,10},{10... | collective-permute-start | bytes 392 | tf_op jit(solution)/shard_map/ppermute | solution.py:44
  9.7 0.6 compare_reduce_fusion
  10.4 0.7 broadcast_select_fusion.1
  11.1 3.1 %collective-permute-start.6 = (f32[2,32]{1,0:T(2,128)S(1)}, f32[2,32]{1,0:T(2,128)S(1)}, u32[]{:S(2)}, u32[]{:S(2)}) collective-permute-start(f32[2,32]{1,0:T(2,128)S(1)} %maximum_select_fusion.4), channel_id=1, source_target_pairs={{0,16},{8,24},{16,0},{24,8},{1,17},{9,25},{17,1},{25,9},{2,18},{10... | collective-permute-start | bytes 776 | tf_op jit(solution)/shard_map/ppermute | solution.py:44
  14.6 0.5 copy-done.2
  15.1 0.4 broadcast_multiply_fusion
  15.6 2.0 %fusion.6 = f32[32,4,32,128]{3,2,1,0:T(8,128)S(1)} fusion(f32[32,4,32,128]{3,2,1,0:T(8,128)S(1)} %pad_maximum_fusion, f32[32,6,32,128]{3,2,1,0:T(8,128)S(1)} %broadcast_multiply_fusion, f32[32,2,32,128]{3,2,1,0:T(8,128)S(1)} %slice.228, f32[32,2,32,128]{3,2,1,0:T(8,128)S(1)} %bitcast.140, f32[32,2,32,128]{3,2,1,0:T(8,128)S(1)} %slice.227), kind=kLoop, calls=%fused_computation.16 | loop fusion | flops 5767168 | bytes 9437184 | tf_op jit(solution)/shard_map/add | solution.py:88
  17.6 0.7 fusion.25
  18.4 1.7 %convolution_bitcast_fusion = f32[4,8,64,128]{3,1,2,0:T(8,128)S(1)} fusion(f32[4,8,64,128]{3,2,1,0:T(8,128)S(1)} %bitcast.143, f32[1,32,32]{2,1,0:T(8,128)S(1)} %copy-done.3), kind=kOutput, calls=%fused_computation.21 | convolution fusion | flops 100663296 | bytes 2101248 | tf_op jit(solution)/shard_map/dot_general | solution.py:90
  20.3 0.5 multiply_reduce_fusion
  21.3 2.0 %collective-permute-start.4 = (f32[67712]{0:T(1024)S(1)}, f32[67712]{0:T(1024)S(1)}, u32[]{:S(2)}, u32[]{:S(2)}) collective-permute-start(f32[67712]{0:T(1024)S(1)} %get-tuple-element.59), channel_id=1, source_target_pairs={{0,24},{8,0},{16,8},{24,16},{1,25},{9,1},{17,9},{25,17},{2,26},{10... | collective-permute-start | bytes 812552 | tf_op jit(solution)/shard_map/ppermute | solution.py:118
  23.4 1.1 %collective-permute-start.3 = (f32[67712]{0:T(1024)S(1)}, f32[67712]{0:T(1024)S(1)}, u32[]{:S(2)}, u32[]{:S(2)}) collective-permute-start(f32[67712]{0:T(1024)S(1)} %get-tuple-element.58), channel_id=1, source_target_pairs={{0,16},{8,24},{16,0},{24,8},{1,17},{9,25},{17,1},{25,9},{2,18},{10... | collective-permute-start | bytes 812552 | tf_op jit(solution)/shard_map/ppermute | solution.py:118
  24.7 3.2 %collective-permute-done.4 = f32[67712]{0:T(1024)S(1)} collective-permute-done((f32[67712]{0:T(1024)S(1)}, f32[67712]{0:T(1024)S(1)}, u32[]{:S(2)}, u32[]{:S(2)}) %collective-permute-start.4) | collective-permute-done | bytes 270880 | tf_op jit(solution)/shard_map/ppermute | solution.py:118
  28.1 9.6 %collective-permute-done.3 = f32[67712]{0:T(1024)S(1)} collective-permute-done((f32[67712]{0:T(1024)S(1)}, f32[67712]{0:T(1024)S(1)}, u32[]{:S(2)}, u32[]{:S(2)}) %collective-permute-start.3) | collective-permute-done | bytes 270880 | tf_op jit(solution)/shard_map/ppermute | solution.py:118
  38.1 1.0 pad_maximum_fusion.2
  39.2 1.1 %gather_fusion = f32[4,67712]{1,0:T(4,128)S(1)} fusion(f32[4,67712]{1,0:T(4,128)S(1)} %pad_maximum_fusion.2, s32[1024]{0:T(1024)S(1)} %pad_clamp_fusion), kind=kCustom, calls=%fused_computation | custom fusion | bytes 2166800 | tf_op jit(solution)/shard_map/jit(_take)/gather | solution.py:120
  40.6 0.8 fusion.47
  42.4 12.9 %collective-permute-start.10 = (f32[1,9,128]{2,1,0:T(8,128)S(1)}, f32[1,9,128]{2,1,0:T(8,128)S(1)}, u32[]{:S(2)}, u32[]{:S(2)}) collective-permute-start(f32[1,9,128]{2,1,0:T(8,128)S(1)} %fusion.42), channel_id=1, source_target_pairs={{0,1},{1,0},{2,3},{3,2},{4,5},{5,4},{6,7},{7,6},{8,9},{9,8},{10,11... | collective-permute-start | bytes 13832 | tf_op jit(solution)/shard_map/ppermute | solution.py:44
  55.5 0.7 collective-permute-done.10
  56.2 12.3 %collective-permute-start.11 = (f32[2,9,128]{2,1,0:T(8,128)S(1)}, f32[2,9,128]{2,1,0:T(8,128)S(1)}, u32[]{:S(2)}, u32[]{:S(2)}) collective-permute-start(f32[2,9,128]{2,1,0:T(8,128)S(1)} %maximum_select_fusion.2), channel_id=1, source_target_pairs={{0,2},{1,3},{2,0},{3,1},{4,6},{5,7},{6,4},{7,5},{8,10},{9,11},{10,... | collective-permute-start | bytes 27656 | tf_op jit(solution)/shard_map/ppermute | solution.py:44
  68.6 1.6 %collective-permute-done.11 = f32[2,9,128]{2,1,0:T(8,128)S(1)} collective-permute-done((f32[2,9,128]{2,1,0:T(8,128)S(1)}, f32[2,9,128]{2,1,0:T(8,128)S(1)}, u32[]{:S(2)}, u32[]{:S(2)}) %collective-permute-start.11) | collective-permute-done | bytes 9248 | tf_op jit(solution)/shard_map/ppermute | solution.py:44
  70.2 5.8 %collective-permute-start.12 = (f32[4,9,128]{2,1,0:T(8,128)S(1)}, f32[4,9,128]{2,1,0:T(8,128)S(1)}, u32[]{:S(2)}, u32[]{:S(2)}) collective-permute-start(f32[4,9,128]{2,1,0:T(8,128)S(1)} %maximum_select_fusion.1), channel_id=1, source_target_pairs={{0,4},{1,5},{2,6},{3,7},{4,0},{5,1},{6,2},{7,3},{8,12},{9,13},{10,... | collective-permute-start | bytes 55304 | tf_op jit(solution)/shard_map/ppermute | solution.py:44
  76.2 2.7 %collective-permute-start.8 = (f32[32,2,8,128]{3,2,1,0:T(8,128)S(1)}, f32[32,2,8,128]{3,2,1,0:T(8,128)S(1)}, u32[]{:S(2)}, u32[]{:S(2)}) collective-permute-start(f32[32,2,8,128]{3,2,1,0:T(8,128)S(1)} %get-tuple-element.47), channel_id=1, source_target_pairs={{0,16},{8,24},{16,0},{24,8},{1,17},{9,25},{17,1},{25,9},{2,18},{10... | collective-permute-start | bytes 786440 | tf_op jit(solution)/shard_map/ppermute | solution.py:148
  78.9 1.9 %collective-permute-start.7 = (f32[32,2,8,128]{3,2,1,0:T(8,128)S(1)}, f32[32,2,8,128]{3,2,1,0:T(8,128)S(1)}, u32[]{:S(2)}, u32[]{:S(2)}) collective-permute-start(f32[32,2,8,128]{3,2,1,0:T(8,128)S(1)} %get-tuple-element.48), channel_id=1, source_target_pairs={{0,8},{8,16},{16,24},{24,0},{1,9},{9,17},{17,25},{25,1},{2,10},{10... | collective-permute-start | bytes 786440 | tf_op jit(solution)/shard_map/ppermute | solution.py:148
  81.0 0.8 fusion.30
  81.8 2.1 %collective-permute-done.9 = f32[32,2,8,128]{3,2,1,0:T(8,128)S(1)} collective-permute-done((f32[32,2,8,128]{3,2,1,0:T(8,128)S(1)}, f32[32,2,8,128]{3,2,1,0:T(8,128)S(1)}, u32[]{:S(2)}, u32[]{:S(2)}) %collective-permute-start.9) | collective-permute-done | bytes 262176 | tf_op jit(solution)/shard_map/ppermute | solution.py:148
  83.8 17.0 %collective-permute-done.8 = f32[32,2,8,128]{3,2,1,0:T(8,128)S(1)} collective-permute-done((f32[32,2,8,128]{3,2,1,0:T(8,128)S(1)}, f32[32,2,8,128]{3,2,1,0:T(8,128)S(1)}, u32[]{:S(2)}, u32[]{:S(2)}) %collective-permute-start.8) | collective-permute-done | bytes 262176 | tf_op jit(solution)/shard_map/ppermute | solution.py:148
  101.0 0.6 gather_fusion.1
  101.6 1.2 %copy_bitcast_fusion = f32[1,32,2,32,128]{4,3,2,1,0:T(8,128)} fusion(f32[4,32,2,8,128]{4,3,2,1,0:T(8,128)S(1)} %gather_fusion.1, pred[4]{0:T(512)(128)(4,1)S(1)} %compare_and_fusion), kind=kLoop, calls=%fused_computation.52 | loop fusion | flops 262144 | bytes 2097156 | tf_op jit(solution)/shard_map/broadcast_in_dim;reshape | solution.py:163
  (73 shorter events, 4.1 us)
Async XLA Ops:
  0.6 41.6 %copy-start = (bf16[1,8,64,128]{3,2,1,0:T(8,128)(2,1)S(1)}, bf16[1,8,64,128]{3,2,1,0:T(8,128)(2,1)}, u32[]{:S(2)}) copy-start(bf16[1,8,64,128]{3,2,1,0:T(8,128)(2,1)} %param.22) | copy-start | bytes 393220
  0.6 5.8 %copy-start.5 = (f32[1,32]{1,0:T(1,128)S(1)}, f32[1,32]{1,0:T(1,128)}, u32[]{:S(2)}) copy-start(f32[1,32]{1,0:T(1,128)} %param.19) | copy-start | bytes 388
  0.7 8.9 %copy-start.6 = (f32[1,32]{1,0:T(1,128)S(1)}, f32[1,32]{1,0:T(1,128)}, u32[]{:S(2)}) copy-start(f32[1,32]{1,0:T(1,128)} %param.21) | copy-start | bytes 388
  0.7 9.7 %copy-start.8 = (s32[1,8]{1,0:T(1,128)S(1)}, s32[1,8]{1,0:T(1,128)}, u32[]{:S(2)}) copy-start(s32[1,8]{1,0:T(1,128)} %param.23) | copy-start | bytes 100
  2.0 12.2 %collective-permute-start.1 = (f32[33,2,32,128]{3,2,1,0:T(8,128)S(1)}, f32[33,2,32,128]{3,2,1,0:T(8,128)S(1)}, u32[]{:S(2)}, u32[]{:S(2)}) collective-permute-start(f32[33,2,32,128]{3,2,1,0:T(8,128)S(1)} %pad_maximum_fusion.3), channel_id=1, source_target_pairs={{1,0},{2,1},{3,2},{4,3},{5,4},{6,5},{7,6},{9,8},{10,9},{11,10},{12... | collective-permute-start | bytes 3244040 | tf_op jit(solution)/shard_map/ppermute | solution.py:82
  3.3 10.9 %collective-permute-start = (f32[33,2,32,128]{3,2,1,0:T(8,128)S(1)}, f32[33,2,32,128]{3,2,1,0:T(8,128)S(1)}, u32[]{:S(2)}, u32[]{:S(2)}) collective-permute-start(f32[33,2,32,128]{3,2,1,0:T(8,128)S(1)} %pad_maximum_fusion.3), channel_id=1, source_target_pairs={{0,1},{1,2},{2,3},{3,4},{4,5},{5,6},{6,7},{8,9},{9,10},{10,11},{11... | collective-permute-start | bytes 3244040 | tf_op jit(solution)/shard_map/ppermute | solution.py:79
  6.5 4.6 %collective-permute-start.5 = (f32[1,32]{1,0:T(1,128)S(1)}, f32[1,32]{1,0:T(1,128)S(1)}, u32[]{:S(2)}, u32[]{:S(2)}) collective-permute-start(f32[1,32]{1,0:T(1,128)S(1)} %copy-done.5), channel_id=1, source_target_pairs={{0,8},{8,0},{16,24},{24,16},{1,9},{9,1},{17,25},{25,17},{2,10},{10... | collective-permute-start | bytes 392 | tf_op jit(solution)/shard_map/ppermute | solution.py:44
  11.1 3.2 %copy-start.1 = (f32[1,32,2,32,128]{4,3,2,1,0:T(8,128)S(1)}, f32[1,32,2,32,128]{4,3,2,1,0:T(8,128)}, u32[]{:S(2)}) copy-start(f32[1,32,2,32,128]{4,3,2,1,0:T(8,128)} %param.15) | copy-start | bytes 3145732
  11.1 13.3 %collective-permute-start.6 = (f32[2,32]{1,0:T(2,128)S(1)}, f32[2,32]{1,0:T(2,128)S(1)}, u32[]{:S(2)}, u32[]{:S(2)}) collective-permute-start(f32[2,32]{1,0:T(2,128)S(1)} %maximum_select_fusion.4), channel_id=1, source_target_pairs={{0,16},{8,24},{16,0},{24,8},{1,17},{9,25},{17,1},{25,9},{2,18},{10... | collective-permute-start | bytes 776 | tf_op jit(solution)/shard_map/ppermute | solution.py:44
  14.4 0.8 copy-start.2
  14.4 0.8 copy-start.7
  17.6 0.8 copy-start.3
  18.4 1.9 %copy-start.4 = (f32[1,32]{1,0:T(1,128)S(1)}, f32[1,32]{1,0:T(1,128)}, u32[]{:S(2)}) copy-start(f32[1,32]{1,0:T(1,128)} %param.20) | copy-start | bytes 388
  21.3 6.6 %collective-permute-start.4 = (f32[67712]{0:T(1024)S(1)}, f32[67712]{0:T(1024)S(1)}, u32[]{:S(2)}, u32[]{:S(2)}) collective-permute-start(f32[67712]{0:T(1024)S(1)} %get-tuple-element.59), channel_id=1, source_target_pairs={{0,24},{8,0},{16,8},{24,16},{1,25},{9,1},{17,9},{25,17},{2,26},{10... | collective-permute-start | bytes 812552 | tf_op jit(solution)/shard_map/ppermute | solution.py:118
  23.4 14.4 %collective-permute-start.3 = (f32[67712]{0:T(1024)S(1)}, f32[67712]{0:T(1024)S(1)}, u32[]{:S(2)}, u32[]{:S(2)}) collective-permute-start(f32[67712]{0:T(1024)S(1)} %get-tuple-element.58), channel_id=1, source_target_pairs={{0,16},{8,24},{16,0},{24,8},{1,17},{9,25},{17,1},{25,9},{2,18},{10... | collective-permute-start | bytes 812552 | tf_op jit(solution)/shard_map/ppermute | solution.py:118
  24.4 13.5 %collective-permute-start.2 = (f32[67712]{0:T(1024)S(1)}, f32[67712]{0:T(1024)S(1)}, u32[]{:S(2)}, u32[]{:S(2)}) collective-permute-start(f32[67712]{0:T(1024)S(1)} %get-tuple-element.57), channel_id=1, source_target_pairs={{0,8},{8,16},{16,24},{24,0},{1,9},{9,17},{17,25},{25,1},{2,10},{10... | collective-permute-start | bytes 812552 | tf_op jit(solution)/shard_map/ppermute | solution.py:118
  42.4 13.8 %collective-permute-start.10 = (f32[1,9,128]{2,1,0:T(8,128)S(1)}, f32[1,9,128]{2,1,0:T(8,128)S(1)}, u32[]{:S(2)}, u32[]{:S(2)}) collective-permute-start(f32[1,9,128]{2,1,0:T(8,128)S(1)} %fusion.42), channel_id=1, source_target_pairs={{0,1},{1,0},{2,3},{3,2},{4,5},{5,4},{6,7},{7,6},{8,9},{9,8},{10,11... | collective-permute-start | bytes 13832 | tf_op jit(solution)/shard_map/ppermute | solution.py:44
  56.2 14.1 %collective-permute-start.11 = (f32[2,9,128]{2,1,0:T(8,128)S(1)}, f32[2,9,128]{2,1,0:T(8,128)S(1)}, u32[]{:S(2)}, u32[]{:S(2)}) collective-permute-start(f32[2,9,128]{2,1,0:T(8,128)S(1)} %maximum_select_fusion.2), channel_id=1, source_target_pairs={{0,2},{1,3},{2,0},{3,1},{4,6},{5,7},{6,4},{7,5},{8,10},{9,11},{10,... | collective-permute-start | bytes 27656 | tf_op jit(solution)/shard_map/ppermute | solution.py:44
  70.2 10.6 %collective-permute-start.12 = (f32[4,9,128]{2,1,0:T(8,128)S(1)}, f32[4,9,128]{2,1,0:T(8,128)S(1)}, u32[]{:S(2)}, u32[]{:S(2)}) collective-permute-start(f32[4,9,128]{2,1,0:T(8,128)S(1)} %maximum_select_fusion.1), channel_id=1, source_target_pairs={{0,4},{1,5},{2,6},{3,7},{4,0},{5,1},{6,2},{7,3},{8,12},{9,13},{10,... | collective-permute-start | bytes 55304 | tf_op jit(solution)/shard_map/ppermute | solution.py:44
  76.2 7.7 %collective-permute-start.9 = (f32[32,2,8,128]{3,2,1,0:T(8,128)S(1)}, f32[32,2,8,128]{3,2,1,0:T(8,128)S(1)}, u32[]{:S(2)}, u32[]{:S(2)}) collective-permute-start(f32[32,2,8,128]{3,2,1,0:T(8,128)S(1)} %get-tuple-element.46), channel_id=1, source_target_pairs={{0,24},{8,0},{16,8},{24,16},{1,25},{9,1},{17,9},{25,17},{2,26},{10... | collective-permute-start | bytes 786440 | tf_op jit(solution)/shard_map/ppermute | solution.py:148
  76.2 24.6 %collective-permute-start.8 = (f32[32,2,8,128]{3,2,1,0:T(8,128)S(1)}, f32[32,2,8,128]{3,2,1,0:T(8,128)S(1)}, u32[]{:S(2)}, u32[]{:S(2)}) collective-permute-start(f32[32,2,8,128]{3,2,1,0:T(8,128)S(1)} %get-tuple-element.47), channel_id=1, source_target_pairs={{0,16},{8,24},{16,0},{24,8},{1,17},{9,25},{17,1},{25,9},{2,18},{10... | collective-permute-start | bytes 786440 | tf_op jit(solution)/shard_map/ppermute | solution.py:148
  78.9 22.0 %collective-permute-start.7 = (f32[32,2,8,128]{3,2,1,0:T(8,128)S(1)}, f32[32,2,8,128]{3,2,1,0:T(8,128)S(1)}, u32[]{:S(2)}, u32[]{:S(2)}) collective-permute-start(f32[32,2,8,128]{3,2,1,0:T(8,128)S(1)} %get-tuple-element.48), channel_id=1, source_target_pairs={{0,8},{8,16},{16,24},{24,0},{1,9},{9,17},{17,25},{25,1},{2,10},{10... | collective-permute-start | bytes 786440 | tf_op jit(solution)/shard_map/ppermute | solution.py:148

commit v16 on v15

--- a/solution.py
+++ b/solution.py
@@ -146,6 +146,7 @@
     for d in shifts:
         outgoing = lax.dynamic_index_in_dim(results, (me_s + d) % groups, 0, keepdims=False)
         back.append(lax.ppermute(outgoing, "species", [(i, (i + d) % groups) for i in range(groups)]))
+    payload, back = lax.optimization_barrier((payload, back))
     mine_slabs = jnp.take(jnp.stack(back), (me_s - jnp.arange(groups)) % groups, axis=0)
     carried = jnp.moveaxis(mine_slabs, 0, 2).reshape(own_part.shape)
     gathered = gather_all(payload, "space")

time: 103 us -> 102 us (level)
  the two profiles are of different devices: /device:TPU:0 before, /device:TPU:28 now
where the time goes in v16:
time: 102 us
  waiting for transfers between devices  66.7 us (65%)
  starting transfers between devices  16.4 us (16%)
  other arithmetic  9.72 us (10%)
  local copies, waits for them, and re-layouts  4.93 us (5%)
  matrix products  3.34 us (3%)
  between operations  1.09 us (1%)
    ppermute x3, waiting for transfers between devices, body(): lax.ppermute(outgoing, 'species', [(i, (i + d) % groups) for i in range(g...  21.9 us
    ppermute x3, waiting for transfers between devices, body(): lax.ppermute(message((me_s + d) % groups), 'species', [(i, (i + d) % grou...  17.1 us
    ppermute x1, waiting for transfers between devices, body(): lax.ppermute(mine[:, :halo], 'space', [(i + 1, i) for i in range(count -...  16.2 us
    ppermute x5, waiting for transfers between devices, gather_all(): other = lax.ppermute(held, axis, [(i, i ^ span) for i in range(count)])  8.47 us
    ppermute x3, starting transfers between devices, body(): lax.ppermute(outgoing, 'species', [(i, (i + d) % groups) for i in range(g...  6.87 us
    ppermute x3, starting transfers between devices, body(): lax.ppermute(message((me_s + d) % groups), 'species', [(i, (i + d) % grou...  3.88 us
    ppermute x1, waiting for transfers between devices, body(): lax.ppermute(mine[:, mine.shape[1] - halo:], 'space', [(i, i + 1) for i i...  3 us
    ppermute x1, starting transfers between devices, body(): lax.ppermute(mine[:, :halo], 'space', [(i + 1, i) for i in range(count -...  2.78 us
  transfers between devices with their start and end apart: 13, of which 10 were waited for; matrix products, arithmetic and copies ran while one was open for 10% of the time, Pallas kernels for 0%

profile of v16, /device:TPU:28, one launch (start us, length us, event | category | flops | bytes accessed | tf_op | source)
XLA Modules:
  0.0 102.2 jit_solution(16920889568588923503)
XLA Ops:
  0.7 1.4 %pad_maximum_fusion.3 = f32[33,2,32,128]{3,2,1,0:T(8,128)S(1)} fusion(f32[1,2,32,128]{3,2,1,0:T(8,128)} %bitcast.159, f32[32,2,32,128]{3,2,1,0:T(8,128)} %bitcast.140), kind=kLoop, calls=%fused_computation.39 | loop fusion | flops 270336 | bytes 2162688 | tf_op jit(solution)/shard_map/concatenate | solution.py:78
  2.0 2.8 %collective-permute-start.1 = (f32[33,2,32,128]{3,2,1,0:T(8,128)S(1)}, f32[33,2,32,128]{3,2,1,0:T(8,128)S(1)}, u32[]{:S(2)}, u32[]{:S(2)}) collective-permute-start(f32[33,2,32,128]{3,2,1,0:T(8,128)S(1)} %pad_maximum_fusion.3), channel_id=1, source_target_pairs={{1,0},{2,1},{3,2},{4,3},{5,4},{6,5},{7,6},{9,8},{10,9},{11,10},{12... | collective-permute-start | bytes 3244040 | tf_op jit(solution)/shard_map/ppermute | solution.py:82
  4.8 1.9 %collective-permute-start = (f32[33,2,32,128]{3,2,1,0:T(8,128)S(1)}, f32[33,2,32,128]{3,2,1,0:T(8,128)S(1)}, u32[]{:S(2)}, u32[]{:S(2)}) collective-permute-start(f32[33,2,32,128]{3,2,1,0:T(8,128)S(1)} %pad_maximum_fusion.3), channel_id=1, source_target_pairs={{0,1},{1,2},{2,3},{3,4},{4,5},{5,6},{6,7},{8,9},{9,10},{10,11},{11... | collective-permute-start | bytes 3244040 | tf_op jit(solution)/shard_map/ppermute | solution.py:79
  6.8 0.5 collective-permute-start.5
  7.4 0.6 compare_reduce_fusion
  8.1 0.7 broadcast_select_fusion.1
  8.8 1.6 %collective-permute-done.5 = f32[1,32]{1,0:T(1,128)S(1)} collective-permute-done((f32[1,32]{1,0:T(1,128)S(1)}, f32[1,32]{1,0:T(1,128)S(1)}, u32[]{:S(2)}, u32[]{:S(2)}) %collective-permute-start.5) | collective-permute-done | bytes 160 | tf_op jit(solution)/shard_map/ppermute | solution.py:44
  10.8 16.2 %collective-permute-done.1 = f32[33,2,32,128]{3,2,1,0:T(8,128)S(1)} collective-permute-done((f32[33,2,32,128]{3,2,1,0:T(8,128)S(1)}, f32[33,2,32,128]{3,2,1,0:T(8,128)S(1)}, u32[]{:S(2)}, u32[]{:S(2)}) %collective-permute-start.1) | collective-permute-done | bytes 1081376 | tf_op jit(solution)/shard_map/ppermute | solution.py:82
  27.1 3.0 %collective-permute-done = f32[33,2,32,128]{3,2,1,0:T(8,128)S(1)} collective-permute-done((f32[33,2,32,128]{3,2,1,0:T(8,128)S(1)}, f32[33,2,32,128]{3,2,1,0:T(8,128)S(1)}, u32[]{:S(2)}, u32[]{:S(2)}) %collective-permute-start) | collective-permute-done | bytes 1081376 | tf_op jit(solution)/shard_map/ppermute | solution.py:79
  30.4 0.5 copy-done.2
  30.9 0.4 broadcast_multiply_fusion
  31.4 2.0 %fusion.6 = f32[32,4,32,128]{3,2,1,0:T(8,128)S(1)} fusion(f32[32,4,32,128]{3,2,1,0:T(8,128)S(1)} %pad_maximum_fusion, f32[32,6,32,128]{3,2,1,0:T(8,128)S(1)} %broadcast_multiply_fusion, f32[32,2,32,128]{3,2,1,0:T(8,128)S(1)} %slice.228, f32[32,2,32,128]{3,2,1,0:T(8,128)S(1)} %bitcast.142, f32[32,2,32,128]{3,2,1,0:T(8,128)S(1)} %slice.227), kind=kLoop, calls=%fused_computation.16 | loop fusion | flops 5767168 | bytes 9437184 | tf_op jit(solution)/shard_map/add | solution.py:88
  33.5 0.7 fusion.25
  34.2 1.7 %convolution_bitcast_fusion = f32[4,8,64,128]{3,1,2,0:T(8,128)S(1)} fusion(f32[4,8,64,128]{3,2,1,0:T(8,128)S(1)} %bitcast.145, f32[1,32,32]{2,1,0:T(8,128)S(1)} %copy-done.3), kind=kOutput, calls=%fused_computation.21 | convolution fusion | flops 100663296 | bytes 2101248 | tf_op jit(solution)/shard_map/dot_general | solution.py:90
  36.1 0.5 multiply_reduce_fusion
  37.1 0.5 collective-permute-start.4
  38.0 3.0 %collective-permute-start.2 = (f32[67712]{0:T(1024)S(1)}, f32[67712]{0:T(1024)S(1)}, u32[]{:S(2)}, u32[]{:S(2)}) collective-permute-start(f32[67712]{0:T(1024)S(1)} %get-tuple-element.67), channel_id=1, source_target_pairs={{0,8},{8,16},{16,24},{24,0},{1,9},{9,17},{17,25},{25,1},{2,10},{10... | collective-permute-start | bytes 812552 | tf_op jit(solution)/shard_map/ppermute | solution.py:118
  41.2 7.4 %collective-permute-done.4 = f32[67712]{0:T(1024)S(1)} collective-permute-done((f32[67712]{0:T(1024)S(1)}, f32[67712]{0:T(1024)S(1)}, u32[]{:S(2)}, u32[]{:S(2)}) %collective-permute-start.4) | collective-permute-done | bytes 270880 | tf_op jit(solution)/shard_map/ppermute | solution.py:118
  48.8 9.7 %collective-permute-done.3 = f32[67712]{0:T(1024)S(1)} collective-permute-done((f32[67712]{0:T(1024)S(1)}, f32[67712]{0:T(1024)S(1)}, u32[]{:S(2)}, u32[]{:S(2)}) %collective-permute-start.3) | collective-permute-done | bytes 270880 | tf_op jit(solution)/shard_map/ppermute | solution.py:118
  58.9 1.0 %pad_maximum_fusion.2 = f32[4,67712]{1,0:T(4,128)S(1)} fusion(f32[1,67712]{1,0:T(1,128)S(1)} %stack.39, f32[1,67712]{1,0:T(1,128)S(1)} %stack.38, f32[1,67712]{1,0:T(1,128)S(1)} %stack.37, f32[1,67712]{1,0:T(1,128)S(1)} %stack.36), kind=kLoop, calls=%fused_computation.38 | loop fusion | flops 812544 | bytes 2166784 | tf_op jit(solution)/shard_map/stack | solution.py:120
  60.0 1.1 %gather_fusion = f32[4,67712]{1,0:T(4,128)S(1)} fusion(f32[4,67712]{1,0:T(4,128)S(1)} %pad_maximum_fusion.2, s32[1024]{0:T(1024)S(1)} %pad_clamp_fusion), kind=kCustom, calls=%fused_computation | custom fusion | bytes 2166800 | tf_op jit(solution)/shard_map/jit(_take)/gather | solution.py:120
  61.4 0.8 fusion.46
  63.3 5.2 %collective-permute-start.7 = (f32[32,2,8,128]{3,2,1,0:T(8,128)S(1)}, f32[32,2,8,128]{3,2,1,0:T(8,128)S(1)}, u32[]{:S(2)}, u32[]{:S(2)}) collective-permute-start(f32[32,2,8,128]{3,2,1,0:T(8,128)S(1)} %get-tuple-element.57), channel_id=1, source_target_pairs={{0,8},{8,16},{16,24},{24,0},{1,9},{9,17},{17,25},{25,1},{2,10},{10... | collective-permute-start | bytes 786440 | tf_op jit(solution)/shard_map/ppermute | solution.py:148
  68.4 1.7 %collective-permute-start.8 = (f32[32,2,8,128]{3,2,1,0:T(8,128)S(1)}, f32[32,2,8,128]{3,2,1,0:T(8,128)S(1)}, u32[]{:S(2)}, u32[]{:S(2)}) collective-permute-start(f32[32,2,8,128]{3,2,1,0:T(8,128)S(1)} %get-tuple-element.56), channel_id=1, source_target_pairs={{0,16},{8,24},{16,0},{24,8},{1,17},{9,25},{17,1},{25,9},{2,18},{10... | collective-permute-start | bytes 786440 | tf_op jit(solution)/shard_map/ppermute | solution.py:148
  70.5 4.7 %collective-permute-done.7 = f32[32,2,8,128]{3,2,1,0:T(8,128)S(1)} collective-permute-done((f32[32,2,8,128]{3,2,1,0:T(8,128)S(1)}, f32[32,2,8,128]{3,2,1,0:T(8,128)S(1)}, u32[]{:S(2)}, u32[]{:S(2)}) %collective-permute-start.7) | collective-permute-done | bytes 262176 | tf_op jit(solution)/shard_map/ppermute | solution.py:148
  75.2 17.2 %collective-permute-done.8 = f32[32,2,8,128]{3,2,1,0:T(8,128)S(1)} collective-permute-done((f32[32,2,8,128]{3,2,1,0:T(8,128)S(1)}, f32[32,2,8,128]{3,2,1,0:T(8,128)S(1)}, u32[]{:S(2)}, u32[]{:S(2)}) %collective-permute-start.8) | collective-permute-done | bytes 262176 | tf_op jit(solution)/shard_map/ppermute | solution.py:148
  92.4 1.2 %collective-permute-done.10 = f32[1,9,128]{2,1,0:T(8,128)S(1)} collective-permute-done((f32[1,9,128]{2,1,0:T(8,128)S(1)}, f32[1,9,128]{2,1,0:T(8,128)S(1)}, u32[]{:S(2)}, u32[]{:S(2)}) %collective-permute-start.10) | collective-permute-done | bytes 4640 | tf_op jit(solution)/shard_map/ppermute | solution.py:44
  93.7 0.6 gather_fusion.1
  94.3 3.0 %collective-permute-done.11 = f32[2,9,128]{2,1,0:T(8,128)S(1)} collective-permute-done((f32[2,9,128]{2,1,0:T(8,128)S(1)}, f32[2,9,128]{2,1,0:T(8,128)S(1)}, u32[]{:S(2)}, u32[]{:S(2)}) %collective-permute-start.11) | collective-permute-done | bytes 9248 | tf_op jit(solution)/shard_map/ppermute | solution.py:44
  97.3 1.2 %copy_bitcast_fusion = f32[1,32,2,32,128]{4,3,2,1,0:T(8,128)} fusion(f32[4,32,2,8,128]{4,3,2,1,0:T(8,128)S(1)} %gather_fusion.1, pred[4]{0:T(512)(128)(4,1)S(1)} %compare_and_fusion), kind=kLoop, calls=%fused_computation.52 | loop fusion | flops 262144 | bytes 2097156 | tf_op jit(solution)/shard_map/broadcast_in_dim;reshape | solution.py:164
  98.5 2.7 %collective-permute-done.12 = f32[4,9,128]{2,1,0:T(8,128)S(1)} collective-permute-done((f32[4,9,128]{2,1,0:T(8,128)S(1)}, f32[4,9,128]{2,1,0:T(8,128)S(1)}, u32[]{:S(2)}, u32[]{:S(2)}) %collective-permute-start.12) | collective-permute-done | bytes 18464 | tf_op jit(solution)/shard_map/ppermute | solution.py:44
  101.4 0.8 fusion.30
  (73 shorter events, 4.8 us)
Async XLA Ops:
  0.6 69.6 %copy-start = (bf16[1,8,64,128]{3,2,1,0:T(8,128)(2,1)S(1)}, bf16[1,8,64,128]{3,2,1,0:T(8,128)(2,1)}, u32[]{:S(2)}) copy-start(bf16[1,8,64,128]{3,2,1,0:T(8,128)(2,1)} %param.22) | copy-start | bytes 393220
  0.6 6.1 %copy-start.5 = (f32[1,32]{1,0:T(1,128)S(1)}, f32[1,32]{1,0:T(1,128)}, u32[]{:S(2)}) copy-start(f32[1,32]{1,0:T(1,128)} %param.19) | copy-start | bytes 388
  0.7 6.6 %copy-start.6 = (f32[1,32]{1,0:T(1,128)S(1)}, f32[1,32]{1,0:T(1,128)}, u32[]{:S(2)}) copy-start(f32[1,32]{1,0:T(1,128)} %param.21) | copy-start | bytes 388
  0.7 7.5 %copy-start.8 = (s32[1,8]{1,0:T(1,128)S(1)}, s32[1,8]{1,0:T(1,128)}, u32[]{:S(2)}) copy-start(s32[1,8]{1,0:T(1,128)} %param.23) | copy-start | bytes 100
  2.0 25.0 %collective-permute-start.1 = (f32[33,2,32,128]{3,2,1,0:T(8,128)S(1)}, f32[33,2,32,128]{3,2,1,0:T(8,128)S(1)}, u32[]{:S(2)}, u32[]{:S(2)}) collective-permute-start(f32[33,2,32,128]{3,2,1,0:T(8,128)S(1)} %pad_maximum_fusion.3), channel_id=1, source_target_pairs={{1,0},{2,1},{3,2},{4,3},{5,4},{6,5},{7,6},{9,8},{10,9},{11,10},{12... | collective-permute-start | bytes 3244040 | tf_op jit(solution)/shard_map/ppermute | solution.py:82
  4.8 25.3 %collective-permute-start = (f32[33,2,32,128]{3,2,1,0:T(8,128)S(1)}, f32[33,2,32,128]{3,2,1,0:T(8,128)S(1)}, u32[]{:S(2)}, u32[]{:S(2)}) collective-permute-start(f32[33,2,32,128]{3,2,1,0:T(8,128)S(1)} %pad_maximum_fusion.3), channel_id=1, source_target_pairs={{0,1},{1,2},{2,3},{3,4},{4,5},{5,6},{6,7},{8,9},{9,10},{10,11},{11... | collective-permute-start | bytes 3244040 | tf_op jit(solution)/shard_map/ppermute | solution.py:79
  6.8 3.6 %collective-permute-start.5 = (f32[1,32]{1,0:T(1,128)S(1)}, f32[1,32]{1,0:T(1,128)S(1)}, u32[]{:S(2)}, u32[]{:S(2)}) collective-permute-start(f32[1,32]{1,0:T(1,128)S(1)} %copy-done.5), channel_id=1, source_target_pairs={{0,8},{8,0},{16,24},{24,16},{1,9},{9,1},{17,25},{25,17},{2,10},{10... | collective-permute-start | bytes 392 | tf_op jit(solution)/shard_map/ppermute | solution.py:44
  10.4 19.8 %copy-start.1 = (f32[1,32,2,32,128]{4,3,2,1,0:T(8,128)S(1)}, f32[1,32,2,32,128]{4,3,2,1,0:T(8,128)}, u32[]{:S(2)}) copy-start(f32[1,32,2,32,128]{4,3,2,1,0:T(8,128)} %param.15) | copy-start | bytes 3145732
  10.4 30.6 %collective-permute-start.6 = (f32[2,32]{1,0:T(2,128)S(1)}, f32[2,32]{1,0:T(2,128)S(1)}, u32[]{:S(2)}, u32[]{:S(2)}) collective-permute-start(f32[2,32]{1,0:T(2,128)S(1)} %maximum_select_fusion.4), channel_id=1, source_target_pairs={{0,16},{8,24},{16,0},{24,8},{1,17},{9,25},{17,1},{25,9},{2,18},{10... | collective-permute-start | bytes 776 | tf_op jit(solution)/shard_map/ppermute | solution.py:44
  30.2 0.8 copy-start.2
  30.2 0.8 copy-start.7
  33.4 0.8 copy-start.3
  34.2 1.9 %copy-start.4 = (f32[1,32]{1,0:T(1,128)S(1)}, f32[1,32]{1,0:T(1,128)}, u32[]{:S(2)}) copy-start(f32[1,32]{1,0:T(1,128)} %param.20) | copy-start | bytes 388
  37.1 11.5 %collective-permute-start.4 = (f32[67712]{0:T(1024)S(1)}, f32[67712]{0:T(1024)S(1)}, u32[]{:S(2)}, u32[]{:S(2)}) collective-permute-start(f32[67712]{0:T(1024)S(1)} %get-tuple-element.69), channel_id=1, source_target_pairs={{0,24},{8,0},{16,8},{24,16},{1,25},{9,1},{17,9},{25,17},{2,26},{10... | collective-permute-start | bytes 812552 | tf_op jit(solution)/shard_map/ppermute | solution.py:118
  37.6 20.9 %collective-permute-start.3 = (f32[67712]{0:T(1024)S(1)}, f32[67712]{0:T(1024)S(1)}, u32[]{:S(2)}, u32[]{:S(2)}) collective-permute-start(f32[67712]{0:T(1024)S(1)} %get-tuple-element.68), channel_id=1, source_target_pairs={{0,16},{8,24},{16,0},{24,8},{1,17},{9,25},{17,1},{25,9},{2,18},{10... | collective-permute-start | bytes 812552 | tf_op jit(solution)/shard_map/ppermute | solution.py:118
  38.0 20.7 %collective-permute-start.2 = (f32[67712]{0:T(1024)S(1)}, f32[67712]{0:T(1024)S(1)}, u32[]{:S(2)}, u32[]{:S(2)}) collective-permute-start(f32[67712]{0:T(1024)S(1)} %get-tuple-element.67), channel_id=1, source_target_pairs={{0,8},{8,16},{16,24},{24,0},{1,9},{9,17},{17,25},{25,1},{2,10},{10... | collective-permute-start | bytes 812552 | tf_op jit(solution)/shard_map/ppermute | solution.py:118
  63.3 11.9 %collective-permute-start.7 = (f32[32,2,8,128]{3,2,1,0:T(8,128)S(1)}, f32[32,2,8,128]{3,2,1,0:T(8,128)S(1)}, u32[]{:S(2)}, u32[]{:S(2)}) collective-permute-start(f32[32,2,8,128]{3,2,1,0:T(8,128)S(1)} %get-tuple-element.57), channel_id=1, source_target_pairs={{0,8},{8,16},{16,24},{24,0},{1,9},{9,17},{17,25},{25,1},{2,10},{10... | collective-permute-start | bytes 786440 | tf_op jit(solution)/shard_map/ppermute | solution.py:148
  68.4 24.0 %collective-permute-start.8 = (f32[32,2,8,128]{3,2,1,0:T(8,128)S(1)}, f32[32,2,8,128]{3,2,1,0:T(8,128)S(1)}, u32[]{:S(2)}, u32[]{:S(2)}) collective-permute-start(f32[32,2,8,128]{3,2,1,0:T(8,128)S(1)} %get-tuple-element.56), channel_id=1, source_target_pairs={{0,16},{8,24},{16,0},{24,8},{1,17},{9,25},{17,1},{25,9},{2,18},{10... | collective-permute-start | bytes 786440 | tf_op jit(solution)/shard_map/ppermute | solution.py:148
  70.1 22.3 %collective-permute-start.9 = (f32[32,2,8,128]{3,2,1,0:T(8,128)S(1)}, f32[32,2,8,128]{3,2,1,0:T(8,128)S(1)}, u32[]{:S(2)}, u32[]{:S(2)}) collective-permute-start(f32[32,2,8,128]{3,2,1,0:T(8,128)S(1)} %get-tuple-element.55), channel_id=1, source_target_pairs={{0,24},{8,0},{16,8},{24,16},{1,25},{9,1},{17,9},{25,17},{2,26},{10... | collective-permute-start | bytes 786440 | tf_op jit(solution)/shard_map/ppermute | solution.py:148
  92.4 1.2 %collective-permute-start.10 = (f32[1,9,128]{2,1,0:T(8,128)S(1)}, f32[1,9,128]{2,1,0:T(8,128)S(1)}, u32[]{:S(2)}, u32[]{:S(2)}) collective-permute-start(f32[1,9,128]{2,1,0:T(8,128)S(1)} %bitcast.160), channel_id=1, source_target_pairs={{0,1},{1,0},{2,3},{3,2},{4,5},{5,4},{6,7},{7,6},{8,9},{9,8},{10,11... | collective-permute-start | bytes 13832 | tf_op jit(solution)/shard_map/ppermute | solution.py:44
  93.6 3.7 %collective-permute-start.11 = (f32[2,9,128]{2,1,0:T(8,128)S(1)}, f32[2,9,128]{2,1,0:T(8,128)S(1)}, u32[]{:S(2)}, u32[]{:S(2)}) collective-permute-start(f32[2,9,128]{2,1,0:T(8,128)S(1)} %maximum_select_fusion.2), channel_id=1, source_target_pairs={{0,2},{1,3},{2,0},{3,1},{4,6},{5,7},{6,4},{7,5},{8,10},{9,11},{10,... | collective-permute-start | bytes 27656 | tf_op jit(solution)/shard_map/ppermute | solution.py:44
  97.3 3.9 %collective-permute-start.12 = (f32[4,9,128]{2,1,0:T(8,128)S(1)}, f32[4,9,128]{2,1,0:T(8,128)S(1)}, u32[]{:S(2)}, u32[]{:S(2)}) collective-permute-start(f32[4,9,128]{2,1,0:T(8,128)S(1)} %maximum_select_fusion.1), channel_id=1, source_target_pairs={{0,4},{1,5},{2,6},{3,7},{4,0},{5,1},{6,2},{7,3},{8,12},{9,13},{10,... | collective-permute-start | bytes 55304 | tf_op jit(solution)/shard_map/ppermute | solution.py:44

commit v17 on v12

--- a/solution.py
+++ b/solution.py
@@ -106,14 +106,12 @@
     bounds[-1] = bins
     pieces = [own_part[bounds[c]:bounds[c + 1]] for c in range(CHUNKS)]
     scales = [chain[bounds[c]:bounds[c + 1]][:, None, None, None] for c in range(CHUNKS)]
-    for wave in range(CHUNKS + groups - 2):
-        for c in range(CHUNKS):
-            s = wave - c
-            if 0 <= s < groups - 1:
-                arrived = lax.ppermute(pieces[c], "species", [(s, s + 1)])
-                pieces[c] = pieces[c] + scales[c] * arrived
-    packed, pieces = lax.optimization_barrier((packed, pieces))
-    carried = jnp.concatenate(pieces, axis=0)
+    landed = []
+    for c in range(CHUNKS):
+        arrived = lax.ppermute(pieces[c], "species", [(0, 1)])
+        if c == 0:
+            packed, arrived = lax.optimization_barrier((packed, arrived))
+        landed.append(arrived)
     me_g = lax.axis_index("species")
     everyone = packed[None]
     span = 1
@@ -142,6 +140,16 @@
     lines, pixels = contribution.shape
     ids = jnp.zeros((1, pixels), jnp.float32).at[0, :lines].set(sky_blocks[0].astype(jnp.float32))
     payload = jnp.concatenate([contribution, ids], axis=0)
+    payload, landed[-1] = lax.optimization_barrier((payload, landed[-1]))
+    for c in range(CHUNKS):
+        pieces[c] = pieces[c] + scales[c] * landed[c]
+    for wave in range(1, CHUNKS + groups - 2):
+        for c in range(CHUNKS):
+            s = wave - c
+            if 1 <= s < groups - 1:
+                arrived = lax.ppermute(pieces[c], "species", [(s, s + 1)])
+                pieces[c] = pieces[c] + scales[c] * arrived
+    carried = jnp.concatenate(pieces, axis=0)
     gathered = gather_all(payload, "space")
     mine = lax.axis_index("space") * rows + jnp.arange(rows, dtype=jnp.int32)
     onehot = (

time: 116 us -> 104 us (0.90)
  waiting for transfers between devices: 83.8 us -> 64.8 us
  starting transfers between devices: 16.4 us -> 23.9 us
    ppermute x12 -> x8, waiting for transfers between devices: 47.6 us -> 35.7 us  [body(): arrived = lax.ppermute(pieces[c], 'species', [(s, s + 1)])]
    ppermute x2, starting transfers between devices: 0.14 us -> 7.62 us  [body(): lax.ppermute(everyone, 'species', [(i, i ^ span) for i in range(groups)])]
    ppermute x2, waiting for transfers between devices: 7.33 us -> 2.74 us  [body(): lax.ppermute(everyone, 'species', [(i, i ^ span) for i in range(groups)])]
    ppermute x12 -> x8, starting transfers between devices: 10.6 us -> 7.88 us  [body(): arrived = lax.ppermute(pieces[c], 'species', [(s, s + 1)])]
    ppermute x0 -> x4, starting transfers between devices: none -> 2.71 us  [body(): arrived = lax.ppermute(pieces[c], 'species', [(0, 1)])]
    ppermute x3, waiting for transfers between devices: 7.72 us -> 5.79 us  [gather_all(): other = lax.ppermute(held, axis, [(i, i ^ span) for i in range(count)])]
  transfers between devices with their start and end apart: 19 -> 19, of which waited for: 11 -> 11; matrix products, arithmetic and copies ran while one was open for 3% -> 5% of each run, Pallas kernels for 0% -> 0%
where the time goes in v17:
time: 104 us
  waiting for transfers between devices  64.8 us (62%)
  starting transfers between devices  23.9 us (23%)
  other arithmetic  8.89 us (9%)
  matrix products  3.36 us (3%)
  local copies, waits for them, and re-layouts  1.66 us (2%)
  between operations  1.18 us (1%)
    ppermute x8, waiting for transfers between devices, body(): arrived = lax.ppermute(pieces[c], 'species', [(s, s + 1)])  35.7 us
    ppermute x1, waiting for transfers between devices, body(): lax.ppermute(mine[:, :halo], 'space', [(i + 1, i) for i in range(count -...  10.5 us
    ppermute x1, waiting for transfers between devices, body(): lax.ppermute(mine[:, mine.shape[1] - halo:], 'space', [(i, i + 1) for i i...  10 us
    ppermute x8, starting transfers between devices, body(): arrived = lax.ppermute(pieces[c], 'species', [(s, s + 1)])  7.88 us
    ppermute x2, starting transfers between devices, body(): lax.ppermute(everyone, 'species', [(i, i ^ span) for i in range(groups)])  7.62 us
    ppermute x3, waiting for transfers between devices, gather_all(): other = lax.ppermute(held, axis, [(i, i ^ span) for i in range(count)])  5.79 us
    ppermute x1, starting transfers between devices, body(): lax.ppermute(mine[:, :halo], 'space', [(i + 1, i) for i in range(count -...  3.64 us
    ppermute x2, waiting for transfers between devices, body(): lax.ppermute(everyone, 'species', [(i, i ^ span) for i in range(groups)])  2.74 us
  transfers between devices with their start and end apart: 19, of which 11 were waited for; matrix products, arithmetic and copies ran while one was open for 5% of the time, Pallas kernels for 0%

profile of v17, /device:TPU:26, one launch (start us, length us, event | category | flops | bytes accessed | tf_op | source)
XLA Modules:
  0.0 103.7 jit_solution(12456367862140955578)
XLA Ops:
  0.7 1.4 %pad_maximum_fusion.2 = f32[33,2,32,128]{3,2,1,0:T(8,128)S(1)} fusion(f32[1,2,32,128]{3,2,1,0:T(8,128)} %bitcast.120, f32[32,2,32,128]{3,2,1,0:T(8,128)} %bitcast.115), kind=kLoop, calls=%fused_computation.36 | loop fusion | flops 270336 | bytes 2162688 | tf_op jit(solution)/shard_map/concatenate | solution.py:77
  2.1 1.9 %collective-permute-start = (f32[33,2,32,128]{3,2,1,0:T(8,128)S(1)}, f32[33,2,32,128]{3,2,1,0:T(8,128)S(1)}, u32[]{:S(2)}, u32[]{:S(2)}) collective-permute-start(f32[33,2,32,128]{3,2,1,0:T(8,128)S(1)} %pad_maximum_fusion.2), channel_id=1, source_target_pairs={{0,1},{1,2},{2,3},{3,4},{4,5},{5,6},{6,7},{8,9},{9,10},{10,11},{11... | collective-permute-start | bytes 3244040 | tf_op jit(solution)/shard_map/ppermute | solution.py:78
  4.0 3.6 %collective-permute-start.1 = (f32[33,2,32,128]{3,2,1,0:T(8,128)S(1)}, f32[33,2,32,128]{3,2,1,0:T(8,128)S(1)}, u32[]{:S(2)}, u32[]{:S(2)}) collective-permute-start(f32[33,2,32,128]{3,2,1,0:T(8,128)S(1)} %pad_maximum_fusion.2), channel_id=1, source_target_pairs={{1,0},{2,1},{3,2},{4,3},{5,4},{6,5},{7,6},{9,8},{10,9},{11,10},{12... | collective-permute-start | bytes 3244040 | tf_op jit(solution)/shard_map/ppermute | solution.py:81
  8.5 10.0 %collective-permute-done = f32[33,2,32,128]{3,2,1,0:T(8,128)S(1)} collective-permute-done((f32[33,2,32,128]{3,2,1,0:T(8,128)S(1)}, f32[33,2,32,128]{3,2,1,0:T(8,128)S(1)}, u32[]{:S(2)}, u32[]{:S(2)}) %collective-permute-start) | collective-permute-done | bytes 1081376 | tf_op jit(solution)/shard_map/ppermute | solution.py:78
  18.6 10.5 %collective-permute-done.1 = f32[33,2,32,128]{3,2,1,0:T(8,128)S(1)} collective-permute-done((f32[33,2,32,128]{3,2,1,0:T(8,128)S(1)}, f32[33,2,32,128]{3,2,1,0:T(8,128)S(1)}, u32[]{:S(2)}, u32[]{:S(2)}) %collective-permute-start.1) | collective-permute-done | bytes 1081376 | tf_op jit(solution)/shard_map/ppermute | solution.py:81
  30.5 2.0 %fusion.6 = f32[32,4,32,128]{3,2,1,0:T(8,128)S(1)} fusion(f32[32,4,32,128]{3,2,1,0:T(8,128)S(1)} %pad_maximum_fusion, f32[32,6,32,128]{3,2,1,0:T(8,128)S(1)} %broadcast_multiply_fusion, f32[32,2,32,128]{3,2,1,0:T(8,128)S(1)} %slice.216, f32[32,2,32,128]{3,2,1,0:T(8,128)S(1)} %bitcast.117, f32[32,2,32,128]{3,2,1,0:T(8,128)S(1)} %slice.215), kind=kLoop, calls=%fused_computation.14 | loop fusion | flops 5767168 | bytes 9437184 | tf_op jit(solution)/shard_map/add | solution.py:87
  32.5 0.7 fusion.25
  33.3 1.7 %convolution_bitcast_fusion = f32[4,8,64,128]{3,1,2,0:T(8,128)S(1)} fusion(f32[4,8,64,128]{3,2,1,0:T(8,128)S(1)} %bitcast.118, f32[1,32,32]{2,1,0:T(8,128)S(1)} %copy-done.3), kind=kOutput, calls=%fused_computation.19 | convolution fusion | flops 100663296 | bytes 2101248 | tf_op jit(solution)/shard_map/dot_general | solution.py:89
  35.7 0.7 collective-permute-start.2
  36.4 0.7 broadcast_select_fusion
  38.0 0.7 collective-permute-start.13
  38.7 0.7 collective-permute-start.5
  39.4 0.7 collective-permute-start.8
  40.0 1.2 %collective-permute-done.11 = f32[1,34,64]{2,1,0:T(8,128)S(1)} collective-permute-done((f32[1,34,64]{2,1,0:T(8,128)S(1)}, f32[1,34,64]{2,1,0:T(8,128)S(1)}, u32[]{:S(2)}, u32[]{:S(2)}) %collective-permute-start.11) | collective-permute-done | bytes 8736 | tf_op jit(solution)/shard_map/ppermute | solution.py:119
  41.2 7.1 %collective-permute-start.12 = (f32[2,34,64]{2,1,0:T(8,128)S(1)}, f32[2,34,64]{2,1,0:T(8,128)S(1)}, u32[]{:S(2)}, u32[]{:S(2)}) collective-permute-start(f32[2,34,64]{2,1,0:T(8,128)S(1)} %maximum_select_fusion.2), channel_id=1, source_target_pairs={{0,16},{8,24},{16,0},{24,8},{1,17},{9,25},{17,1},{25,9},{2,18},{10... | collective-permute-start | bytes 52232 | tf_op jit(solution)/shard_map/ppermute | solution.py:119
  48.4 0.7 collective-permute-start.3
  49.1 1.6 %collective-permute-done.12 = f32[2,34,64]{2,1,0:T(8,128)S(1)} collective-permute-done((f32[2,34,64]{2,1,0:T(8,128)S(1)}, f32[2,34,64]{2,1,0:T(8,128)S(1)}, u32[]{:S(2)}, u32[]{:S(2)}) %collective-permute-start.12) | collective-permute-done | bytes 17440 | tf_op jit(solution)/shard_map/ppermute | solution.py:119
  51.8 0.7 collective-permute-start.6
  52.7 0.7 collective-permute-start.9
  53.8 1.3 %collective-permute-start.4 = (f32[5,2,32,128]{3,2,1,0:T(8,128)S(1)}, f32[5,2,32,128]{3,2,1,0:T(8,128)S(1)}, u32[]{:S(2)}, u32[]{:S(2)}) collective-permute-start(f32[5,2,32,128]{3,2,1,0:T(8,128)S(1)} %multiply_add_fusion.10), channel_id=1, source_target_pairs={{16,24},{17,25},{18,26},{19,27},{20,28},{21,29},{22,30},{23,31}} | collective-permute-start | bytes 491528 | tf_op jit(solution)/shard_map/ppermute | solution.py:150
  55.1 2.3 %collective-permute-done.17 = f32[2,9,128]{2,1,0:T(8,128)S(1)} collective-permute-done((f32[2,9,128]{2,1,0:T(8,128)S(1)}, f32[2,9,128]{2,1,0:T(8,128)S(1)}, u32[]{:S(2)}, u32[]{:S(2)}) %collective-permute-start.17) | collective-permute-done | bytes 9248 | tf_op jit(solution)/shard_map/ppermute | solution.py:44
  57.6 0.7 collective-permute-start.14
  58.3 3.1 %collective-permute-done.18 = f32[4,9,128]{2,1,0:T(8,128)S(1)} collective-permute-done((f32[4,9,128]{2,1,0:T(8,128)S(1)}, f32[4,9,128]{2,1,0:T(8,128)S(1)}, u32[]{:S(2)}, u32[]{:S(2)}) %collective-permute-start.18) | collective-permute-done | bytes 18464 | tf_op jit(solution)/shard_map/ppermute | solution.py:44
  61.5 0.8 fusion.30
  62.4 1.3 %collective-permute-start.7 = (f32[7,2,32,128]{3,2,1,0:T(8,128)S(1)}, f32[7,2,32,128]{3,2,1,0:T(8,128)S(1)}, u32[]{:S(2)}, u32[]{:S(2)}) collective-permute-start(f32[7,2,32,128]{3,2,1,0:T(8,128)S(1)} %multiply_add_fusion.7), channel_id=1, source_target_pairs={{16,24},{17,25},{18,26},{19,27},{20,28},{21,29},{22,30},{23,31}} | collective-permute-start | bytes 688136 | tf_op jit(solution)/shard_map/ppermute | solution.py:150
  63.7 15.8 %collective-permute-done.4 = f32[5,2,32,128]{3,2,1,0:T(8,128)S(1)} collective-permute-done((f32[5,2,32,128]{3,2,1,0:T(8,128)S(1)}, f32[5,2,32,128]{3,2,1,0:T(8,128)S(1)}, u32[]{:S(2)}, u32[]{:S(2)}) %collective-permute-start.4) | collective-permute-done | bytes 163872 | tf_op jit(solution)/shard_map/ppermute | solution.py:150
  79.7 1.3 %collective-permute-start.10 = (f32[9,2,32,128]{3,2,1,0:T(8,128)S(1)}, f32[9,2,32,128]{3,2,1,0:T(8,128)S(1)}, u32[]{:S(2)}, u32[]{:S(2)}) collective-permute-start(f32[9,2,32,128]{3,2,1,0:T(8,128)S(1)} %multiply_add_fusion.4), channel_id=1, source_target_pairs={{16,24},{17,25},{18,26},{19,27},{20,28},{21,29},{22,30},{23,31}} | collective-permute-start | bytes 884744 | tf_op jit(solution)/shard_map/ppermute | solution.py:150
  81.1 1.3 %collective-permute-start.15 = (f32[11,2,32,128]{3,2,1,0:T(8,128)S(1)}, f32[11,2,32,128]{3,2,1,0:T(8,128)S(1)}, u32[]{:S(2)}, u32[]{:S(2)}) collective-permute-start(f32[11,2,32,128]{3,2,1,0:T(8,128)S(1)} %multiply_add_fusion.1), channel_id=1, source_target_pairs={{16,24},{17,25},{18,26},{19,27},{20,28},{21,29},{22,30},{23,31}} | collective-permute-start | bytes 1081352 | tf_op jit(solution)/shard_map/ppermute | solution.py:150
  82.4 6.0 %collective-permute-done.7 = f32[7,2,32,128]{3,2,1,0:T(8,128)S(1)} collective-permute-done((f32[7,2,32,128]{3,2,1,0:T(8,128)S(1)}, f32[7,2,32,128]{3,2,1,0:T(8,128)S(1)}, u32[]{:S(2)}, u32[]{:S(2)}) %collective-permute-start.7) | collective-permute-done | bytes 229408 | tf_op jit(solution)/shard_map/ppermute | solution.py:150
  88.5 5.6 %collective-permute-done.10 = f32[9,2,32,128]{3,2,1,0:T(8,128)S(1)} collective-permute-done((f32[9,2,32,128]{3,2,1,0:T(8,128)S(1)}, f32[9,2,32,128]{3,2,1,0:T(8,128)S(1)}, u32[]{:S(2)}, u32[]{:S(2)}) %collective-permute-start.10) | collective-permute-done | bytes 294944 | tf_op jit(solution)/shard_map/ppermute | solution.py:150
  94.2 8.3 %collective-permute-done.15 = f32[11,2,32,128]{3,2,1,0:T(8,128)S(1)} collective-permute-done((f32[11,2,32,128]{3,2,1,0:T(8,128)S(1)}, f32[11,2,32,128]{3,2,1,0:T(8,128)S(1)}, u32[]{:S(2)}, u32[]{:S(2)}) %collective-permute-start.15) | collective-permute-done | bytes 360480 | tf_op jit(solution)/shard_map/ppermute | solution.py:150
  102.6 1.1 %maximum_bitcast_fusion = f32[1,32,2,32,128]{4,3,2,1,0:T(8,128)} fusion(f32[11,2,32,128]{3,2,1,0:T(8,128)S(1)} %multiply_add_fusion, f32[9,2,32,128]{3,2,1,0:T(8,128)S(1)} %multiply_add_fusion.3, f32[7,2,32,128]{3,2,1,0:T(8,128)S(1)} %multiply_add_fusion.6, f32[5,2,32,128]{3,2,1,0:T(8,128)S(1)} %multiply_add_fusion.9), kind=kLoop, calls=%fused_computation.47 | loop fusion | flops 786432 | bytes 2097152 | tf_op jit(solution)/shard_map/broadcast_in_dim | solution.py:165
  (82 shorter events, 6.5 us)
Async XLA Ops:
  0.6 50.9 %copy-start = (bf16[1,8,64,128]{3,2,1,0:T(8,128)(2,1)S(1)}, bf16[1,8,64,128]{3,2,1,0:T(8,128)(2,1)}, u32[]{:S(2)}) copy-start(bf16[1,8,64,128]{3,2,1,0:T(8,128)(2,1)} %param.22) | copy-start | bytes 393220
  0.6 7.6 %copy-start.5 = (f32[1,32]{1,0:T(1,128)S(1)}, f32[1,32]{1,0:T(1,128)}, u32[]{:S(2)}) copy-start(f32[1,32]{1,0:T(1,128)} %param.19) | copy-start | bytes 388
  2.1 16.5 %collective-permute-start = (f32[33,2,32,128]{3,2,1,0:T(8,128)S(1)}, f32[33,2,32,128]{3,2,1,0:T(8,128)S(1)}, u32[]{:S(2)}, u32[]{:S(2)}) collective-permute-start(f32[33,2,32,128]{3,2,1,0:T(8,128)S(1)} %pad_maximum_fusion.2), channel_id=1, source_target_pairs={{0,1},{1,2},{2,3},{3,4},{4,5},{5,6},{6,7},{8,9},{9,10},{10,11},{11... | collective-permute-start | bytes 3244040 | tf_op jit(solution)/shard_map/ppermute | solution.py:78
  4.0 25.1 %collective-permute-start.1 = (f32[33,2,32,128]{3,2,1,0:T(8,128)S(1)}, f32[33,2,32,128]{3,2,1,0:T(8,128)S(1)}, u32[]{:S(2)}, u32[]{:S(2)}) collective-permute-start(f32[33,2,32,128]{3,2,1,0:T(8,128)S(1)} %pad_maximum_fusion.2), channel_id=1, source_target_pairs={{1,0},{2,1},{3,2},{4,3},{5,4},{6,5},{7,6},{9,8},{10,9},{11,10},{12... | collective-permute-start | bytes 3244040 | tf_op jit(solution)/shard_map/ppermute | solution.py:81
  8.5 20.7 %copy-start.1 = (f32[1,32,2,32,128]{4,3,2,1,0:T(8,128)S(1)}, f32[1,32,2,32,128]{4,3,2,1,0:T(8,128)}, u32[]{:S(2)}) copy-start(f32[1,32,2,32,128]{4,3,2,1,0:T(8,128)} %param.15) | copy-start | bytes 3145732
  29.2 0.8 copy-start.2
  29.3 0.8 copy-start.7
  32.5 0.8 copy-start.3
  33.3 1.9 %copy-start.4 = (f32[1,32]{1,0:T(1,128)S(1)}, f32[1,32]{1,0:T(1,128)}, u32[]{:S(2)}) copy-start(f32[1,32]{1,0:T(1,128)} %param.20) | copy-start | bytes 388
  35.0 1.4 %copy-start.8 = (s32[1,8]{1,0:T(1,128)S(1)}, s32[1,8]{1,0:T(1,128)}, u32[]{:S(2)}) copy-start(s32[1,8]{1,0:T(1,128)} %param.23) | copy-start | bytes 100
  35.0 2.1 %copy-start.6 = (f32[1,32]{1,0:T(1,128)S(1)}, f32[1,32]{1,0:T(1,128)}, u32[]{:S(2)}) copy-start(f32[1,32]{1,0:T(1,128)} %param.21) | copy-start | bytes 388
  35.7 1.6 %collective-permute-start.2 = (f32[5,2,32,128]{3,2,1,0:T(8,128)S(1)}, f32[5,2,32,128]{3,2,1,0:T(8,128)S(1)}, u32[]{:S(2)}, u32[]{:S(2)}) collective-permute-start(f32[5,2,32,128]{3,2,1,0:T(8,128)S(1)} %slice.224), channel_id=1, source_target_pairs={{0,8},{1,9},{2,10},{3,11},{4,12},{5,13},{6,14},{7,15}} | collective-permute-start | bytes 491528 | tf_op jit(solution)/shard_map/ppermute | solution.py:111
  37.4 3.8 %collective-permute-start.11 = (f32[1,34,64]{2,1,0:T(8,128)S(1)}, f32[1,34,64]{2,1,0:T(8,128)S(1)}, u32[]{:S(2)}, u32[]{:S(2)}) collective-permute-start(f32[1,34,64]{2,1,0:T(8,128)S(1)} %bitcast.121), channel_id=1, source_target_pairs={{0,8},{8,0},{16,24},{24,16},{1,9},{9,1},{17,25},{25,17},{2,10},{10... | collective-permute-start | bytes 26120 | tf_op jit(solution)/shard_map/ppermute | solution.py:119
  38.0 14.5 %collective-permute-start.13 = (f32[11,2,32,128]{3,2,1,0:T(8,128)S(1)}, f32[11,2,32,128]{3,2,1,0:T(8,128)S(1)}, u32[]{:S(2)}, u32[]{:S(2)}) collective-permute-start(f32[11,2,32,128]{3,2,1,0:T(8,128)S(1)} %slice.227), channel_id=1, source_target_pairs={{0,8},{1,9},{2,10},{3,11},{4,12},{5,13},{6,14},{7,15}} | collective-permute-start | bytes 1081352 | tf_op jit(solution)/shard_map/ppermute | solution.py:111
  38.7 13.0 %collective-permute-start.5 = (f32[7,2,32,128]{3,2,1,0:T(8,128)S(1)}, f32[7,2,32,128]{3,2,1,0:T(8,128)S(1)}, u32[]{:S(2)}, u32[]{:S(2)}) collective-permute-start(f32[7,2,32,128]{3,2,1,0:T(8,128)S(1)} %slice.225), channel_id=1, source_target_pairs={{0,8},{1,9},{2,10},{3,11},{4,12},{5,13},{6,14},{7,15}} | collective-permute-start | bytes 688136 | tf_op jit(solution)/shard_map/ppermute | solution.py:111
  39.4 13.2 %collective-permute-start.8 = (f32[9,2,32,128]{3,2,1,0:T(8,128)S(1)}, f32[9,2,32,128]{3,2,1,0:T(8,128)S(1)}, u32[]{:S(2)}, u32[]{:S(2)}) collective-permute-start(f32[9,2,32,128]{3,2,1,0:T(8,128)S(1)} %slice.226), channel_id=1, source_target_pairs={{0,8},{1,9},{2,10},{3,11},{4,12},{5,13},{6,14},{7,15}} | collective-permute-start | bytes 884744 | tf_op jit(solution)/shard_map/ppermute | solution.py:111
  41.2 9.4 %collective-permute-start.12 = (f32[2,34,64]{2,1,0:T(8,128)S(1)}, f32[2,34,64]{2,1,0:T(8,128)S(1)}, u32[]{:S(2)}, u32[]{:S(2)}) collective-permute-start(f32[2,34,64]{2,1,0:T(8,128)S(1)} %maximum_select_fusion.2), channel_id=1, source_target_pairs={{0,16},{8,24},{16,0},{24,8},{1,17},{9,25},{17,1},{25,9},{2,18},{10... | collective-permute-start | bytes 52232 | tf_op jit(solution)/shard_map/ppermute | solution.py:119
  48.4 5.3 %collective-permute-start.3 = (f32[5,2,32,128]{3,2,1,0:T(8,128)S(1)}, f32[5,2,32,128]{3,2,1,0:T(8,128)S(1)}, u32[]{:S(2)}, u32[]{:S(2)}) collective-permute-start(f32[5,2,32,128]{3,2,1,0:T(8,128)S(1)} %multiply_add_fusion.11), channel_id=1, source_target_pairs={{8,16},{9,17},{10,18},{11,19},{12,20},{13,21},{14,22},{15,23}} | collective-permute-start | bytes 491528 | tf_op jit(solution)/shard_map/ppermute | solution.py:150
  51.8 10.5 %collective-permute-start.6 = (f32[7,2,32,128]{3,2,1,0:T(8,128)S(1)}, f32[7,2,32,128]{3,2,1,0:T(8,128)S(1)}, u32[]{:S(2)}, u32[]{:S(2)}) collective-permute-start(f32[7,2,32,128]{3,2,1,0:T(8,128)S(1)} %multiply_add_fusion.8), channel_id=1, source_target_pairs={{8,16},{9,17},{10,18},{11,19},{12,20},{13,21},{14,22},{15,23}} | collective-permute-start | bytes 688136 | tf_op jit(solution)/shard_map/ppermute | solution.py:150
  52.5 1.2 %collective-permute-start.16 = (f32[1,9,128]{2,1,0:T(8,128)S(1)}, f32[1,9,128]{2,1,0:T(8,128)S(1)}, u32[]{:S(2)}, u32[]{:S(2)}) collective-permute-start(f32[1,9,128]{2,1,0:T(8,128)S(1)} %bitcast.123), channel_id=1, source_target_pairs={{0,1},{1,0},{2,3},{3,2},{4,5},{5,4},{6,7},{7,6},{8,9},{9,8},{10,11... | collective-permute-start | bytes 13832 | tf_op jit(solution)/shard_map/ppermute | solution.py:44
  52.7 26.9 %collective-permute-start.9 = (f32[9,2,32,128]{3,2,1,0:T(8,128)S(1)}, f32[9,2,32,128]{3,2,1,0:T(8,128)S(1)}, u32[]{:S(2)}, u32[]{:S(2)}) collective-permute-start(f32[9,2,32,128]{3,2,1,0:T(8,128)S(1)} %multiply_add_fusion.5), channel_id=1, source_target_pairs={{8,16},{9,17},{10,18},{11,19},{12,20},{13,21},{14,22},{15,23}} | collective-permute-start | bytes 884744 | tf_op jit(solution)/shard_map/ppermute | solution.py:150
  53.7 3.7 %collective-permute-start.17 = (f32[2,9,128]{2,1,0:T(8,128)S(1)}, f32[2,9,128]{2,1,0:T(8,128)S(1)}, u32[]{:S(2)}, u32[]{:S(2)}) collective-permute-start(f32[2,9,128]{2,1,0:T(8,128)S(1)} %maximum_select_fusion.4), channel_id=1, source_target_pairs={{0,2},{1,3},{2,0},{3,1},{4,6},{5,7},{6,4},{7,5},{8,10},{9,11},{10,... | collective-permute-start | bytes 27656 | tf_op jit(solution)/shard_map/ppermute | solution.py:44
  53.8 25.7 %collective-permute-start.4 = (f32[5,2,32,128]{3,2,1,0:T(8,128)S(1)}, f32[5,2,32,128]{3,2,1,0:T(8,128)S(1)}, u32[]{:S(2)}, u32[]{:S(2)}) collective-permute-start(f32[5,2,32,128]{3,2,1,0:T(8,128)S(1)} %multiply_add_fusion.10), channel_id=1, source_target_pairs={{16,24},{17,25},{18,26},{19,27},{20,28},{21,29},{22,30},{23,31}} | collective-permute-start | bytes 491528 | tf_op jit(solution)/shard_map/ppermute | solution.py:150
  57.5 3.9 %collective-permute-start.18 = (f32[4,9,128]{2,1,0:T(8,128)S(1)}, f32[4,9,128]{2,1,0:T(8,128)S(1)}, u32[]{:S(2)}, u32[]{:S(2)}) collective-permute-start(f32[4,9,128]{2,1,0:T(8,128)S(1)} %maximum_select_fusion.3), channel_id=1, source_target_pairs={{0,4},{1,5},{2,6},{3,7},{4,0},{5,1},{6,2},{7,3},{8,12},{9,13},{10,... | collective-permute-start | bytes 55304 | tf_op jit(solution)/shard_map/ppermute | solution.py:44
  57.6 23.4 %collective-permute-start.14 = (f32[11,2,32,128]{3,2,1,0:T(8,128)S(1)}, f32[11,2,32,128]{3,2,1,0:T(8,128)S(1)}, u32[]{:S(2)}, u32[]{:S(2)}) collective-permute-start(f32[11,2,32,128]{3,2,1,0:T(8,128)S(1)} %multiply_add_fusion.2), channel_id=1, source_target_pairs={{8,16},{9,17},{10,18},{11,19},{12,20},{13,21},{14,22},{15,23}} | collective-permute-start | bytes 1081352 | tf_op jit(solution)/shard_map/ppermute | solution.py:150
  62.4 26.0 %collective-permute-start.7 = (f32[7,2,32,128]{3,2,1,0:T(8,128)S(1)}, f32[7,2,32,128]{3,2,1,0:T(8,128)S(1)}, u32[]{:S(2)}, u32[]{:S(2)}) collective-permute-start(f32[7,2,32,128]{3,2,1,0:T(8,128)S(1)} %multiply_add_fusion.7), channel_id=1, source_target_pairs={{16,24},{17,25},{18,26},{19,27},{20,28},{21,29},{22,30},{23,31}} | collective-permute-start | bytes 688136 | tf_op jit(solution)/shard_map/ppermute | solution.py:150
  79.7 14.4 %collective-permute-start.10 = (f32[9,2,32,128]{3,2,1,0:T(8,128)S(1)}, f32[9,2,32,128]{3,2,1,0:T(8,128)S(1)}, u32[]{:S(2)}, u32[]{:S(2)}) collective-permute-start(f32[9,2,32,128]{3,2,1,0:T(8,128)S(1)} %multiply_add_fusion.4), channel_id=1, source_target_pairs={{16,24},{17,25},{18,26},{19,27},{20,28},{21,29},{22,30},{23,31}} | collective-permute-start | bytes 884744 | tf_op jit(solution)/shard_map/ppermute | solution.py:150
  81.1 21.4 %collective-permute-start.15 = (f32[11,2,32,128]{3,2,1,0:T(8,128)S(1)}, f32[11,2,32,128]{3,2,1,0:T(8,128)S(1)}, u32[]{:S(2)}, u32[]{:S(2)}) collective-permute-start(f32[11,2,32,128]{3,2,1,0:T(8,128)S(1)} %multiply_add_fusion.1), channel_id=1, source_target_pairs={{16,24},{17,25},{18,26},{19,27},{20,28},{21,29},{22,30},{23,31}} | collective-permute-start | bytes 1081352 | tf_op jit(solution)/shard_map/ppermute | solution.py:150

commit v18 on v15

--- a/solution.py
+++ b/solution.py
@@ -146,6 +146,7 @@
     for d in shifts:
         outgoing = lax.dynamic_index_in_dim(results, (me_s + d) % groups, 0, keepdims=False)
         back.append(lax.ppermute(outgoing, "species", [(i, (i + d) % groups) for i in range(groups)]))
+    payload, back[1] = lax.optimization_barrier((payload, back[1]))
     mine_slabs = jnp.take(jnp.stack(back), (me_s - jnp.arange(groups)) % groups, axis=0)
     carried = jnp.moveaxis(mine_slabs, 0, 2).reshape(own_part.shape)
     gathered = gather_all(payload, "space")

time: 103 us -> 99.5 us (0.966)
  waiting for transfers between devices: 34.3 us -> 26.3 us
  starting transfers between devices: 49.4 us -> 53.8 us
    ppermute x3, waiting for transfers between devices: 19.1 us -> 10.9 us  [body(): lax.ppermute(outgoing, 'species', [(i, (i + d) % groups) for i in range(g...]
    ppermute x5, starting transfers between devices: 37.2 us -> 43 us  [gather_all(): other = lax.ppermute(held, axis, [(i, i ^ span) for i in range(count)])]
    ppermute x3, starting transfers between devices: 4.67 us -> 3.35 us  [body(): lax.ppermute(outgoing, 'species', [(i, (i + d) % groups) for i in range(g...]
  transfers between devices with their start and end apart: 13 -> 13, of which waited for: 6 -> 6; matrix products, arithmetic and copies ran while one was open for 10% -> 12% of each run, Pallas kernels for 0% -> 0%
where the time goes in v18:
time: 99.5 us; the launch traced here: 99.2 us
  starting transfers between devices  53.8 us (54%)
  waiting for transfers between devices  26.3 us (26%)
  other arithmetic  9.7 us (10%)
  local copies, waits for them, and re-layouts  4.94 us (5%)
  matrix products  3.34 us (3%)
  between operations  1.1 us (1%)
    ppermute x5, starting transfers between devices, gather_all(): other = lax.ppermute(held, axis, [(i, i ^ span) for i in range(count)])  43 us
    ppermute x3, waiting for transfers between devices, body(): lax.ppermute(message((me_s + d) % groups), 'species', [(i, (i + d) % grou...  12.9 us
    ppermute x3, waiting for transfers between devices, body(): lax.ppermute(outgoing, 'species', [(i, (i + d) % groups) for i in range(g...  10.9 us
    ppermute x3, starting transfers between devices, body(): lax.ppermute(outgoing, 'species', [(i, (i + d) % groups) for i in range(g...  3.35 us
    ppermute x1, starting transfers between devices, body(): lax.ppermute(mine[:, mine.shape[1] - halo:], 'space', [(i, i + 1) for i i...  3.1 us
    ppermute x3, starting transfers between devices, body(): lax.ppermute(message((me_s + d) % groups), 'species', [(i, (i + d) % grou...  3.1 us
    add x2, other arithmetic, body(): inner + wide_factor[:, 1 + step:wide_factor.shape[1] - 1 - step] * (besid...  2.71 us
    ppermute x5, waiting for transfers between devices, gather_all(): other = lax.ppermute(held, axis, [(i, i ^ span) for i in range(count)])  2.54 us
  transfers between devices with their start and end apart: 13, of which 6 were waited for; matrix products, arithmetic and copies ran while one was open for 12% of the time, Pallas kernels for 0%

profile of v18, /device:TPU:0, one launch (start us, length us, event | category | flops | bytes accessed | tf_op | source)
XLA Modules:
  0.0 99.2 jit_solution(1648299900459688735)
XLA Ops:
  0.7 1.4 %pad_maximum_fusion.3 = f32[33,2,32,128]{3,2,1,0:T(8,128)S(1)} fusion(f32[1,2,32,128]{3,2,1,0:T(8,128)} %bitcast.155, f32[32,2,32,128]{3,2,1,0:T(8,128)} %bitcast.137), kind=kLoop, calls=%fused_computation.39 | loop fusion | flops 270336 | bytes 2162688 | tf_op jit(solution)/shard_map/concatenate | solution.py:78
  2.0 1.3 %collective-permute-start.1 = (f32[33,2,32,128]{3,2,1,0:T(8,128)S(1)}, f32[33,2,32,128]{3,2,1,0:T(8,128)S(1)}, u32[]{:S(2)}, u32[]{:S(2)}) collective-permute-start(f32[33,2,32,128]{3,2,1,0:T(8,128)S(1)} %pad_maximum_fusion.3), channel_id=1, source_target_pairs={{1,0},{2,1},{3,2},{4,3},{5,4},{6,5},{7,6},{9,8},{10,9},{11,10},{12... | collective-permute-start | bytes 3244040 | tf_op jit(solution)/shard_map/ppermute | solution.py:82
  3.3 3.1 %collective-permute-start = (f32[33,2,32,128]{3,2,1,0:T(8,128)S(1)}, f32[33,2,32,128]{3,2,1,0:T(8,128)S(1)}, u32[]{:S(2)}, u32[]{:S(2)}) collective-permute-start(f32[33,2,32,128]{3,2,1,0:T(8,128)S(1)} %pad_maximum_fusion.3), channel_id=1, source_target_pairs={{0,1},{1,2},{2,3},{3,4},{4,5},{5,6},{6,7},{8,9},{9,10},{10,11},{11... | collective-permute-start | bytes 3244040 | tf_op jit(solution)/shard_map/ppermute | solution.py:79
  6.5 3.1 %collective-permute-start.5 = (f32[1,32]{1,0:T(1,128)S(1)}, f32[1,32]{1,0:T(1,128)S(1)}, u32[]{:S(2)}, u32[]{:S(2)}) collective-permute-start(f32[1,32]{1,0:T(1,128)S(1)} %copy-done.5), channel_id=1, source_target_pairs={{0,8},{8,0},{16,24},{24,16},{1,9},{9,1},{17,25},{25,17},{2,10},{10... | collective-permute-start | bytes 392 | tf_op jit(solution)/shard_map/ppermute | solution.py:44
  9.7 0.6 compare_reduce_fusion
  10.4 0.7 broadcast_select_fusion.1
  11.1 3.1 %collective-permute-start.6 = (f32[2,32]{1,0:T(2,128)S(1)}, f32[2,32]{1,0:T(2,128)S(1)}, u32[]{:S(2)}, u32[]{:S(2)}) collective-permute-start(f32[2,32]{1,0:T(2,128)S(1)} %maximum_select_fusion.4), channel_id=1, source_target_pairs={{0,16},{8,24},{16,0},{24,8},{1,17},{9,25},{17,1},{25,9},{2,18},{10... | collective-permute-start | bytes 776 | tf_op jit(solution)/shard_map/ppermute | solution.py:44
  14.6 0.5 copy-done.2
  15.1 0.4 broadcast_multiply_fusion
  15.6 2.0 %fusion.6 = f32[32,4,32,128]{3,2,1,0:T(8,128)S(1)} fusion(f32[32,4,32,128]{3,2,1,0:T(8,128)S(1)} %pad_maximum_fusion, f32[32,6,32,128]{3,2,1,0:T(8,128)S(1)} %broadcast_multiply_fusion, f32[32,2,32,128]{3,2,1,0:T(8,128)S(1)} %slice.228, f32[32,2,32,128]{3,2,1,0:T(8,128)S(1)} %bitcast.139, f32[32,2,32,128]{3,2,1,0:T(8,128)S(1)} %slice.227), kind=kLoop, calls=%fused_computation.16 | loop fusion | flops 5767168 | bytes 9437184 | tf_op jit(solution)/shard_map/add | solution.py:88
  17.6 0.7 fusion.25
  18.4 1.7 %convolution_bitcast_fusion = f32[4,8,64,128]{3,1,2,0:T(8,128)S(1)} fusion(f32[4,8,64,128]{3,2,1,0:T(8,128)S(1)} %bitcast.142, f32[1,32,32]{2,1,0:T(8,128)S(1)} %copy-done.3), kind=kOutput, calls=%fused_computation.21 | convolution fusion | flops 100663296 | bytes 2101248 | tf_op jit(solution)/shard_map/dot_general | solution.py:90
  20.3 0.5 multiply_reduce_fusion
  21.3 2.0 %collective-permute-start.4 = (f32[67712]{0:T(1024)S(1)}, f32[67712]{0:T(1024)S(1)}, u32[]{:S(2)}, u32[]{:S(2)}) collective-permute-start(f32[67712]{0:T(1024)S(1)} %get-tuple-element.63), channel_id=1, source_target_pairs={{0,24},{8,0},{16,8},{24,16},{1,25},{9,1},{17,9},{25,17},{2,26},{10... | collective-permute-start | bytes 812552 | tf_op jit(solution)/shard_map/ppermute | solution.py:118
  23.4 1.1 %collective-permute-start.3 = (f32[67712]{0:T(1024)S(1)}, f32[67712]{0:T(1024)S(1)}, u32[]{:S(2)}, u32[]{:S(2)}) collective-permute-start(f32[67712]{0:T(1024)S(1)} %get-tuple-element.62), channel_id=1, source_target_pairs={{0,16},{8,24},{16,0},{24,8},{1,17},{9,25},{17,1},{25,9},{2,18},{10... | collective-permute-start | bytes 812552 | tf_op jit(solution)/shard_map/ppermute | solution.py:118
  24.7 3.2 %collective-permute-done.4 = f32[67712]{0:T(1024)S(1)} collective-permute-done((f32[67712]{0:T(1024)S(1)}, f32[67712]{0:T(1024)S(1)}, u32[]{:S(2)}, u32[]{:S(2)}) %collective-permute-start.4) | collective-permute-done | bytes 270880 | tf_op jit(solution)/shard_map/ppermute | solution.py:118
  28.1 9.6 %collective-permute-done.3 = f32[67712]{0:T(1024)S(1)} collective-permute-done((f32[67712]{0:T(1024)S(1)}, f32[67712]{0:T(1024)S(1)}, u32[]{:S(2)}, u32[]{:S(2)}) %collective-permute-start.3) | collective-permute-done | bytes 270880 | tf_op jit(solution)/shard_map/ppermute | solution.py:118
  38.1 1.0 %pad_maximum_fusion.2 = f32[4,67712]{1,0:T(4,128)S(1)} fusion(f32[1,67712]{1,0:T(1,128)S(1)} %stack.37, f32[1,67712]{1,0:T(1,128)S(1)} %stack.36, f32[1,67712]{1,0:T(1,128)S(1)} %stack.35, f32[1,67712]{1,0:T(1,128)S(1)} %stack.34), kind=kLoop, calls=%fused_computation.38 | loop fusion | flops 812544 | bytes 2166784 | tf_op jit(solution)/shard_map/stack | solution.py:120
  39.2 1.1 %gather_fusion = f32[4,67712]{1,0:T(4,128)S(1)} fusion(f32[4,67712]{1,0:T(4,128)S(1)} %pad_maximum_fusion.2, s32[1024]{0:T(1024)S(1)} %pad_clamp_fusion), kind=kCustom, calls=%fused_computation | custom fusion | bytes 2166800 | tf_op jit(solution)/shard_map/jit(_take)/gather | solution.py:120
  40.6 0.8 fusion.46
  41.8 1.3 %collective-permute-start.8 = (f32[32,2,8,128]{3,2,1,0:T(8,128)S(1)}, f32[32,2,8,128]{3,2,1,0:T(8,128)S(1)}, u32[]{:S(2)}, u32[]{:S(2)}) collective-permute-start(f32[32,2,8,128]{3,2,1,0:T(8,128)S(1)} %get-tuple-element.51), channel_id=1, source_target_pairs={{0,16},{8,24},{16,0},{24,8},{1,17},{9,25},{17,1},{25,9},{2,18},{10... | collective-permute-start | bytes 786440 | tf_op jit(solution)/shard_map/ppermute | solution.py:148
  43.8 2.0 %collective-permute-start.7 = (f32[32,2,8,128]{3,2,1,0:T(8,128)S(1)}, f32[32,2,8,128]{3,2,1,0:T(8,128)S(1)}, u32[]{:S(2)}, u32[]{:S(2)}) collective-permute-start(f32[32,2,8,128]{3,2,1,0:T(8,128)S(1)} %get-tuple-element.52), channel_id=1, source_target_pairs={{0,8},{8,16},{16,24},{24,0},{1,9},{9,17},{17,25},{25,1},{2,10},{10... | collective-permute-start | bytes 786440 | tf_op jit(solution)/shard_map/ppermute | solution.py:148
  46.1 10.9 %collective-permute-done.7 = f32[32,2,8,128]{3,2,1,0:T(8,128)S(1)} collective-permute-done((f32[32,2,8,128]{3,2,1,0:T(8,128)S(1)}, f32[32,2,8,128]{3,2,1,0:T(8,128)S(1)}, u32[]{:S(2)}, u32[]{:S(2)}) %collective-permute-start.7) | collective-permute-done | bytes 262176 | tf_op jit(solution)/shard_map/ppermute | solution.py:148
  57.0 21.1 %collective-permute-start.10 = (f32[1,9,128]{2,1,0:T(8,128)S(1)}, f32[1,9,128]{2,1,0:T(8,128)S(1)}, u32[]{:S(2)}, u32[]{:S(2)}) collective-permute-start(f32[1,9,128]{2,1,0:T(8,128)S(1)} %bitcast.156), channel_id=1, source_target_pairs={{0,1},{1,0},{2,3},{3,2},{4,5},{5,4},{6,7},{7,6},{8,9},{9,8},{10,11... | collective-permute-start | bytes 13832 | tf_op jit(solution)/shard_map/ppermute | solution.py:44
  78.1 0.8 collective-permute-done.10
  79.0 10.6 %collective-permute-start.11 = (f32[2,9,128]{2,1,0:T(8,128)S(1)}, f32[2,9,128]{2,1,0:T(8,128)S(1)}, u32[]{:S(2)}, u32[]{:S(2)}) collective-permute-start(f32[2,9,128]{2,1,0:T(8,128)S(1)} %maximum_select_fusion.2), channel_id=1, source_target_pairs={{0,2},{1,3},{2,0},{3,1},{4,6},{5,7},{6,4},{7,5},{8,10},{9,11},{10,... | collective-permute-start | bytes 27656 | tf_op jit(solution)/shard_map/ppermute | solution.py:44
  89.7 0.6 gather_fusion.1
  90.3 1.0 %collective-permute-done.11 = f32[2,9,128]{2,1,0:T(8,128)S(1)} collective-permute-done((f32[2,9,128]{2,1,0:T(8,128)S(1)}, f32[2,9,128]{2,1,0:T(8,128)S(1)}, u32[]{:S(2)}, u32[]{:S(2)}) %collective-permute-start.11) | collective-permute-done | bytes 9248 | tf_op jit(solution)/shard_map/ppermute | solution.py:44
  91.3 5.1 %collective-permute-start.12 = (f32[4,9,128]{2,1,0:T(8,128)S(1)}, f32[4,9,128]{2,1,0:T(8,128)S(1)}, u32[]{:S(2)}, u32[]{:S(2)}) collective-permute-start(f32[4,9,128]{2,1,0:T(8,128)S(1)} %maximum_select_fusion.1), channel_id=1, source_target_pairs={{0,4},{1,5},{2,6},{3,7},{4,0},{5,1},{6,2},{7,3},{8,12},{9,13},{10,... | collective-permute-start | bytes 55304 | tf_op jit(solution)/shard_map/ppermute | solution.py:44
  96.4 1.2 %copy_bitcast_fusion = f32[1,32,2,32,128]{4,3,2,1,0:T(8,128)} fusion(f32[4,32,2,8,128]{4,3,2,1,0:T(8,128)S(1)} %gather_fusion.1, pred[4]{0:T(512)(128)(4,1)S(1)} %compare_and_fusion), kind=kLoop, calls=%fused_computation.52 | loop fusion | flops 262144 | bytes 2097156 | tf_op jit(solution)/shard_map/broadcast_in_dim;reshape | solution.py:164
  97.6 0.7 collective-permute-done.12
  98.4 0.8 fusion.30
  (73 shorter events, 4.1 us)
Async XLA Ops:
  0.6 45.3 %copy-start = (bf16[1,8,64,128]{3,2,1,0:T(8,128)(2,1)S(1)}, bf16[1,8,64,128]{3,2,1,0:T(8,128)(2,1)}, u32[]{:S(2)}) copy-start(bf16[1,8,64,128]{3,2,1,0:T(8,128)(2,1)} %param.22) | copy-start | bytes 393220
  0.6 5.8 %copy-start.5 = (f32[1,32]{1,0:T(1,128)S(1)}, f32[1,32]{1,0:T(1,128)}, u32[]{:S(2)}) copy-start(f32[1,32]{1,0:T(1,128)} %param.19) | copy-start | bytes 388
  0.7 8.9 %copy-start.6 = (f32[1,32]{1,0:T(1,128)S(1)}, f32[1,32]{1,0:T(1,128)}, u32[]{:S(2)}) copy-start(f32[1,32]{1,0:T(1,128)} %param.21) | copy-start | bytes 388
  0.7 9.7 %copy-start.8 = (s32[1,8]{1,0:T(1,128)S(1)}, s32[1,8]{1,0:T(1,128)}, u32[]{:S(2)}) copy-start(s32[1,8]{1,0:T(1,128)} %param.23) | copy-start | bytes 100
  2.0 12.2 %collective-permute-start.1 = (f32[33,2,32,128]{3,2,1,0:T(8,128)S(1)}, f32[33,2,32,128]{3,2,1,0:T(8,128)S(1)}, u32[]{:S(2)}, u32[]{:S(2)}) collective-permute-start(f32[33,2,32,128]{3,2,1,0:T(8,128)S(1)} %pad_maximum_fusion.3), channel_id=1, source_target_pairs={{1,0},{2,1},{3,2},{4,3},{5,4},{6,5},{7,6},{9,8},{10,9},{11,10},{12... | collective-permute-start | bytes 3244040 | tf_op jit(solution)/shard_map/ppermute | solution.py:82
  3.3 10.9 %collective-permute-start = (f32[33,2,32,128]{3,2,1,0:T(8,128)S(1)}, f32[33,2,32,128]{3,2,1,0:T(8,128)S(1)}, u32[]{:S(2)}, u32[]{:S(2)}) collective-permute-start(f32[33,2,32,128]{3,2,1,0:T(8,128)S(1)} %pad_maximum_fusion.3), channel_id=1, source_target_pairs={{0,1},{1,2},{2,3},{3,4},{4,5},{5,6},{6,7},{8,9},{9,10},{10,11},{11... | collective-permute-start | bytes 3244040 | tf_op jit(solution)/shard_map/ppermute | solution.py:79
  6.5 4.6 %collective-permute-start.5 = (f32[1,32]{1,0:T(1,128)S(1)}, f32[1,32]{1,0:T(1,128)S(1)}, u32[]{:S(2)}, u32[]{:S(2)}) collective-permute-start(f32[1,32]{1,0:T(1,128)S(1)} %copy-done.5), channel_id=1, source_target_pairs={{0,8},{8,0},{16,24},{24,16},{1,9},{9,1},{17,25},{25,17},{2,10},{10... | collective-permute-start | bytes 392 | tf_op jit(solution)/shard_map/ppermute | solution.py:44
  11.1 3.3 %copy-start.1 = (f32[1,32,2,32,128]{4,3,2,1,0:T(8,128)S(1)}, f32[1,32,2,32,128]{4,3,2,1,0:T(8,128)}, u32[]{:S(2)}) copy-start(f32[1,32,2,32,128]{4,3,2,1,0:T(8,128)} %param.15) | copy-start | bytes 3145732
  11.1 13.3 %collective-permute-start.6 = (f32[2,32]{1,0:T(2,128)S(1)}, f32[2,32]{1,0:T(2,128)S(1)}, u32[]{:S(2)}, u32[]{:S(2)}) collective-permute-start(f32[2,32]{1,0:T(2,128)S(1)} %maximum_select_fusion.4), channel_id=1, source_target_pairs={{0,16},{8,24},{16,0},{24,8},{1,17},{9,25},{17,1},{25,9},{2,18},{10... | collective-permute-start | bytes 776 | tf_op jit(solution)/shard_map/ppermute | solution.py:44
  14.4 0.8 copy-start.2
  14.4 0.8 copy-start.7
  17.6 0.8 copy-start.3
  18.4 1.9 %copy-start.4 = (f32[1,32]{1,0:T(1,128)S(1)}, f32[1,32]{1,0:T(1,128)}, u32[]{:S(2)}) copy-start(f32[1,32]{1,0:T(1,128)} %param.20) | copy-start | bytes 388
  21.3 6.6 %collective-permute-start.4 = (f32[67712]{0:T(1024)S(1)}, f32[67712]{0:T(1024)S(1)}, u32[]{:S(2)}, u32[]{:S(2)}) collective-permute-start(f32[67712]{0:T(1024)S(1)} %get-tuple-element.63), channel_id=1, source_target_pairs={{0,24},{8,0},{16,8},{24,16},{1,25},{9,1},{17,9},{25,17},{2,26},{10... | collective-permute-start | bytes 812552 | tf_op jit(solution)/shard_map/ppermute | solution.py:118
  23.4 14.4 %collective-permute-start.3 = (f32[67712]{0:T(1024)S(1)}, f32[67712]{0:T(1024)S(1)}, u32[]{:S(2)}, u32[]{:S(2)}) collective-permute-start(f32[67712]{0:T(1024)S(1)} %get-tuple-element.62), channel_id=1, source_target_pairs={{0,16},{8,24},{16,0},{24,8},{1,17},{9,25},{17,1},{25,9},{2,18},{10... | collective-permute-start | bytes 812552 | tf_op jit(solution)/shard_map/ppermute | solution.py:118
  24.4 13.5 %collective-permute-start.2 = (f32[67712]{0:T(1024)S(1)}, f32[67712]{0:T(1024)S(1)}, u32[]{:S(2)}, u32[]{:S(2)}) collective-permute-start(f32[67712]{0:T(1024)S(1)} %get-tuple-element.61), channel_id=1, source_target_pairs={{0,8},{8,16},{16,24},{24,0},{1,9},{9,17},{17,25},{25,1},{2,10},{10... | collective-permute-start | bytes 812552 | tf_op jit(solution)/shard_map/ppermute | solution.py:118
  41.7 47.9 %collective-permute-start.9 = (f32[32,2,8,128]{3,2,1,0:T(8,128)S(1)}, f32[32,2,8,128]{3,2,1,0:T(8,128)S(1)}, u32[]{:S(2)}, u32[]{:S(2)}) collective-permute-start(f32[32,2,8,128]{3,2,1,0:T(8,128)S(1)} %get-tuple-element.50), channel_id=1, source_target_pairs={{0,24},{8,0},{16,8},{24,16},{1,25},{9,1},{17,9},{25,17},{2,26},{10... | collective-permute-start | bytes 786440 | tf_op jit(solution)/shard_map/ppermute | solution.py:148
  41.8 47.8 %collective-permute-start.8 = (f32[32,2,8,128]{3,2,1,0:T(8,128)S(1)}, f32[32,2,8,128]{3,2,1,0:T(8,128)S(1)}, u32[]{:S(2)}, u32[]{:S(2)}) collective-permute-start(f32[32,2,8,128]{3,2,1,0:T(8,128)S(1)} %get-tuple-element.51), channel_id=1, source_target_pairs={{0,16},{8,24},{16,0},{24,8},{1,17},{9,25},{17,1},{25,9},{2,18},{10... | collective-permute-start | bytes 786440 | tf_op jit(solution)/shard_map/ppermute | solution.py:148
  43.8 13.1 %collective-permute-start.7 = (f32[32,2,8,128]{3,2,1,0:T(8,128)S(1)}, f32[32,2,8,128]{3,2,1,0:T(8,128)S(1)}, u32[]{:S(2)}, u32[]{:S(2)}) collective-permute-start(f32[32,2,8,128]{3,2,1,0:T(8,128)S(1)} %get-tuple-element.52), channel_id=1, source_target_pairs={{0,8},{8,16},{16,24},{24,0},{1,9},{9,17},{17,25},{25,1},{2,10},{10... | collective-permute-start | bytes 786440 | tf_op jit(solution)/shard_map/ppermute | solution.py:148
  57.0 22.0 %collective-permute-start.10 = (f32[1,9,128]{2,1,0:T(8,128)S(1)}, f32[1,9,128]{2,1,0:T(8,128)S(1)}, u32[]{:S(2)}, u32[]{:S(2)}) collective-permute-start(f32[1,9,128]{2,1,0:T(8,128)S(1)} %bitcast.156), channel_id=1, source_target_pairs={{0,1},{1,0},{2,3},{3,2},{4,5},{5,4},{6,7},{7,6},{8,9},{9,8},{10,11... | collective-permute-start | bytes 13832 | tf_op jit(solution)/shard_map/ppermute | solution.py:44
  79.0 12.3 %collective-permute-start.11 = (f32[2,9,128]{2,1,0:T(8,128)S(1)}, f32[2,9,128]{2,1,0:T(8,128)S(1)}, u32[]{:S(2)}, u32[]{:S(2)}) collective-permute-start(f32[2,9,128]{2,1,0:T(8,128)S(1)} %maximum_select_fusion.2), channel_id=1, source_target_pairs={{0,2},{1,3},{2,0},{3,1},{4,6},{5,7},{6,4},{7,5},{8,10},{9,11},{10,... | collective-permute-start | bytes 27656 | tf_op jit(solution)/shard_map/ppermute | solution.py:44
  91.3 7.0 %collective-permute-start.12 = (f32[4,9,128]{2,1,0:T(8,128)S(1)}, f32[4,9,128]{2,1,0:T(8,128)S(1)}, u32[]{:S(2)}, u32[]{:S(2)}) collective-permute-start(f32[4,9,128]{2,1,0:T(8,128)S(1)} %maximum_select_fusion.1), channel_id=1, source_target_pairs={{0,4},{1,5},{2,6},{3,7},{4,0},{5,1},{6,2},{7,3},{8,12},{9,13},{10,... | collective-permute-start | bytes 55304 | tf_op jit(solution)/shard_map/ppermute | solution.py:44

commit v19 on v15

--- a/solution.py
+++ b/solution.py
@@ -146,6 +146,7 @@
     for d in shifts:
         outgoing = lax.dynamic_index_in_dim(results, (me_s + d) % groups, 0, keepdims=False)
         back.append(lax.ppermute(outgoing, "species", [(i, (i + d) % groups) for i in range(groups)]))
+    payload, back[-1] = lax.optimization_barrier((payload, back[-1]))
     mine_slabs = jnp.take(jnp.stack(back), (me_s - jnp.arange(groups)) % groups, axis=0)
     carried = jnp.moveaxis(mine_slabs, 0, 2).reshape(own_part.shape)
     gathered = gather_all(payload, "space")

time: 103 us -> 100 us (0.971)
  waiting for transfers between devices: 34.3 us -> 22.1 us
  starting transfers between devices: 49.4 us -> 58.8 us
    ppermute x3, waiting for transfers between devices: 19.1 us -> 6.66 us  [body(): lax.ppermute(outgoing, 'species', [(i, (i + d) % groups) for i in range(g...]
    ppermute x5, starting transfers between devices: 37.2 us -> 48 us  [gather_all(): other = lax.ppermute(held, axis, [(i, i ^ span) for i in range(count)])]
    ppermute x3, starting transfers between devices: 4.67 us -> 3.33 us  [body(): lax.ppermute(outgoing, 'species', [(i, (i + d) % groups) for i in range(g...]
  transfers between devices with their start and end apart: 13 -> 13, of which waited for: 6 -> 6; matrix products, arithmetic and copies ran while one was open for 10% -> 11% of each run, Pallas kernels for 0% -> 0%
where the time goes in v19:
time: 100 us
  starting transfers between devices  58.8 us (59%)
  waiting for transfers between devices  22.1 us (22%)
  other arithmetic  9.72 us (10%)
  local copies, waits for them, and re-layouts  4.93 us (5%)
  matrix products  3.34 us (3%)
  between operations  1.1 us (1%)
    ppermute x5, starting transfers between devices, gather_all(): other = lax.ppermute(held, axis, [(i, i ^ span) for i in range(count)])  48 us
    ppermute x3, waiting for transfers between devices, body(): lax.ppermute(message((me_s + d) % groups), 'species', [(i, (i + d) % grou...  12.9 us
    ppermute x3, waiting for transfers between devices, body(): lax.ppermute(outgoing, 'species', [(i, (i + d) % groups) for i in range(g...  6.66 us
    ppermute x3, starting transfers between devices, body(): lax.ppermute(outgoing, 'species', [(i, (i + d) % groups) for i in range(g...  3.33 us
    ppermute x1, starting transfers between devices, body(): lax.ppermute(mine[:, mine.shape[1] - halo:], 'space', [(i, i + 1) for i i...  3.1 us
    ppermute x3, starting transfers between devices, body(): lax.ppermute(message((me_s + d) % groups), 'species', [(i, (i + d) % grou...  3.1 us
    add x2, other arithmetic, body(): inner + wide_factor[:, 1 + step:wide_factor.shape[1] - 1 - step] * (besid...  2.71 us
    ppermute x5, waiting for transfers between devices, gather_all(): other = lax.ppermute(held, axis, [(i, i ^ span) for i in range(count)])  2.54 us
  transfers between devices with their start and end apart: 13, of which 6 were waited for; matrix products, arithmetic and copies ran while one was open for 11% of the time, Pallas kernels for 0%

profile of v19, /device:TPU:0, one launch (start us, length us, event | category | flops | bytes accessed | tf_op | source)
XLA Modules:
  0.0 100.0 jit_solution(698810804419738213)
XLA Ops:
  0.7 1.4 %pad_maximum_fusion.3 = f32[33,2,32,128]{3,2,1,0:T(8,128)S(1)} fusion(f32[1,2,32,128]{3,2,1,0:T(8,128)} %bitcast.155, f32[32,2,32,128]{3,2,1,0:T(8,128)} %bitcast.137), kind=kLoop, calls=%fused_computation.39 | loop fusion | flops 270336 | bytes 2162688 | tf_op jit(solution)/shard_map/concatenate | solution.py:78
  2.0 1.3 %collective-permute-start.1 = (f32[33,2,32,128]{3,2,1,0:T(8,128)S(1)}, f32[33,2,32,128]{3,2,1,0:T(8,128)S(1)}, u32[]{:S(2)}, u32[]{:S(2)}) collective-permute-start(f32[33,2,32,128]{3,2,1,0:T(8,128)S(1)} %pad_maximum_fusion.3), channel_id=1, source_target_pairs={{1,0},{2,1},{3,2},{4,3},{5,4},{6,5},{7,6},{9,8},{10,9},{11,10},{12... | collective-permute-start | bytes 3244040 | tf_op jit(solution)/shard_map/ppermute | solution.py:82
  3.3 3.1 %collective-permute-start = (f32[33,2,32,128]{3,2,1,0:T(8,128)S(1)}, f32[33,2,32,128]{3,2,1,0:T(8,128)S(1)}, u32[]{:S(2)}, u32[]{:S(2)}) collective-permute-start(f32[33,2,32,128]{3,2,1,0:T(8,128)S(1)} %pad_maximum_fusion.3), channel_id=1, source_target_pairs={{0,1},{1,2},{2,3},{3,4},{4,5},{5,6},{6,7},{8,9},{9,10},{10,11},{11... | collective-permute-start | bytes 3244040 | tf_op jit(solution)/shard_map/ppermute | solution.py:79
  6.5 3.1 %collective-permute-start.5 = (f32[1,32]{1,0:T(1,128)S(1)}, f32[1,32]{1,0:T(1,128)S(1)}, u32[]{:S(2)}, u32[]{:S(2)}) collective-permute-start(f32[1,32]{1,0:T(1,128)S(1)} %copy-done.5), channel_id=1, source_target_pairs={{0,8},{8,0},{16,24},{24,16},{1,9},{9,1},{17,25},{25,17},{2,10},{10... | collective-permute-start | bytes 392 | tf_op jit(solution)/shard_map/ppermute | solution.py:44
  9.7 0.6 compare_reduce_fusion
  10.4 0.7 broadcast_select_fusion.1
  11.1 3.1 %collective-permute-start.6 = (f32[2,32]{1,0:T(2,128)S(1)}, f32[2,32]{1,0:T(2,128)S(1)}, u32[]{:S(2)}, u32[]{:S(2)}) collective-permute-start(f32[2,32]{1,0:T(2,128)S(1)} %maximum_select_fusion.4), channel_id=1, source_target_pairs={{0,16},{8,24},{16,0},{24,8},{1,17},{9,25},{17,1},{25,9},{2,18},{10... | collective-permute-start | bytes 776 | tf_op jit(solution)/shard_map/ppermute | solution.py:44
  14.6 0.5 copy-done.2
  15.1 0.4 broadcast_multiply_fusion
  15.6 2.0 %fusion.6 = f32[32,4,32,128]{3,2,1,0:T(8,128)S(1)} fusion(f32[32,4,32,128]{3,2,1,0:T(8,128)S(1)} %pad_maximum_fusion, f32[32,6,32,128]{3,2,1,0:T(8,128)S(1)} %broadcast_multiply_fusion, f32[32,2,32,128]{3,2,1,0:T(8,128)S(1)} %slice.228, f32[32,2,32,128]{3,2,1,0:T(8,128)S(1)} %bitcast.139, f32[32,2,32,128]{3,2,1,0:T(8,128)S(1)} %slice.227), kind=kLoop, calls=%fused_computation.16 | loop fusion | flops 5767168 | bytes 9437184 | tf_op jit(solution)/shard_map/add | solution.py:88
  17.6 0.7 fusion.25
  18.4 1.7 %convolution_bitcast_fusion = f32[4,8,64,128]{3,1,2,0:T(8,128)S(1)} fusion(f32[4,8,64,128]{3,2,1,0:T(8,128)S(1)} %bitcast.142, f32[1,32,32]{2,1,0:T(8,128)S(1)} %copy-done.3), kind=kOutput, calls=%fused_computation.21 | convolution fusion | flops 100663296 | bytes 2101248 | tf_op jit(solution)/shard_map/dot_general | solution.py:90
  20.3 0.5 multiply_reduce_fusion
  21.3 2.0 %collective-permute-start.4 = (f32[67712]{0:T(1024)S(1)}, f32[67712]{0:T(1024)S(1)}, u32[]{:S(2)}, u32[]{:S(2)}) collective-permute-start(f32[67712]{0:T(1024)S(1)} %get-tuple-element.63), channel_id=1, source_target_pairs={{0,24},{8,0},{16,8},{24,16},{1,25},{9,1},{17,9},{25,17},{2,26},{10... | collective-permute-start | bytes 812552 | tf_op jit(solution)/shard_map/ppermute | solution.py:118
  23.4 1.1 %collective-permute-start.3 = (f32[67712]{0:T(1024)S(1)}, f32[67712]{0:T(1024)S(1)}, u32[]{:S(2)}, u32[]{:S(2)}) collective-permute-start(f32[67712]{0:T(1024)S(1)} %get-tuple-element.62), channel_id=1, source_target_pairs={{0,16},{8,24},{16,0},{24,8},{1,17},{9,25},{17,1},{25,9},{2,18},{10... | collective-permute-start | bytes 812552 | tf_op jit(solution)/shard_map/ppermute | solution.py:118
  24.7 3.2 %collective-permute-done.4 = f32[67712]{0:T(1024)S(1)} collective-permute-done((f32[67712]{0:T(1024)S(1)}, f32[67712]{0:T(1024)S(1)}, u32[]{:S(2)}, u32[]{:S(2)}) %collective-permute-start.4) | collective-permute-done | bytes 270880 | tf_op jit(solution)/shard_map/ppermute | solution.py:118
  28.1 9.6 %collective-permute-done.3 = f32[67712]{0:T(1024)S(1)} collective-permute-done((f32[67712]{0:T(1024)S(1)}, f32[67712]{0:T(1024)S(1)}, u32[]{:S(2)}, u32[]{:S(2)}) %collective-permute-start.3) | collective-permute-done | bytes 270880 | tf_op jit(solution)/shard_map/ppermute | solution.py:118
  38.1 1.0 %pad_maximum_fusion.2 = f32[4,67712]{1,0:T(4,128)S(1)} fusion(f32[1,67712]{1,0:T(1,128)S(1)} %stack.37, f32[1,67712]{1,0:T(1,128)S(1)} %stack.36, f32[1,67712]{1,0:T(1,128)S(1)} %stack.35, f32[1,67712]{1,0:T(1,128)S(1)} %stack.34), kind=kLoop, calls=%fused_computation.38 | loop fusion | flops 812544 | bytes 2166784 | tf_op jit(solution)/shard_map/stack | solution.py:120
  39.2 1.1 %gather_fusion = f32[4,67712]{1,0:T(4,128)S(1)} fusion(f32[4,67712]{1,0:T(4,128)S(1)} %pad_maximum_fusion.2, s32[1024]{0:T(1024)S(1)} %pad_clamp_fusion), kind=kCustom, calls=%fused_computation | custom fusion | bytes 2166800 | tf_op jit(solution)/shard_map/jit(_take)/gather | solution.py:120
  40.6 0.8 fusion.46
  42.5 1.3 %collective-permute-start.8 = (f32[32,2,8,128]{3,2,1,0:T(8,128)S(1)}, f32[32,2,8,128]{3,2,1,0:T(8,128)S(1)}, u32[]{:S(2)}, u32[]{:S(2)}) collective-permute-start(f32[32,2,8,128]{3,2,1,0:T(8,128)S(1)} %get-tuple-element.51), channel_id=1, source_target_pairs={{0,16},{8,24},{16,0},{24,8},{1,17},{9,25},{17,1},{25,9},{2,18},{10... | collective-permute-start | bytes 786440 | tf_op jit(solution)/shard_map/ppermute | solution.py:148
  43.9 1.9 %collective-permute-start.7 = (f32[32,2,8,128]{3,2,1,0:T(8,128)S(1)}, f32[32,2,8,128]{3,2,1,0:T(8,128)S(1)}, u32[]{:S(2)}, u32[]{:S(2)}) collective-permute-start(f32[32,2,8,128]{3,2,1,0:T(8,128)S(1)} %get-tuple-element.52), channel_id=1, source_target_pairs={{0,8},{8,16},{16,24},{24,0},{1,9},{9,17},{17,25},{25,1},{2,10},{10... | collective-permute-start | bytes 786440 | tf_op jit(solution)/shard_map/ppermute | solution.py:148
  46.1 6.7 %collective-permute-done.9 = f32[32,2,8,128]{3,2,1,0:T(8,128)S(1)} collective-permute-done((f32[32,2,8,128]{3,2,1,0:T(8,128)S(1)}, f32[32,2,8,128]{3,2,1,0:T(8,128)S(1)}, u32[]{:S(2)}, u32[]{:S(2)}) %collective-permute-start.9) | collective-permute-done | bytes 262176 | tf_op jit(solution)/shard_map/ppermute | solution.py:148
  52.8 17.3 %collective-permute-start.10 = (f32[1,9,128]{2,1,0:T(8,128)S(1)}, f32[1,9,128]{2,1,0:T(8,128)S(1)}, u32[]{:S(2)}, u32[]{:S(2)}) collective-permute-start(f32[1,9,128]{2,1,0:T(8,128)S(1)} %bitcast.156), channel_id=1, source_target_pairs={{0,1},{1,0},{2,3},{3,2},{4,5},{5,4},{6,7},{7,6},{8,9},{9,8},{10,11... | collective-permute-start | bytes 13832 | tf_op jit(solution)/shard_map/ppermute | solution.py:44
  70.1 0.8 collective-permute-done.10
  70.9 4.7 %collective-permute-start.11 = (f32[2,9,128]{2,1,0:T(8,128)S(1)}, f32[2,9,128]{2,1,0:T(8,128)S(1)}, u32[]{:S(2)}, u32[]{:S(2)}) collective-permute-start(f32[2,9,128]{2,1,0:T(8,128)S(1)} %maximum_select_fusion.2), channel_id=1, source_target_pairs={{0,2},{1,3},{2,0},{3,1},{4,6},{5,7},{6,4},{7,5},{8,10},{9,11},{10,... | collective-permute-start | bytes 27656 | tf_op jit(solution)/shard_map/ppermute | solution.py:44
  75.7 0.6 gather_fusion.1
  76.4 1.0 collective-permute-done.11
  77.4 19.8 %collective-permute-start.12 = (f32[4,9,128]{2,1,0:T(8,128)S(1)}, f32[4,9,128]{2,1,0:T(8,128)S(1)}, u32[]{:S(2)}, u32[]{:S(2)}) collective-permute-start(f32[4,9,128]{2,1,0:T(8,128)S(1)} %maximum_select_fusion.1), channel_id=1, source_target_pairs={{0,4},{1,5},{2,6},{3,7},{4,0},{5,1},{6,2},{7,3},{8,12},{9,13},{10,... | collective-permute-start | bytes 55304 | tf_op jit(solution)/shard_map/ppermute | solution.py:44
  97.1 1.2 %copy_bitcast_fusion = f32[1,32,2,32,128]{4,3,2,1,0:T(8,128)} fusion(f32[4,32,2,8,128]{4,3,2,1,0:T(8,128)S(1)} %gather_fusion.1, pred[4]{0:T(512)(128)(4,1)S(1)} %compare_and_fusion), kind=kLoop, calls=%fused_computation.52 | loop fusion | flops 262144 | bytes 2097156 | tf_op jit(solution)/shard_map/broadcast_in_dim;reshape | solution.py:164
  98.3 0.7 collective-permute-done.12
  99.1 0.8 fusion.30
  (73 shorter events, 4.2 us)
Async XLA Ops:
  0.6 45.3 %copy-start = (bf16[1,8,64,128]{3,2,1,0:T(8,128)(2,1)S(1)}, bf16[1,8,64,128]{3,2,1,0:T(8,128)(2,1)}, u32[]{:S(2)}) copy-start(bf16[1,8,64,128]{3,2,1,0:T(8,128)(2,1)} %param.22) | copy-start | bytes 393220
  0.6 5.8 %copy-start.5 = (f32[1,32]{1,0:T(1,128)S(1)}, f32[1,32]{1,0:T(1,128)}, u32[]{:S(2)}) copy-start(f32[1,32]{1,0:T(1,128)} %param.19) | copy-start | bytes 388
  0.7 8.9 %copy-start.6 = (f32[1,32]{1,0:T(1,128)S(1)}, f32[1,32]{1,0:T(1,128)}, u32[]{:S(2)}) copy-start(f32[1,32]{1,0:T(1,128)} %param.21) | copy-start | bytes 388
  0.7 9.7 %copy-start.8 = (s32[1,8]{1,0:T(1,128)S(1)}, s32[1,8]{1,0:T(1,128)}, u32[]{:S(2)}) copy-start(s32[1,8]{1,0:T(1,128)} %param.23) | copy-start | bytes 100
  2.0 12.2 %collective-permute-start.1 = (f32[33,2,32,128]{3,2,1,0:T(8,128)S(1)}, f32[33,2,32,128]{3,2,1,0:T(8,128)S(1)}, u32[]{:S(2)}, u32[]{:S(2)}) collective-permute-start(f32[33,2,32,128]{3,2,1,0:T(8,128)S(1)} %pad_maximum_fusion.3), channel_id=1, source_target_pairs={{1,0},{2,1},{3,2},{4,3},{5,4},{6,5},{7,6},{9,8},{10,9},{11,10},{12... | collective-permute-start | bytes 3244040 | tf_op jit(solution)/shard_map/ppermute | solution.py:82
  3.3 10.9 %collective-permute-start = (f32[33,2,32,128]{3,2,1,0:T(8,128)S(1)}, f32[33,2,32,128]{3,2,1,0:T(8,128)S(1)}, u32[]{:S(2)}, u32[]{:S(2)}) collective-permute-start(f32[33,2,32,128]{3,2,1,0:T(8,128)S(1)} %pad_maximum_fusion.3), channel_id=1, source_target_pairs={{0,1},{1,2},{2,3},{3,4},{4,5},{5,6},{6,7},{8,9},{9,10},{10,11},{11... | collective-permute-start | bytes 3244040 | tf_op jit(solution)/shard_map/ppermute | solution.py:79
  6.5 4.6 %collective-permute-start.5 = (f32[1,32]{1,0:T(1,128)S(1)}, f32[1,32]{1,0:T(1,128)S(1)}, u32[]{:S(2)}, u32[]{:S(2)}) collective-permute-start(f32[1,32]{1,0:T(1,128)S(1)} %copy-done.5), channel_id=1, source_target_pairs={{0,8},{8,0},{16,24},{24,16},{1,9},{9,1},{17,25},{25,17},{2,10},{10... | collective-permute-start | bytes 392 | tf_op jit(solution)/shard_map/ppermute | solution.py:44
  11.1 3.3 %copy-start.1 = (f32[1,32,2,32,128]{4,3,2,1,0:T(8,128)S(1)}, f32[1,32,2,32,128]{4,3,2,1,0:T(8,128)}, u32[]{:S(2)}) copy-start(f32[1,32,2,32,128]{4,3,2,1,0:T(8,128)} %param.15) | copy-start | bytes 3145732
  11.1 13.3 %collective-permute-start.6 = (f32[2,32]{1,0:T(2,128)S(1)}, f32[2,32]{1,0:T(2,128)S(1)}, u32[]{:S(2)}, u32[]{:S(2)}) collective-permute-start(f32[2,32]{1,0:T(2,128)S(1)} %maximum_select_fusion.4), channel_id=1, source_target_pairs={{0,16},{8,24},{16,0},{24,8},{1,17},{9,25},{17,1},{25,9},{2,18},{10... | collective-permute-start | bytes 776 | tf_op jit(solution)/shard_map/ppermute | solution.py:44
  14.4 0.8 copy-start.2
  14.4 0.8 copy-start.7
  17.6 0.8 copy-start.3
  18.4 1.9 %copy-start.4 = (f32[1,32]{1,0:T(1,128)S(1)}, f32[1,32]{1,0:T(1,128)}, u32[]{:S(2)}) copy-start(f32[1,32]{1,0:T(1,128)} %param.20) | copy-start | bytes 388
  21.3 6.6 %collective-permute-start.4 = (f32[67712]{0:T(1024)S(1)}, f32[67712]{0:T(1024)S(1)}, u32[]{:S(2)}, u32[]{:S(2)}) collective-permute-start(f32[67712]{0:T(1024)S(1)} %get-tuple-element.63), channel_id=1, source_target_pairs={{0,24},{8,0},{16,8},{24,16},{1,25},{9,1},{17,9},{25,17},{2,26},{10... | collective-permute-start | bytes 812552 | tf_op jit(solution)/shard_map/ppermute | solution.py:118
  23.4 14.4 %collective-permute-start.3 = (f32[67712]{0:T(1024)S(1)}, f32[67712]{0:T(1024)S(1)}, u32[]{:S(2)}, u32[]{:S(2)}) collective-permute-start(f32[67712]{0:T(1024)S(1)} %get-tuple-element.62), channel_id=1, source_target_pairs={{0,16},{8,24},{16,0},{24,8},{1,17},{9,25},{17,1},{25,9},{2,18},{10... | collective-permute-start | bytes 812552 | tf_op jit(solution)/shard_map/ppermute | solution.py:118
  24.4 13.5 %collective-permute-start.2 = (f32[67712]{0:T(1024)S(1)}, f32[67712]{0:T(1024)S(1)}, u32[]{:S(2)}, u32[]{:S(2)}) collective-permute-start(f32[67712]{0:T(1024)S(1)} %get-tuple-element.61), channel_id=1, source_target_pairs={{0,8},{8,16},{16,24},{24,0},{1,9},{9,17},{17,25},{25,1},{2,10},{10... | collective-permute-start | bytes 812552 | tf_op jit(solution)/shard_map/ppermute | solution.py:118
  42.5 10.3 %collective-permute-start.9 = (f32[32,2,8,128]{3,2,1,0:T(8,128)S(1)}, f32[32,2,8,128]{3,2,1,0:T(8,128)S(1)}, u32[]{:S(2)}, u32[]{:S(2)}) collective-permute-start(f32[32,2,8,128]{3,2,1,0:T(8,128)S(1)} %get-tuple-element.50), channel_id=1, source_target_pairs={{0,24},{8,0},{16,8},{24,16},{1,25},{9,1},{17,9},{25,17},{2,26},{10... | collective-permute-start | bytes 786440 | tf_op jit(solution)/shard_map/ppermute | solution.py:148
  42.5 33.1 %collective-permute-start.8 = (f32[32,2,8,128]{3,2,1,0:T(8,128)S(1)}, f32[32,2,8,128]{3,2,1,0:T(8,128)S(1)}, u32[]{:S(2)}, u32[]{:S(2)}) collective-permute-start(f32[32,2,8,128]{3,2,1,0:T(8,128)S(1)} %get-tuple-element.51), channel_id=1, source_target_pairs={{0,16},{8,24},{16,0},{24,8},{1,17},{9,25},{17,1},{25,9},{2,18},{10... | collective-permute-start | bytes 786440 | tf_op jit(solution)/shard_map/ppermute | solution.py:148
  43.9 31.8 %collective-permute-start.7 = (f32[32,2,8,128]{3,2,1,0:T(8,128)S(1)}, f32[32,2,8,128]{3,2,1,0:T(8,128)S(1)}, u32[]{:S(2)}, u32[]{:S(2)}) collective-permute-start(f32[32,2,8,128]{3,2,1,0:T(8,128)S(1)} %get-tuple-element.52), channel_id=1, source_target_pairs={{0,8},{8,16},{16,24},{24,0},{1,9},{9,17},{17,25},{25,1},{2,10},{10... | collective-permute-start | bytes 786440 | tf_op jit(solution)/shard_map/ppermute | solution.py:148
  52.8 18.1 %collective-permute-start.10 = (f32[1,9,128]{2,1,0:T(8,128)S(1)}, f32[1,9,128]{2,1,0:T(8,128)S(1)}, u32[]{:S(2)}, u32[]{:S(2)}) collective-permute-start(f32[1,9,128]{2,1,0:T(8,128)S(1)} %bitcast.156), channel_id=1, source_target_pairs={{0,1},{1,0},{2,3},{3,2},{4,5},{5,4},{6,7},{7,6},{8,9},{9,8},{10,11... | collective-permute-start | bytes 13832 | tf_op jit(solution)/shard_map/ppermute | solution.py:44
  70.9 6.4 %collective-permute-start.11 = (f32[2,9,128]{2,1,0:T(8,128)S(1)}, f32[2,9,128]{2,1,0:T(8,128)S(1)}, u32[]{:S(2)}, u32[]{:S(2)}) collective-permute-start(f32[2,9,128]{2,1,0:T(8,128)S(1)} %maximum_select_fusion.2), channel_id=1, source_target_pairs={{0,2},{1,3},{2,0},{3,1},{4,6},{5,7},{6,4},{7,5},{8,10},{9,11},{10,... | collective-permute-start | bytes 27656 | tf_op jit(solution)/shard_map/ppermute | solution.py:44
  77.4 21.7 %collective-permute-start.12 = (f32[4,9,128]{2,1,0:T(8,128)S(1)}, f32[4,9,128]{2,1,0:T(8,128)S(1)}, u32[]{:S(2)}, u32[]{:S(2)}) collective-permute-start(f32[4,9,128]{2,1,0:T(8,128)S(1)} %maximum_select_fusion.1), channel_id=1, source_target_pairs={{0,4},{1,5},{2,6},{3,7},{4,0},{5,1},{6,2},{7,3},{8,12},{9,13},{10,... | collective-permute-start | bytes 55304 | tf_op jit(solution)/shard_map/ppermute | solution.py:44

commit v20 on v7

--- a/solution.py
+++ b/solution.py
@@ -74,13 +74,15 @@
     factor = rate * space_factor[None]
     halo = SUBSTEPS
     count = lax.axis_size("space")
-    mine = jnp.concatenate([field, space_factor[None]], axis=0)
-    from_left = lax.ppermute(
-        mine[:, mine.shape[1] - halo:], "space", [(i, i + 1) for i in range(count - 1)]
-    )
-    from_right = lax.ppermute(mine[:, :halo], "space", [(i + 1, i) for i in range(count - 1)])
-    wide = jnp.concatenate([from_left[:bins], field, from_right[:bins]], axis=1)
-    wide_factor = rate * jnp.concatenate([from_left[bins], space_factor, from_right[bins]], axis=0)[None]
+    right_pairs = [(i, i + 1) for i in range(count - 1)]
+    left_pairs = [(i + 1, i) for i in range(count - 1)]
+    layers = field.shape[1]
+    from_left = lax.ppermute(field[:, layers - halo:], "space", right_pairs)
+    from_right = lax.ppermute(field[:, :halo], "space", left_pairs)
+    factor_left = lax.ppermute(space_factor[layers - halo:], "space", right_pairs)
+    factor_right = lax.ppermute(space_factor[:halo], "space", left_pairs)
+    wide = jnp.concatenate([from_left, field, from_right], axis=1)
+    wide_factor = rate * jnp.concatenate([factor_left, space_factor, factor_right], axis=0)[None]
     for step in range(SUBSTEPS):
         inner = wide[:, 1:-1]
         beside = wide[:, 2:] + wide[:, :-2] + cross_sum(inner)

time: 96.9 us -> 96.4 us (level)
  waiting for transfers between devices: 64.3 us -> 54.9 us
  starting transfers between devices: 17.2 us -> 22.9 us
  local copies, waits for them, and re-layouts: 1.6 us -> 4.82 us
    ppermute x2 -> x4, waiting for transfers between devices: 20.4 us -> 11.3 us  [the longest x1 10.7 us: body(): factor_right = lax.ppermute(space_factor[:halo], 'space', left_pairs)]
    ppermute x2 -> x4, starting transfers between devices: 5.56 us -> 11.3 us  [the longest x1 3.64 us: body(): factor_right = lax.ppermute(space_factor[:halo], 'space', left_pairs)]
    mul x4, local copies, waits for them, and re-layouts: 0.22 us -> 2.84 us  [body(): pieces[c] = pieces[c] + scales[c] * arrived]
    scatter x2, local copies, waits for them, and re-layouts: 0.16 us -> 1.42 us  [body(): jnp.zeros((2, cols), jnp.float32).at[0, :bins].set(chain).at[1, :bins]]
  transfers between devices with their start and end apart: 19 -> 21, of which waited for: 11 -> 11; matrix products, arithmetic and copies ran while one was open for 5% -> 11% of each run, Pallas kernels for 0% -> 0%
where the time goes in v20:
time: 96.4 us; the launch traced here: 95.9 us
  waiting for transfers between devices  54.9 us (57%)
  starting transfers between devices  22.9 us (24%)
  other arithmetic  8.82 us (9%)
  local copies, waits for them, and re-layouts  4.82 us (5%)
  matrix products  3.35 us (3%)
  between operations  1.12 us (1%)
    ppermute x12, waiting for transfers between devices, body(): arrived = lax.ppermute(pieces[c], 'species', [(s, s + 1)])  32.7 us
    ppermute x1, waiting for transfers between devices, body(): factor_right = lax.ppermute(space_factor[:halo], 'space', left_pairs)  10.7 us
    ppermute x12, starting transfers between devices, body(): arrived = lax.ppermute(pieces[c], 'species', [(s, s + 1)])  10.6 us
    ppermute x3, waiting for transfers between devices, gather_all(): other = lax.ppermute(held, axis, [(i, i ^ span) for i in range(count)])  5.74 us
    ppermute x2, waiting for transfers between devices, body(): lax.ppermute(everyone, 'species', [(i, i ^ span) for i in range(groups)])  5.13 us
    ppermute x1, starting transfers between devices, body(): factor_right = lax.ppermute(space_factor[:halo], 'space', left_pairs)  3.64 us
    ppermute x1, starting transfers between devices, body(): from_right = lax.ppermute(field[:, :halo], 'space', left_pairs)  3.64 us
    mul x4, local copies, waits for them, and re-layouts, body(): pieces[c] = pieces[c] + scales[c] * arrived  2.84 us
  transfers between devices with their start and end apart: 21, of which 11 were waited for; matrix products, arithmetic and copies ran while one was open for 11% of the time, Pallas kernels for 0%

profile of v20, /device:TPU:26, one launch (start us, length us, event | category | flops | bytes accessed | tf_op | source)
XLA Modules:
  0.0 95.9 jit_solution(11947192363439085241)
XLA Ops:
  0.7 2.1 %collective-permute-start = (f32[32,2,32,128]{3,2,1,0:T(8,128)}, f32[32,2,32,128]{3,2,1,0:T(8,128)S(1)}, u32[]{:S(2)}, u32[]{:S(2)}) collective-permute-start(f32[32,2,32,128]{3,2,1,0:T(8,128)} %bitcast.111), channel_id=1, source_target_pairs={{0,1},{1,2},{2,3},{3,4},{4,5},{5,6},{6,7},{8,9},{9,10},{10,11},{11... | collective-permute-start | bytes 3145736 | tf_op jit(solution)/shard_map/ppermute | solution.py:80
  2.7 3.6 %collective-permute-start.1 = (f32[32,2,32,128]{3,2,1,0:T(8,128)}, f32[32,2,32,128]{3,2,1,0:T(8,128)S(1)}, u32[]{:S(2)}, u32[]{:S(2)}) collective-permute-start(f32[32,2,32,128]{3,2,1,0:T(8,128)} %bitcast.112), channel_id=1, source_target_pairs={{1,0},{2,1},{3,2},{4,3},{5,4},{6,5},{7,6},{9,8},{10,9},{11,10},{12... | collective-permute-start | bytes 3145736 | tf_op jit(solution)/shard_map/ppermute | solution.py:81
  6.4 1.9 %collective-permute-start.2 = (f32[2,32,128]{2,1,0:T(8,128)}, f32[2,32,128]{2,1,0:T(8,128)S(1)}, u32[]{:S(2)}, u32[]{:S(2)}) collective-permute-start(f32[2,32,128]{2,1,0:T(8,128)} %param.16), channel_id=1, source_target_pairs={{0,1},{1,2},{2,3},{3,4},{4,5},{5,6},{6,7},{8,9},{9,10},{10,11},{11... | collective-permute-start | bytes 98312 | tf_op jit(solution)/shard_map/ppermute | solution.py:82
  8.3 3.6 %collective-permute-start.3 = (f32[2,32,128]{2,1,0:T(8,128)}, f32[2,32,128]{2,1,0:T(8,128)S(1)}, u32[]{:S(2)}, u32[]{:S(2)}) collective-permute-start(f32[2,32,128]{2,1,0:T(8,128)} %param.16), channel_id=1, source_target_pairs={{1,0},{2,1},{3,2},{4,3},{5,4},{6,5},{7,6},{9,8},{10,9},{11,10},{12... | collective-permute-start | bytes 98312 | tf_op jit(solution)/shard_map/ppermute | solution.py:83
  12.6 0.7 slice_bitcast_fusion.15
  13.3 0.7 slice_bitcast_fusion.14
  14.1 0.7 slice_bitcast_fusion.13
  15.4 0.8 scatter.11
  17.5 10.7 %collective-permute-done.3 = f32[2,32,128]{2,1,0:T(8,128)S(1)} collective-permute-done((f32[2,32,128]{2,1,0:T(8,128)}, f32[2,32,128]{2,1,0:T(8,128)S(1)}, u32[]{:S(2)}, u32[]{:S(2)}) %collective-permute-start.3) | collective-permute-done | bytes 32800 | tf_op jit(solution)/shard_map/ppermute | solution.py:83
  28.2 0.8 pad_maximum_fusion.2
  28.9 1.1 %broadcast_multiply_fusion = f32[32,6,32,128]{3,2,1,0:T(8,128)S(1)} fusion(f32[6,32,128]{2,1,0:T(8,128)S(1)} %pad_maximum_fusion.2, f32[32]{0:T(128)} %bitcast.121), kind=kLoop, calls=%fused_computation.18 | loop fusion | flops 786432 | bytes 3244160 | tf_op jit(solution)/shard_map/mul | solution.py:85
  30.2 1.9 %fusion.6 = f32[32,4,32,128]{3,2,1,0:T(8,128)S(1)} fusion(f32[32,4,32,128]{3,2,1,0:T(8,128)S(1)} %pad_maximum_fusion, f32[32,6,32,128]{3,2,1,0:T(8,128)S(1)} %broadcast_multiply_fusion, f32[32,2,32,128]{3,2,1,0:T(8,128)S(1)} %collective-permute-done.1, f32[32,2,32,128]{3,2,1,0:T(8,128)S(1)} %bitcast.114, f32[32,2,32,128]{3,2,1,0:T(8,128)S(1)} %collective-permute-done), kind=kLoop, calls=%fused_computation.14 | loop fusion | flops 5767168 | bytes 9437184 | tf_op jit(solution)/shard_map/add | solution.py:89
  32.3 0.7 fusion.25
  33.0 1.7 %convolution_bitcast_fusion = f32[4,8,64,128]{3,1,2,0:T(8,128)S(1)} fusion(f32[4,8,64,128]{3,2,1,0:T(8,128)S(1)} %bitcast.115, f32[1,32,32]{2,1,0:T(8,128)S(1)} %copy-done.2), kind=kOutput, calls=%fused_computation.19 | convolution fusion | flops 100663296 | bytes 2101248 | tf_op jit(solution)/shard_map/dot_general | solution.py:91
  36.7 2.7 %collective-permute-done.4 = f32[1,34,64]{2,1,0:T(8,128)S(1)} collective-permute-done((f32[1,34,64]{2,1,0:T(8,128)S(1)}, f32[1,34,64]{2,1,0:T(8,128)S(1)}, u32[]{:S(2)}, u32[]{:S(2)}) %collective-permute-start.4) | collective-permute-done | bytes 8736 | tf_op jit(solution)/shard_map/ppermute | solution.py:108
  39.9 0.7 collective-permute-start.15
  42.0 0.7 collective-permute-start.11
  42.7 2.5 %collective-permute-done.14 = f32[2,34,64]{2,1,0:T(8,128)S(1)} collective-permute-done((f32[2,34,64]{2,1,0:T(8,128)S(1)}, f32[2,34,64]{2,1,0:T(8,128)S(1)}, u32[]{:S(2)}, u32[]{:S(2)}) %collective-permute-start.14) | collective-permute-done | bytes 17440 | tf_op jit(solution)/shard_map/ppermute | solution.py:108
  47.9 0.7 collective-permute-start.12
  49.0 1.3 %collective-permute-start.7 = (f32[5,2,32,128]{3,2,1,0:T(8,128)S(1)}, f32[5,2,32,128]{3,2,1,0:T(8,128)S(1)}, u32[]{:S(2)}, u32[]{:S(2)}) collective-permute-start(f32[5,2,32,128]{3,2,1,0:T(8,128)S(1)} %multiply_add_fusion.10), channel_id=1, source_target_pairs={{16,24},{17,25},{18,26},{19,27},{20,28},{21,29},{22,30},{23,31}} | collective-permute-start | bytes 491528 | tf_op jit(solution)/shard_map/ppermute | solution.py:145
  50.3 2.3 %collective-permute-done.19 = f32[2,9,128]{2,1,0:T(8,128)S(1)} collective-permute-done((f32[2,9,128]{2,1,0:T(8,128)S(1)}, f32[2,9,128]{2,1,0:T(8,128)S(1)}, u32[]{:S(2)}, u32[]{:S(2)}) %collective-permute-start.19) | collective-permute-done | bytes 9248 | tf_op jit(solution)/shard_map/ppermute | solution.py:44
  52.8 0.7 collective-permute-start.16
  53.5 3.1 %collective-permute-done.20 = f32[4,9,128]{2,1,0:T(8,128)S(1)} collective-permute-done((f32[4,9,128]{2,1,0:T(8,128)S(1)}, f32[4,9,128]{2,1,0:T(8,128)S(1)}, u32[]{:S(2)}, u32[]{:S(2)}) %collective-permute-start.20) | collective-permute-done | bytes 18464 | tf_op jit(solution)/shard_map/ppermute | solution.py:44
  56.7 0.8 fusion.30
  57.6 1.3 %collective-permute-start.10 = (f32[7,2,32,128]{3,2,1,0:T(8,128)S(1)}, f32[7,2,32,128]{3,2,1,0:T(8,128)S(1)}, u32[]{:S(2)}, u32[]{:S(2)}) collective-permute-start(f32[7,2,32,128]{3,2,1,0:T(8,128)S(1)} %multiply_add_fusion.7), channel_id=1, source_target_pairs={{16,24},{17,25},{18,26},{19,27},{20,28},{21,29},{22,30},{23,31}} | collective-permute-start | bytes 688136 | tf_op jit(solution)/shard_map/ppermute | solution.py:145
  58.9 10.1 %collective-permute-done.7 = f32[5,2,32,128]{3,2,1,0:T(8,128)S(1)} collective-permute-done((f32[5,2,32,128]{3,2,1,0:T(8,128)S(1)}, f32[5,2,32,128]{3,2,1,0:T(8,128)S(1)}, u32[]{:S(2)}, u32[]{:S(2)}) %collective-permute-start.7) | collective-permute-done | bytes 163872 | tf_op jit(solution)/shard_map/ppermute | solution.py:145
  69.2 1.3 %collective-permute-start.13 = (f32[9,2,32,128]{3,2,1,0:T(8,128)S(1)}, f32[9,2,32,128]{3,2,1,0:T(8,128)S(1)}, u32[]{:S(2)}, u32[]{:S(2)}) collective-permute-start(f32[9,2,32,128]{3,2,1,0:T(8,128)S(1)} %multiply_add_fusion.4), channel_id=1, source_target_pairs={{16,24},{17,25},{18,26},{19,27},{20,28},{21,29},{22,30},{23,31}} | collective-permute-start | bytes 884744 | tf_op jit(solution)/shard_map/ppermute | solution.py:145
  70.7 1.3 %collective-permute-start.17 = (f32[11,2,32,128]{3,2,1,0:T(8,128)S(1)}, f32[11,2,32,128]{3,2,1,0:T(8,128)S(1)}, u32[]{:S(2)}, u32[]{:S(2)}) collective-permute-start(f32[11,2,32,128]{3,2,1,0:T(8,128)S(1)} %multiply_add_fusion.1), channel_id=1, source_target_pairs={{16,24},{17,25},{18,26},{19,27},{20,28},{21,29},{22,30},{23,31}} | collective-permute-start | bytes 1081352 | tf_op jit(solution)/shard_map/ppermute | solution.py:145
  72.0 4.1 %collective-permute-done.10 = f32[7,2,32,128]{3,2,1,0:T(8,128)S(1)} collective-permute-done((f32[7,2,32,128]{3,2,1,0:T(8,128)S(1)}, f32[7,2,32,128]{3,2,1,0:T(8,128)S(1)}, u32[]{:S(2)}, u32[]{:S(2)}) %collective-permute-start.10) | collective-permute-done | bytes 229408 | tf_op jit(solution)/shard_map/ppermute | solution.py:145
  76.2 9.4 %collective-permute-done.13 = f32[9,2,32,128]{3,2,1,0:T(8,128)S(1)} collective-permute-done((f32[9,2,32,128]{3,2,1,0:T(8,128)S(1)}, f32[9,2,32,128]{3,2,1,0:T(8,128)S(1)}, u32[]{:S(2)}, u32[]{:S(2)}) %collective-permute-start.13) | collective-permute-done | bytes 294944 | tf_op jit(solution)/shard_map/ppermute | solution.py:145
  85.7 9.0 %collective-permute-done.17 = f32[11,2,32,128]{3,2,1,0:T(8,128)S(1)} collective-permute-done((f32[11,2,32,128]{3,2,1,0:T(8,128)S(1)}, f32[11,2,32,128]{3,2,1,0:T(8,128)S(1)}, u32[]{:S(2)}, u32[]{:S(2)}) %collective-permute-start.17) | collective-permute-done | bytes 360480 | tf_op jit(solution)/shard_map/ppermute | solution.py:145
  94.8 1.1 %maximum_bitcast_fusion = f32[1,32,2,32,128]{4,3,2,1,0:T(8,128)} fusion(f32[11,2,32,128]{3,2,1,0:T(8,128)S(1)} %multiply_add_fusion, f32[9,2,32,128]{3,2,1,0:T(8,128)S(1)} %multiply_add_fusion.3, f32[7,2,32,128]{3,2,1,0:T(8,128)S(1)} %multiply_add_fusion.6, f32[5,2,32,128]{3,2,1,0:T(8,128)S(1)} %multiply_add_fusion.9), kind=kLoop, calls=%fused_computation.46 | loop fusion | flops 786432 | bytes 2097152 | tf_op jit(solution)/shard_map/broadcast_in_dim | solution.py:162
  (73 shorter events, 10.6 us)
Async XLA Ops:
  0.6 45.3 %copy-start = (bf16[1,8,64,128]{3,2,1,0:T(8,128)(2,1)S(1)}, bf16[1,8,64,128]{3,2,1,0:T(8,128)(2,1)}, u32[]{:S(2)}) copy-start(bf16[1,8,64,128]{3,2,1,0:T(8,128)(2,1)} %param.22) | copy-start | bytes 393220
  0.6 29.4 %copy-start.1 = (f32[1,32,2,32,128]{4,3,2,1,0:T(8,128)S(1)}, f32[1,32,2,32,128]{4,3,2,1,0:T(8,128)}, u32[]{:S(2)}) copy-start(f32[1,32,2,32,128]{4,3,2,1,0:T(8,128)} %param.15) | copy-start | bytes 3145732
  0.7 29.4 %collective-permute-start = (f32[32,2,32,128]{3,2,1,0:T(8,128)}, f32[32,2,32,128]{3,2,1,0:T(8,128)S(1)}, u32[]{:S(2)}, u32[]{:S(2)}) collective-permute-start(f32[32,2,32,128]{3,2,1,0:T(8,128)} %bitcast.111), channel_id=1, source_target_pairs={{0,1},{1,2},{2,3},{3,4},{4,5},{5,6},{6,7},{8,9},{9,10},{10,11},{11... | collective-permute-start | bytes 3145736 | tf_op jit(solution)/shard_map/ppermute | solution.py:80
  2.7 27.3 %collective-permute-start.1 = (f32[32,2,32,128]{3,2,1,0:T(8,128)}, f32[32,2,32,128]{3,2,1,0:T(8,128)S(1)}, u32[]{:S(2)}, u32[]{:S(2)}) collective-permute-start(f32[32,2,32,128]{3,2,1,0:T(8,128)} %bitcast.112), channel_id=1, source_target_pairs={{1,0},{2,1},{3,2},{4,3},{5,4},{6,5},{7,6},{9,8},{10,9},{11,10},{12... | collective-permute-start | bytes 3145736 | tf_op jit(solution)/shard_map/ppermute | solution.py:81
  6.4 11.1 %collective-permute-start.2 = (f32[2,32,128]{2,1,0:T(8,128)}, f32[2,32,128]{2,1,0:T(8,128)S(1)}, u32[]{:S(2)}, u32[]{:S(2)}) collective-permute-start(f32[2,32,128]{2,1,0:T(8,128)} %param.16), channel_id=1, source_target_pairs={{0,1},{1,2},{2,3},{3,4},{4,5},{5,6},{6,7},{8,9},{9,10},{10,11},{11... | collective-permute-start | bytes 98312 | tf_op jit(solution)/shard_map/ppermute | solution.py:82
  8.3 19.9 %collective-permute-start.3 = (f32[2,32,128]{2,1,0:T(8,128)}, f32[2,32,128]{2,1,0:T(8,128)S(1)}, u32[]{:S(2)}, u32[]{:S(2)}) collective-permute-start(f32[2,32,128]{2,1,0:T(8,128)} %param.16), channel_id=1, source_target_pairs={{1,0},{2,1},{3,2},{4,3},{5,4},{6,5},{7,6},{9,8},{10,9},{11,10},{12... | collective-permute-start | bytes 98312 | tf_op jit(solution)/shard_map/ppermute | solution.py:83
  32.3 0.8 copy-start.2
  33.0 1.9 %copy-start.3 = (f32[1,32]{1,0:T(1,128)S(1)}, f32[1,32]{1,0:T(1,128)}, u32[]{:S(2)}) copy-start(f32[1,32]{1,0:T(1,128)} %param.20) | copy-start | bytes 388
  34.7 1.3 %copy-start.4 = (s32[1,8]{1,0:T(1,128)S(1)}, s32[1,8]{1,0:T(1,128)}, u32[]{:S(2)}) copy-start(s32[1,8]{1,0:T(1,128)} %param.23) | copy-start | bytes 100
  35.5 3.8 %collective-permute-start.4 = (f32[1,34,64]{2,1,0:T(8,128)S(1)}, f32[1,34,64]{2,1,0:T(8,128)S(1)}, u32[]{:S(2)}, u32[]{:S(2)}) collective-permute-start(f32[1,34,64]{2,1,0:T(8,128)S(1)} %maximum_bitcast_fusion.1), channel_id=1, source_target_pairs={{0,8},{8,0},{16,24},{24,16},{1,9},{9,1},{17,25},{25,17},{2,10},{10... | collective-permute-start | bytes 26120 | tf_op jit(solution)/shard_map/ppermute | solution.py:108
  39.4 5.7 %collective-permute-start.14 = (f32[2,34,64]{2,1,0:T(8,128)S(1)}, f32[2,34,64]{2,1,0:T(8,128)S(1)}, u32[]{:S(2)}, u32[]{:S(2)}) collective-permute-start(f32[2,34,64]{2,1,0:T(8,128)S(1)} %maximum_select_fusion.2), channel_id=1, source_target_pairs={{0,16},{8,24},{16,0},{24,8},{1,17},{9,25},{17,1},{25,9},{2,18},{10... | collective-permute-start | bytes 52232 | tf_op jit(solution)/shard_map/ppermute | solution.py:108
  39.9 7.8 %collective-permute-start.15 = (f32[11,2,32,128]{3,2,1,0:T(8,128)S(1)}, f32[11,2,32,128]{3,2,1,0:T(8,128)S(1)}, u32[]{:S(2)}, u32[]{:S(2)}) collective-permute-start(f32[11,2,32,128]{3,2,1,0:T(8,128)S(1)} %slice.184), channel_id=1, source_target_pairs={{0,8},{1,9},{2,10},{3,11},{4,12},{5,13},{6,14},{7,15}} | collective-permute-start | bytes 1081352 | tf_op jit(solution)/shard_map/ppermute | solution.py:145
  40.6 5.5 %collective-permute-start.5 = (f32[5,2,32,128]{3,2,1,0:T(8,128)S(1)}, f32[5,2,32,128]{3,2,1,0:T(8,128)S(1)}, u32[]{:S(2)}, u32[]{:S(2)}) collective-permute-start(f32[5,2,32,128]{3,2,1,0:T(8,128)S(1)} %slice.178), channel_id=1, source_target_pairs={{0,8},{1,9},{2,10},{3,11},{4,12},{5,13},{6,14},{7,15}} | collective-permute-start | bytes 491528 | tf_op jit(solution)/shard_map/ppermute | solution.py:145
  41.3 5.6 %collective-permute-start.8 = (f32[7,2,32,128]{3,2,1,0:T(8,128)S(1)}, f32[7,2,32,128]{3,2,1,0:T(8,128)S(1)}, u32[]{:S(2)}, u32[]{:S(2)}) collective-permute-start(f32[7,2,32,128]{3,2,1,0:T(8,128)S(1)} %slice.180), channel_id=1, source_target_pairs={{0,8},{1,9},{2,10},{3,11},{4,12},{5,13},{6,14},{7,15}} | collective-permute-start | bytes 688136 | tf_op jit(solution)/shard_map/ppermute | solution.py:145
  42.0 5.9 %collective-permute-start.11 = (f32[9,2,32,128]{3,2,1,0:T(8,128)S(1)}, f32[9,2,32,128]{3,2,1,0:T(8,128)S(1)}, u32[]{:S(2)}, u32[]{:S(2)}) collective-permute-start(f32[9,2,32,128]{3,2,1,0:T(8,128)S(1)} %slice.182), channel_id=1, source_target_pairs={{0,8},{1,9},{2,10},{3,11},{4,12},{5,13},{6,14},{7,15}} | collective-permute-start | bytes 884744 | tf_op jit(solution)/shard_map/ppermute | solution.py:145
  46.2 2.7 %collective-permute-start.6 = (f32[5,2,32,128]{3,2,1,0:T(8,128)S(1)}, f32[5,2,32,128]{3,2,1,0:T(8,128)S(1)}, u32[]{:S(2)}, u32[]{:S(2)}) collective-permute-start(f32[5,2,32,128]{3,2,1,0:T(8,128)S(1)} %multiply_add_fusion.11), channel_id=1, source_target_pairs={{8,16},{9,17},{10,18},{11,19},{12,20},{13,21},{14,22},{15,23}} | collective-permute-start | bytes 491528 | tf_op jit(solution)/shard_map/ppermute | solution.py:145
  47.0 10.5 %collective-permute-start.9 = (f32[7,2,32,128]{3,2,1,0:T(8,128)S(1)}, f32[7,2,32,128]{3,2,1,0:T(8,128)S(1)}, u32[]{:S(2)}, u32[]{:S(2)}) collective-permute-start(f32[7,2,32,128]{3,2,1,0:T(8,128)S(1)} %multiply_add_fusion.8), channel_id=1, source_target_pairs={{8,16},{9,17},{10,18},{11,19},{12,20},{13,21},{14,22},{15,23}} | collective-permute-start | bytes 688136 | tf_op jit(solution)/shard_map/ppermute | solution.py:145
  47.7 1.2 %collective-permute-start.18 = (f32[1,9,128]{2,1,0:T(8,128)S(1)}, f32[1,9,128]{2,1,0:T(8,128)S(1)}, u32[]{:S(2)}, u32[]{:S(2)}) collective-permute-start(f32[1,9,128]{2,1,0:T(8,128)S(1)} %bitcast.117), channel_id=1, source_target_pairs={{0,1},{1,0},{2,3},{3,2},{4,5},{5,4},{6,7},{7,6},{8,9},{9,8},{10,11... | collective-permute-start | bytes 13832 | tf_op jit(solution)/shard_map/ppermute | solution.py:44
  47.9 21.2 %collective-permute-start.12 = (f32[9,2,32,128]{3,2,1,0:T(8,128)S(1)}, f32[9,2,32,128]{3,2,1,0:T(8,128)S(1)}, u32[]{:S(2)}, u32[]{:S(2)}) collective-permute-start(f32[9,2,32,128]{3,2,1,0:T(8,128)S(1)} %multiply_add_fusion.5), channel_id=1, source_target_pairs={{8,16},{9,17},{10,18},{11,19},{12,20},{13,21},{14,22},{15,23}} | collective-permute-start | bytes 884744 | tf_op jit(solution)/shard_map/ppermute | solution.py:145
  48.9 3.7 %collective-permute-start.19 = (f32[2,9,128]{2,1,0:T(8,128)S(1)}, f32[2,9,128]{2,1,0:T(8,128)S(1)}, u32[]{:S(2)}, u32[]{:S(2)}) collective-permute-start(f32[2,9,128]{2,1,0:T(8,128)S(1)} %maximum_select_fusion.4), channel_id=1, source_target_pairs={{0,2},{1,3},{2,0},{3,1},{4,6},{5,7},{6,4},{7,5},{8,10},{9,11},{10,... | collective-permute-start | bytes 27656 | tf_op jit(solution)/shard_map/ppermute | solution.py:44
  49.0 20.0 %collective-permute-start.7 = (f32[5,2,32,128]{3,2,1,0:T(8,128)S(1)}, f32[5,2,32,128]{3,2,1,0:T(8,128)S(1)}, u32[]{:S(2)}, u32[]{:S(2)}) collective-permute-start(f32[5,2,32,128]{3,2,1,0:T(8,128)S(1)} %multiply_add_fusion.10), channel_id=1, source_target_pairs={{16,24},{17,25},{18,26},{19,27},{20,28},{21,29},{22,30},{23,31}} | collective-permute-start | bytes 491528 | tf_op jit(solution)/shard_map/ppermute | solution.py:145
  52.7 3.9 %collective-permute-start.20 = (f32[4,9,128]{2,1,0:T(8,128)S(1)}, f32[4,9,128]{2,1,0:T(8,128)S(1)}, u32[]{:S(2)}, u32[]{:S(2)}) collective-permute-start(f32[4,9,128]{2,1,0:T(8,128)S(1)} %maximum_select_fusion.3), channel_id=1, source_target_pairs={{0,4},{1,5},{2,6},{3,7},{4,0},{5,1},{6,2},{7,3},{8,12},{9,13},{10,... | collective-permute-start | bytes 55304 | tf_op jit(solution)/shard_map/ppermute | solution.py:44
  52.8 17.7 %collective-permute-start.16 = (f32[11,2,32,128]{3,2,1,0:T(8,128)S(1)}, f32[11,2,32,128]{3,2,1,0:T(8,128)S(1)}, u32[]{:S(2)}, u32[]{:S(2)}) collective-permute-start(f32[11,2,32,128]{3,2,1,0:T(8,128)S(1)} %multiply_add_fusion.2), channel_id=1, source_target_pairs={{8,16},{9,17},{10,18},{11,19},{12,20},{13,21},{14,22},{15,23}} | collective-permute-start | bytes 1081352 | tf_op jit(solution)/shard_map/ppermute | solution.py:145
  57.6 18.5 %collective-permute-start.10 = (f32[7,2,32,128]{3,2,1,0:T(8,128)S(1)}, f32[7,2,32,128]{3,2,1,0:T(8,128)S(1)}, u32[]{:S(2)}, u32[]{:S(2)}) collective-permute-start(f32[7,2,32,128]{3,2,1,0:T(8,128)S(1)} %multiply_add_fusion.7), channel_id=1, source_target_pairs={{16,24},{17,25},{18,26},{19,27},{20,28},{21,29},{22,30},{23,31}} | collective-permute-start | bytes 688136 | tf_op jit(solution)/shard_map/ppermute | solution.py:145
  69.2 16.4 %collective-permute-start.13 = (f32[9,2,32,128]{3,2,1,0:T(8,128)S(1)}, f32[9,2,32,128]{3,2,1,0:T(8,128)S(1)}, u32[]{:S(2)}, u32[]{:S(2)}) collective-permute-start(f32[9,2,32,128]{3,2,1,0:T(8,128)S(1)} %multiply_add_fusion.4), channel_id=1, source_target_pairs={{16,24},{17,25},{18,26},{19,27},{20,28},{21,29},{22,30},{23,31}} | collective-permute-start | bytes 884744 | tf_op jit(solution)/shard_map/ppermute | solution.py:145
  70.7 24.0 %collective-permute-start.17 = (f32[11,2,32,128]{3,2,1,0:T(8,128)S(1)}, f32[11,2,32,128]{3,2,1,0:T(8,128)S(1)}, u32[]{:S(2)}, u32[]{:S(2)}) collective-permute-start(f32[11,2,32,128]{3,2,1,0:T(8,128)S(1)} %multiply_add_fusion.1), channel_id=1, source_target_pairs={{16,24},{17,25},{18,26},{19,27},{20,28},{21,29},{22,30},{23,31}} | collective-permute-start | bytes 1081352 | tf_op jit(solution)/shard_map/ppermute | solution.py:145

commit v21 on v20

--- a/solution.py
+++ b/solution.py
@@ -146,7 +146,9 @@
                 if s == 0 and c == CHUNKS - 1:
                     payload, arrived = lax.optimization_barrier((payload, arrived))
                 pieces[c] = pieces[c] + scales[c] * arrived
-    carried = jnp.concatenate(pieces, axis=0)
+    carried = own_part
+    for c in range(CHUNKS):
+        carried = lax.dynamic_update_slice_in_dim(carried, pieces[c], bounds[c], axis=0)
     gathered = gather_all(payload, "space")
     mine = lax.axis_index("space") * rows + jnp.arange(rows, dtype=jnp.int32)
     onehot = (

time: 96.4 us -> 105 us (1.089)
  waiting for transfers between devices: 54.9 us -> 63.3 us
  other arithmetic: 8.82 us -> 7.75 us
    ppermute x12, waiting for transfers between devices: 32.7 us -> 41.1 us  [body(): arrived = lax.ppermute(pieces[c], 'species', [(s, s + 1)])]
    broadcast_in_dim x1 -> x0, other arithmetic: 1.09 us -> none  [body(): return (carried[None], sky)]
  transfers between devices with their start and end apart: 21 -> 21, of which waited for: 11 -> 11; matrix products, arithmetic and copies ran while one was open for 11% -> 10% of each run, Pallas kernels for 0% -> 0%
where the time goes in v21:
time: 105 us; the launch traced here: 104 us
  waiting for transfers between devices  63.3 us (60%)
  starting transfers between devices  22.9 us (22%)
  other arithmetic  7.75 us (7%)
  local copies, waits for them, and re-layouts  5.78 us (6%)
  matrix products  3.36 us (3%)
  between operations  1.12 us (1%)
    ppermute x12, waiting for transfers between devices, body(): arrived = lax.ppermute(pieces[c], 'species', [(s, s + 1)])  41.1 us
    ppermute x1, waiting for transfers between devices, body(): factor_right = lax.ppermute(space_factor[:halo], 'space', left_pairs)  10.7 us
    ppermute x12, starting transfers between devices, body(): arrived = lax.ppermute(pieces[c], 'species', [(s, s + 1)])  10.6 us
    ppermute x3, waiting for transfers between devices, gather_all(): other = lax.ppermute(held, axis, [(i, i ^ span) for i in range(count)])  5.74 us
    ppermute x2, waiting for transfers between devices, body(): lax.ppermute(everyone, 'species', [(i, i ^ span) for i in range(groups)])  5.13 us
    ppermute x1, starting transfers between devices, body(): factor_right = lax.ppermute(space_factor[:halo], 'space', left_pairs)  3.64 us
    ppermute x1, starting transfers between devices, body(): from_right = lax.ppermute(field[:, :halo], 'space', left_pairs)  3.64 us
    mul x4, local copies, waits for them, and re-layouts, body(): pieces[c] = pieces[c] + scales[c] * arrived  2.84 us
  transfers between devices with their start and end apart: 21, of which 11 were waited for; matrix products, arithmetic and copies ran while one was open for 10% of the time, Pallas kernels for 0%

profile of v21, /device:TPU:26, one launch (start us, length us, event | category | flops | bytes accessed | tf_op | source)
XLA Modules:
  0.0 104.2 jit_solution(8767328025405355051)
XLA Ops:
  0.7 2.1 %collective-permute-start = (f32[32,2,32,128]{3,2,1,0:T(8,128)}, f32[32,2,32,128]{3,2,1,0:T(8,128)S(1)}, u32[]{:S(2)}, u32[]{:S(2)}) collective-permute-start(f32[32,2,32,128]{3,2,1,0:T(8,128)} %bitcast.119), channel_id=1, source_target_pairs={{0,1},{1,2},{2,3},{3,4},{4,5},{5,6},{6,7},{8,9},{9,10},{10,11},{11... | collective-permute-start | bytes 3145736 | tf_op jit(solution)/shard_map/ppermute | solution.py:80
  2.7 3.6 %collective-permute-start.1 = (f32[32,2,32,128]{3,2,1,0:T(8,128)}, f32[32,2,32,128]{3,2,1,0:T(8,128)S(1)}, u32[]{:S(2)}, u32[]{:S(2)}) collective-permute-start(f32[32,2,32,128]{3,2,1,0:T(8,128)} %bitcast.120), channel_id=1, source_target_pairs={{1,0},{2,1},{3,2},{4,3},{5,4},{6,5},{7,6},{9,8},{10,9},{11,10},{12... | collective-permute-start | bytes 3145736 | tf_op jit(solution)/shard_map/ppermute | solution.py:81
  6.4 1.9 %collective-permute-start.2 = (f32[2,32,128]{2,1,0:T(8,128)}, f32[2,32,128]{2,1,0:T(8,128)S(1)}, u32[]{:S(2)}, u32[]{:S(2)}) collective-permute-start(f32[2,32,128]{2,1,0:T(8,128)} %param.16), channel_id=1, source_target_pairs={{0,1},{1,2},{2,3},{3,4},{4,5},{5,6},{6,7},{8,9},{9,10},{10,11},{11... | collective-permute-start | bytes 98312 | tf_op jit(solution)/shard_map/ppermute | solution.py:82
  8.3 3.6 %collective-permute-start.3 = (f32[2,32,128]{2,1,0:T(8,128)}, f32[2,32,128]{2,1,0:T(8,128)S(1)}, u32[]{:S(2)}, u32[]{:S(2)}) collective-permute-start(f32[2,32,128]{2,1,0:T(8,128)} %param.16), channel_id=1, source_target_pairs={{1,0},{2,1},{3,2},{4,3},{5,4},{6,5},{7,6},{9,8},{10,9},{11,10},{12... | collective-permute-start | bytes 98312 | tf_op jit(solution)/shard_map/ppermute | solution.py:83
  11.9 0.7 slice_bitcast_fusion.13
  12.7 0.7 slice_bitcast_fusion.14
  13.4 0.7 slice_bitcast_fusion.15
  15.4 0.8 scatter.11
  17.5 10.7 %collective-permute-done.3 = f32[2,32,128]{2,1,0:T(8,128)S(1)} collective-permute-done((f32[2,32,128]{2,1,0:T(8,128)}, f32[2,32,128]{2,1,0:T(8,128)S(1)}, u32[]{:S(2)}, u32[]{:S(2)}) %collective-permute-start.3) | collective-permute-done | bytes 32800 | tf_op jit(solution)/shard_map/ppermute | solution.py:83
  28.2 0.8 pad_maximum_fusion.2
  28.9 1.1 %broadcast_multiply_fusion = f32[32,6,32,128]{3,2,1,0:T(8,128)S(1)} fusion(f32[6,32,128]{2,1,0:T(8,128)S(1)} %pad_maximum_fusion.2, f32[32]{0:T(128)} %bitcast.129), kind=kLoop, calls=%fused_computation.18 | loop fusion | flops 786432 | bytes 3244160 | tf_op jit(solution)/shard_map/mul | solution.py:85
  30.2 1.9 %fusion.6 = f32[32,4,32,128]{3,2,1,0:T(8,128)S(1)} fusion(f32[32,4,32,128]{3,2,1,0:T(8,128)S(1)} %pad_maximum_fusion, f32[32,6,32,128]{3,2,1,0:T(8,128)S(1)} %broadcast_multiply_fusion, f32[32,2,32,128]{3,2,1,0:T(8,128)S(1)} %collective-permute-done.1, f32[32,2,32,128]{3,2,1,0:T(8,128)S(1)} %bitcast.122, f32[32,2,32,128]{3,2,1,0:T(8,128)S(1)} %collective-permute-done), kind=kLoop, calls=%fused_computation.14 | loop fusion | flops 5767168 | bytes 9437184 | tf_op jit(solution)/shard_map/add | solution.py:89
  32.3 0.7 fusion.25
  33.0 1.7 %convolution_bitcast_fusion = f32[4,8,64,128]{3,1,2,0:T(8,128)S(1)} fusion(f32[4,8,64,128]{3,2,1,0:T(8,128)S(1)} %bitcast.123, f32[1,32,32]{2,1,0:T(8,128)S(1)} %copy-done.3), kind=kOutput, calls=%fused_computation.19 | convolution fusion | flops 100663296 | bytes 2101248 | tf_op jit(solution)/shard_map/dot_general | solution.py:91
  36.7 2.7 %collective-permute-done.4 = f32[1,34,64]{2,1,0:T(8,128)S(1)} collective-permute-done((f32[1,34,64]{2,1,0:T(8,128)S(1)}, f32[1,34,64]{2,1,0:T(8,128)S(1)}, u32[]{:S(2)}, u32[]{:S(2)}) %collective-permute-start.4) | collective-permute-done | bytes 8736 | tf_op jit(solution)/shard_map/ppermute | solution.py:108
  39.9 0.7 collective-permute-start.15
  40.6 0.7 collective-permute-start.11
  42.7 2.5 %collective-permute-done.14 = f32[2,34,64]{2,1,0:T(8,128)S(1)} collective-permute-done((f32[2,34,64]{2,1,0:T(8,128)S(1)}, f32[2,34,64]{2,1,0:T(8,128)S(1)}, u32[]{:S(2)}, u32[]{:S(2)}) %collective-permute-start.14) | collective-permute-done | bytes 17440 | tf_op jit(solution)/shard_map/ppermute | solution.py:108
  47.9 0.7 collective-permute-start.12
  49.0 1.3 %collective-permute-start.7 = (f32[5,2,32,128]{3,2,1,0:T(8,128)S(1)}, f32[5,2,32,128]{3,2,1,0:T(8,128)S(1)}, u32[]{:S(2)}, u32[]{:S(2)}) collective-permute-start(f32[5,2,32,128]{3,2,1,0:T(8,128)S(1)} %multiply_add_fusion.6), channel_id=1, source_target_pairs={{16,24},{17,25},{18,26},{19,27},{20,28},{21,29},{22,30},{23,31}} | collective-permute-start | bytes 491528 | tf_op jit(solution)/shard_map/ppermute | solution.py:145
  50.3 2.3 %collective-permute-done.19 = f32[2,9,128]{2,1,0:T(8,128)S(1)} collective-permute-done((f32[2,9,128]{2,1,0:T(8,128)S(1)}, f32[2,9,128]{2,1,0:T(8,128)S(1)}, u32[]{:S(2)}, u32[]{:S(2)}) %collective-permute-start.19) | collective-permute-done | bytes 9248 | tf_op jit(solution)/shard_map/ppermute | solution.py:44
  52.8 0.7 collective-permute-start.16
  53.5 3.1 %collective-permute-done.20 = f32[4,9,128]{2,1,0:T(8,128)S(1)} collective-permute-done((f32[4,9,128]{2,1,0:T(8,128)S(1)}, f32[4,9,128]{2,1,0:T(8,128)S(1)}, u32[]{:S(2)}, u32[]{:S(2)}) %collective-permute-start.20) | collective-permute-done | bytes 18464 | tf_op jit(solution)/shard_map/ppermute | solution.py:44
  56.7 0.8 fusion.30
  57.6 1.3 %collective-permute-start.10 = (f32[7,2,32,128]{3,2,1,0:T(8,128)S(1)}, f32[7,2,32,128]{3,2,1,0:T(8,128)S(1)}, u32[]{:S(2)}, u32[]{:S(2)}) collective-permute-start(f32[7,2,32,128]{3,2,1,0:T(8,128)S(1)} %multiply_add_fusion.4), channel_id=1, source_target_pairs={{16,24},{17,25},{18,26},{19,27},{20,28},{21,29},{22,30},{23,31}} | collective-permute-start | bytes 688136 | tf_op jit(solution)/shard_map/ppermute | solution.py:145
  58.9 22.4 %collective-permute-done.7 = f32[5,2,32,128]{3,2,1,0:T(8,128)S(1)} collective-permute-done((f32[5,2,32,128]{3,2,1,0:T(8,128)S(1)}, f32[5,2,32,128]{3,2,1,0:T(8,128)S(1)}, u32[]{:S(2)}, u32[]{:S(2)}) %collective-permute-start.7) | collective-permute-done | bytes 163872 | tf_op jit(solution)/shard_map/ppermute | solution.py:145
  81.6 1.3 %collective-permute-start.13 = (f32[9,2,32,128]{3,2,1,0:T(8,128)S(1)}, f32[9,2,32,128]{3,2,1,0:T(8,128)S(1)}, u32[]{:S(2)}, u32[]{:S(2)}) collective-permute-start(f32[9,2,32,128]{3,2,1,0:T(8,128)S(1)} %multiply_add_fusion.2), channel_id=1, source_target_pairs={{16,24},{17,25},{18,26},{19,27},{20,28},{21,29},{22,30},{23,31}} | collective-permute-start | bytes 884744 | tf_op jit(solution)/shard_map/ppermute | solution.py:145
  83.0 1.3 %collective-permute-start.17 = (f32[11,2,32,128]{3,2,1,0:T(8,128)S(1)}, f32[11,2,32,128]{3,2,1,0:T(8,128)S(1)}, u32[]{:S(2)}, u32[]{:S(2)}) collective-permute-start(f32[11,2,32,128]{3,2,1,0:T(8,128)S(1)} %multiply_add_fusion), channel_id=1, source_target_pairs={{16,24},{17,25},{18,26},{19,27},{20,28},{21,29},{22,30},{23,31}} | collective-permute-start | bytes 1081352 | tf_op jit(solution)/shard_map/ppermute | solution.py:145
  84.3 4.8 %collective-permute-done.10 = f32[7,2,32,128]{3,2,1,0:T(8,128)S(1)} collective-permute-done((f32[7,2,32,128]{3,2,1,0:T(8,128)S(1)}, f32[7,2,32,128]{3,2,1,0:T(8,128)S(1)}, u32[]{:S(2)}, u32[]{:S(2)}) %collective-permute-start.10) | collective-permute-done | bytes 229408 | tf_op jit(solution)/shard_map/ppermute | solution.py:145
  89.2 5.5 %collective-permute-done.13 = f32[9,2,32,128]{3,2,1,0:T(8,128)S(1)} collective-permute-done((f32[9,2,32,128]{3,2,1,0:T(8,128)S(1)}, f32[9,2,32,128]{3,2,1,0:T(8,128)S(1)}, u32[]{:S(2)}, u32[]{:S(2)}) %collective-permute-start.13) | collective-permute-done | bytes 294944 | tf_op jit(solution)/shard_map/ppermute | solution.py:145
  94.8 8.3 %collective-permute-done.17 = f32[11,2,32,128]{3,2,1,0:T(8,128)S(1)} collective-permute-done((f32[11,2,32,128]{3,2,1,0:T(8,128)S(1)}, f32[11,2,32,128]{3,2,1,0:T(8,128)S(1)}, u32[]{:S(2)}, u32[]{:S(2)}) %collective-permute-start.17) | collective-permute-done | bytes 360480 | tf_op jit(solution)/shard_map/ppermute | solution.py:145
  103.2 1.0 copy-done.1
  (74 shorter events, 10.7 us)
Async XLA Ops:
  0.6 45.3 %copy-start = (bf16[1,8,64,128]{3,2,1,0:T(8,128)(2,1)S(1)}, bf16[1,8,64,128]{3,2,1,0:T(8,128)(2,1)}, u32[]{:S(2)}) copy-start(bf16[1,8,64,128]{3,2,1,0:T(8,128)(2,1)} %param.22) | copy-start | bytes 393220
  0.6 29.4 %copy-start.2 = (f32[1,32,2,32,128]{4,3,2,1,0:T(8,128)S(1)}, f32[1,32,2,32,128]{4,3,2,1,0:T(8,128)}, u32[]{:S(2)}) copy-start(f32[1,32,2,32,128]{4,3,2,1,0:T(8,128)} %param.15) | copy-start | bytes 3145732
  0.7 29.4 %collective-permute-start = (f32[32,2,32,128]{3,2,1,0:T(8,128)}, f32[32,2,32,128]{3,2,1,0:T(8,128)S(1)}, u32[]{:S(2)}, u32[]{:S(2)}) collective-permute-start(f32[32,2,32,128]{3,2,1,0:T(8,128)} %bitcast.119), channel_id=1, source_target_pairs={{0,1},{1,2},{2,3},{3,4},{4,5},{5,6},{6,7},{8,9},{9,10},{10,11},{11... | collective-permute-start | bytes 3145736 | tf_op jit(solution)/shard_map/ppermute | solution.py:80
  2.7 27.3 %collective-permute-start.1 = (f32[32,2,32,128]{3,2,1,0:T(8,128)}, f32[32,2,32,128]{3,2,1,0:T(8,128)S(1)}, u32[]{:S(2)}, u32[]{:S(2)}) collective-permute-start(f32[32,2,32,128]{3,2,1,0:T(8,128)} %bitcast.120), channel_id=1, source_target_pairs={{1,0},{2,1},{3,2},{4,3},{5,4},{6,5},{7,6},{9,8},{10,9},{11,10},{12... | collective-permute-start | bytes 3145736 | tf_op jit(solution)/shard_map/ppermute | solution.py:81
  6.4 11.1 %collective-permute-start.2 = (f32[2,32,128]{2,1,0:T(8,128)}, f32[2,32,128]{2,1,0:T(8,128)S(1)}, u32[]{:S(2)}, u32[]{:S(2)}) collective-permute-start(f32[2,32,128]{2,1,0:T(8,128)} %param.16), channel_id=1, source_target_pairs={{0,1},{1,2},{2,3},{3,4},{4,5},{5,6},{6,7},{8,9},{9,10},{10,11},{11... | collective-permute-start | bytes 98312 | tf_op jit(solution)/shard_map/ppermute | solution.py:82
  8.3 19.9 %collective-permute-start.3 = (f32[2,32,128]{2,1,0:T(8,128)}, f32[2,32,128]{2,1,0:T(8,128)S(1)}, u32[]{:S(2)}, u32[]{:S(2)}) collective-permute-start(f32[2,32,128]{2,1,0:T(8,128)} %param.16), channel_id=1, source_target_pairs={{1,0},{2,1},{3,2},{4,3},{5,4},{6,5},{7,6},{9,8},{10,9},{11,10},{12... | collective-permute-start | bytes 98312 | tf_op jit(solution)/shard_map/ppermute | solution.py:83
  32.3 0.8 copy-start.3
  33.0 1.9 %copy-start.4 = (f32[1,32]{1,0:T(1,128)S(1)}, f32[1,32]{1,0:T(1,128)}, u32[]{:S(2)}) copy-start(f32[1,32]{1,0:T(1,128)} %param.20) | copy-start | bytes 388
  34.7 1.3 %copy-start.5 = (s32[1,8]{1,0:T(1,128)S(1)}, s32[1,8]{1,0:T(1,128)}, u32[]{:S(2)}) copy-start(s32[1,8]{1,0:T(1,128)} %param.23) | copy-start | bytes 100
  35.5 3.8 %collective-permute-start.4 = (f32[1,34,64]{2,1,0:T(8,128)S(1)}, f32[1,34,64]{2,1,0:T(8,128)S(1)}, u32[]{:S(2)}, u32[]{:S(2)}) collective-permute-start(f32[1,34,64]{2,1,0:T(8,128)S(1)} %maximum_bitcast_fusion), channel_id=1, source_target_pairs={{0,8},{8,0},{16,24},{24,16},{1,9},{9,1},{17,25},{25,17},{2,10},{10... | collective-permute-start | bytes 26120 | tf_op jit(solution)/shard_map/ppermute | solution.py:108
  39.4 5.7 %collective-permute-start.14 = (f32[2,34,64]{2,1,0:T(8,128)S(1)}, f32[2,34,64]{2,1,0:T(8,128)S(1)}, u32[]{:S(2)}, u32[]{:S(2)}) collective-permute-start(f32[2,34,64]{2,1,0:T(8,128)S(1)} %maximum_select_fusion.2), channel_id=1, source_target_pairs={{0,16},{8,24},{16,0},{24,8},{1,17},{9,25},{17,1},{25,9},{2,18},{10... | collective-permute-start | bytes 52232 | tf_op jit(solution)/shard_map/ppermute | solution.py:108
  39.9 7.8 %collective-permute-start.15 = (f32[11,2,32,128]{3,2,1,0:T(8,128)S(1)}, f32[11,2,32,128]{3,2,1,0:T(8,128)S(1)}, u32[]{:S(2)}, u32[]{:S(2)}) collective-permute-start(f32[11,2,32,128]{3,2,1,0:T(8,128)S(1)} %slice.184), channel_id=1, source_target_pairs={{0,8},{1,9},{2,10},{3,11},{4,12},{5,13},{6,14},{7,15}} | collective-permute-start | bytes 1081352 | tf_op jit(solution)/shard_map/ppermute | solution.py:145
  40.6 7.2 %collective-permute-start.11 = (f32[9,2,32,128]{3,2,1,0:T(8,128)S(1)}, f32[9,2,32,128]{3,2,1,0:T(8,128)S(1)}, u32[]{:S(2)}, u32[]{:S(2)}) collective-permute-start(f32[9,2,32,128]{3,2,1,0:T(8,128)S(1)} %slice.182), channel_id=1, source_target_pairs={{0,8},{1,9},{2,10},{3,11},{4,12},{5,13},{6,14},{7,15}} | collective-permute-start | bytes 884744 | tf_op jit(solution)/shard_map/ppermute | solution.py:145
  41.3 5.6 %collective-permute-start.8 = (f32[7,2,32,128]{3,2,1,0:T(8,128)S(1)}, f32[7,2,32,128]{3,2,1,0:T(8,128)S(1)}, u32[]{:S(2)}, u32[]{:S(2)}) collective-permute-start(f32[7,2,32,128]{3,2,1,0:T(8,128)S(1)} %slice.180), channel_id=1, source_target_pairs={{0,8},{1,9},{2,10},{3,11},{4,12},{5,13},{6,14},{7,15}} | collective-permute-start | bytes 688136 | tf_op jit(solution)/shard_map/ppermute | solution.py:145
  42.0 4.1 %collective-permute-start.5 = (f32[5,2,32,128]{3,2,1,0:T(8,128)S(1)}, f32[5,2,32,128]{3,2,1,0:T(8,128)S(1)}, u32[]{:S(2)}, u32[]{:S(2)}) collective-permute-start(f32[5,2,32,128]{3,2,1,0:T(8,128)S(1)} %slice.178), channel_id=1, source_target_pairs={{0,8},{1,9},{2,10},{3,11},{4,12},{5,13},{6,14},{7,15}} | collective-permute-start | bytes 491528 | tf_op jit(solution)/shard_map/ppermute | solution.py:145
  46.2 2.7 %collective-permute-start.6 = (f32[5,2,32,128]{3,2,1,0:T(8,128)S(1)}, f32[5,2,32,128]{3,2,1,0:T(8,128)S(1)}, u32[]{:S(2)}, u32[]{:S(2)}) collective-permute-start(f32[5,2,32,128]{3,2,1,0:T(8,128)S(1)} %multiply_add_fusion.7), channel_id=1, source_target_pairs={{8,16},{9,17},{10,18},{11,19},{12,20},{13,21},{14,22},{15,23}} | collective-permute-start | bytes 491528 | tf_op jit(solution)/shard_map/ppermute | solution.py:145
  47.0 10.5 %collective-permute-start.9 = (f32[7,2,32,128]{3,2,1,0:T(8,128)S(1)}, f32[7,2,32,128]{3,2,1,0:T(8,128)S(1)}, u32[]{:S(2)}, u32[]{:S(2)}) collective-permute-start(f32[7,2,32,128]{3,2,1,0:T(8,128)S(1)} %multiply_add_fusion.5), channel_id=1, source_target_pairs={{8,16},{9,17},{10,18},{11,19},{12,20},{13,21},{14,22},{15,23}} | collective-permute-start | bytes 688136 | tf_op jit(solution)/shard_map/ppermute | solution.py:145
  47.7 1.2 %collective-permute-start.18 = (f32[1,9,128]{2,1,0:T(8,128)S(1)}, f32[1,9,128]{2,1,0:T(8,128)S(1)}, u32[]{:S(2)}, u32[]{:S(2)}) collective-permute-start(f32[1,9,128]{2,1,0:T(8,128)S(1)} %bitcast.125), channel_id=1, source_target_pairs={{0,1},{1,0},{2,3},{3,2},{4,5},{5,4},{6,7},{7,6},{8,9},{9,8},{10,11... | collective-permute-start | bytes 13832 | tf_op jit(solution)/shard_map/ppermute | solution.py:44
  47.9 33.5 %collective-permute-start.12 = (f32[9,2,32,128]{3,2,1,0:T(8,128)S(1)}, f32[9,2,32,128]{3,2,1,0:T(8,128)S(1)}, u32[]{:S(2)}, u32[]{:S(2)}) collective-permute-start(f32[9,2,32,128]{3,2,1,0:T(8,128)S(1)} %multiply_add_fusion.3), channel_id=1, source_target_pairs={{8,16},{9,17},{10,18},{11,19},{12,20},{13,21},{14,22},{15,23}} | collective-permute-start | bytes 884744 | tf_op jit(solution)/shard_map/ppermute | solution.py:145
  48.9 3.7 %collective-permute-start.19 = (f32[2,9,128]{2,1,0:T(8,128)S(1)}, f32[2,9,128]{2,1,0:T(8,128)S(1)}, u32[]{:S(2)}, u32[]{:S(2)}) collective-permute-start(f32[2,9,128]{2,1,0:T(8,128)S(1)} %maximum_select_fusion.4), channel_id=1, source_target_pairs={{0,2},{1,3},{2,0},{3,1},{4,6},{5,7},{6,4},{7,5},{8,10},{9,11},{10,... | collective-permute-start | bytes 27656 | tf_op jit(solution)/shard_map/ppermute | solution.py:44
  49.0 32.3 %collective-permute-start.7 = (f32[5,2,32,128]{3,2,1,0:T(8,128)S(1)}, f32[5,2,32,128]{3,2,1,0:T(8,128)S(1)}, u32[]{:S(2)}, u32[]{:S(2)}) collective-permute-start(f32[5,2,32,128]{3,2,1,0:T(8,128)S(1)} %multiply_add_fusion.6), channel_id=1, source_target_pairs={{16,24},{17,25},{18,26},{19,27},{20,28},{21,29},{22,30},{23,31}} | collective-permute-start | bytes 491528 | tf_op jit(solution)/shard_map/ppermute | solution.py:145
  52.7 3.9 %collective-permute-start.20 = (f32[4,9,128]{2,1,0:T(8,128)S(1)}, f32[4,9,128]{2,1,0:T(8,128)S(1)}, u32[]{:S(2)}, u32[]{:S(2)}) collective-permute-start(f32[4,9,128]{2,1,0:T(8,128)S(1)} %maximum_select_fusion.3), channel_id=1, source_target_pairs={{0,4},{1,5},{2,6},{3,7},{4,0},{5,1},{6,2},{7,3},{8,12},{9,13},{10,... | collective-permute-start | bytes 55304 | tf_op jit(solution)/shard_map/ppermute | solution.py:44
  52.8 30.1 %collective-permute-start.16 = (f32[11,2,32,128]{3,2,1,0:T(8,128)S(1)}, f32[11,2,32,128]{3,2,1,0:T(8,128)S(1)}, u32[]{:S(2)}, u32[]{:S(2)}) collective-permute-start(f32[11,2,32,128]{3,2,1,0:T(8,128)S(1)} %multiply_add_fusion.1), channel_id=1, source_target_pairs={{8,16},{9,17},{10,18},{11,19},{12,20},{13,21},{14,22},{15,23}} | collective-permute-start | bytes 1081352 | tf_op jit(solution)/shard_map/ppermute | solution.py:145
  57.6 31.5 %collective-permute-start.10 = (f32[7,2,32,128]{3,2,1,0:T(8,128)S(1)}, f32[7,2,32,128]{3,2,1,0:T(8,128)S(1)}, u32[]{:S(2)}, u32[]{:S(2)}) collective-permute-start(f32[7,2,32,128]{3,2,1,0:T(8,128)S(1)} %multiply_add_fusion.4), channel_id=1, source_target_pairs={{16,24},{17,25},{18,26},{19,27},{20,28},{21,29},{22,30},{23,31}} | collective-permute-start | bytes 688136 | tf_op jit(solution)/shard_map/ppermute | solution.py:145
  81.6 13.2 %collective-permute-start.13 = (f32[9,2,32,128]{3,2,1,0:T(8,128)S(1)}, f32[9,2,32,128]{3,2,1,0:T(8,128)S(1)}, u32[]{:S(2)}, u32[]{:S(2)}) collective-permute-start(f32[9,2,32,128]{3,2,1,0:T(8,128)S(1)} %multiply_add_fusion.2), channel_id=1, source_target_pairs={{16,24},{17,25},{18,26},{19,27},{20,28},{21,29},{22,30},{23,31}} | collective-permute-start | bytes 884744 | tf_op jit(solution)/shard_map/ppermute | solution.py:145
  83.0 20.1 %collective-permute-start.17 = (f32[11,2,32,128]{3,2,1,0:T(8,128)S(1)}, f32[11,2,32,128]{3,2,1,0:T(8,128)S(1)}, u32[]{:S(2)}, u32[]{:S(2)}) collective-permute-start(f32[11,2,32,128]{3,2,1,0:T(8,128)S(1)} %multiply_add_fusion), channel_id=1, source_target_pairs={{16,24},{17,25},{18,26},{19,27},{20,28},{21,29},{22,30},{23,31}} | collective-permute-start | bytes 1081352 | tf_op jit(solution)/shard_map/ppermute | solution.py:145
  103.2 1.0 copy-start.1

commit v22 on v20

--- a/solution.py
+++ b/solution.py
@@ -91,7 +91,7 @@
     solved = jnp.dot(
         loss_inverse[0],
         field.reshape(bins, -1),
-        precision=HIGH,
+        precision=lax.Precision.HIGH,
         preferred_element_type=jnp.float32,
     ).reshape(field.shape)
     chain = chain_yield[0]

time: 96.4 us -> 95.9 us (level)
  no operation moved by 1% of the time
where the time goes in v22:
time: 95.9 us; the launch traced here: 95.4 us
  waiting for transfers between devices  54.9 us (57%)
  starting transfers between devices  22.9 us (24%)
  other arithmetic  8.82 us (9%)
  local copies, waits for them, and re-layouts  4.82 us (5%)
  matrix products  2.84 us (3%)
  between operations  1.11 us (1%)
    ppermute x12, waiting for transfers between devices, body(): arrived = lax.ppermute(pieces[c], 'species', [(s, s + 1)])  32.7 us
    ppermute x1, waiting for transfers between devices, body(): factor_right = lax.ppermute(space_factor[:halo], 'space', left_pairs)  10.7 us
    ppermute x12, starting transfers between devices, body(): arrived = lax.ppermute(pieces[c], 'species', [(s, s + 1)])  10.6 us
    ppermute x3, waiting for transfers between devices, gather_all(): other = lax.ppermute(held, axis, [(i, i ^ span) for i in range(count)])  5.74 us
    ppermute x2, waiting for transfers between devices, body(): lax.ppermute(everyone, 'species', [(i, i ^ span) for i in range(groups)])  5.13 us
    ppermute x1, starting transfers between devices, body(): factor_right = lax.ppermute(space_factor[:halo], 'space', left_pairs)  3.64 us
    ppermute x1, starting transfers between devices, body(): from_right = lax.ppermute(field[:, :halo], 'space', left_pairs)  3.64 us
    mul x4, local copies, waits for them, and re-layouts, body(): pieces[c] = pieces[c] + scales[c] * arrived  2.84 us
  transfers between devices with their start and end apart: 21, of which 11 were waited for; matrix products, arithmetic and copies ran while one was open for 11% of the time, Pallas kernels for 0%

profile of v22, /device:TPU:26, one launch (start us, length us, event | category | flops | bytes accessed | tf_op | source)
XLA Modules:
  0.0 95.4 jit_solution(202192907400221744)
XLA Ops:
  0.7 2.1 %collective-permute-start = (f32[32,2,32,128]{3,2,1,0:T(8,128)}, f32[32,2,32,128]{3,2,1,0:T(8,128)S(1)}, u32[]{:S(2)}, u32[]{:S(2)}) collective-permute-start(f32[32,2,32,128]{3,2,1,0:T(8,128)} %bitcast.111), channel_id=1, source_target_pairs={{0,1},{1,2},{2,3},{3,4},{4,5},{5,6},{6,7},{8,9},{9,10},{10,11},{11... | collective-permute-start | bytes 3145736 | tf_op jit(solution)/shard_map/ppermute | solution.py:80
  2.7 3.6 %collective-permute-start.1 = (f32[32,2,32,128]{3,2,1,0:T(8,128)}, f32[32,2,32,128]{3,2,1,0:T(8,128)S(1)}, u32[]{:S(2)}, u32[]{:S(2)}) collective-permute-start(f32[32,2,32,128]{3,2,1,0:T(8,128)} %bitcast.112), channel_id=1, source_target_pairs={{1,0},{2,1},{3,2},{4,3},{5,4},{6,5},{7,6},{9,8},{10,9},{11,10},{12... | collective-permute-start | bytes 3145736 | tf_op jit(solution)/shard_map/ppermute | solution.py:81
  6.4 1.9 %collective-permute-start.2 = (f32[2,32,128]{2,1,0:T(8,128)}, f32[2,32,128]{2,1,0:T(8,128)S(1)}, u32[]{:S(2)}, u32[]{:S(2)}) collective-permute-start(f32[2,32,128]{2,1,0:T(8,128)} %param.16), channel_id=1, source_target_pairs={{0,1},{1,2},{2,3},{3,4},{4,5},{5,6},{6,7},{8,9},{9,10},{10,11},{11... | collective-permute-start | bytes 98312 | tf_op jit(solution)/shard_map/ppermute | solution.py:82
  8.3 3.6 %collective-permute-start.3 = (f32[2,32,128]{2,1,0:T(8,128)}, f32[2,32,128]{2,1,0:T(8,128)S(1)}, u32[]{:S(2)}, u32[]{:S(2)}) collective-permute-start(f32[2,32,128]{2,1,0:T(8,128)} %param.16), channel_id=1, source_target_pairs={{1,0},{2,1},{3,2},{4,3},{5,4},{6,5},{7,6},{9,8},{10,9},{11,10},{12... | collective-permute-start | bytes 98312 | tf_op jit(solution)/shard_map/ppermute | solution.py:83
  12.6 0.7 slice_bitcast_fusion.15
  13.3 0.7 slice_bitcast_fusion.14
  14.1 0.7 slice_bitcast_fusion.13
  15.4 0.8 scatter.11
  17.5 10.7 %collective-permute-done.3 = f32[2,32,128]{2,1,0:T(8,128)S(1)} collective-permute-done((f32[2,32,128]{2,1,0:T(8,128)}, f32[2,32,128]{2,1,0:T(8,128)S(1)}, u32[]{:S(2)}, u32[]{:S(2)}) %collective-permute-start.3) | collective-permute-done | bytes 32800 | tf_op jit(solution)/shard_map/ppermute | solution.py:83
  28.2 0.8 pad_maximum_fusion.2
  28.9 1.1 %broadcast_multiply_fusion = f32[32,6,32,128]{3,2,1,0:T(8,128)S(1)} fusion(f32[6,32,128]{2,1,0:T(8,128)S(1)} %pad_maximum_fusion.2, f32[32]{0:T(128)} %bitcast.121), kind=kLoop, calls=%fused_computation.18 | loop fusion | flops 786432 | bytes 3244160 | tf_op jit(solution)/shard_map/mul | solution.py:85
  30.2 1.9 %fusion.6 = f32[32,4,32,128]{3,2,1,0:T(8,128)S(1)} fusion(f32[32,4,32,128]{3,2,1,0:T(8,128)S(1)} %pad_maximum_fusion, f32[32,6,32,128]{3,2,1,0:T(8,128)S(1)} %broadcast_multiply_fusion, f32[32,2,32,128]{3,2,1,0:T(8,128)S(1)} %collective-permute-done.1, f32[32,2,32,128]{3,2,1,0:T(8,128)S(1)} %bitcast.114, f32[32,2,32,128]{3,2,1,0:T(8,128)S(1)} %collective-permute-done), kind=kLoop, calls=%fused_computation.14 | loop fusion | flops 5767168 | bytes 9437184 | tf_op jit(solution)/shard_map/add | solution.py:89
  32.3 0.7 fusion.25
  33.0 1.2 %convolution_bitcast_fusion = f32[4,8,64,128]{3,1,2,0:T(8,128)S(1)} fusion(f32[4,8,64,128]{3,2,1,0:T(8,128)S(1)} %bitcast.115, f32[1,32,32]{2,1,0:T(8,128)S(1)} %copy-done.2), kind=kOutput, calls=%fused_computation.19 | convolution fusion | flops 50331648 | bytes 2101248 | tf_op jit(solution)/shard_map/dot_general | solution.py:91
  36.2 2.7 %collective-permute-done.4 = f32[1,34,64]{2,1,0:T(8,128)S(1)} collective-permute-done((f32[1,34,64]{2,1,0:T(8,128)S(1)}, f32[1,34,64]{2,1,0:T(8,128)S(1)}, u32[]{:S(2)}, u32[]{:S(2)}) %collective-permute-start.4) | collective-permute-done | bytes 8736 | tf_op jit(solution)/shard_map/ppermute | solution.py:108
  39.4 0.7 collective-permute-start.15
  41.4 0.7 collective-permute-start.11
  42.1 2.5 %collective-permute-done.14 = f32[2,34,64]{2,1,0:T(8,128)S(1)} collective-permute-done((f32[2,34,64]{2,1,0:T(8,128)S(1)}, f32[2,34,64]{2,1,0:T(8,128)S(1)}, u32[]{:S(2)}, u32[]{:S(2)}) %collective-permute-start.14) | collective-permute-done | bytes 17440 | tf_op jit(solution)/shard_map/ppermute | solution.py:108
  47.4 0.7 collective-permute-start.12
  48.5 1.3 %collective-permute-start.7 = (f32[5,2,32,128]{3,2,1,0:T(8,128)S(1)}, f32[5,2,32,128]{3,2,1,0:T(8,128)S(1)}, u32[]{:S(2)}, u32[]{:S(2)}) collective-permute-start(f32[5,2,32,128]{3,2,1,0:T(8,128)S(1)} %multiply_add_fusion.10), channel_id=1, source_target_pairs={{16,24},{17,25},{18,26},{19,27},{20,28},{21,29},{22,30},{23,31}} | collective-permute-start | bytes 491528 | tf_op jit(solution)/shard_map/ppermute | solution.py:145
  49.8 2.3 %collective-permute-done.19 = f32[2,9,128]{2,1,0:T(8,128)S(1)} collective-permute-done((f32[2,9,128]{2,1,0:T(8,128)S(1)}, f32[2,9,128]{2,1,0:T(8,128)S(1)}, u32[]{:S(2)}, u32[]{:S(2)}) %collective-permute-start.19) | collective-permute-done | bytes 9248 | tf_op jit(solution)/shard_map/ppermute | solution.py:44
  52.3 0.7 collective-permute-start.16
  53.0 3.1 %collective-permute-done.20 = f32[4,9,128]{2,1,0:T(8,128)S(1)} collective-permute-done((f32[4,9,128]{2,1,0:T(8,128)S(1)}, f32[4,9,128]{2,1,0:T(8,128)S(1)}, u32[]{:S(2)}, u32[]{:S(2)}) %collective-permute-start.20) | collective-permute-done | bytes 18464 | tf_op jit(solution)/shard_map/ppermute | solution.py:44
  56.2 0.8 fusion.30
  57.1 1.3 %collective-permute-start.10 = (f32[7,2,32,128]{3,2,1,0:T(8,128)S(1)}, f32[7,2,32,128]{3,2,1,0:T(8,128)S(1)}, u32[]{:S(2)}, u32[]{:S(2)}) collective-permute-start(f32[7,2,32,128]{3,2,1,0:T(8,128)S(1)} %multiply_add_fusion.7), channel_id=1, source_target_pairs={{16,24},{17,25},{18,26},{19,27},{20,28},{21,29},{22,30},{23,31}} | collective-permute-start | bytes 688136 | tf_op jit(solution)/shard_map/ppermute | solution.py:145
  58.4 10.1 %collective-permute-done.7 = f32[5,2,32,128]{3,2,1,0:T(8,128)S(1)} collective-permute-done((f32[5,2,32,128]{3,2,1,0:T(8,128)S(1)}, f32[5,2,32,128]{3,2,1,0:T(8,128)S(1)}, u32[]{:S(2)}, u32[]{:S(2)}) %collective-permute-start.7) | collective-permute-done | bytes 163872 | tf_op jit(solution)/shard_map/ppermute | solution.py:145
  68.7 1.3 %collective-permute-start.13 = (f32[9,2,32,128]{3,2,1,0:T(8,128)S(1)}, f32[9,2,32,128]{3,2,1,0:T(8,128)S(1)}, u32[]{:S(2)}, u32[]{:S(2)}) collective-permute-start(f32[9,2,32,128]{3,2,1,0:T(8,128)S(1)} %multiply_add_fusion.4), channel_id=1, source_target_pairs={{16,24},{17,25},{18,26},{19,27},{20,28},{21,29},{22,30},{23,31}} | collective-permute-start | bytes 884744 | tf_op jit(solution)/shard_map/ppermute | solution.py:145
  70.1 1.3 %collective-permute-start.17 = (f32[11,2,32,128]{3,2,1,0:T(8,128)S(1)}, f32[11,2,32,128]{3,2,1,0:T(8,128)S(1)}, u32[]{:S(2)}, u32[]{:S(2)}) collective-permute-start(f32[11,2,32,128]{3,2,1,0:T(8,128)S(1)} %multiply_add_fusion.1), channel_id=1, source_target_pairs={{16,24},{17,25},{18,26},{19,27},{20,28},{21,29},{22,30},{23,31}} | collective-permute-start | bytes 1081352 | tf_op jit(solution)/shard_map/ppermute | solution.py:145
  71.4 4.1 %collective-permute-done.10 = f32[7,2,32,128]{3,2,1,0:T(8,128)S(1)} collective-permute-done((f32[7,2,32,128]{3,2,1,0:T(8,128)S(1)}, f32[7,2,32,128]{3,2,1,0:T(8,128)S(1)}, u32[]{:S(2)}, u32[]{:S(2)}) %collective-permute-start.10) | collective-permute-done | bytes 229408 | tf_op jit(solution)/shard_map/ppermute | solution.py:145
  75.7 9.4 %collective-permute-done.13 = f32[9,2,32,128]{3,2,1,0:T(8,128)S(1)} collective-permute-done((f32[9,2,32,128]{3,2,1,0:T(8,128)S(1)}, f32[9,2,32,128]{3,2,1,0:T(8,128)S(1)}, u32[]{:S(2)}, u32[]{:S(2)}) %collective-permute-start.13) | collective-permute-done | bytes 294944 | tf_op jit(solution)/shard_map/ppermute | solution.py:145
  85.2 9.0 %collective-permute-done.17 = f32[11,2,32,128]{3,2,1,0:T(8,128)S(1)} collective-permute-done((f32[11,2,32,128]{3,2,1,0:T(8,128)S(1)}, f32[11,2,32,128]{3,2,1,0:T(8,128)S(1)}, u32[]{:S(2)}, u32[]{:S(2)}) %collective-permute-start.17) | collective-permute-done | bytes 360480 | tf_op jit(solution)/shard_map/ppermute | solution.py:145
  94.3 1.1 %maximum_bitcast_fusion = f32[1,32,2,32,128]{4,3,2,1,0:T(8,128)} fusion(f32[11,2,32,128]{3,2,1,0:T(8,128)S(1)} %multiply_add_fusion, f32[9,2,32,128]{3,2,1,0:T(8,128)S(1)} %multiply_add_fusion.3, f32[7,2,32,128]{3,2,1,0:T(8,128)S(1)} %multiply_add_fusion.6, f32[5,2,32,128]{3,2,1,0:T(8,128)S(1)} %multiply_add_fusion.9), kind=kLoop, calls=%fused_computation.46 | loop fusion | flops 786432 | bytes 2097152 | tf_op jit(solution)/shard_map/broadcast_in_dim | solution.py:162
  (73 shorter events, 10.6 us)
Async XLA Ops:
  0.6 44.8 %copy-start = (bf16[1,8,64,128]{3,2,1,0:T(8,128)(2,1)S(1)}, bf16[1,8,64,128]{3,2,1,0:T(8,128)(2,1)}, u32[]{:S(2)}) copy-start(bf16[1,8,64,128]{3,2,1,0:T(8,128)(2,1)} %param.22) | copy-start | bytes 393220
  0.6 29.4 %copy-start.1 = (f32[1,32,2,32,128]{4,3,2,1,0:T(8,128)S(1)}, f32[1,32,2,32,128]{4,3,2,1,0:T(8,128)}, u32[]{:S(2)}) copy-start(f32[1,32,2,32,128]{4,3,2,1,0:T(8,128)} %param.15) | copy-start | bytes 3145732
  0.7 29.4 %collective-permute-start = (f32[32,2,32,128]{3,2,1,0:T(8,128)}, f32[32,2,32,128]{3,2,1,0:T(8,128)S(1)}, u32[]{:S(2)}, u32[]{:S(2)}) collective-permute-start(f32[32,2,32,128]{3,2,1,0:T(8,128)} %bitcast.111), channel_id=1, source_target_pairs={{0,1},{1,2},{2,3},{3,4},{4,5},{5,6},{6,7},{8,9},{9,10},{10,11},{11... | collective-permute-start | bytes 3145736 | tf_op jit(solution)/shard_map/ppermute | solution.py:80
  2.7 27.3 %collective-permute-start.1 = (f32[32,2,32,128]{3,2,1,0:T(8,128)}, f32[32,2,32,128]{3,2,1,0:T(8,128)S(1)}, u32[]{:S(2)}, u32[]{:S(2)}) collective-permute-start(f32[32,2,32,128]{3,2,1,0:T(8,128)} %bitcast.112), channel_id=1, source_target_pairs={{1,0},{2,1},{3,2},{4,3},{5,4},{6,5},{7,6},{9,8},{10,9},{11,10},{12... | collective-permute-start | bytes 3145736 | tf_op jit(solution)/shard_map/ppermute | solution.py:81
  6.4 11.1 %collective-permute-start.2 = (f32[2,32,128]{2,1,0:T(8,128)}, f32[2,32,128]{2,1,0:T(8,128)S(1)}, u32[]{:S(2)}, u32[]{:S(2)}) collective-permute-start(f32[2,32,128]{2,1,0:T(8,128)} %param.16), channel_id=1, source_target_pairs={{0,1},{1,2},{2,3},{3,4},{4,5},{5,6},{6,7},{8,9},{9,10},{10,11},{11... | collective-permute-start | bytes 98312 | tf_op jit(solution)/shard_map/ppermute | solution.py:82
  8.3 19.9 %collective-permute-start.3 = (f32[2,32,128]{2,1,0:T(8,128)}, f32[2,32,128]{2,1,0:T(8,128)S(1)}, u32[]{:S(2)}, u32[]{:S(2)}) collective-permute-start(f32[2,32,128]{2,1,0:T(8,128)} %param.16), channel_id=1, source_target_pairs={{1,0},{2,1},{3,2},{4,3},{5,4},{6,5},{7,6},{9,8},{10,9},{11,10},{12... | collective-permute-start | bytes 98312 | tf_op jit(solution)/shard_map/ppermute | solution.py:83
  32.3 0.8 copy-start.2
  33.0 1.4 %copy-start.3 = (f32[1,32]{1,0:T(1,128)S(1)}, f32[1,32]{1,0:T(1,128)}, u32[]{:S(2)}) copy-start(f32[1,32]{1,0:T(1,128)} %param.20) | copy-start | bytes 388
  34.2 1.3 %copy-start.4 = (s32[1,8]{1,0:T(1,128)S(1)}, s32[1,8]{1,0:T(1,128)}, u32[]{:S(2)}) copy-start(s32[1,8]{1,0:T(1,128)} %param.23) | copy-start | bytes 100
  35.0 3.8 %collective-permute-start.4 = (f32[1,34,64]{2,1,0:T(8,128)S(1)}, f32[1,34,64]{2,1,0:T(8,128)S(1)}, u32[]{:S(2)}, u32[]{:S(2)}) collective-permute-start(f32[1,34,64]{2,1,0:T(8,128)S(1)} %maximum_bitcast_fusion.1), channel_id=1, source_target_pairs={{0,8},{8,0},{16,24},{24,16},{1,9},{9,1},{17,25},{25,17},{2,10},{10... | collective-permute-start | bytes 26120 | tf_op jit(solution)/shard_map/ppermute | solution.py:108
  38.9 5.7 %collective-permute-start.14 = (f32[2,34,64]{2,1,0:T(8,128)S(1)}, f32[2,34,64]{2,1,0:T(8,128)S(1)}, u32[]{:S(2)}, u32[]{:S(2)}) collective-permute-start(f32[2,34,64]{2,1,0:T(8,128)S(1)} %maximum_select_fusion.2), channel_id=1, source_target_pairs={{0,16},{8,24},{16,0},{24,8},{1,17},{9,25},{17,1},{25,9},{2,18},{10... | collective-permute-start | bytes 52232 | tf_op jit(solution)/shard_map/ppermute | solution.py:108
  39.4 7.8 %collective-permute-start.15 = (f32[11,2,32,128]{3,2,1,0:T(8,128)S(1)}, f32[11,2,32,128]{3,2,1,0:T(8,128)S(1)}, u32[]{:S(2)}, u32[]{:S(2)}) collective-permute-start(f32[11,2,32,128]{3,2,1,0:T(8,128)S(1)} %slice.184), channel_id=1, source_target_pairs={{0,8},{1,9},{2,10},{3,11},{4,12},{5,13},{6,14},{7,15}} | collective-permute-start | bytes 1081352 | tf_op jit(solution)/shard_map/ppermute | solution.py:145
  40.1 5.5 %collective-permute-start.5 = (f32[5,2,32,128]{3,2,1,0:T(8,128)S(1)}, f32[5,2,32,128]{3,2,1,0:T(8,128)S(1)}, u32[]{:S(2)}, u32[]{:S(2)}) collective-permute-start(f32[5,2,32,128]{3,2,1,0:T(8,128)S(1)} %slice.178), channel_id=1, source_target_pairs={{0,8},{1,9},{2,10},{3,11},{4,12},{5,13},{6,14},{7,15}} | collective-permute-start | bytes 491528 | tf_op jit(solution)/shard_map/ppermute | solution.py:145
  40.8 5.6 %collective-permute-start.8 = (f32[7,2,32,128]{3,2,1,0:T(8,128)S(1)}, f32[7,2,32,128]{3,2,1,0:T(8,128)S(1)}, u32[]{:S(2)}, u32[]{:S(2)}) collective-permute-start(f32[7,2,32,128]{3,2,1,0:T(8,128)S(1)} %slice.180), channel_id=1, source_target_pairs={{0,8},{1,9},{2,10},{3,11},{4,12},{5,13},{6,14},{7,15}} | collective-permute-start | bytes 688136 | tf_op jit(solution)/shard_map/ppermute | solution.py:145
  41.4 5.9 %collective-permute-start.11 = (f32[9,2,32,128]{3,2,1,0:T(8,128)S(1)}, f32[9,2,32,128]{3,2,1,0:T(8,128)S(1)}, u32[]{:S(2)}, u32[]{:S(2)}) collective-permute-start(f32[9,2,32,128]{3,2,1,0:T(8,128)S(1)} %slice.182), channel_id=1, source_target_pairs={{0,8},{1,9},{2,10},{3,11},{4,12},{5,13},{6,14},{7,15}} | collective-permute-start | bytes 884744 | tf_op jit(solution)/shard_map/ppermute | solution.py:145
  45.7 2.7 %collective-permute-start.6 = (f32[5,2,32,128]{3,2,1,0:T(8,128)S(1)}, f32[5,2,32,128]{3,2,1,0:T(8,128)S(1)}, u32[]{:S(2)}, u32[]{:S(2)}) collective-permute-start(f32[5,2,32,128]{3,2,1,0:T(8,128)S(1)} %multiply_add_fusion.11), channel_id=1, source_target_pairs={{8,16},{9,17},{10,18},{11,19},{12,20},{13,21},{14,22},{15,23}} | collective-permute-start | bytes 491528 | tf_op jit(solution)/shard_map/ppermute | solution.py:145
  46.5 10.5 %collective-permute-start.9 = (f32[7,2,32,128]{3,2,1,0:T(8,128)S(1)}, f32[7,2,32,128]{3,2,1,0:T(8,128)S(1)}, u32[]{:S(2)}, u32[]{:S(2)}) collective-permute-start(f32[7,2,32,128]{3,2,1,0:T(8,128)S(1)} %multiply_add_fusion.8), channel_id=1, source_target_pairs={{8,16},{9,17},{10,18},{11,19},{12,20},{13,21},{14,22},{15,23}} | collective-permute-start | bytes 688136 | tf_op jit(solution)/shard_map/ppermute | solution.py:145
  47.2 1.2 %collective-permute-start.18 = (f32[1,9,128]{2,1,0:T(8,128)S(1)}, f32[1,9,128]{2,1,0:T(8,128)S(1)}, u32[]{:S(2)}, u32[]{:S(2)}) collective-permute-start(f32[1,9,128]{2,1,0:T(8,128)S(1)} %bitcast.117), channel_id=1, source_target_pairs={{0,1},{1,0},{2,3},{3,2},{4,5},{5,4},{6,7},{7,6},{8,9},{9,8},{10,11... | collective-permute-start | bytes 13832 | tf_op jit(solution)/shard_map/ppermute | solution.py:44
  47.4 21.2 %collective-permute-start.12 = (f32[9,2,32,128]{3,2,1,0:T(8,128)S(1)}, f32[9,2,32,128]{3,2,1,0:T(8,128)S(1)}, u32[]{:S(2)}, u32[]{:S(2)}) collective-permute-start(f32[9,2,32,128]{3,2,1,0:T(8,128)S(1)} %multiply_add_fusion.5), channel_id=1, source_target_pairs={{8,16},{9,17},{10,18},{11,19},{12,20},{13,21},{14,22},{15,23}} | collective-permute-start | bytes 884744 | tf_op jit(solution)/shard_map/ppermute | solution.py:145
  48.4 3.7 %collective-permute-start.19 = (f32[2,9,128]{2,1,0:T(8,128)S(1)}, f32[2,9,128]{2,1,0:T(8,128)S(1)}, u32[]{:S(2)}, u32[]{:S(2)}) collective-permute-start(f32[2,9,128]{2,1,0:T(8,128)S(1)} %maximum_select_fusion.4), channel_id=1, source_target_pairs={{0,2},{1,3},{2,0},{3,1},{4,6},{5,7},{6,4},{7,5},{8,10},{9,11},{10,... | collective-permute-start | bytes 27656 | tf_op jit(solution)/shard_map/ppermute | solution.py:44
  48.5 20.0 %collective-permute-start.7 = (f32[5,2,32,128]{3,2,1,0:T(8,128)S(1)}, f32[5,2,32,128]{3,2,1,0:T(8,128)S(1)}, u32[]{:S(2)}, u32[]{:S(2)}) collective-permute-start(f32[5,2,32,128]{3,2,1,0:T(8,128)S(1)} %multiply_add_fusion.10), channel_id=1, source_target_pairs={{16,24},{17,25},{18,26},{19,27},{20,28},{21,29},{22,30},{23,31}} | collective-permute-start | bytes 491528 | tf_op jit(solution)/shard_map/ppermute | solution.py:145
  52.2 3.9 %collective-permute-start.20 = (f32[4,9,128]{2,1,0:T(8,128)S(1)}, f32[4,9,128]{2,1,0:T(8,128)S(1)}, u32[]{:S(2)}, u32[]{:S(2)}) collective-permute-start(f32[4,9,128]{2,1,0:T(8,128)S(1)} %maximum_select_fusion.3), channel_id=1, source_target_pairs={{0,4},{1,5},{2,6},{3,7},{4,0},{5,1},{6,2},{7,3},{8,12},{9,13},{10,... | collective-permute-start | bytes 55304 | tf_op jit(solution)/shard_map/ppermute | solution.py:44
  52.3 17.7 %collective-permute-start.16 = (f32[11,2,32,128]{3,2,1,0:T(8,128)S(1)}, f32[11,2,32,128]{3,2,1,0:T(8,128)S(1)}, u32[]{:S(2)}, u32[]{:S(2)}) collective-permute-start(f32[11,2,32,128]{3,2,1,0:T(8,128)S(1)} %multiply_add_fusion.2), channel_id=1, source_target_pairs={{8,16},{9,17},{10,18},{11,19},{12,20},{13,21},{14,22},{15,23}} | collective-permute-start | bytes 1081352 | tf_op jit(solution)/shard_map/ppermute | solution.py:145
  57.1 18.5 %collective-permute-start.10 = (f32[7,2,32,128]{3,2,1,0:T(8,128)S(1)}, f32[7,2,32,128]{3,2,1,0:T(8,128)S(1)}, u32[]{:S(2)}, u32[]{:S(2)}) collective-permute-start(f32[7,2,32,128]{3,2,1,0:T(8,128)S(1)} %multiply_add_fusion.7), channel_id=1, source_target_pairs={{16,24},{17,25},{18,26},{19,27},{20,28},{21,29},{22,30},{23,31}} | collective-permute-start | bytes 688136 | tf_op jit(solution)/shard_map/ppermute | solution.py:145
  68.7 16.4 %collective-permute-start.13 = (f32[9,2,32,128]{3,2,1,0:T(8,128)S(1)}, f32[9,2,32,128]{3,2,1,0:T(8,128)S(1)}, u32[]{:S(2)}, u32[]{:S(2)}) collective-permute-start(f32[9,2,32,128]{3,2,1,0:T(8,128)S(1)} %multiply_add_fusion.4), channel_id=1, source_target_pairs={{16,24},{17,25},{18,26},{19,27},{20,28},{21,29},{22,30},{23,31}} | collective-permute-start | bytes 884744 | tf_op jit(solution)/shard_map/ppermute | solution.py:145
  70.1 24.0 %collective-permute-start.17 = (f32[11,2,32,128]{3,2,1,0:T(8,128)S(1)}, f32[11,2,32,128]{3,2,1,0:T(8,128)S(1)}, u32[]{:S(2)}, u32[]{:S(2)}) collective-permute-start(f32[11,2,32,128]{3,2,1,0:T(8,128)S(1)} %multiply_add_fusion.1), channel_id=1, source_target_pairs={{16,24},{17,25},{18,26},{19,27},{20,28},{21,29},{22,30},{23,31}} | collective-permute-start | bytes 1081352 | tf_op jit(solution)/shard_map/ppermute | solution.py:145

commit v23 on v22

--- a/solution.py
+++ b/solution.py
@@ -6,7 +6,7 @@
 SUBSTEPS = 2
 NB = 384
 CHUNKS = 4
-HIGH = lax.Precision.HIGHEST
+HIGH = lax.Precision.HIGH
 
 
 def padded_2(cells, sides, width):

time: 95.9 us -> 95.9 us (level)
  no operation moved by 1% of the time
where the time goes in v23:
time: 95.9 us; the launch traced here: 95.4 us
  waiting for transfers between devices  55 us (57%)
  starting transfers between devices  22.9 us (24%)
  other arithmetic  8.82 us (9%)
  local copies, waits for them, and re-layouts  4.81 us (5%)
  matrix products  2.78 us (3%)
  between operations  1.1 us (1%)
    ppermute x12, waiting for transfers between devices, body(): arrived = lax.ppermute(pieces[c], 'species', [(s, s + 1)])  32.8 us
    ppermute x1, waiting for transfers between devices, body(): factor_right = lax.ppermute(space_factor[:halo], 'space', left_pairs)  10.7 us
    ppermute x12, starting transfers between devices, body(): arrived = lax.ppermute(pieces[c], 'species', [(s, s + 1)])  10.6 us
    ppermute x3, waiting for transfers between devices, gather_all(): other = lax.ppermute(held, axis, [(i, i ^ span) for i in range(count)])  5.74 us
    ppermute x2, waiting for transfers between devices, body(): lax.ppermute(everyone, 'species', [(i, i ^ span) for i in range(groups)])  5.13 us
    ppermute x1, starting transfers between devices, body(): factor_right = lax.ppermute(space_factor[:halo], 'space', left_pairs)  3.64 us
    ppermute x1, starting transfers between devices, body(): from_right = lax.ppermute(field[:, :halo], 'space', left_pairs)  3.64 us
    mul x4, local copies, waits for them, and re-layouts, body(): pieces[c] = pieces[c] + scales[c] * arrived  2.84 us
  transfers between devices with their start and end apart: 21, of which 11 were waited for; matrix products, arithmetic and copies ran while one was open for 11% of the time, Pallas kernels for 0%

profile of v23, /device:TPU:26, one launch (start us, length us, event | category | flops | bytes accessed | tf_op | source)
XLA Modules:
  0.0 95.4 jit_solution(11691311598088806743)
XLA Ops:
  0.7 2.1 %collective-permute-start = (f32[32,2,32,128]{3,2,1,0:T(8,128)}, f32[32,2,32,128]{3,2,1,0:T(8,128)S(1)}, u32[]{:S(2)}, u32[]{:S(2)}) collective-permute-start(f32[32,2,32,128]{3,2,1,0:T(8,128)} %bitcast.111), channel_id=1, source_target_pairs={{0,1},{1,2},{2,3},{3,4},{4,5},{5,6},{6,7},{8,9},{9,10},{10,11},{11... | collective-permute-start | bytes 3145736 | tf_op jit(solution)/shard_map/ppermute | solution.py:80
  2.7 3.6 %collective-permute-start.1 = (f32[32,2,32,128]{3,2,1,0:T(8,128)}, f32[32,2,32,128]{3,2,1,0:T(8,128)S(1)}, u32[]{:S(2)}, u32[]{:S(2)}) collective-permute-start(f32[32,2,32,128]{3,2,1,0:T(8,128)} %bitcast.112), channel_id=1, source_target_pairs={{1,0},{2,1},{3,2},{4,3},{5,4},{6,5},{7,6},{9,8},{10,9},{11,10},{12... | collective-permute-start | bytes 3145736 | tf_op jit(solution)/shard_map/ppermute | solution.py:81
  6.4 1.9 %collective-permute-start.2 = (f32[2,32,128]{2,1,0:T(8,128)}, f32[2,32,128]{2,1,0:T(8,128)S(1)}, u32[]{:S(2)}, u32[]{:S(2)}) collective-permute-start(f32[2,32,128]{2,1,0:T(8,128)} %param.16), channel_id=1, source_target_pairs={{0,1},{1,2},{2,3},{3,4},{4,5},{5,6},{6,7},{8,9},{9,10},{10,11},{11... | collective-permute-start | bytes 98312 | tf_op jit(solution)/shard_map/ppermute | solution.py:82
  8.3 3.6 %collective-permute-start.3 = (f32[2,32,128]{2,1,0:T(8,128)}, f32[2,32,128]{2,1,0:T(8,128)S(1)}, u32[]{:S(2)}, u32[]{:S(2)}) collective-permute-start(f32[2,32,128]{2,1,0:T(8,128)} %param.16), channel_id=1, source_target_pairs={{1,0},{2,1},{3,2},{4,3},{5,4},{6,5},{7,6},{9,8},{10,9},{11,10},{12... | collective-permute-start | bytes 98312 | tf_op jit(solution)/shard_map/ppermute | solution.py:83
  12.6 0.7 slice_bitcast_fusion.15
  13.3 0.7 slice_bitcast_fusion.14
  14.1 0.7 slice_bitcast_fusion.13
  15.4 0.8 scatter.11
  17.5 10.7 %collective-permute-done.3 = f32[2,32,128]{2,1,0:T(8,128)S(1)} collective-permute-done((f32[2,32,128]{2,1,0:T(8,128)}, f32[2,32,128]{2,1,0:T(8,128)S(1)}, u32[]{:S(2)}, u32[]{:S(2)}) %collective-permute-start.3) | collective-permute-done | bytes 32800 | tf_op jit(solution)/shard_map/ppermute | solution.py:83
  28.2 0.8 pad_maximum_fusion.2
  28.9 1.1 %broadcast_multiply_fusion = f32[32,6,32,128]{3,2,1,0:T(8,128)S(1)} fusion(f32[6,32,128]{2,1,0:T(8,128)S(1)} %pad_maximum_fusion.2, f32[32]{0:T(128)} %bitcast.121), kind=kLoop, calls=%fused_computation.18 | loop fusion | flops 786432 | bytes 3244160 | tf_op jit(solution)/shard_map/mul | solution.py:85
  30.2 1.9 %fusion.6 = f32[32,4,32,128]{3,2,1,0:T(8,128)S(1)} fusion(f32[32,4,32,128]{3,2,1,0:T(8,128)S(1)} %pad_maximum_fusion, f32[32,6,32,128]{3,2,1,0:T(8,128)S(1)} %broadcast_multiply_fusion, f32[32,2,32,128]{3,2,1,0:T(8,128)S(1)} %collective-permute-done.1, f32[32,2,32,128]{3,2,1,0:T(8,128)S(1)} %bitcast.114, f32[32,2,32,128]{3,2,1,0:T(8,128)S(1)} %collective-permute-done), kind=kLoop, calls=%fused_computation.14 | loop fusion | flops 5767168 | bytes 9437184 | tf_op jit(solution)/shard_map/add | solution.py:89
  32.3 0.7 fusion.25
  33.0 1.2 %convolution_bitcast_fusion = f32[4,8,64,128]{3,1,2,0:T(8,128)S(1)} fusion(f32[4,8,64,128]{3,2,1,0:T(8,128)S(1)} %bitcast.115, f32[1,32,32]{2,1,0:T(8,128)S(1)} %copy-done.2), kind=kOutput, calls=%fused_computation.19 | convolution fusion | flops 50331648 | bytes 2101248 | tf_op jit(solution)/shard_map/dot_general | solution.py:91
  36.2 2.7 %collective-permute-done.4 = f32[1,34,64]{2,1,0:T(8,128)S(1)} collective-permute-done((f32[1,34,64]{2,1,0:T(8,128)S(1)}, f32[1,34,64]{2,1,0:T(8,128)S(1)}, u32[]{:S(2)}, u32[]{:S(2)}) %collective-permute-start.4) | collective-permute-done | bytes 8736 | tf_op jit(solution)/shard_map/ppermute | solution.py:108
  39.4 0.7 collective-permute-start.15
  41.4 0.7 collective-permute-start.11
  42.1 2.5 %collective-permute-done.14 = f32[2,34,64]{2,1,0:T(8,128)S(1)} collective-permute-done((f32[2,34,64]{2,1,0:T(8,128)S(1)}, f32[2,34,64]{2,1,0:T(8,128)S(1)}, u32[]{:S(2)}, u32[]{:S(2)}) %collective-permute-start.14) | collective-permute-done | bytes 17440 | tf_op jit(solution)/shard_map/ppermute | solution.py:108
  47.4 0.7 collective-permute-start.12
  48.5 1.3 %collective-permute-start.7 = (f32[5,2,32,128]{3,2,1,0:T(8,128)S(1)}, f32[5,2,32,128]{3,2,1,0:T(8,128)S(1)}, u32[]{:S(2)}, u32[]{:S(2)}) collective-permute-start(f32[5,2,32,128]{3,2,1,0:T(8,128)S(1)} %multiply_add_fusion.10), channel_id=1, source_target_pairs={{16,24},{17,25},{18,26},{19,27},{20,28},{21,29},{22,30},{23,31}} | collective-permute-start | bytes 491528 | tf_op jit(solution)/shard_map/ppermute | solution.py:145
  49.8 2.3 %collective-permute-done.19 = f32[2,9,128]{2,1,0:T(8,128)S(1)} collective-permute-done((f32[2,9,128]{2,1,0:T(8,128)S(1)}, f32[2,9,128]{2,1,0:T(8,128)S(1)}, u32[]{:S(2)}, u32[]{:S(2)}) %collective-permute-start.19) | collective-permute-done | bytes 9248 | tf_op jit(solution)/shard_map/ppermute | solution.py:44
  52.2 0.7 collective-permute-start.16
  52.9 3.1 %collective-permute-done.20 = f32[4,9,128]{2,1,0:T(8,128)S(1)} collective-permute-done((f32[4,9,128]{2,1,0:T(8,128)S(1)}, f32[4,9,128]{2,1,0:T(8,128)S(1)}, u32[]{:S(2)}, u32[]{:S(2)}) %collective-permute-start.20) | collective-permute-done | bytes 18464 | tf_op jit(solution)/shard_map/ppermute | solution.py:44
  56.1 0.8 fusion.30
  57.0 1.3 %collective-permute-start.10 = (f32[7,2,32,128]{3,2,1,0:T(8,128)S(1)}, f32[7,2,32,128]{3,2,1,0:T(8,128)S(1)}, u32[]{:S(2)}, u32[]{:S(2)}) collective-permute-start(f32[7,2,32,128]{3,2,1,0:T(8,128)S(1)} %multiply_add_fusion.7), channel_id=1, source_target_pairs={{16,24},{17,25},{18,26},{19,27},{20,28},{21,29},{22,30},{23,31}} | collective-permute-start | bytes 688136 | tf_op jit(solution)/shard_map/ppermute | solution.py:145
  58.3 10.2 %collective-permute-done.7 = f32[5,2,32,128]{3,2,1,0:T(8,128)S(1)} collective-permute-done((f32[5,2,32,128]{3,2,1,0:T(8,128)S(1)}, f32[5,2,32,128]{3,2,1,0:T(8,128)S(1)}, u32[]{:S(2)}, u32[]{:S(2)}) %collective-permute-start.7) | collective-permute-done | bytes 163872 | tf_op jit(solution)/shard_map/ppermute | solution.py:145
  68.7 1.3 %collective-permute-start.13 = (f32[9,2,32,128]{3,2,1,0:T(8,128)S(1)}, f32[9,2,32,128]{3,2,1,0:T(8,128)S(1)}, u32[]{:S(2)}, u32[]{:S(2)}) collective-permute-start(f32[9,2,32,128]{3,2,1,0:T(8,128)S(1)} %multiply_add_fusion.4), channel_id=1, source_target_pairs={{16,24},{17,25},{18,26},{19,27},{20,28},{21,29},{22,30},{23,31}} | collective-permute-start | bytes 884744 | tf_op jit(solution)/shard_map/ppermute | solution.py:145
  70.1 1.3 %collective-permute-start.17 = (f32[11,2,32,128]{3,2,1,0:T(8,128)S(1)}, f32[11,2,32,128]{3,2,1,0:T(8,128)S(1)}, u32[]{:S(2)}, u32[]{:S(2)}) collective-permute-start(f32[11,2,32,128]{3,2,1,0:T(8,128)S(1)} %multiply_add_fusion.1), channel_id=1, source_target_pairs={{16,24},{17,25},{18,26},{19,27},{20,28},{21,29},{22,30},{23,31}} | collective-permute-start | bytes 1081352 | tf_op jit(solution)/shard_map/ppermute | solution.py:145
  71.4 4.1 %collective-permute-done.10 = f32[7,2,32,128]{3,2,1,0:T(8,128)S(1)} collective-permute-done((f32[7,2,32,128]{3,2,1,0:T(8,128)S(1)}, f32[7,2,32,128]{3,2,1,0:T(8,128)S(1)}, u32[]{:S(2)}, u32[]{:S(2)}) %collective-permute-start.10) | collective-permute-done | bytes 229408 | tf_op jit(solution)/shard_map/ppermute | solution.py:145
  75.6 9.4 %collective-permute-done.13 = f32[9,2,32,128]{3,2,1,0:T(8,128)S(1)} collective-permute-done((f32[9,2,32,128]{3,2,1,0:T(8,128)S(1)}, f32[9,2,32,128]{3,2,1,0:T(8,128)S(1)}, u32[]{:S(2)}, u32[]{:S(2)}) %collective-permute-start.13) | collective-permute-done | bytes 294944 | tf_op jit(solution)/shard_map/ppermute | solution.py:145
  85.2 9.0 %collective-permute-done.17 = f32[11,2,32,128]{3,2,1,0:T(8,128)S(1)} collective-permute-done((f32[11,2,32,128]{3,2,1,0:T(8,128)S(1)}, f32[11,2,32,128]{3,2,1,0:T(8,128)S(1)}, u32[]{:S(2)}, u32[]{:S(2)}) %collective-permute-start.17) | collective-permute-done | bytes 360480 | tf_op jit(solution)/shard_map/ppermute | solution.py:145
  94.3 1.1 %maximum_bitcast_fusion = f32[1,32,2,32,128]{4,3,2,1,0:T(8,128)} fusion(f32[11,2,32,128]{3,2,1,0:T(8,128)S(1)} %multiply_add_fusion, f32[9,2,32,128]{3,2,1,0:T(8,128)S(1)} %multiply_add_fusion.3, f32[7,2,32,128]{3,2,1,0:T(8,128)S(1)} %multiply_add_fusion.6, f32[5,2,32,128]{3,2,1,0:T(8,128)S(1)} %multiply_add_fusion.9), kind=kLoop, calls=%fused_computation.46 | loop fusion | flops 786432 | bytes 2097152 | tf_op jit(solution)/shard_map/broadcast_in_dim | solution.py:162
  (73 shorter events, 10.6 us)
Async XLA Ops:
  0.6 44.7 %copy-start = (bf16[1,8,64,128]{3,2,1,0:T(8,128)(2,1)S(1)}, bf16[1,8,64,128]{3,2,1,0:T(8,128)(2,1)}, u32[]{:S(2)}) copy-start(bf16[1,8,64,128]{3,2,1,0:T(8,128)(2,1)} %param.22) | copy-start | bytes 393220
  0.6 29.4 %copy-start.1 = (f32[1,32,2,32,128]{4,3,2,1,0:T(8,128)S(1)}, f32[1,32,2,32,128]{4,3,2,1,0:T(8,128)}, u32[]{:S(2)}) copy-start(f32[1,32,2,32,128]{4,3,2,1,0:T(8,128)} %param.15) | copy-start | bytes 3145732
  0.7 29.4 %collective-permute-start = (f32[32,2,32,128]{3,2,1,0:T(8,128)}, f32[32,2,32,128]{3,2,1,0:T(8,128)S(1)}, u32[]{:S(2)}, u32[]{:S(2)}) collective-permute-start(f32[32,2,32,128]{3,2,1,0:T(8,128)} %bitcast.111), channel_id=1, source_target_pairs={{0,1},{1,2},{2,3},{3,4},{4,5},{5,6},{6,7},{8,9},{9,10},{10,11},{11... | collective-permute-start | bytes 3145736 | tf_op jit(solution)/shard_map/ppermute | solution.py:80
  2.7 27.3 %collective-permute-start.1 = (f32[32,2,32,128]{3,2,1,0:T(8,128)}, f32[32,2,32,128]{3,2,1,0:T(8,128)S(1)}, u32[]{:S(2)}, u32[]{:S(2)}) collective-permute-start(f32[32,2,32,128]{3,2,1,0:T(8,128)} %bitcast.112), channel_id=1, source_target_pairs={{1,0},{2,1},{3,2},{4,3},{5,4},{6,5},{7,6},{9,8},{10,9},{11,10},{12... | collective-permute-start | bytes 3145736 | tf_op jit(solution)/shard_map/ppermute | solution.py:81
  6.4 11.1 %collective-permute-start.2 = (f32[2,32,128]{2,1,0:T(8,128)}, f32[2,32,128]{2,1,0:T(8,128)S(1)}, u32[]{:S(2)}, u32[]{:S(2)}) collective-permute-start(f32[2,32,128]{2,1,0:T(8,128)} %param.16), channel_id=1, source_target_pairs={{0,1},{1,2},{2,3},{3,4},{4,5},{5,6},{6,7},{8,9},{9,10},{10,11},{11... | collective-permute-start | bytes 98312 | tf_op jit(solution)/shard_map/ppermute | solution.py:82
  8.3 19.9 %collective-permute-start.3 = (f32[2,32,128]{2,1,0:T(8,128)}, f32[2,32,128]{2,1,0:T(8,128)S(1)}, u32[]{:S(2)}, u32[]{:S(2)}) collective-permute-start(f32[2,32,128]{2,1,0:T(8,128)} %param.16), channel_id=1, source_target_pairs={{1,0},{2,1},{3,2},{4,3},{5,4},{6,5},{7,6},{9,8},{10,9},{11,10},{12... | collective-permute-start | bytes 98312 | tf_op jit(solution)/shard_map/ppermute | solution.py:83
  32.3 0.8 copy-start.2
  33.0 1.4 %copy-start.3 = (f32[1,32]{1,0:T(1,128)S(1)}, f32[1,32]{1,0:T(1,128)}, u32[]{:S(2)}) copy-start(f32[1,32]{1,0:T(1,128)} %param.20) | copy-start | bytes 388
  34.2 1.3 %copy-start.4 = (s32[1,8]{1,0:T(1,128)S(1)}, s32[1,8]{1,0:T(1,128)}, u32[]{:S(2)}) copy-start(s32[1,8]{1,0:T(1,128)} %param.23) | copy-start | bytes 100
  35.0 3.8 %collective-permute-start.4 = (f32[1,34,64]{2,1,0:T(8,128)S(1)}, f32[1,34,64]{2,1,0:T(8,128)S(1)}, u32[]{:S(2)}, u32[]{:S(2)}) collective-permute-start(f32[1,34,64]{2,1,0:T(8,128)S(1)} %maximum_bitcast_fusion.1), channel_id=1, source_target_pairs={{0,8},{8,0},{16,24},{24,16},{1,9},{9,1},{17,25},{25,17},{2,10},{10... | collective-permute-start | bytes 26120 | tf_op jit(solution)/shard_map/ppermute | solution.py:108
  38.9 5.7 %collective-permute-start.14 = (f32[2,34,64]{2,1,0:T(8,128)S(1)}, f32[2,34,64]{2,1,0:T(8,128)S(1)}, u32[]{:S(2)}, u32[]{:S(2)}) collective-permute-start(f32[2,34,64]{2,1,0:T(8,128)S(1)} %maximum_select_fusion.2), channel_id=1, source_target_pairs={{0,16},{8,24},{16,0},{24,8},{1,17},{9,25},{17,1},{25,9},{2,18},{10... | collective-permute-start | bytes 52232 | tf_op jit(solution)/shard_map/ppermute | solution.py:108
  39.4 7.7 %collective-permute-start.15 = (f32[11,2,32,128]{3,2,1,0:T(8,128)S(1)}, f32[11,2,32,128]{3,2,1,0:T(8,128)S(1)}, u32[]{:S(2)}, u32[]{:S(2)}) collective-permute-start(f32[11,2,32,128]{3,2,1,0:T(8,128)S(1)} %slice.184), channel_id=1, source_target_pairs={{0,8},{1,9},{2,10},{3,11},{4,12},{5,13},{6,14},{7,15}} | collective-permute-start | bytes 1081352 | tf_op jit(solution)/shard_map/ppermute | solution.py:145
  40.1 5.4 %collective-permute-start.5 = (f32[5,2,32,128]{3,2,1,0:T(8,128)S(1)}, f32[5,2,32,128]{3,2,1,0:T(8,128)S(1)}, u32[]{:S(2)}, u32[]{:S(2)}) collective-permute-start(f32[5,2,32,128]{3,2,1,0:T(8,128)S(1)} %slice.178), channel_id=1, source_target_pairs={{0,8},{1,9},{2,10},{3,11},{4,12},{5,13},{6,14},{7,15}} | collective-permute-start | bytes 491528 | tf_op jit(solution)/shard_map/ppermute | solution.py:145
  40.8 5.5 %collective-permute-start.8 = (f32[7,2,32,128]{3,2,1,0:T(8,128)S(1)}, f32[7,2,32,128]{3,2,1,0:T(8,128)S(1)}, u32[]{:S(2)}, u32[]{:S(2)}) collective-permute-start(f32[7,2,32,128]{3,2,1,0:T(8,128)S(1)} %slice.180), channel_id=1, source_target_pairs={{0,8},{1,9},{2,10},{3,11},{4,12},{5,13},{6,14},{7,15}} | collective-permute-start | bytes 688136 | tf_op jit(solution)/shard_map/ppermute | solution.py:145
  41.4 5.8 %collective-permute-start.11 = (f32[9,2,32,128]{3,2,1,0:T(8,128)S(1)}, f32[9,2,32,128]{3,2,1,0:T(8,128)S(1)}, u32[]{:S(2)}, u32[]{:S(2)}) collective-permute-start(f32[9,2,32,128]{3,2,1,0:T(8,128)S(1)} %slice.182), channel_id=1, source_target_pairs={{0,8},{1,9},{2,10},{3,11},{4,12},{5,13},{6,14},{7,15}} | collective-permute-start | bytes 884744 | tf_op jit(solution)/shard_map/ppermute | solution.py:145
  45.6 2.7 %collective-permute-start.6 = (f32[5,2,32,128]{3,2,1,0:T(8,128)S(1)}, f32[5,2,32,128]{3,2,1,0:T(8,128)S(1)}, u32[]{:S(2)}, u32[]{:S(2)}) collective-permute-start(f32[5,2,32,128]{3,2,1,0:T(8,128)S(1)} %multiply_add_fusion.11), channel_id=1, source_target_pairs={{8,16},{9,17},{10,18},{11,19},{12,20},{13,21},{14,22},{15,23}} | collective-permute-start | bytes 491528 | tf_op jit(solution)/shard_map/ppermute | solution.py:145
  46.4 10.5 %collective-permute-start.9 = (f32[7,2,32,128]{3,2,1,0:T(8,128)S(1)}, f32[7,2,32,128]{3,2,1,0:T(8,128)S(1)}, u32[]{:S(2)}, u32[]{:S(2)}) collective-permute-start(f32[7,2,32,128]{3,2,1,0:T(8,128)S(1)} %multiply_add_fusion.8), channel_id=1, source_target_pairs={{8,16},{9,17},{10,18},{11,19},{12,20},{13,21},{14,22},{15,23}} | collective-permute-start | bytes 688136 | tf_op jit(solution)/shard_map/ppermute | solution.py:145
  47.1 1.2 %collective-permute-start.18 = (f32[1,9,128]{2,1,0:T(8,128)S(1)}, f32[1,9,128]{2,1,0:T(8,128)S(1)}, u32[]{:S(2)}, u32[]{:S(2)}) collective-permute-start(f32[1,9,128]{2,1,0:T(8,128)S(1)} %bitcast.117), channel_id=1, source_target_pairs={{0,1},{1,0},{2,3},{3,2},{4,5},{5,4},{6,7},{7,6},{8,9},{9,8},{10,11... | collective-permute-start | bytes 13832 | tf_op jit(solution)/shard_map/ppermute | solution.py:44
  47.4 21.3 %collective-permute-start.12 = (f32[9,2,32,128]{3,2,1,0:T(8,128)S(1)}, f32[9,2,32,128]{3,2,1,0:T(8,128)S(1)}, u32[]{:S(2)}, u32[]{:S(2)}) collective-permute-start(f32[9,2,32,128]{3,2,1,0:T(8,128)S(1)} %multiply_add_fusion.5), channel_id=1, source_target_pairs={{8,16},{9,17},{10,18},{11,19},{12,20},{13,21},{14,22},{15,23}} | collective-permute-start | bytes 884744 | tf_op jit(solution)/shard_map/ppermute | solution.py:145
  48.4 3.7 %collective-permute-start.19 = (f32[2,9,128]{2,1,0:T(8,128)S(1)}, f32[2,9,128]{2,1,0:T(8,128)S(1)}, u32[]{:S(2)}, u32[]{:S(2)}) collective-permute-start(f32[2,9,128]{2,1,0:T(8,128)S(1)} %maximum_select_fusion.4), channel_id=1, source_target_pairs={{0,2},{1,3},{2,0},{3,1},{4,6},{5,7},{6,4},{7,5},{8,10},{9,11},{10,... | collective-permute-start | bytes 27656 | tf_op jit(solution)/shard_map/ppermute | solution.py:44
  48.5 20.1 %collective-permute-start.7 = (f32[5,2,32,128]{3,2,1,0:T(8,128)S(1)}, f32[5,2,32,128]{3,2,1,0:T(8,128)S(1)}, u32[]{:S(2)}, u32[]{:S(2)}) collective-permute-start(f32[5,2,32,128]{3,2,1,0:T(8,128)S(1)} %multiply_add_fusion.10), channel_id=1, source_target_pairs={{16,24},{17,25},{18,26},{19,27},{20,28},{21,29},{22,30},{23,31}} | collective-permute-start | bytes 491528 | tf_op jit(solution)/shard_map/ppermute | solution.py:145
  52.1 3.9 %collective-permute-start.20 = (f32[4,9,128]{2,1,0:T(8,128)S(1)}, f32[4,9,128]{2,1,0:T(8,128)S(1)}, u32[]{:S(2)}, u32[]{:S(2)}) collective-permute-start(f32[4,9,128]{2,1,0:T(8,128)S(1)} %maximum_select_fusion.3), channel_id=1, source_target_pairs={{0,4},{1,5},{2,6},{3,7},{4,0},{5,1},{6,2},{7,3},{8,12},{9,13},{10,... | collective-permute-start | bytes 55304 | tf_op jit(solution)/shard_map/ppermute | solution.py:44
  52.2 17.8 %collective-permute-start.16 = (f32[11,2,32,128]{3,2,1,0:T(8,128)S(1)}, f32[11,2,32,128]{3,2,1,0:T(8,128)S(1)}, u32[]{:S(2)}, u32[]{:S(2)}) collective-permute-start(f32[11,2,32,128]{3,2,1,0:T(8,128)S(1)} %multiply_add_fusion.2), channel_id=1, source_target_pairs={{8,16},{9,17},{10,18},{11,19},{12,20},{13,21},{14,22},{15,23}} | collective-permute-start | bytes 1081352 | tf_op jit(solution)/shard_map/ppermute | solution.py:145
  57.0 18.5 %collective-permute-start.10 = (f32[7,2,32,128]{3,2,1,0:T(8,128)S(1)}, f32[7,2,32,128]{3,2,1,0:T(8,128)S(1)}, u32[]{:S(2)}, u32[]{:S(2)}) collective-permute-start(f32[7,2,32,128]{3,2,1,0:T(8,128)S(1)} %multiply_add_fusion.7), channel_id=1, source_target_pairs={{16,24},{17,25},{18,26},{19,27},{20,28},{21,29},{22,30},{23,31}} | collective-permute-start | bytes 688136 | tf_op jit(solution)/shard_map/ppermute | solution.py:145
  68.7 16.4 %collective-permute-start.13 = (f32[9,2,32,128]{3,2,1,0:T(8,128)S(1)}, f32[9,2,32,128]{3,2,1,0:T(8,128)S(1)}, u32[]{:S(2)}, u32[]{:S(2)}) collective-permute-start(f32[9,2,32,128]{3,2,1,0:T(8,128)S(1)} %multiply_add_fusion.4), channel_id=1, source_target_pairs={{16,24},{17,25},{18,26},{19,27},{20,28},{21,29},{22,30},{23,31}} | collective-permute-start | bytes 884744 | tf_op jit(solution)/shard_map/ppermute | solution.py:145
  70.1 24.0 %collective-permute-start.17 = (f32[11,2,32,128]{3,2,1,0:T(8,128)S(1)}, f32[11,2,32,128]{3,2,1,0:T(8,128)S(1)}, u32[]{:S(2)}, u32[]{:S(2)}) collective-permute-start(f32[11,2,32,128]{3,2,1,0:T(8,128)S(1)} %multiply_add_fusion.1), channel_id=1, source_target_pairs={{16,24},{17,25},{18,26},{19,27},{20,28},{21,29},{22,30},{23,31}} | collective-permute-start | bytes 1081352 | tf_op jit(solution)/shard_map/ppermute | solution.py:145

commit v24 on v22

--- a/solution.py
+++ b/solution.py
@@ -133,8 +133,8 @@
     payload = jnp.concatenate([contribution, ids], axis=0)
     base = bins // CHUNKS
     bounds = [0]
-    for c in range(CHUNKS):
-        bounds.append(bounds[-1] + base + 2 * c - (CHUNKS - 1))
+    for step in (-2, -1, 1, 2):
+        bounds.append(bounds[-1] + base + step)
     bounds[-1] = bins
     pieces = [own_part[bounds[c]:bounds[c + 1]] for c in range(CHUNKS)]
     scales = [chain[bounds[c]:bounds[c + 1]][:, None, None, None] for c in range(CHUNKS)]

time: 95.9 us -> 94.5 us (0.985)
  waiting for transfers between devices: 54.9 us -> 53.5 us
    ppermute x12, waiting for transfers between devices: 32.7 us -> 30.7 us  [body(): arrived = lax.ppermute(pieces[c], 'species', [(s, s + 1)])]
where the time goes in v24:
time: 94.5 us; the launch traced here: 94 us
  waiting for transfers between devices  53.5 us (57%)
  starting transfers between devices  22.9 us (24%)
  other arithmetic  8.83 us (9%)
  local copies, waits for them, and re-layouts  4.82 us (5%)
  matrix products  2.84 us (3%)
  between operations  1.11 us (1%)
    ppermute x12, waiting for transfers between devices, body(): arrived = lax.ppermute(pieces[c], 'species', [(s, s + 1)])  30.7 us
    ppermute x1, waiting for transfers between devices, body(): factor_right = lax.ppermute(space_factor[:halo], 'space', left_pairs)  10.7 us
    ppermute x12, starting transfers between devices, body(): arrived = lax.ppermute(pieces[c], 'species', [(s, s + 1)])  10.6 us
    ppermute x3, waiting for transfers between devices, gather_all(): other = lax.ppermute(held, axis, [(i, i ^ span) for i in range(count)])  6.35 us
    ppermute x2, waiting for transfers between devices, body(): lax.ppermute(everyone, 'species', [(i, i ^ span) for i in range(groups)])  5.13 us
    ppermute x1, starting transfers between devices, body(): factor_right = lax.ppermute(space_factor[:halo], 'space', left_pairs)  3.64 us
    ppermute x1, starting transfers between devices, body(): from_right = lax.ppermute(field[:, :halo], 'space', left_pairs)  3.64 us
    mul x4, local copies, waits for them, and re-layouts, body(): pieces[c] = pieces[c] + scales[c] * arrived  2.84 us
  transfers between devices with their start and end apart: 21, of which 11 were waited for; matrix products, arithmetic and copies ran while one was open for 11% of the time, Pallas kernels for 0%

profile of v24, /device:TPU:26, one launch (start us, length us, event | category | flops | bytes accessed | tf_op | source)
XLA Modules:
  0.0 94.0 jit_solution(12507071446467078321)
XLA Ops:
  0.7 2.1 %collective-permute-start = (f32[32,2,32,128]{3,2,1,0:T(8,128)}, f32[32,2,32,128]{3,2,1,0:T(8,128)S(1)}, u32[]{:S(2)}, u32[]{:S(2)}) collective-permute-start(f32[32,2,32,128]{3,2,1,0:T(8,128)} %bitcast.111), channel_id=1, source_target_pairs={{0,1},{1,2},{2,3},{3,4},{4,5},{5,6},{6,7},{8,9},{9,10},{10,11},{11... | collective-permute-start | bytes 3145736 | tf_op jit(solution)/shard_map/ppermute | solution.py:80
  2.7 3.6 %collective-permute-start.1 = (f32[32,2,32,128]{3,2,1,0:T(8,128)}, f32[32,2,32,128]{3,2,1,0:T(8,128)S(1)}, u32[]{:S(2)}, u32[]{:S(2)}) collective-permute-start(f32[32,2,32,128]{3,2,1,0:T(8,128)} %bitcast.112), channel_id=1, source_target_pairs={{1,0},{2,1},{3,2},{4,3},{5,4},{6,5},{7,6},{9,8},{10,9},{11,10},{12... | collective-permute-start | bytes 3145736 | tf_op jit(solution)/shard_map/ppermute | solution.py:81
  6.4 1.9 %collective-permute-start.2 = (f32[2,32,128]{2,1,0:T(8,128)}, f32[2,32,128]{2,1,0:T(8,128)S(1)}, u32[]{:S(2)}, u32[]{:S(2)}) collective-permute-start(f32[2,32,128]{2,1,0:T(8,128)} %param.16), channel_id=1, source_target_pairs={{0,1},{1,2},{2,3},{3,4},{4,5},{5,6},{6,7},{8,9},{9,10},{10,11},{11... | collective-permute-start | bytes 98312 | tf_op jit(solution)/shard_map/ppermute | solution.py:82
  8.3 3.6 %collective-permute-start.3 = (f32[2,32,128]{2,1,0:T(8,128)}, f32[2,32,128]{2,1,0:T(8,128)S(1)}, u32[]{:S(2)}, u32[]{:S(2)}) collective-permute-start(f32[2,32,128]{2,1,0:T(8,128)} %param.16), channel_id=1, source_target_pairs={{1,0},{2,1},{3,2},{4,3},{5,4},{6,5},{7,6},{9,8},{10,9},{11,10},{12... | collective-permute-start | bytes 98312 | tf_op jit(solution)/shard_map/ppermute | solution.py:83
  12.6 0.7 slice_bitcast_fusion.15
  13.3 0.7 slice_bitcast_fusion.14
  14.1 0.7 slice_bitcast_fusion.13
  15.4 0.8 scatter.11
  17.5 10.7 %collective-permute-done.3 = f32[2,32,128]{2,1,0:T(8,128)S(1)} collective-permute-done((f32[2,32,128]{2,1,0:T(8,128)}, f32[2,32,128]{2,1,0:T(8,128)S(1)}, u32[]{:S(2)}, u32[]{:S(2)}) %collective-permute-start.3) | collective-permute-done | bytes 32800 | tf_op jit(solution)/shard_map/ppermute | solution.py:83
  28.2 0.8 pad_maximum_fusion.2
  28.9 1.1 %broadcast_multiply_fusion = f32[32,6,32,128]{3,2,1,0:T(8,128)S(1)} fusion(f32[6,32,128]{2,1,0:T(8,128)S(1)} %pad_maximum_fusion.2, f32[32]{0:T(128)} %bitcast.121), kind=kLoop, calls=%fused_computation.18 | loop fusion | flops 786432 | bytes 3244160 | tf_op jit(solution)/shard_map/mul | solution.py:85
  30.2 1.9 %fusion.6 = f32[32,4,32,128]{3,2,1,0:T(8,128)S(1)} fusion(f32[32,4,32,128]{3,2,1,0:T(8,128)S(1)} %pad_maximum_fusion, f32[32,6,32,128]{3,2,1,0:T(8,128)S(1)} %broadcast_multiply_fusion, f32[32,2,32,128]{3,2,1,0:T(8,128)S(1)} %collective-permute-done.1, f32[32,2,32,128]{3,2,1,0:T(8,128)S(1)} %bitcast.114, f32[32,2,32,128]{3,2,1,0:T(8,128)S(1)} %collective-permute-done), kind=kLoop, calls=%fused_computation.14 | loop fusion | flops 5767168 | bytes 9437184 | tf_op jit(solution)/shard_map/add | solution.py:89
  32.3 0.7 fusion.25
  33.0 1.2 %convolution_bitcast_fusion = f32[4,8,64,128]{3,1,2,0:T(8,128)S(1)} fusion(f32[4,8,64,128]{3,2,1,0:T(8,128)S(1)} %bitcast.115, f32[1,32,32]{2,1,0:T(8,128)S(1)} %copy-done.2), kind=kOutput, calls=%fused_computation.19 | convolution fusion | flops 50331648 | bytes 2101248 | tf_op jit(solution)/shard_map/dot_general | solution.py:91
  36.2 2.7 %collective-permute-done.4 = f32[1,34,64]{2,1,0:T(8,128)S(1)} collective-permute-done((f32[1,34,64]{2,1,0:T(8,128)S(1)}, f32[1,34,64]{2,1,0:T(8,128)S(1)}, u32[]{:S(2)}, u32[]{:S(2)}) %collective-permute-start.4) | collective-permute-done | bytes 8736 | tf_op jit(solution)/shard_map/ppermute | solution.py:108
  39.4 0.7 collective-permute-start.15
  41.4 0.7 collective-permute-start.11
  42.1 2.5 %collective-permute-done.14 = f32[2,34,64]{2,1,0:T(8,128)S(1)} collective-permute-done((f32[2,34,64]{2,1,0:T(8,128)S(1)}, f32[2,34,64]{2,1,0:T(8,128)S(1)}, u32[]{:S(2)}, u32[]{:S(2)}) %collective-permute-start.14) | collective-permute-done | bytes 17440 | tf_op jit(solution)/shard_map/ppermute | solution.py:108
  47.8 0.7 collective-permute-start.12
  48.4 2.9 %collective-permute-done.19 = f32[2,9,128]{2,1,0:T(8,128)S(1)} collective-permute-done((f32[2,9,128]{2,1,0:T(8,128)S(1)}, f32[2,9,128]{2,1,0:T(8,128)S(1)}, u32[]{:S(2)}, u32[]{:S(2)}) %collective-permute-start.19) | collective-permute-done | bytes 9248 | tf_op jit(solution)/shard_map/ppermute | solution.py:44
  51.5 0.7 collective-permute-start.16
  52.2 3.1 %collective-permute-done.20 = f32[4,9,128]{2,1,0:T(8,128)S(1)} collective-permute-done((f32[4,9,128]{2,1,0:T(8,128)S(1)}, f32[4,9,128]{2,1,0:T(8,128)S(1)}, u32[]{:S(2)}, u32[]{:S(2)}) %collective-permute-start.20) | collective-permute-done | bytes 18464 | tf_op jit(solution)/shard_map/ppermute | solution.py:44
  55.4 0.8 fusion.30
  56.3 1.3 %collective-permute-start.7 = (f32[6,2,32,128]{3,2,1,0:T(8,128)S(1)}, f32[6,2,32,128]{3,2,1,0:T(8,128)S(1)}, u32[]{:S(2)}, u32[]{:S(2)}) collective-permute-start(f32[6,2,32,128]{3,2,1,0:T(8,128)S(1)} %multiply_add_fusion.10), channel_id=1, source_target_pairs={{16,24},{17,25},{18,26},{19,27},{20,28},{21,29},{22,30},{23,31}} | collective-permute-start | bytes 589832 | tf_op jit(solution)/shard_map/ppermute | solution.py:145
  57.7 1.3 %collective-permute-start.10 = (f32[7,2,32,128]{3,2,1,0:T(8,128)S(1)}, f32[7,2,32,128]{3,2,1,0:T(8,128)S(1)}, u32[]{:S(2)}, u32[]{:S(2)}) collective-permute-start(f32[7,2,32,128]{3,2,1,0:T(8,128)S(1)} %multiply_add_fusion.7), channel_id=1, source_target_pairs={{16,24},{17,25},{18,26},{19,27},{20,28},{21,29},{22,30},{23,31}} | collective-permute-start | bytes 688136 | tf_op jit(solution)/shard_map/ppermute | solution.py:145
  59.1 1.3 %collective-permute-start.13 = (f32[9,2,32,128]{3,2,1,0:T(8,128)S(1)}, f32[9,2,32,128]{3,2,1,0:T(8,128)S(1)}, u32[]{:S(2)}, u32[]{:S(2)}) collective-permute-start(f32[9,2,32,128]{3,2,1,0:T(8,128)S(1)} %multiply_add_fusion.4), channel_id=1, source_target_pairs={{16,24},{17,25},{18,26},{19,27},{20,28},{21,29},{22,30},{23,31}} | collective-permute-start | bytes 884744 | tf_op jit(solution)/shard_map/ppermute | solution.py:145
  60.4 8.9 %collective-permute-done.7 = f32[6,2,32,128]{3,2,1,0:T(8,128)S(1)} collective-permute-done((f32[6,2,32,128]{3,2,1,0:T(8,128)S(1)}, f32[6,2,32,128]{3,2,1,0:T(8,128)S(1)}, u32[]{:S(2)}, u32[]{:S(2)}) %collective-permute-start.7) | collective-permute-done | bytes 196640 | tf_op jit(solution)/shard_map/ppermute | solution.py:145
  69.6 1.3 %collective-permute-start.17 = (f32[10,2,32,128]{3,2,1,0:T(8,128)S(1)}, f32[10,2,32,128]{3,2,1,0:T(8,128)S(1)}, u32[]{:S(2)}, u32[]{:S(2)}) collective-permute-start(f32[10,2,32,128]{3,2,1,0:T(8,128)S(1)} %multiply_add_fusion.1), channel_id=1, source_target_pairs={{16,24},{17,25},{18,26},{19,27},{20,28},{21,29},{22,30},{23,31}} | collective-permute-start | bytes 983048 | tf_op jit(solution)/shard_map/ppermute | solution.py:145
  70.9 4.5 %collective-permute-done.10 = f32[7,2,32,128]{3,2,1,0:T(8,128)S(1)} collective-permute-done((f32[7,2,32,128]{3,2,1,0:T(8,128)S(1)}, f32[7,2,32,128]{3,2,1,0:T(8,128)S(1)}, u32[]{:S(2)}, u32[]{:S(2)}) %collective-permute-start.10) | collective-permute-done | bytes 229408 | tf_op jit(solution)/shard_map/ppermute | solution.py:145
  75.4 9.7 %collective-permute-done.13 = f32[9,2,32,128]{3,2,1,0:T(8,128)S(1)} collective-permute-done((f32[9,2,32,128]{3,2,1,0:T(8,128)S(1)}, f32[9,2,32,128]{3,2,1,0:T(8,128)S(1)}, u32[]{:S(2)}, u32[]{:S(2)}) %collective-permute-start.13) | collective-permute-done | bytes 294944 | tf_op jit(solution)/shard_map/ppermute | solution.py:145
  85.2 7.6 %collective-permute-done.17 = f32[10,2,32,128]{3,2,1,0:T(8,128)S(1)} collective-permute-done((f32[10,2,32,128]{3,2,1,0:T(8,128)S(1)}, f32[10,2,32,128]{3,2,1,0:T(8,128)S(1)}, u32[]{:S(2)}, u32[]{:S(2)}) %collective-permute-start.17) | collective-permute-done | bytes 327712 | tf_op jit(solution)/shard_map/ppermute | solution.py:145
  92.9 1.1 %maximum_bitcast_fusion = f32[1,32,2,32,128]{4,3,2,1,0:T(8,128)} fusion(f32[10,2,32,128]{3,2,1,0:T(8,128)S(1)} %multiply_add_fusion, f32[9,2,32,128]{3,2,1,0:T(8,128)S(1)} %multiply_add_fusion.3, f32[7,2,32,128]{3,2,1,0:T(8,128)S(1)} %multiply_add_fusion.6, f32[6,2,32,128]{3,2,1,0:T(8,128)S(1)} %multiply_add_fusion.9), kind=kLoop, calls=%fused_computation.46 | loop fusion | flops 786432 | bytes 2097152 | tf_op jit(solution)/shard_map/broadcast_in_dim | solution.py:162
  (73 shorter events, 10.6 us)
Async XLA Ops:
  0.6 44.8 %copy-start = (bf16[1,8,64,128]{3,2,1,0:T(8,128)(2,1)S(1)}, bf16[1,8,64,128]{3,2,1,0:T(8,128)(2,1)}, u32[]{:S(2)}) copy-start(bf16[1,8,64,128]{3,2,1,0:T(8,128)(2,1)} %param.22) | copy-start | bytes 393220
  0.6 29.4 %copy-start.1 = (f32[1,32,2,32,128]{4,3,2,1,0:T(8,128)S(1)}, f32[1,32,2,32,128]{4,3,2,1,0:T(8,128)}, u32[]{:S(2)}) copy-start(f32[1,32,2,32,128]{4,3,2,1,0:T(8,128)} %param.15) | copy-start | bytes 3145732
  0.7 29.4 %collective-permute-start = (f32[32,2,32,128]{3,2,1,0:T(8,128)}, f32[32,2,32,128]{3,2,1,0:T(8,128)S(1)}, u32[]{:S(2)}, u32[]{:S(2)}) collective-permute-start(f32[32,2,32,128]{3,2,1,0:T(8,128)} %bitcast.111), channel_id=1, source_target_pairs={{0,1},{1,2},{2,3},{3,4},{4,5},{5,6},{6,7},{8,9},{9,10},{10,11},{11... | collective-permute-start | bytes 3145736 | tf_op jit(solution)/shard_map/ppermute | solution.py:80
  2.7 27.3 %collective-permute-start.1 = (f32[32,2,32,128]{3,2,1,0:T(8,128)}, f32[32,2,32,128]{3,2,1,0:T(8,128)S(1)}, u32[]{:S(2)}, u32[]{:S(2)}) collective-permute-start(f32[32,2,32,128]{3,2,1,0:T(8,128)} %bitcast.112), channel_id=1, source_target_pairs={{1,0},{2,1},{3,2},{4,3},{5,4},{6,5},{7,6},{9,8},{10,9},{11,10},{12... | collective-permute-start | bytes 3145736 | tf_op jit(solution)/shard_map/ppermute | solution.py:81
  6.4 11.1 %collective-permute-start.2 = (f32[2,32,128]{2,1,0:T(8,128)}, f32[2,32,128]{2,1,0:T(8,128)S(1)}, u32[]{:S(2)}, u32[]{:S(2)}) collective-permute-start(f32[2,32,128]{2,1,0:T(8,128)} %param.16), channel_id=1, source_target_pairs={{0,1},{1,2},{2,3},{3,4},{4,5},{5,6},{6,7},{8,9},{9,10},{10,11},{11... | collective-permute-start | bytes 98312 | tf_op jit(solution)/shard_map/ppermute | solution.py:82
  8.3 19.9 %collective-permute-start.3 = (f32[2,32,128]{2,1,0:T(8,128)}, f32[2,32,128]{2,1,0:T(8,128)S(1)}, u32[]{:S(2)}, u32[]{:S(2)}) collective-permute-start(f32[2,32,128]{2,1,0:T(8,128)} %param.16), channel_id=1, source_target_pairs={{1,0},{2,1},{3,2},{4,3},{5,4},{6,5},{7,6},{9,8},{10,9},{11,10},{12... | collective-permute-start | bytes 98312 | tf_op jit(solution)/shard_map/ppermute | solution.py:83
  32.3 0.8 copy-start.2
  33.0 1.4 %copy-start.3 = (f32[1,32]{1,0:T(1,128)S(1)}, f32[1,32]{1,0:T(1,128)}, u32[]{:S(2)}) copy-start(f32[1,32]{1,0:T(1,128)} %param.20) | copy-start | bytes 388
  34.2 1.3 %copy-start.4 = (s32[1,8]{1,0:T(1,128)S(1)}, s32[1,8]{1,0:T(1,128)}, u32[]{:S(2)}) copy-start(s32[1,8]{1,0:T(1,128)} %param.23) | copy-start | bytes 100
  35.0 3.8 %collective-permute-start.4 = (f32[1,34,64]{2,1,0:T(8,128)S(1)}, f32[1,34,64]{2,1,0:T(8,128)S(1)}, u32[]{:S(2)}, u32[]{:S(2)}) collective-permute-start(f32[1,34,64]{2,1,0:T(8,128)S(1)} %maximum_bitcast_fusion.1), channel_id=1, source_target_pairs={{0,8},{8,0},{16,24},{24,16},{1,9},{9,1},{17,25},{25,17},{2,10},{10... | collective-permute-start | bytes 26120 | tf_op jit(solution)/shard_map/ppermute | solution.py:108
  38.9 5.7 %collective-permute-start.14 = (f32[2,34,64]{2,1,0:T(8,128)S(1)}, f32[2,34,64]{2,1,0:T(8,128)S(1)}, u32[]{:S(2)}, u32[]{:S(2)}) collective-permute-start(f32[2,34,64]{2,1,0:T(8,128)S(1)} %maximum_select_fusion.2), channel_id=1, source_target_pairs={{0,16},{8,24},{16,0},{24,8},{1,17},{9,25},{17,1},{25,9},{2,18},{10... | collective-permute-start | bytes 52232 | tf_op jit(solution)/shard_map/ppermute | solution.py:108
  39.4 7.0 %collective-permute-start.15 = (f32[10,2,32,128]{3,2,1,0:T(8,128)S(1)}, f32[10,2,32,128]{3,2,1,0:T(8,128)S(1)}, u32[]{:S(2)}, u32[]{:S(2)}) collective-permute-start(f32[10,2,32,128]{3,2,1,0:T(8,128)S(1)} %slice.184), channel_id=1, source_target_pairs={{0,8},{1,9},{2,10},{3,11},{4,12},{5,13},{6,14},{7,15}} | collective-permute-start | bytes 983048 | tf_op jit(solution)/shard_map/ppermute | solution.py:145
  40.1 5.5 %collective-permute-start.5 = (f32[6,2,32,128]{3,2,1,0:T(8,128)S(1)}, f32[6,2,32,128]{3,2,1,0:T(8,128)S(1)}, u32[]{:S(2)}, u32[]{:S(2)}) collective-permute-start(f32[6,2,32,128]{3,2,1,0:T(8,128)S(1)} %slice.178), channel_id=1, source_target_pairs={{0,8},{1,9},{2,10},{3,11},{4,12},{5,13},{6,14},{7,15}} | collective-permute-start | bytes 589832 | tf_op jit(solution)/shard_map/ppermute | solution.py:145
  40.8 5.8 %collective-permute-start.8 = (f32[7,2,32,128]{3,2,1,0:T(8,128)S(1)}, f32[7,2,32,128]{3,2,1,0:T(8,128)S(1)}, u32[]{:S(2)}, u32[]{:S(2)}) collective-permute-start(f32[7,2,32,128]{3,2,1,0:T(8,128)S(1)} %slice.180), channel_id=1, source_target_pairs={{0,8},{1,9},{2,10},{3,11},{4,12},{5,13},{6,14},{7,15}} | collective-permute-start | bytes 688136 | tf_op jit(solution)/shard_map/ppermute | solution.py:145
  41.4 6.2 %collective-permute-start.11 = (f32[9,2,32,128]{3,2,1,0:T(8,128)S(1)}, f32[9,2,32,128]{3,2,1,0:T(8,128)S(1)}, u32[]{:S(2)}, u32[]{:S(2)}) collective-permute-start(f32[9,2,32,128]{3,2,1,0:T(8,128)S(1)} %slice.182), channel_id=1, source_target_pairs={{0,8},{1,9},{2,10},{3,11},{4,12},{5,13},{6,14},{7,15}} | collective-permute-start | bytes 884744 | tf_op jit(solution)/shard_map/ppermute | solution.py:145
  45.7 10.5 %collective-permute-start.6 = (f32[6,2,32,128]{3,2,1,0:T(8,128)S(1)}, f32[6,2,32,128]{3,2,1,0:T(8,128)S(1)}, u32[]{:S(2)}, u32[]{:S(2)}) collective-permute-start(f32[6,2,32,128]{3,2,1,0:T(8,128)S(1)} %multiply_add_fusion.11), channel_id=1, source_target_pairs={{8,16},{9,17},{10,18},{11,19},{12,20},{13,21},{14,22},{15,23}} | collective-permute-start | bytes 589832 | tf_op jit(solution)/shard_map/ppermute | solution.py:145
  46.4 1.2 %collective-permute-start.18 = (f32[1,9,128]{2,1,0:T(8,128)S(1)}, f32[1,9,128]{2,1,0:T(8,128)S(1)}, u32[]{:S(2)}, u32[]{:S(2)}) collective-permute-start(f32[1,9,128]{2,1,0:T(8,128)S(1)} %bitcast.117), channel_id=1, source_target_pairs={{0,1},{1,0},{2,3},{3,2},{4,5},{5,4},{6,7},{7,6},{8,9},{9,8},{10,11... | collective-permute-start | bytes 13832 | tf_op jit(solution)/shard_map/ppermute | solution.py:44
  46.6 11.0 %collective-permute-start.9 = (f32[7,2,32,128]{3,2,1,0:T(8,128)S(1)}, f32[7,2,32,128]{3,2,1,0:T(8,128)S(1)}, u32[]{:S(2)}, u32[]{:S(2)}) collective-permute-start(f32[7,2,32,128]{3,2,1,0:T(8,128)S(1)} %multiply_add_fusion.8), channel_id=1, source_target_pairs={{8,16},{9,17},{10,18},{11,19},{12,20},{13,21},{14,22},{15,23}} | collective-permute-start | bytes 688136 | tf_op jit(solution)/shard_map/ppermute | solution.py:145
  47.6 3.7 %collective-permute-start.19 = (f32[2,9,128]{2,1,0:T(8,128)S(1)}, f32[2,9,128]{2,1,0:T(8,128)S(1)}, u32[]{:S(2)}, u32[]{:S(2)}) collective-permute-start(f32[2,9,128]{2,1,0:T(8,128)S(1)} %maximum_select_fusion.4), channel_id=1, source_target_pairs={{0,2},{1,3},{2,0},{3,1},{4,6},{5,7},{6,4},{7,5},{8,10},{9,11},{10,... | collective-permute-start | bytes 27656 | tf_op jit(solution)/shard_map/ppermute | solution.py:44
  47.8 11.3 %collective-permute-start.12 = (f32[9,2,32,128]{3,2,1,0:T(8,128)S(1)}, f32[9,2,32,128]{3,2,1,0:T(8,128)S(1)}, u32[]{:S(2)}, u32[]{:S(2)}) collective-permute-start(f32[9,2,32,128]{3,2,1,0:T(8,128)S(1)} %multiply_add_fusion.5), channel_id=1, source_target_pairs={{8,16},{9,17},{10,18},{11,19},{12,20},{13,21},{14,22},{15,23}} | collective-permute-start | bytes 884744 | tf_op jit(solution)/shard_map/ppermute | solution.py:145
  51.4 3.9 %collective-permute-start.20 = (f32[4,9,128]{2,1,0:T(8,128)S(1)}, f32[4,9,128]{2,1,0:T(8,128)S(1)}, u32[]{:S(2)}, u32[]{:S(2)}) collective-permute-start(f32[4,9,128]{2,1,0:T(8,128)S(1)} %maximum_select_fusion.3), channel_id=1, source_target_pairs={{0,4},{1,5},{2,6},{3,7},{4,0},{5,1},{6,2},{7,3},{8,12},{9,13},{10,... | collective-permute-start | bytes 55304 | tf_op jit(solution)/shard_map/ppermute | solution.py:44
  51.5 18.0 %collective-permute-start.16 = (f32[10,2,32,128]{3,2,1,0:T(8,128)S(1)}, f32[10,2,32,128]{3,2,1,0:T(8,128)S(1)}, u32[]{:S(2)}, u32[]{:S(2)}) collective-permute-start(f32[10,2,32,128]{3,2,1,0:T(8,128)S(1)} %multiply_add_fusion.2), channel_id=1, source_target_pairs={{8,16},{9,17},{10,18},{11,19},{12,20},{13,21},{14,22},{15,23}} | collective-permute-start | bytes 983048 | tf_op jit(solution)/shard_map/ppermute | solution.py:145
  56.3 13.1 %collective-permute-start.7 = (f32[6,2,32,128]{3,2,1,0:T(8,128)S(1)}, f32[6,2,32,128]{3,2,1,0:T(8,128)S(1)}, u32[]{:S(2)}, u32[]{:S(2)}) collective-permute-start(f32[6,2,32,128]{3,2,1,0:T(8,128)S(1)} %multiply_add_fusion.10), channel_id=1, source_target_pairs={{16,24},{17,25},{18,26},{19,27},{20,28},{21,29},{22,30},{23,31}} | collective-permute-start | bytes 589832 | tf_op jit(solution)/shard_map/ppermute | solution.py:145
  57.7 17.6 %collective-permute-start.10 = (f32[7,2,32,128]{3,2,1,0:T(8,128)S(1)}, f32[7,2,32,128]{3,2,1,0:T(8,128)S(1)}, u32[]{:S(2)}, u32[]{:S(2)}) collective-permute-start(f32[7,2,32,128]{3,2,1,0:T(8,128)S(1)} %multiply_add_fusion.7), channel_id=1, source_target_pairs={{16,24},{17,25},{18,26},{19,27},{20,28},{21,29},{22,30},{23,31}} | collective-permute-start | bytes 688136 | tf_op jit(solution)/shard_map/ppermute | solution.py:145
  59.1 26.0 %collective-permute-start.13 = (f32[9,2,32,128]{3,2,1,0:T(8,128)S(1)}, f32[9,2,32,128]{3,2,1,0:T(8,128)S(1)}, u32[]{:S(2)}, u32[]{:S(2)}) collective-permute-start(f32[9,2,32,128]{3,2,1,0:T(8,128)S(1)} %multiply_add_fusion.4), channel_id=1, source_target_pairs={{16,24},{17,25},{18,26},{19,27},{20,28},{21,29},{22,30},{23,31}} | collective-permute-start | bytes 884744 | tf_op jit(solution)/shard_map/ppermute | solution.py:145
  69.6 23.2 %collective-permute-start.17 = (f32[10,2,32,128]{3,2,1,0:T(8,128)S(1)}, f32[10,2,32,128]{3,2,1,0:T(8,128)S(1)}, u32[]{:S(2)}, u32[]{:S(2)}) collective-permute-start(f32[10,2,32,128]{3,2,1,0:T(8,128)S(1)} %multiply_add_fusion.1), channel_id=1, source_target_pairs={{16,24},{17,25},{18,26},{19,27},{20,28},{21,29},{22,30},{23,31}} | collective-permute-start | bytes 983048 | tf_op jit(solution)/shard_map/ppermute | solution.py:145

commit v25 on v24

--- a/solution.py
+++ b/solution.py
@@ -133,7 +133,7 @@
     payload = jnp.concatenate([contribution, ids], axis=0)
     base = bins // CHUNKS
     bounds = [0]
-    for step in (-2, -1, 1, 2):
+    for step in (-3, 0, 1, 2):
         bounds.append(bounds[-1] + base + step)
     bounds[-1] = bins
     pieces = [own_part[bounds[c]:bounds[c + 1]] for c in range(CHUNKS)]

time: 94.5 us -> 94.5 us (level)
  no operation moved by 1% of the time
where the time goes in v25:
time: 94.5 us; the launch traced here: 94 us
  waiting for transfers between devices  53.5 us (57%)
  starting transfers between devices  22.9 us (24%)
  other arithmetic  8.83 us (9%)
  local copies, waits for them, and re-layouts  4.82 us (5%)
  matrix products  2.84 us (3%)
  between operations  1.12 us (1%)
    ppermute x12, waiting for transfers between devices, body(): arrived = lax.ppermute(pieces[c], 'species', [(s, s + 1)])  31.3 us
    ppermute x1, waiting for transfers between devices, body(): factor_right = lax.ppermute(space_factor[:halo], 'space', left_pairs)  10.7 us
    ppermute x12, starting transfers between devices, body(): arrived = lax.ppermute(pieces[c], 'species', [(s, s + 1)])  10.6 us
    ppermute x3, waiting for transfers between devices, gather_all(): other = lax.ppermute(held, axis, [(i, i ^ span) for i in range(count)])  5.75 us
    ppermute x2, waiting for transfers between devices, body(): lax.ppermute(everyone, 'species', [(i, i ^ span) for i in range(groups)])  5.13 us
    ppermute x1, starting transfers between devices, body(): factor_right = lax.ppermute(space_factor[:halo], 'space', left_pairs)  3.64 us
    ppermute x1, starting transfers between devices, body(): from_right = lax.ppermute(field[:, :halo], 'space', left_pairs)  3.64 us
    mul x4, local copies, waits for them, and re-layouts, body(): pieces[c] = pieces[c] + scales[c] * arrived  2.84 us
  transfers between devices with their start and end apart: 21, of which 11 were waited for; matrix products, arithmetic and copies ran while one was open for 11% of the time, Pallas kernels for 0%

profile of v25, /device:TPU:26, one launch (start us, length us, event | category | flops | bytes accessed | tf_op | source)
XLA Modules:
  0.0 94.0 jit_solution(16884318378269042110)
XLA Ops:
  0.7 2.1 %collective-permute-start = (f32[32,2,32,128]{3,2,1,0:T(8,128)}, f32[32,2,32,128]{3,2,1,0:T(8,128)S(1)}, u32[]{:S(2)}, u32[]{:S(2)}) collective-permute-start(f32[32,2,32,128]{3,2,1,0:T(8,128)} %bitcast.111), channel_id=1, source_target_pairs={{0,1},{1,2},{2,3},{3,4},{4,5},{5,6},{6,7},{8,9},{9,10},{10,11},{11... | collective-permute-start | bytes 3145736 | tf_op jit(solution)/shard_map/ppermute | solution.py:80
  2.7 3.6 %collective-permute-start.1 = (f32[32,2,32,128]{3,2,1,0:T(8,128)}, f32[32,2,32,128]{3,2,1,0:T(8,128)S(1)}, u32[]{:S(2)}, u32[]{:S(2)}) collective-permute-start(f32[32,2,32,128]{3,2,1,0:T(8,128)} %bitcast.112), channel_id=1, source_target_pairs={{1,0},{2,1},{3,2},{4,3},{5,4},{6,5},{7,6},{9,8},{10,9},{11,10},{12... | collective-permute-start | bytes 3145736 | tf_op jit(solution)/shard_map/ppermute | solution.py:81
  6.4 1.9 %collective-permute-start.2 = (f32[2,32,128]{2,1,0:T(8,128)}, f32[2,32,128]{2,1,0:T(8,128)S(1)}, u32[]{:S(2)}, u32[]{:S(2)}) collective-permute-start(f32[2,32,128]{2,1,0:T(8,128)} %param.16), channel_id=1, source_target_pairs={{0,1},{1,2},{2,3},{3,4},{4,5},{5,6},{6,7},{8,9},{9,10},{10,11},{11... | collective-permute-start | bytes 98312 | tf_op jit(solution)/shard_map/ppermute | solution.py:82
  8.3 3.6 %collective-permute-start.3 = (f32[2,32,128]{2,1,0:T(8,128)}, f32[2,32,128]{2,1,0:T(8,128)S(1)}, u32[]{:S(2)}, u32[]{:S(2)}) collective-permute-start(f32[2,32,128]{2,1,0:T(8,128)} %param.16), channel_id=1, source_target_pairs={{1,0},{2,1},{3,2},{4,3},{5,4},{6,5},{7,6},{9,8},{10,9},{11,10},{12... | collective-permute-start | bytes 98312 | tf_op jit(solution)/shard_map/ppermute | solution.py:83
  12.6 0.7 slice_bitcast_fusion.15
  13.3 0.7 slice_bitcast_fusion.14
  14.1 0.7 slice_bitcast_fusion.13
  15.4 0.8 scatter.11
  17.5 10.7 %collective-permute-done.3 = f32[2,32,128]{2,1,0:T(8,128)S(1)} collective-permute-done((f32[2,32,128]{2,1,0:T(8,128)}, f32[2,32,128]{2,1,0:T(8,128)S(1)}, u32[]{:S(2)}, u32[]{:S(2)}) %collective-permute-start.3) | collective-permute-done | bytes 32800 | tf_op jit(solution)/shard_map/ppermute | solution.py:83
  28.2 0.8 pad_maximum_fusion.2
  28.9 1.1 %broadcast_multiply_fusion = f32[32,6,32,128]{3,2,1,0:T(8,128)S(1)} fusion(f32[6,32,128]{2,1,0:T(8,128)S(1)} %pad_maximum_fusion.2, f32[32]{0:T(128)} %bitcast.121), kind=kLoop, calls=%fused_computation.18 | loop fusion | flops 786432 | bytes 3244160 | tf_op jit(solution)/shard_map/mul | solution.py:85
  30.2 1.9 %fusion.6 = f32[32,4,32,128]{3,2,1,0:T(8,128)S(1)} fusion(f32[32,4,32,128]{3,2,1,0:T(8,128)S(1)} %pad_maximum_fusion, f32[32,6,32,128]{3,2,1,0:T(8,128)S(1)} %broadcast_multiply_fusion, f32[32,2,32,128]{3,2,1,0:T(8,128)S(1)} %collective-permute-done.1, f32[32,2,32,128]{3,2,1,0:T(8,128)S(1)} %bitcast.114, f32[32,2,32,128]{3,2,1,0:T(8,128)S(1)} %collective-permute-done), kind=kLoop, calls=%fused_computation.14 | loop fusion | flops 5767168 | bytes 9437184 | tf_op jit(solution)/shard_map/add | solution.py:89
  32.3 0.7 fusion.25
  33.0 1.2 %convolution_bitcast_fusion = f32[4,8,64,128]{3,1,2,0:T(8,128)S(1)} fusion(f32[4,8,64,128]{3,2,1,0:T(8,128)S(1)} %bitcast.115, f32[1,32,32]{2,1,0:T(8,128)S(1)} %copy-done.2), kind=kOutput, calls=%fused_computation.19 | convolution fusion | flops 50331648 | bytes 2101248 | tf_op jit(solution)/shard_map/dot_general | solution.py:91
  36.2 2.7 %collective-permute-done.4 = f32[1,34,64]{2,1,0:T(8,128)S(1)} collective-permute-done((f32[1,34,64]{2,1,0:T(8,128)S(1)}, f32[1,34,64]{2,1,0:T(8,128)S(1)}, u32[]{:S(2)}, u32[]{:S(2)}) %collective-permute-start.4) | collective-permute-done | bytes 8736 | tf_op jit(solution)/shard_map/ppermute | solution.py:108
  39.4 0.7 collective-permute-start.15
  41.4 0.7 collective-permute-start.11
  42.1 2.5 %collective-permute-done.14 = f32[2,34,64]{2,1,0:T(8,128)S(1)} collective-permute-done((f32[2,34,64]{2,1,0:T(8,128)S(1)}, f32[2,34,64]{2,1,0:T(8,128)S(1)}, u32[]{:S(2)}, u32[]{:S(2)}) %collective-permute-start.14) | collective-permute-done | bytes 17440 | tf_op jit(solution)/shard_map/ppermute | solution.py:108
  47.4 0.7 collective-permute-start.12
  48.5 1.3 %collective-permute-start.7 = (f32[5,2,32,128]{3,2,1,0:T(8,128)S(1)}, f32[5,2,32,128]{3,2,1,0:T(8,128)S(1)}, u32[]{:S(2)}, u32[]{:S(2)}) collective-permute-start(f32[5,2,32,128]{3,2,1,0:T(8,128)S(1)} %multiply_add_fusion.10), channel_id=1, source_target_pairs={{16,24},{17,25},{18,26},{19,27},{20,28},{21,29},{22,30},{23,31}} | collective-permute-start | bytes 491528 | tf_op jit(solution)/shard_map/ppermute | solution.py:145
  49.8 2.3 %collective-permute-done.19 = f32[2,9,128]{2,1,0:T(8,128)S(1)} collective-permute-done((f32[2,9,128]{2,1,0:T(8,128)S(1)}, f32[2,9,128]{2,1,0:T(8,128)S(1)}, u32[]{:S(2)}, u32[]{:S(2)}) %collective-permute-start.19) | collective-permute-done | bytes 9248 | tf_op jit(solution)/shard_map/ppermute | solution.py:44
  52.3 0.7 collective-permute-start.16
  53.0 3.1 %collective-permute-done.20 = f32[4,9,128]{2,1,0:T(8,128)S(1)} collective-permute-done((f32[4,9,128]{2,1,0:T(8,128)S(1)}, f32[4,9,128]{2,1,0:T(8,128)S(1)}, u32[]{:S(2)}, u32[]{:S(2)}) %collective-permute-start.20) | collective-permute-done | bytes 18464 | tf_op jit(solution)/shard_map/ppermute | solution.py:44
  56.2 0.8 fusion.30
  57.0 10.8 %collective-permute-done.7 = f32[5,2,32,128]{3,2,1,0:T(8,128)S(1)} collective-permute-done((f32[5,2,32,128]{3,2,1,0:T(8,128)S(1)}, f32[5,2,32,128]{3,2,1,0:T(8,128)S(1)}, u32[]{:S(2)}, u32[]{:S(2)}) %collective-permute-start.7) | collective-permute-done | bytes 163872 | tf_op jit(solution)/shard_map/ppermute | solution.py:145
  68.0 1.3 %collective-permute-start.10 = (f32[8,2,32,128]{3,2,1,0:T(8,128)S(1)}, f32[8,2,32,128]{3,2,1,0:T(8,128)S(1)}, u32[]{:S(2)}, u32[]{:S(2)}) collective-permute-start(f32[8,2,32,128]{3,2,1,0:T(8,128)S(1)} %multiply_add_fusion.7), channel_id=1, source_target_pairs={{16,24},{17,25},{18,26},{19,27},{20,28},{21,29},{22,30},{23,31}} | collective-permute-start | bytes 786440 | tf_op jit(solution)/shard_map/ppermute | solution.py:145
  69.4 1.3 %collective-permute-start.13 = (f32[9,2,32,128]{3,2,1,0:T(8,128)S(1)}, f32[9,2,32,128]{3,2,1,0:T(8,128)S(1)}, u32[]{:S(2)}, u32[]{:S(2)}) collective-permute-start(f32[9,2,32,128]{3,2,1,0:T(8,128)S(1)} %multiply_add_fusion.4), channel_id=1, source_target_pairs={{16,24},{17,25},{18,26},{19,27},{20,28},{21,29},{22,30},{23,31}} | collective-permute-start | bytes 884744 | tf_op jit(solution)/shard_map/ppermute | solution.py:145
  70.8 1.3 %collective-permute-start.17 = (f32[10,2,32,128]{3,2,1,0:T(8,128)S(1)}, f32[10,2,32,128]{3,2,1,0:T(8,128)S(1)}, u32[]{:S(2)}, u32[]{:S(2)}) collective-permute-start(f32[10,2,32,128]{3,2,1,0:T(8,128)S(1)} %multiply_add_fusion.1), channel_id=1, source_target_pairs={{16,24},{17,25},{18,26},{19,27},{20,28},{21,29},{22,30},{23,31}} | collective-permute-start | bytes 983048 | tf_op jit(solution)/shard_map/ppermute | solution.py:145
  72.1 4.5 %collective-permute-done.10 = f32[8,2,32,128]{3,2,1,0:T(8,128)S(1)} collective-permute-done((f32[8,2,32,128]{3,2,1,0:T(8,128)S(1)}, f32[8,2,32,128]{3,2,1,0:T(8,128)S(1)}, u32[]{:S(2)}, u32[]{:S(2)}) %collective-permute-start.10) | collective-permute-done | bytes 262176 | tf_op jit(solution)/shard_map/ppermute | solution.py:145
  76.7 8.4 %collective-permute-done.13 = f32[9,2,32,128]{3,2,1,0:T(8,128)S(1)} collective-permute-done((f32[9,2,32,128]{3,2,1,0:T(8,128)S(1)}, f32[9,2,32,128]{3,2,1,0:T(8,128)S(1)}, u32[]{:S(2)}, u32[]{:S(2)}) %collective-permute-start.13) | collective-permute-done | bytes 294944 | tf_op jit(solution)/shard_map/ppermute | solution.py:145
  85.2 7.6 %collective-permute-done.17 = f32[10,2,32,128]{3,2,1,0:T(8,128)S(1)} collective-permute-done((f32[10,2,32,128]{3,2,1,0:T(8,128)S(1)}, f32[10,2,32,128]{3,2,1,0:T(8,128)S(1)}, u32[]{:S(2)}, u32[]{:S(2)}) %collective-permute-start.17) | collective-permute-done | bytes 327712 | tf_op jit(solution)/shard_map/ppermute | solution.py:145
  92.9 1.1 %maximum_bitcast_fusion = f32[1,32,2,32,128]{4,3,2,1,0:T(8,128)} fusion(f32[10,2,32,128]{3,2,1,0:T(8,128)S(1)} %multiply_add_fusion, f32[9,2,32,128]{3,2,1,0:T(8,128)S(1)} %multiply_add_fusion.3, f32[8,2,32,128]{3,2,1,0:T(8,128)S(1)} %multiply_add_fusion.6, f32[5,2,32,128]{3,2,1,0:T(8,128)S(1)} %multiply_add_fusion.9), kind=kLoop, calls=%fused_computation.46 | loop fusion | flops 786432 | bytes 2097152 | tf_op jit(solution)/shard_map/broadcast_in_dim | solution.py:162
  (73 shorter events, 10.6 us)
Async XLA Ops:
  0.6 44.8 %copy-start = (bf16[1,8,64,128]{3,2,1,0:T(8,128)(2,1)S(1)}, bf16[1,8,64,128]{3,2,1,0:T(8,128)(2,1)}, u32[]{:S(2)}) copy-start(bf16[1,8,64,128]{3,2,1,0:T(8,128)(2,1)} %param.22) | copy-start | bytes 393220
  0.6 29.4 %copy-start.1 = (f32[1,32,2,32,128]{4,3,2,1,0:T(8,128)S(1)}, f32[1,32,2,32,128]{4,3,2,1,0:T(8,128)}, u32[]{:S(2)}) copy-start(f32[1,32,2,32,128]{4,3,2,1,0:T(8,128)} %param.15) | copy-start | bytes 3145732
  0.7 29.4 %collective-permute-start = (f32[32,2,32,128]{3,2,1,0:T(8,128)}, f32[32,2,32,128]{3,2,1,0:T(8,128)S(1)}, u32[]{:S(2)}, u32[]{:S(2)}) collective-permute-start(f32[32,2,32,128]{3,2,1,0:T(8,128)} %bitcast.111), channel_id=1, source_target_pairs={{0,1},{1,2},{2,3},{3,4},{4,5},{5,6},{6,7},{8,9},{9,10},{10,11},{11... | collective-permute-start | bytes 3145736 | tf_op jit(solution)/shard_map/ppermute | solution.py:80
  2.7 27.3 %collective-permute-start.1 = (f32[32,2,32,128]{3,2,1,0:T(8,128)}, f32[32,2,32,128]{3,2,1,0:T(8,128)S(1)}, u32[]{:S(2)}, u32[]{:S(2)}) collective-permute-start(f32[32,2,32,128]{3,2,1,0:T(8,128)} %bitcast.112), channel_id=1, source_target_pairs={{1,0},{2,1},{3,2},{4,3},{5,4},{6,5},{7,6},{9,8},{10,9},{11,10},{12... | collective-permute-start | bytes 3145736 | tf_op jit(solution)/shard_map/ppermute | solution.py:81
  6.4 11.1 %collective-permute-start.2 = (f32[2,32,128]{2,1,0:T(8,128)}, f32[2,32,128]{2,1,0:T(8,128)S(1)}, u32[]{:S(2)}, u32[]{:S(2)}) collective-permute-start(f32[2,32,128]{2,1,0:T(8,128)} %param.16), channel_id=1, source_target_pairs={{0,1},{1,2},{2,3},{3,4},{4,5},{5,6},{6,7},{8,9},{9,10},{10,11},{11... | collective-permute-start | bytes 98312 | tf_op jit(solution)/shard_map/ppermute | solution.py:82
  8.3 19.9 %collective-permute-start.3 = (f32[2,32,128]{2,1,0:T(8,128)}, f32[2,32,128]{2,1,0:T(8,128)S(1)}, u32[]{:S(2)}, u32[]{:S(2)}) collective-permute-start(f32[2,32,128]{2,1,0:T(8,128)} %param.16), channel_id=1, source_target_pairs={{1,0},{2,1},{3,2},{4,3},{5,4},{6,5},{7,6},{9,8},{10,9},{11,10},{12... | collective-permute-start | bytes 98312 | tf_op jit(solution)/shard_map/ppermute | solution.py:83
  32.3 0.8 copy-start.2
  33.0 1.4 %copy-start.3 = (f32[1,32]{1,0:T(1,128)S(1)}, f32[1,32]{1,0:T(1,128)}, u32[]{:S(2)}) copy-start(f32[1,32]{1,0:T(1,128)} %param.20) | copy-start | bytes 388
  34.2 1.3 %copy-start.4 = (s32[1,8]{1,0:T(1,128)S(1)}, s32[1,8]{1,0:T(1,128)}, u32[]{:S(2)}) copy-start(s32[1,8]{1,0:T(1,128)} %param.23) | copy-start | bytes 100
  35.0 3.8 %collective-permute-start.4 = (f32[1,34,64]{2,1,0:T(8,128)S(1)}, f32[1,34,64]{2,1,0:T(8,128)S(1)}, u32[]{:S(2)}, u32[]{:S(2)}) collective-permute-start(f32[1,34,64]{2,1,0:T(8,128)S(1)} %maximum_bitcast_fusion.1), channel_id=1, source_target_pairs={{0,8},{8,0},{16,24},{24,16},{1,9},{9,1},{17,25},{25,17},{2,10},{10... | collective-permute-start | bytes 26120 | tf_op jit(solution)/shard_map/ppermute | solution.py:108
  38.9 5.7 %collective-permute-start.14 = (f32[2,34,64]{2,1,0:T(8,128)S(1)}, f32[2,34,64]{2,1,0:T(8,128)S(1)}, u32[]{:S(2)}, u32[]{:S(2)}) collective-permute-start(f32[2,34,64]{2,1,0:T(8,128)S(1)} %maximum_select_fusion.2), channel_id=1, source_target_pairs={{0,16},{8,24},{16,0},{24,8},{1,17},{9,25},{17,1},{25,9},{2,18},{10... | collective-permute-start | bytes 52232 | tf_op jit(solution)/shard_map/ppermute | solution.py:108
  39.4 7.8 %collective-permute-start.15 = (f32[10,2,32,128]{3,2,1,0:T(8,128)S(1)}, f32[10,2,32,128]{3,2,1,0:T(8,128)S(1)}, u32[]{:S(2)}, u32[]{:S(2)}) collective-permute-start(f32[10,2,32,128]{3,2,1,0:T(8,128)S(1)} %slice.184), channel_id=1, source_target_pairs={{0,8},{1,9},{2,10},{3,11},{4,12},{5,13},{6,14},{7,15}} | collective-permute-start | bytes 983048 | tf_op jit(solution)/shard_map/ppermute | solution.py:145
  40.1 5.5 %collective-permute-start.5 = (f32[5,2,32,128]{3,2,1,0:T(8,128)S(1)}, f32[5,2,32,128]{3,2,1,0:T(8,128)S(1)}, u32[]{:S(2)}, u32[]{:S(2)}) collective-permute-start(f32[5,2,32,128]{3,2,1,0:T(8,128)S(1)} %slice.178), channel_id=1, source_target_pairs={{0,8},{1,9},{2,10},{3,11},{4,12},{5,13},{6,14},{7,15}} | collective-permute-start | bytes 491528 | tf_op jit(solution)/shard_map/ppermute | solution.py:145
  40.8 5.6 %collective-permute-start.8 = (f32[8,2,32,128]{3,2,1,0:T(8,128)S(1)}, f32[8,2,32,128]{3,2,1,0:T(8,128)S(1)}, u32[]{:S(2)}, u32[]{:S(2)}) collective-permute-start(f32[8,2,32,128]{3,2,1,0:T(8,128)S(1)} %slice.180), channel_id=1, source_target_pairs={{0,8},{1,9},{2,10},{3,11},{4,12},{5,13},{6,14},{7,15}} | collective-permute-start | bytes 786440 | tf_op jit(solution)/shard_map/ppermute | solution.py:145
  41.4 5.9 %collective-permute-start.11 = (f32[9,2,32,128]{3,2,1,0:T(8,128)S(1)}, f32[9,2,32,128]{3,2,1,0:T(8,128)S(1)}, u32[]{:S(2)}, u32[]{:S(2)}) collective-permute-start(f32[9,2,32,128]{3,2,1,0:T(8,128)S(1)} %slice.182), channel_id=1, source_target_pairs={{0,8},{1,9},{2,10},{3,11},{4,12},{5,13},{6,14},{7,15}} | collective-permute-start | bytes 884744 | tf_op jit(solution)/shard_map/ppermute | solution.py:145
  45.7 2.7 %collective-permute-start.6 = (f32[5,2,32,128]{3,2,1,0:T(8,128)S(1)}, f32[5,2,32,128]{3,2,1,0:T(8,128)S(1)}, u32[]{:S(2)}, u32[]{:S(2)}) collective-permute-start(f32[5,2,32,128]{3,2,1,0:T(8,128)S(1)} %multiply_add_fusion.11), channel_id=1, source_target_pairs={{8,16},{9,17},{10,18},{11,19},{12,20},{13,21},{14,22},{15,23}} | collective-permute-start | bytes 491528 | tf_op jit(solution)/shard_map/ppermute | solution.py:145
  46.5 21.4 %collective-permute-start.9 = (f32[8,2,32,128]{3,2,1,0:T(8,128)S(1)}, f32[8,2,32,128]{3,2,1,0:T(8,128)S(1)}, u32[]{:S(2)}, u32[]{:S(2)}) collective-permute-start(f32[8,2,32,128]{3,2,1,0:T(8,128)S(1)} %multiply_add_fusion.8), channel_id=1, source_target_pairs={{8,16},{9,17},{10,18},{11,19},{12,20},{13,21},{14,22},{15,23}} | collective-permute-start | bytes 786440 | tf_op jit(solution)/shard_map/ppermute | solution.py:145
  47.2 1.2 %collective-permute-start.18 = (f32[1,9,128]{2,1,0:T(8,128)S(1)}, f32[1,9,128]{2,1,0:T(8,128)S(1)}, u32[]{:S(2)}, u32[]{:S(2)}) collective-permute-start(f32[1,9,128]{2,1,0:T(8,128)S(1)} %bitcast.117), channel_id=1, source_target_pairs={{0,1},{1,0},{2,3},{3,2},{4,5},{5,4},{6,7},{7,6},{8,9},{9,8},{10,11... | collective-permute-start | bytes 13832 | tf_op jit(solution)/shard_map/ppermute | solution.py:44
  47.4 21.9 %collective-permute-start.12 = (f32[9,2,32,128]{3,2,1,0:T(8,128)S(1)}, f32[9,2,32,128]{3,2,1,0:T(8,128)S(1)}, u32[]{:S(2)}, u32[]{:S(2)}) collective-permute-start(f32[9,2,32,128]{3,2,1,0:T(8,128)S(1)} %multiply_add_fusion.5), channel_id=1, source_target_pairs={{8,16},{9,17},{10,18},{11,19},{12,20},{13,21},{14,22},{15,23}} | collective-permute-start | bytes 884744 | tf_op jit(solution)/shard_map/ppermute | solution.py:145
  48.4 3.7 %collective-permute-start.19 = (f32[2,9,128]{2,1,0:T(8,128)S(1)}, f32[2,9,128]{2,1,0:T(8,128)S(1)}, u32[]{:S(2)}, u32[]{:S(2)}) collective-permute-start(f32[2,9,128]{2,1,0:T(8,128)S(1)} %maximum_select_fusion.4), channel_id=1, source_target_pairs={{0,2},{1,3},{2,0},{3,1},{4,6},{5,7},{6,4},{7,5},{8,10},{9,11},{10,... | collective-permute-start | bytes 27656 | tf_op jit(solution)/shard_map/ppermute | solution.py:44
  48.5 19.3 %collective-permute-start.7 = (f32[5,2,32,128]{3,2,1,0:T(8,128)S(1)}, f32[5,2,32,128]{3,2,1,0:T(8,128)S(1)}, u32[]{:S(2)}, u32[]{:S(2)}) collective-permute-start(f32[5,2,32,128]{3,2,1,0:T(8,128)S(1)} %multiply_add_fusion.10), channel_id=1, source_target_pairs={{16,24},{17,25},{18,26},{19,27},{20,28},{21,29},{22,30},{23,31}} | collective-permute-start | bytes 491528 | tf_op jit(solution)/shard_map/ppermute | solution.py:145
  52.2 3.9 %collective-permute-start.20 = (f32[4,9,128]{2,1,0:T(8,128)S(1)}, f32[4,9,128]{2,1,0:T(8,128)S(1)}, u32[]{:S(2)}, u32[]{:S(2)}) collective-permute-start(f32[4,9,128]{2,1,0:T(8,128)S(1)} %maximum_select_fusion.3), channel_id=1, source_target_pairs={{0,4},{1,5},{2,6},{3,7},{4,0},{5,1},{6,2},{7,3},{8,12},{9,13},{10,... | collective-permute-start | bytes 55304 | tf_op jit(solution)/shard_map/ppermute | solution.py:44
  52.3 18.4 %collective-permute-start.16 = (f32[10,2,32,128]{3,2,1,0:T(8,128)S(1)}, f32[10,2,32,128]{3,2,1,0:T(8,128)S(1)}, u32[]{:S(2)}, u32[]{:S(2)}) collective-permute-start(f32[10,2,32,128]{3,2,1,0:T(8,128)S(1)} %multiply_add_fusion.2), channel_id=1, source_target_pairs={{8,16},{9,17},{10,18},{11,19},{12,20},{13,21},{14,22},{15,23}} | collective-permute-start | bytes 983048 | tf_op jit(solution)/shard_map/ppermute | solution.py:145
  68.0 8.6 %collective-permute-start.10 = (f32[8,2,32,128]{3,2,1,0:T(8,128)S(1)}, f32[8,2,32,128]{3,2,1,0:T(8,128)S(1)}, u32[]{:S(2)}, u32[]{:S(2)}) collective-permute-start(f32[8,2,32,128]{3,2,1,0:T(8,128)S(1)} %multiply_add_fusion.7), channel_id=1, source_target_pairs={{16,24},{17,25},{18,26},{19,27},{20,28},{21,29},{22,30},{23,31}} | collective-permute-start | bytes 786440 | tf_op jit(solution)/shard_map/ppermute | solution.py:145
  69.4 15.7 %collective-permute-start.13 = (f32[9,2,32,128]{3,2,1,0:T(8,128)S(1)}, f32[9,2,32,128]{3,2,1,0:T(8,128)S(1)}, u32[]{:S(2)}, u32[]{:S(2)}) collective-permute-start(f32[9,2,32,128]{3,2,1,0:T(8,128)S(1)} %multiply_add_fusion.4), channel_id=1, source_target_pairs={{16,24},{17,25},{18,26},{19,27},{20,28},{21,29},{22,30},{23,31}} | collective-permute-start | bytes 884744 | tf_op jit(solution)/shard_map/ppermute | solution.py:145
  70.8 21.9 %collective-permute-start.17 = (f32[10,2,32,128]{3,2,1,0:T(8,128)S(1)}, f32[10,2,32,128]{3,2,1,0:T(8,128)S(1)}, u32[]{:S(2)}, u32[]{:S(2)}) collective-permute-start(f32[10,2,32,128]{3,2,1,0:T(8,128)S(1)} %multiply_add_fusion.1), channel_id=1, source_target_pairs={{16,24},{17,25},{18,26},{19,27},{20,28},{21,29},{22,30},{23,31}} | collective-permute-start | bytes 983048 | tf_op jit(solution)/shard_map/ppermute | solution.py:145
